TPU v7x, 32 devices: a whole 2x2x4 slice. The times are simulated.
32 devices in a mesh: seq: 8 (over z, y), chan: 4 (over x, core).
Axes of the slice: x: 2, y: 2, z: 4, core: 2. Of those that a mesh axis runs over, the one named last changes fastest.
Arguments:
- query_mr: bfloat16 [1024, 8192], P('seq', 'chan'), may hold values from -6 to 6
- key_mr: bfloat16 [1024, 8192], P('seq', 'chan'), may hold values from -6 to 6
- value_mr: bfloat16 [1024, 8192], P('seq', 'chan'), may hold values from -6 to 6
- query_li: bfloat16 [1024, 8192], P('seq', 'chan'), may hold values from -6 to 6
- key_li: bfloat16 [1024, 8192], P('seq', 'chan'), may hold values from -6 to 6
- cotangent: bfloat16 [1024, 8192], P('seq', 'chan'), may hold values from -40 to 40
- mr_filter: float32 [512, 128], P('chan'), may hold values from -3.535534 to 3.535534
- norm_gain: float32 [8192], P('chan'), may hold values from 0.1 to 1.9
- li_decay: float32 [512, 16], P('chan'), may hold values from 0.00048828125 to 0.03
- li_residue: float32 [512, 16], P('chan'), may hold values from -1 to 1
Outputs:
- out_li: bfloat16 [1024, 8192], P('seq', 'chan')
- grad_query_mr: bfloat16 [1024, 8192], P('seq', 'chan')
- grad_key_mr: bfloat16 [1024, 8192], P('seq', 'chan')
- grad_value_mr: bfloat16 [1024, 8192], P('seq', 'chan')
- grad_query_li: bfloat16 [1024, 8192], P('seq', 'chan')
- grad_key_li: bfloat16 [1024, 8192], P('seq', 'chan')
- grad_gain: float32 [8192], P('chan')
- grad_filter: float32 [512, 128], P('chan')
All inputs are finite; a program needn't handle non-finite values.
Results may differ from a plain program's by a relative error of at most 0.025.
Values may be sent and summed in bfloat16 or wider, within the bound.
No kernel may reach another device: no remote copies, remote signals or barrier semaphores. Data moves between devices by JAX's collectives and lax.ppermute only.
A program may use at most 192 MiB of HBM per device.

v0:
```python
import functools

import jax
import jax.numpy as jnp
from jax import lax
from jax.experimental import pallas as pl
from jax.experimental.pallas import tpu as pltpu
from jax.sharding import PartitionSpec as P

D = 8192
G = 512
LANES = 128
BLOCK_LANES = 512
HIGHEST = lax.Precision.HIGHEST


def from_behind(value, axis, steps):
    count = lax.axis_size(axis)
    initial, last = (max(0, -steps), min(count, count - steps))
    return lax.ppermute(value, axis, [(source, source + steps) for source in range(initial, last)])


def _split(value):
    high = value.astype(jnp.bfloat16)
    return high, (value - high.astype(jnp.float32)).astype(jnp.bfloat16)


def _band_kernel(*refs, group_size, split, tri, two_inputs, modal, sub):
    refs = list(refs)
    h_ref = refs.pop(0)
    top_ref = refs.pop(0)
    bot_ref = refs.pop(0) if two_inputs else None
    if modal is not None:
        dec_ref, wt_ref, ent_ref = refs.pop(0), refs.pop(0), refs.pop(0)
    out_ref = refs.pop(0)
    rows = out_ref.shape[0]
    width = h_ref.shape[1]
    groups_here = LANES // group_size
    lane_group = lax.broadcasted_iota(jnp.int32, (rows, LANES), 1) // group_size
    row_id = lax.broadcasted_iota(jnp.int32, (rows, width), 0)
    col_id = lax.broadcasted_iota(jnp.int32, (rows, width), 1)
    if modal is not None:
        modes = dec_ref.shape[1]
        offsets = lax.broadcasted_iota(jnp.int32, (rows, modes), 0).astype(jnp.float32)
        dist = offsets + 1.0 if modal == "forward" else float(rows) - offsets

    def body(j, carry):
        lanes = pl.ds(pl.multiple_of(j * LANES, LANES), LANES)
        if two_inputs:
            x = jnp.concatenate([top_ref[:, lanes], bot_ref[:, lanes]], axis=0)
        else:
            x = top_ref[:, lanes]
        bands = []
        for k in range(groups_here):
            band_row = h_ref[pl.ds(j * groups_here + k, 1), :]
            band = pltpu.roll(jnp.broadcast_to(band_row, (rows, width)), 0, 1, stride=1, stride_axis=0)
            if tri == "lower":
                band = jnp.where(col_id <= row_id, band, 0.0)
            elif tri == "upper":
                band = jnp.where(col_id >= row_id, band, 0.0)
            bands.append(band)
        stacked = jnp.concatenate(bands, axis=0)
        if split:
            high, low = _split(stacked)
            y = jnp.dot(high, x, preferred_element_type=jnp.float32)
            y = y + jnp.dot(low, x, preferred_element_type=jnp.float32)
        else:
            y = jnp.dot(stacked.astype(jnp.bfloat16), x, preferred_element_type=jnp.float32)
        if modal is not None:
            ent_high, ent_low = _split(ent_ref[:, lanes])
            out_w = []
            for k in range(groups_here):
                rate = dec_ref[pl.ds(j * groups_here + k, 1), :]
                weight = wt_ref[pl.ds(j * groups_here + k, 1), :]
                out_w.append(weight * jnp.exp(-rate * dist))
            a_high, a_low = _split(jnp.concatenate(out_w, axis=0))
            y = y + jnp.dot(a_high, ent_high, preferred_element_type=jnp.float32)
            y = y + jnp.dot(a_low, ent_high, preferred_element_type=jnp.float32)
            y = y + jnp.dot(a_high, ent_low, preferred_element_type=jnp.float32)
        acc = y[:rows]
        for k in range(1, groups_here):
            acc = jnp.where(lane_group == k, y[k * rows:(k + 1) * rows], acc)
        out_ref[:, lanes] = acc
        return carry

    lax.fori_loop(0, sub, body, 0)


def band_conv(band_rows, top, bottom=None, modal_args=None, *, group_size, split, tri, modal=None):
    rows, chans = top.shape
    block = min(BLOCK_LANES, chans)
    groups_block = block // group_size
    width = band_rows.shape[1]
    two_inputs = bottom is not None
    in_specs = [
        pl.BlockSpec((groups_block, width), lambda b: (b, 0)),
        pl.BlockSpec((rows, block), lambda b: (0, b)),
    ]
    args = [band_rows, top]
    if two_inputs:
        in_specs.append(pl.BlockSpec((rows, block), lambda b: (0, b)))
        args.append(bottom)
    if modal is not None:
        decays, weights, entering = modal_args
        modes = decays.shape[1]
        in_specs += [
            pl.BlockSpec((groups_block, modes), lambda b: (b, 0)),
            pl.BlockSpec((groups_block, modes), lambda b: (b, 0)),
            pl.BlockSpec((modes, block), lambda b: (0, b)),
        ]
        args += [decays, weights, entering]
    kernel = functools.partial(
        _band_kernel,
        group_size=group_size,
        split=split,
        tri=tri,
        two_inputs=two_inputs,
        modal=modal,
        sub=block // LANES,
    )
    return pl.pallas_call(
        kernel,
        grid=(chans // block,),
        in_specs=in_specs,
        out_specs=pl.BlockSpec((rows, block), lambda b: (0, b)),
        out_shape=jax.ShapeDtypeStruct((rows, chans), jnp.float32),
        compiler_params=pltpu.CompilerParams(dimension_semantics=("parallel",)),
    )(*args)


def _state_kernel(e_ref, x_ref, s_ref, *, group_size, sub):
    modes = s_ref.shape[0]
    groups_here = LANES // group_size
    state_group = lax.broadcasted_iota(jnp.int32, (modes, LANES), 1) // group_size

    def body(j, carry):
        lanes = pl.ds(pl.multiple_of(j * LANES, LANES), LANES)
        x = x_ref[:, lanes]
        weights = e_ref[pl.ds(j * groups_here, groups_here)]
        high, low = _split(weights.reshape(groups_here * modes, weights.shape[2]))
        y = jnp.dot(high, x, preferred_element_type=jnp.float32)
        y = y + jnp.dot(low, x, preferred_element_type=jnp.float32)
        acc = y[:modes]
        for k in range(1, groups_here):
            acc = jnp.where(state_group == k, y[k * modes:(k + 1) * modes], acc)
        s_ref[:, lanes] = acc
        return carry

    lax.fori_loop(0, sub, body, 0)


def modal_states(state_rows, x, *, group_size):
    rows, chans = x.shape
    block = min(BLOCK_LANES, chans)
    groups_block = block // group_size
    modes = state_rows.shape[1]
    kernel = functools.partial(_state_kernel, group_size=group_size, sub=block // LANES)
    return pl.pallas_call(
        kernel,
        grid=(chans // block,),
        in_specs=[
            pl.BlockSpec((groups_block, modes, rows), lambda b: (b, 0, 0)),
            pl.BlockSpec((rows, block), lambda b: (0, b)),
        ],
        out_specs=pl.BlockSpec((modes, block), lambda b: (0, b)),
        out_shape=jax.ShapeDtypeStruct((modes, chans), jnp.float32),
        compiler_params=pltpu.CompilerParams(dimension_semantics=("parallel",)),
    )(state_rows, x)


def _gram_kernel(back_ref, top_ref, bot_ref, f_ref, *, group_size, sub):
    rows = back_ref.shape[0]
    groups_here = LANES // group_size
    r_id = lax.broadcasted_iota(jnp.int32, (rows, rows), 0)
    c_id = lax.broadcasted_iota(jnp.int32, (rows, rows), 1)
    exchange = jnp.where(r_id + c_id == rows - 1, 1.0, 0.0).astype(jnp.bfloat16)
    lane_group = lax.broadcasted_iota(jnp.int32, (rows, LANES), 1) // group_size

    def body(j, carry):
        lanes = pl.ds(pl.multiple_of(j * LANES, LANES), LANES)
        back = back_ref[:, lanes]
        x = jnp.concatenate([top_ref[:, lanes], bot_ref[:, lanes]], axis=0)
        back_rev = jnp.dot(exchange, back, preferred_element_type=jnp.float32).astype(jnp.bfloat16)
        masked = jnp.concatenate(
            [jnp.where(lane_group == k, back_rev, jnp.zeros_like(back_rev)) for k in range(groups_here)],
            axis=0,
        )
        gram = lax.dot_general(
            masked, x, (((1,), (1,)), ((), ())), preferred_element_type=jnp.float32
        )
        sums = []
        for k in range(groups_here):
            skew = pltpu.roll(gram[k * rows:(k + 1) * rows], 0, 1, stride=1, stride_axis=0)
            sums.append(jnp.sum(skew, axis=0, keepdims=True))
        f_ref[pl.ds(pl.multiple_of(j * groups_here, groups_here), groups_here), :] = jnp.concatenate(sums, 0)
        return carry

    lax.fori_loop(0, sub, body, 0)


def gram_diag(back, top, bottom, *, group_size):
    rows, chans = back.shape
    block = min(BLOCK_LANES, chans)
    groups_block = block // group_size
    group_count = chans // group_size
    kernel = functools.partial(_gram_kernel, group_size=group_size, sub=block // LANES)
    return pl.pallas_call(
        kernel,
        grid=(chans // block,),
        in_specs=[
            pl.BlockSpec((rows, block), lambda b: (0, b)),
            pl.BlockSpec((rows, block), lambda b: (0, b)),
            pl.BlockSpec((rows, block), lambda b: (0, b)),
        ],
        out_specs=pl.BlockSpec((groups_block, 2 * rows), lambda b: (b, 0)),
        out_shape=jax.ShapeDtypeStruct((group_count, 2 * rows), jnp.float32),
        compiler_params=pltpu.CompilerParams(dimension_semantics=("parallel",)),
    )(back, top, bottom)


def gather_seq(value):
    count = lax.axis_size("seq")
    tiled = jnp.broadcast_to(value[None], (count,) + value.shape)
    return lax.all_to_all(tiled, "seq", split_axis=0, concat_axis=0, tiled=True)


def entering_states(states, decays, block_len, group_size, forward):
    gathered = gather_seq(states)
    count = gathered.shape[0]
    here = lax.axis_index("seq")
    rates = jnp.repeat(decays.T, group_size, axis=1)
    source = jnp.arange(count)
    if forward:
        gap = here - 1 - source
    else:
        gap = source - here - 1
    valid = gap >= 0
    steps = jnp.maximum(gap, 0).astype(jnp.float32)
    coef = jnp.exp(-rates[None] * (float(block_len) * steps)[:, None, None])
    coef = jnp.where(valid[:, None, None], coef, 0.0)
    return jnp.sum(coef * gathered, axis=0)


def on_device(
    query_mr,
    key_mr,
    value_mr,
    query_li,
    key_li,
    cotangent,
    mr_filter,
    norm_gain,
    li_decay,
    li_residue,
):
    row_count, chan_count = query_mr.shape
    group_count, tap_count = mr_filter.shape
    group_size = chan_count // group_count
    assert row_count == tap_count
    grad_scale = float(row_count * lax.axis_size("seq")) ** (-0.5)

    taps_mr = mr_filter.astype(jnp.bfloat16).astype(jnp.float32)
    zero_col = jnp.zeros((group_count, 1), jnp.float32)
    fwd_rows = jnp.concatenate(
        [zero_col, jnp.flip(taps_mr, 1), jnp.zeros((group_count, tap_count - 1), jnp.float32)], 1
    )
    bwd_rows = jnp.concatenate([taps_mr, jnp.zeros_like(taps_mr)], 1)

    mixed_mr = (key_mr.astype(jnp.float32) * value_mr.astype(jnp.float32)).astype(jnp.bfloat16)
    rim_rows = from_behind(mixed_mr, "seq", 1)
    conv_mr = band_conv(fwd_rows, rim_rows, mixed_mr, group_size=group_size, split=False, tri=None)
    out_mr = (query_mr.astype(jnp.float32) * conv_mr).astype(jnp.bfloat16)
    out_full = out_mr.astype(jnp.float32)
    squares = lax.psum(jnp.sum(out_full * out_full, axis=1), "chan")
    inv_rms = lax.rsqrt(squares / D + 1e-06)[:, None]
    normed = out_full * inv_rms * norm_gain
    mixed_li = key_li.astype(jnp.float32) * normed
    cotan_full = cotangent.astype(jnp.float32)
    back_li = cotan_full * query_li.astype(jnp.float32)

    offsets = jnp.arange(row_count, dtype=jnp.float32)
    weights_res = li_residue * jnp.sqrt(2.0 * li_decay)
    taps_li = jnp.einsum(
        "gr,grd->gd", weights_res, jnp.exp(-li_decay[:, :, None] * offsets), precision=HIGHEST
    )
    li_fwd_rows = jnp.concatenate([taps_li[:, :1], jnp.flip(taps_li[:, 1:], 1)], 1)
    fwd_states = jnp.exp(-li_decay[:, :, None] * (row_count - 1.0 - offsets))
    bwd_states = jnp.exp(-li_decay[:, :, None] * offsets)

    back_li_bf = back_li.astype(jnp.bfloat16)
    mixed_li_bf = mixed_li.astype(jnp.bfloat16)
    grad_st = modal_states(bwd_states, back_li_bf, group_size=group_size)
    grad_st, conv_mr = lax.optimization_barrier((grad_st, conv_mr))
    grad_ent = entering_states(grad_st, li_decay, row_count, group_size, False)
    grad_mixed_li = band_conv(
        taps_li, back_li_bf, None, (li_decay, weights_res, grad_ent),
        group_size=group_size, split=True, tri="upper", modal="backward",
    )
    conv_st = modal_states(fwd_states, mixed_li_bf, group_size=group_size)
    conv_ent = entering_states(conv_st, li_decay, row_count, group_size, True)
    conv_li = band_conv(
        li_fwd_rows, mixed_li_bf, None, (li_decay, weights_res, conv_ent),
        group_size=group_size, split=True, tri="lower", modal="forward",
    )

    out_li = (query_li.astype(jnp.float32) * conv_li).astype(jnp.bfloat16)
    grad_query_li = (cotan_full * conv_li).astype(jnp.bfloat16)
    grad_key_li = (grad_mixed_li * normed).astype(jnp.bfloat16)
    grad_normed = grad_mixed_li * key_li.astype(jnp.float32)
    gain_part = jnp.sum(grad_normed * out_full * inv_rms, axis=0)
    weighted = grad_normed * norm_gain
    cross_dots = lax.psum(jnp.sum(weighted * out_full, axis=1), "chan")[:, None]
    grad_out_mr = inv_rms * weighted - out_full * inv_rms**3 * cross_dots / D
    grad_query_mr = (grad_out_mr * conv_mr).astype(jnp.bfloat16)
    back_mr = (grad_out_mr * query_mr.astype(jnp.float32)).astype(jnp.bfloat16)
    after_rim = from_behind(back_mr, "seq", -1)
    grad_mixed_mr = band_conv(bwd_rows, back_mr, after_rim, group_size=group_size, split=False, tri=None)
    grad_key_mr = (grad_mixed_mr * value_mr.astype(jnp.float32)).astype(jnp.bfloat16)
    grad_value_mr = (grad_mixed_mr * key_mr.astype(jnp.float32)).astype(jnp.bfloat16)
    diag_sums = gram_diag(back_mr, rim_rows, mixed_mr, group_size=group_size)
    filter_part = jnp.flip(diag_sums[:, tap_count:], 1)
    packed = jnp.concatenate([gain_part, filter_part.reshape(-1)])
    param_sums = jnp.sum(gather_seq(packed), axis=0) * grad_scale
    grad_gain = param_sums[:chan_count]
    grad_filter = param_sums[chan_count:].reshape(group_count, tap_count)
    return (
        out_li,
        grad_query_mr,
        grad_key_mr,
        grad_value_mr,
        grad_query_li,
        grad_key_li,
        grad_gain,
        grad_filter,
    )


def solution(mesh):
    in_specs = (
        P("seq", "chan"),
        P("seq", "chan"),
        P("seq", "chan"),
        P("seq", "chan"),
        P("seq", "chan"),
        P("seq", "chan"),
        P("chan", None),
        P("chan"),
        P("chan", None),
        P("chan", None),
    )
    out_specs = (
        P("seq", "chan"),
        P("seq", "chan"),
        P("seq", "chan"),
        P("seq", "chan"),
        P("seq", "chan"),
        P("seq", "chan"),
        P("chan"),
        P("chan", None),
    )
    return jax.shard_map(
        on_device, mesh=mesh, in_specs=in_specs, out_specs=out_specs, check_vma=False
    )
```

profile of v0, /device:TPU:0, one launch (start us, length us, event | category | flops | bytes accessed | tf_op | source)
XLA Modules:
  0.0 173.9 jit_solution(15404114498000557068)
XLA Ops:
  2.0 5.0 %collective-permute-start = (bf16[128,2048]{1,0:T(8,128)(2,1)S(1)}, bf16[128,2048]{1,0:T(8,128)(2,1)S(1)}, u32[]{:S(2)}, u32[]{:S(2)}) collective-permute-start(bf16[128,2048]{1,0:T(8,128)(2,1)S(1)} %fusion.5.refs_2_.bot_ref), channel_id=1, source_target_pairs={{0,4},{4,8},{8,12},{12,16},{16,20},{20,24},{24,28},{1,5},{5,9},{9,... | collective-permute-start | bytes 1572872 | tf_op jit(solution)/shard_map/ppermute | solution.py:20
  8.2 1.7 multiply_exponential_fusion
  9.9 8.3 %collective-permute-done.refs_1_.top_ref = bf16[128,2048]{1,0:T(8,128)(2,1)S(1)} collective-permute-done((bf16[128,2048]{1,0:T(8,128)(2,1)S(1)}, bf16[128,2048]{1,0:T(8,128)(2,1)S(1)}, u32[]{:S(2)}, u32[]{:S(2)}) %collective-permute-start) | collective-permute-done | bytes 524320 | tf_op jit(solution)/shard_map/ppermute | solution.py:20
  19.0 7.5 %shard_map.161 = f32[128,2048]{1,0:T(8,128)} custom-call(f32[128,256]{1,0:T(8,128)} %maximum_maximum_fusion.refs_0_, bf16[128,2048]{1,0:T(8,128)(2,1)} %copy-done.4, bf16[128,2048]{1,0:T(8,128)(2,1)} %copy-done.2), custom_call_target="tpu_custom_call" | custom-call | tf_op jit(solution)/shard_map/pallas_call | solution.py:121
  28.0 5.7 %psum.14 = f32[128]{0:T(128)S(1)} all-reduce(f32[128]{0:T(128)S(1)} %get-tuple-element.16), channel_id=1, replica_groups=mesh['seq'=8,'chan'=4] {'chan'}, use_global_device_ids=true, to_apply=%region_1.2 | all-reduce | flops 128 | bytes 1024 | tf_op jit(solution)/shard_map/psum | solution.py:274
  34.8 4.5 %shard_map.162 = f32[16,2048]{1,0:T(8,128)} custom-call(f32[128,16,128]{2,1,0:T(8,128)} %get-tuple-element.25.e_ref, bf16[128,2048]{1,0:T(8,128)(2,1)} %fusion.1.x_ref.refs_1_), custom_call_target="tpu_custom_call" | custom-call | tf_op jit(solution)/shard_map/pallas_call | solution.py:158
  39.3 2.0 %broadcast_in_dim.35 = f32[8,16,2048]{2,1,0:T(8,128)} broadcast(f32[16,2048]{1,0:T(8,128)} %shard_map.162), dimensions={1,2} | broadcast | bytes 1179648 | tf_op jit(solution)/shard_map/broadcast_in_dim | solution.py:223
  41.3 6.9 %all-to-all-start = ((f32[8,16,2048]{2,1,0:T(8,128)}), f32[8,16,2048]{2,1,0:T(8,128)S(1)}, u32[]{:S(2)}, u32[]{:S(2)}) async-start(f32[8,16,2048]{2,1,0:T(8,128)} %broadcast_in_dim.35), calls=%async_computation | async-start | bytes 2097152 | tf_op jit(solution)/shard_map/all_to_all | solution.py:224
  49.1 4.5 %shard_map.164 = f32[16,2048]{1,0:T(8,128)} custom-call(f32[128,16,128]{2,1,0:T(8,128)} %get-tuple-element.26.e_ref, bf16[128,2048]{1,0:T(8,128)(2,1)} %fusion.7.x_ref.refs_1_), custom_call_target="tpu_custom_call" | custom-call | tf_op jit(solution)/shard_map/pallas_call | solution.py:158
  53.6 20.3 %all-to-all-done = f32[8,16,2048]{2,1,0:T(8,128)S(1)} async-done(((f32[8,16,2048]{2,1,0:T(8,128)}), f32[8,16,2048]{2,1,0:T(8,128)S(1)}, u32[]{:S(2)}, u32[]{:S(2)}) %all-to-all-start) | async-done | bytes 1048608 | tf_op jit(solution)/shard_map/all_to_all | solution.py:224
  73.9 2.0 %broadcast_in_dim.37 = f32[8,16,2048]{2,1,0:T(8,128)} broadcast(f32[16,2048]{1,0:T(8,128)} %shard_map.164), dimensions={1,2} | broadcast | bytes 1179648 | tf_op jit(solution)/shard_map/broadcast_in_dim | solution.py:223
  75.9 3.6 %all-to-all-start.1 = ((f32[8,16,2048]{2,1,0:T(8,128)}), f32[8,16,2048]{2,1,0:T(8,128)S(1)}, u32[]{:S(2)}, u32[]{:S(2)}) async-start(f32[8,16,2048]{2,1,0:T(8,128)} %broadcast_in_dim.37), calls=%async_computation.1 | async-start | bytes 2097152 | tf_op jit(solution)/shard_map/all_to_all | solution.py:224
  82.2 1.8 %neg.22 = f32[16,2048]{1,0:T(8,128)S(1)} reshape(f32[16,128,16]{2,1,0:T(8,128)} %broadcast_in_dim.33) | data formatting | bytes 262144 | tf_op jit(solution)/shard_map/neg | solution.py:239
  87.4 18.1 %all-to-all-done.1 = f32[8,16,2048]{2,1,0:T(8,128)S(1)} async-done(((f32[8,16,2048]{2,1,0:T(8,128)}), f32[8,16,2048]{2,1,0:T(8,128)S(1)}, u32[]{:S(2)}, u32[]{:S(2)}) %all-to-all-start.1) | async-done | bytes 1048608 | tf_op jit(solution)/shard_map/all_to_all | solution.py:224
  106.6 10.3 %shard_map.165 = f32[128,2048]{1,0:T(8,128)} custom-call(f32[128,128]{1,0:T(8,128)} %bitcast.15, bf16[128,2048]{1,0:T(8,128)(2,1)} %fusion.7.x_ref.refs_1_, f32[128,16]{1,0:T(8,128)} %copy.46.refs_2_, f32[128,16]{1,0:T(8,128)} %copy-done.13, f32[16,2048]{1,0:T(8,128)} %get-tuple-element.14.refs_4_), custom_call_target="tpu_custom_call" | custom-call | tf_op jit(solution)/shard_map/pallas_call | solution.py:121
  116.9 2.6 %fusion.18 = (f32[2048]{0:T(1024)S(1)}, f32[128]{0:T(128)S(1)}, bf16[128,2048]{1,0:T(8,128)(2,1)}) fusion(bf16[128,2048]{1,0:T(8,128)(2,1)S(1)} %get-tuple-element.17, f32[128]{0:T(128)S(1)} %get-tuple-element.31, f32[128,2048]{1,0:T(8,128)} %shard_map.165, bf16[128,2048]{1,0:T(8,128)(2,1)S(1)} %copy-done.3, f32[2048]{0:T(1024)S(1)} %copy-done.15), kind=kLoop, calls=%fused_computation.33 | loop fusion | flops 3405696 | bytes 2638848 | tf_op jit(solution)/shard_map/reduce_sum | solution.py:310
  119.5 5.6 %psum.15 = f32[128]{0:T(128)S(1)} all-reduce(f32[128]{0:T(128)S(1)} %get-tuple-element.13), channel_id=1, replica_groups=mesh['seq'=8,'chan'=4] {'chan'}, use_global_device_ids=true, to_apply=%region_5.6 | all-reduce | flops 128 | bytes 1024 | tf_op jit(solution)/shard_map/psum | solution.py:312
  125.2 2.6 %fusion.3 = (bf16[128,2048]{1,0:T(8,128)(2,1)}, bf16[128,2048]{1,0:T(8,128)(2,1)}) fusion(bf16[128,2048]{1,0:T(8,128)(2,1)} %param.10, f32[128]{0:T(128)S(1)} %psum.15, f32[128]{0:T(128)S(1)} %get-tuple-element.30, bf16[128,2048]{1,0:T(8,128)(2,1)S(1)} %get-tuple-element.17, f32[2048]{0:T(1024)S(1)} %copy-done.15, f32[128,2048]{1,0:T(8,128)S(1)} %copy-done, ...), kind=kLoop, calls=%fused_computation.18 | loop fusion | flops 3670016 | bytes 4728320 | tf_op jit(solution)/shard_map/convert_element_type | solution.py:315
  129.0 11.4 %shard_map.167 = f32[128,256]{1,0:T(8,128)} custom-call(bf16[128,2048]{1,0:T(8,128)(2,1)} %get-tuple-element.18.refs_1_.back_ref, bf16[128,2048]{1,0:T(8,128)(2,1)} %copy-done.4, bf16[128,2048]{1,0:T(8,128)(2,1)} %copy-done.2), custom_call_target="tpu_custom_call" | custom-call | tf_op jit(solution)/shard_map/pallas_call | solution.py:207
  142.5 6.1 %all-to-all-start.2 = ((f32[8,1,18432]{2,1,0:T(1,128)}), f32[8,1,18432]{2,1,0:T(1,128)S(1)}, u32[]{:S(2)}, u32[]{:S(2)}) async-start(f32[8,1,18432]{2,1,0:T(1,128)} %broadcast_in_dim.38), calls=%async_computation.2 | async-start | bytes 1179648 | tf_op jit(solution)/shard_map/all_to_all | solution.py:224
  148.6 10.4 %shard_map.163 = f32[128,2048]{1,0:T(8,128)} custom-call(f32[128,128]{1,0:T(8,128)} %pad_maximum_fusion.1.refs_0_, bf16[128,2048]{1,0:T(8,128)(2,1)} %fusion.1.x_ref.refs_1_, f32[128,16]{1,0:T(8,128)} %copy.46.refs_2_, f32[128,16]{1,0:T(8,128)} %copy-done.13, f32[16,2048]{1,0:T(8,128)} %get-tuple-element.15.refs_4_), custom_call_target="tpu_custom_call" | custom-call | tf_op jit(solution)/shard_map/pallas_call | solution.py:121
  159.1 2.5 %fusion.8 = (bf16[128,2048]{1,0:T(8,128)(2,1)}, bf16[128,2048]{1,0:T(8,128)(2,1)}) fusion(f32[128,2048]{1,0:T(8,128)} %shard_map.163, bf16[128,2048]{1,0:T(8,128)(2,1)S(1)} %copy-done.8, bf16[128,2048]{1,0:T(8,128)(2,1)S(1)} %copy-done.6), kind=kLoop, calls=%fused_computation.23 | loop fusion | flops 1572864 | bytes 3145728 | tf_op jit(solution)/shard_map/convert_element_type | solution.py:307
  162.3 7.5 %shard_map.166 = f32[128,2048]{1,0:T(8,128)} custom-call(f32[128,256]{1,0:T(8,128)} %concatenate.14.refs_0_, bf16[128,2048]{1,0:T(8,128)(2,1)} %get-tuple-element.18.refs_1_.back_ref, bf16[128,2048]{1,0:T(8,128)(2,1)} %copy-done.14), custom_call_target="tpu_custom_call" | custom-call | tf_op jit(solution)/shard_map/pallas_call | solution.py:121
  169.8 2.5 %fusion.4 = (bf16[128,2048]{1,0:T(8,128)(2,1)}, bf16[128,2048]{1,0:T(8,128)(2,1)}) fusion(f32[128,2048]{1,0:T(8,128)} %shard_map.166, bf16[128,2048]{1,0:T(8,128)(2,1)S(1)} %copy-done.10, bf16[128,2048]{1,0:T(8,128)(2,1)S(1)} %copy-done.9), kind=kLoop, calls=%fused_computation.19 | loop fusion | flops 1572864 | bytes 3145728 | tf_op jit(solution)/shard_map/convert_element_type | solution.py:319
  (77 shorter events, 19.7 us)
Async XLA Ops:
  0.6 6.4 %copy-start.16 = (f32[128,128]{1,0:T(8,128)S(1)}, f32[128,128]{1,0:T(8,128)}, u32[]{:S(2)}) copy-start(f32[128,128]{1,0:T(8,128)} %param.16) | copy-start | bytes 196612
  2.0 7.9 %copy-start.2 = (bf16[128,2048]{1,0:T(8,128)(2,1)}, bf16[128,2048]{1,0:T(8,128)(2,1)S(1)}, u32[]{:S(2)}) copy-start(bf16[128,2048]{1,0:T(8,128)(2,1)S(1)} %fusion.5.refs_2_.bot_ref) | copy-start | bytes 1572868
  2.0 5.1 %copy-start.17 = (f32[128,16]{0,1:T(8,128)S(1)}, f32[128,16]{0,1:T(8,128)}, u32[]{:S(2)}) copy-start(f32[128,16]{0,1:T(8,128)} %param.18) | copy-start | bytes 24580
  2.0 16.2 %collective-permute-start = (bf16[128,2048]{1,0:T(8,128)(2,1)S(1)}, bf16[128,2048]{1,0:T(8,128)(2,1)S(1)}, u32[]{:S(2)}, u32[]{:S(2)}) collective-permute-start(bf16[128,2048]{1,0:T(8,128)(2,1)S(1)} %fusion.5.refs_2_.bot_ref), channel_id=1, source_target_pairs={{0,4},{4,8},{8,12},{12,16},{16,20},{20,24},{24,28},{1,5},{5,9},{9,... | collective-permute-start | bytes 1572872 | tf_op jit(solution)/shard_map/ppermute | solution.py:20
  9.9 16.6 %copy-start.11 = (bf16[128,2048]{1,0:T(8,128)(2,1)S(1)}, bf16[128,2048]{1,0:T(8,128)(2,1)}, u32[]{:S(2)}) copy-start(bf16[128,2048]{1,0:T(8,128)(2,1)} %param.10) | copy-start | bytes 1572868
  18.2 0.8 copy-start.4
  26.5 7.3 %copy-start.3 = (bf16[128,2048]{1,0:T(8,128)(2,1)S(1)}, bf16[128,2048]{1,0:T(8,128)(2,1)}, u32[]{:S(2)}) copy-start(bf16[128,2048]{1,0:T(8,128)(2,1)} %param.14) | copy-start | bytes 1572868
  28.0 5.7 %copy-start.15 = (f32[2048]{0:T(1024)S(1)}, f32[2048]{0:T(1024)}, u32[]{:S(2)}) copy-start(f32[2048]{0:T(1024)} %param.17) | copy-start | bytes 24580
  41.3 6.9 %copy-start.5 = (bf16[128,2048]{1,0:T(8,128)(2,1)S(1)}, bf16[128,2048]{1,0:T(8,128)(2,1)}, u32[]{:S(2)}) copy-start(bf16[128,2048]{1,0:T(8,128)(2,1)} %param.13) | copy-start | bytes 1572868
  41.3 6.9 %copy-start.7 = (bf16[128,2048]{1,0:T(8,128)(2,1)S(1)}, bf16[128,2048]{1,0:T(8,128)(2,1)}, u32[]{:S(2)}) copy-start(bf16[128,2048]{1,0:T(8,128)(2,1)} %param.15) | copy-start | bytes 1572868
  41.3 32.7 %all-to-all-start = ((f32[8,16,2048]{2,1,0:T(8,128)}), f32[8,16,2048]{2,1,0:T(8,128)S(1)}, u32[]{:S(2)}, u32[]{:S(2)}) async-start(f32[8,16,2048]{2,1,0:T(8,128)} %broadcast_in_dim.35), calls=%async_computation | async-start | bytes 2097152 | tf_op jit(solution)/shard_map/all_to_all | solution.py:224
  75.9 29.5 %all-to-all-start.1 = ((f32[8,16,2048]{2,1,0:T(8,128)}), f32[8,16,2048]{2,1,0:T(8,128)S(1)}, u32[]{:S(2)}, u32[]{:S(2)}) async-start(f32[8,16,2048]{2,1,0:T(8,128)} %broadcast_in_dim.37), calls=%async_computation.1 | async-start | bytes 2097152 | tf_op jit(solution)/shard_map/all_to_all | solution.py:224
  84.1 0.7 copy-start.18
  84.9 1.2 copy-start.13
  116.9 8.2 %copy-start = (f32[128,2048]{1,0:T(8,128)S(1)}, f32[128,2048]{1,0:T(8,128)}, u32[]{:S(2)}) copy-start(f32[128,2048]{1,0:T(8,128)} %shard_map.165) | copy-start | bytes 3145732
  116.9 8.2 %copy-start.1 = (f32[128,2048]{1,0:T(8,128)S(1)}, f32[128,2048]{1,0:T(8,128)}, u32[]{:S(2)}) copy-start(f32[128,2048]{1,0:T(8,128)} %shard_map.161) | copy-start | bytes 3145732
  127.8 33.8 %collective-permute-start.1 = (bf16[128,2048]{1,0:T(8,128)(2,1)}, bf16[128,2048]{1,0:T(8,128)(2,1)S(1)}, u32[]{:S(2)}, u32[]{:S(2)}) collective-permute-start(bf16[128,2048]{1,0:T(8,128)(2,1)} %get-tuple-element.18.refs_1_.back_ref), channel_id=1, source_target_pairs={{4,0},{8,4},{12,8},{16,12},{20,16},{24,20},{28,24},{5,1},{9,5},{13... | collective-permute-start | bytes 1572872 | tf_op jit(solution)/shard_map/ppermute | solution.py:20
  140.5 0.8 slice-start
  142.5 29.7 %all-to-all-start.2 = ((f32[8,1,18432]{2,1,0:T(1,128)}), f32[8,1,18432]{2,1,0:T(1,128)S(1)}, u32[]{:S(2)}, u32[]{:S(2)}) async-start(f32[8,1,18432]{2,1,0:T(1,128)} %broadcast_in_dim.38), calls=%async_computation.2 | async-start | bytes 1179648 | tf_op jit(solution)/shard_map/all_to_all | solution.py:224
  148.6 10.4 %copy-start.6 = (bf16[128,2048]{1,0:T(8,128)(2,1)S(1)}, bf16[128,2048]{1,0:T(8,128)(2,1)}, u32[]{:S(2)}) copy-start(bf16[128,2048]{1,0:T(8,128)(2,1)} %param.13) | copy-start | bytes 1572868
  148.6 10.4 %copy-start.8 = (bf16[128,2048]{1,0:T(8,128)(2,1)S(1)}, bf16[128,2048]{1,0:T(8,128)(2,1)}, u32[]{:S(2)}) copy-start(bf16[128,2048]{1,0:T(8,128)(2,1)} %param.15) | copy-start | bytes 1572868
  161.5 8.3 %copy-start.9 = (bf16[128,2048]{1,0:T(8,128)(2,1)S(1)}, bf16[128,2048]{1,0:T(8,128)(2,1)}, u32[]{:S(2)}) copy-start(bf16[128,2048]{1,0:T(8,128)(2,1)} %param.12) | copy-start | bytes 1572868
  161.5 8.3 %copy-start.10 = (bf16[128,2048]{1,0:T(8,128)(2,1)S(1)}, bf16[128,2048]{1,0:T(8,128)(2,1)}, u32[]{:S(2)}) copy-start(bf16[128,2048]{1,0:T(8,128)(2,1)} %param.11) | copy-start | bytes 1572868
  161.5 0.8 copy-start.14
  (1 other events, 0.6 us)
where the time goes:
time: 175 us; the launch traced here: 174 us
  Pallas kernels  56 us (32%)
  waiting for transfers between devices  46.7 us (27%)
  starting transfers between devices  22.9 us (13%)
  other arithmetic  19.9 us (11%)
  local copies, waits for them, and re-layouts  15.1 us (9%)
  blocking collectives  11.3 us (6%)
    all_to_all x3, waiting for transfers between devices, gather_seq(): return lax.all_to_all(tiled, 'seq', split_axis=0, concat_axis=0, tiled=True)  38.4 us
    pallas_call x4, Pallas kernels, band_conv(): pl.pallas_call(kernel, grid=(chans // block,), in_specs=in_specs, out_spe...  35.6 us
    all_to_all x3, starting transfers between devices, gather_seq(): return lax.all_to_all(tiled, 'seq', split_axis=0, concat_axis=0, tiled=True)  16.6 us
    pallas_call x1, Pallas kernels, gram_diag(): pl.pallas_call(kernel, grid=(chans // block,), in_specs=[pl.BlockSpec((ro...  11.4 us
    pallas_call x2, Pallas kernels, modal_states(): pl.pallas_call(kernel, grid=(chans // block,), in_specs=[pl.BlockSpec((gr...  9 us
    ppermute x2, waiting for transfers between devices, from_behind(): lax.ppermute(value, axis, [(source, source + steps) for source in range(i...  8.35 us
    ppermute x2, starting transfers between devices, from_behind(): lax.ppermute(value, axis, [(source, source + steps) for source in range(i...  6.32 us
    psum x1, blocking collectives, on_device(): squares = lax.psum(jnp.sum(out_full * out_full, axis=1), 'chan')  5.72 us
  transfers between devices with their start and end apart: 5, of which 3 were waited for; matrix products, arithmetic and copies ran while one was open for 10% of the time, Pallas kernels for 19%

commit v1 on v0

--- a/solution.py
+++ b/solution.py
@@ -168,6 +168,58 @@
     )(state_rows, x)
 
 
+def _modal_kernel(dec_ref, wt_ref, ent_ref, loc_ref, out_ref, *, group_size, forward, sub):
+    rows = out_ref.shape[0]
+    modes = dec_ref.shape[1]
+    groups_here = LANES // group_size
+    lane_group = lax.broadcasted_iota(jnp.int32, (rows, LANES), 1) // group_size
+    offsets = lax.broadcasted_iota(jnp.int32, (rows, modes), 0).astype(jnp.float32)
+    dist = offsets + 1.0 if forward else float(rows) - offsets
+
+    def body(j, carry):
+        lanes = pl.ds(pl.multiple_of(j * LANES, LANES), LANES)
+        ent_high, ent_low = _split(ent_ref[:, lanes])
+        out_w = []
+        for k in range(groups_here):
+            rate = dec_ref[pl.ds(j * groups_here + k, 1), :]
+            weight = wt_ref[pl.ds(j * groups_here + k, 1), :]
+            out_w.append(weight * jnp.exp(-rate * dist))
+        a_high, a_low = _split(jnp.concatenate(out_w, axis=0))
+        y = jnp.dot(a_high, ent_high, preferred_element_type=jnp.float32)
+        y = y + jnp.dot(a_low, ent_high, preferred_element_type=jnp.float32)
+        y = y + jnp.dot(a_high, ent_low, preferred_element_type=jnp.float32)
+        acc = y[:rows]
+        for k in range(1, groups_here):
+            acc = jnp.where(lane_group == k, y[k * rows:(k + 1) * rows], acc)
+        out_ref[:, lanes] = loc_ref[:, lanes] + acc
+        return carry
+
+    lax.fori_loop(0, sub, body, 0)
+
+
+def modal_out(decays, weights, entering, local, *, group_size, forward):
+    rows, chans = local.shape
+    block = min(BLOCK_LANES, chans)
+    groups_block = block // group_size
+    modes = decays.shape[1]
+    kernel = functools.partial(
+        _modal_kernel, group_size=group_size, forward=forward, sub=block // LANES
+    )
+    return pl.pallas_call(
+        kernel,
+        grid=(chans // block,),
+        in_specs=[
+            pl.BlockSpec((groups_block, modes), lambda b: (b, 0)),
+            pl.BlockSpec((groups_block, modes), lambda b: (b, 0)),
+            pl.BlockSpec((modes, block), lambda b: (0, b)),
+            pl.BlockSpec((rows, block), lambda b: (0, b)),
+        ],
+        out_specs=pl.BlockSpec((rows, block), lambda b: (0, b)),
+        out_shape=jax.ShapeDtypeStruct((rows, chans), jnp.float32),
+        compiler_params=pltpu.CompilerParams(dimension_semantics=("parallel",)),
+    )(decays, weights, entering, local)
+
+
 def _gram_kernel(back_ref, top_ref, bot_ref, f_ref, *, group_size, sub):
     rows = back_ref.shape[0]
     groups_here = LANES // group_size
@@ -224,8 +276,7 @@
     return lax.all_to_all(tiled, "seq", split_axis=0, concat_axis=0, tiled=True)
 
 
-def entering_states(states, decays, block_len, group_size, forward):
-    gathered = gather_seq(states)
+def entering_states(gathered, decays, block_len, group_size, forward):
     count = gathered.shape[0]
     here = lax.axis_index("seq")
     rates = jnp.repeat(decays.T, group_size, axis=1)
@@ -289,19 +340,19 @@
 
     back_li_bf = back_li.astype(jnp.bfloat16)
     mixed_li_bf = mixed_li.astype(jnp.bfloat16)
+    modes = li_decay.shape[1]
     grad_st = modal_states(bwd_states, back_li_bf, group_size=group_size)
-    grad_st, conv_mr = lax.optimization_barrier((grad_st, conv_mr))
-    grad_ent = entering_states(grad_st, li_decay, row_count, group_size, False)
-    grad_mixed_li = band_conv(
-        taps_li, back_li_bf, None, (li_decay, weights_res, grad_ent),
-        group_size=group_size, split=True, tri="upper", modal="backward",
-    )
     conv_st = modal_states(fwd_states, mixed_li_bf, group_size=group_size)
-    conv_ent = entering_states(conv_st, li_decay, row_count, group_size, True)
-    conv_li = band_conv(
-        li_fwd_rows, mixed_li_bf, None, (li_decay, weights_res, conv_ent),
-        group_size=group_size, split=True, tri="lower", modal="forward",
-    )
+    both_st = gather_seq(jnp.concatenate([grad_st, conv_st], 0).astype(jnp.bfloat16))
+    both_st = both_st.astype(jnp.float32)
+    grad_loc = band_conv(taps_li, back_li_bf, group_size=group_size, split=True, tri="upper")
+    conv_loc = band_conv(li_fwd_rows, mixed_li_bf, group_size=group_size, split=True, tri="lower")
+    grad_ent = entering_states(both_st[:, :modes], li_decay, row_count, group_size, False)
+    conv_ent = entering_states(both_st[:, modes:], li_decay, row_count, group_size, True)
+    grad_mixed_li = modal_out(
+        li_decay, weights_res, grad_ent, grad_loc, group_size=group_size, forward=False
+    )
+    conv_li = modal_out(li_decay, weights_res, conv_ent, conv_loc, group_size=group_size, forward=True)
 
     out_li = (query_li.astype(jnp.float32) * conv_li).astype(jnp.bfloat16)
     grad_query_li = (cotan_full * conv_li).astype(jnp.bfloat16)

time: 175 us -> 138 us (0.79)
  waiting for transfers between devices: 46.7 us -> 5.21 us
  Pallas kernels: 56 us -> 66.1 us
  local copies, waits for them, and re-layouts: 15.1 us -> 9.86 us
  starting transfers between devices: 22.9 us -> 18.6 us
  other arithmetic: 19.9 us -> 23.5 us
    all_to_all x3 -> x2, waiting for transfers between devices: 38.4 us -> 4.74 us  [gather_seq(): return lax.all_to_all(tiled, 'seq', split_axis=0, concat_axis=0, tiled=True)]
    pallas_call x0 -> x2, Pallas kernels: none -> 15.9 us  [modal_out(): pl.pallas_call(kernel, grid=(chans // block,), in_specs=[pl.BlockSpec((gr...]
    ppermute x2, waiting for transfers between devices: 8.35 us -> 0.47 us  [from_behind(): lax.ppermute(value, axis, [(source, source + steps) for source in range(i...]
    pallas_call x4, Pallas kernels: 35.6 us -> 29.8 us  [band_conv(): pl.pallas_call(kernel, grid=(chans // block,), in_specs=in_specs, out_spe...]
    all_to_all x3 -> x2, starting transfers between devices: 16.6 us -> 12.4 us  [gather_seq(): return lax.all_to_all(tiled, 'seq', split_axis=0, concat_axis=0, tiled=True)]
    broadcast_in_dim x3 -> x2, local copies, waits for them, and re-layouts: 5.11 us -> 2.25 us  [gather_seq(): tiled = jnp.broadcast_to(value[None], (count,) + value.shape)]
    another operation x0 -> x2, other arithmetic: none -> 1.85 us
  transfers between devices with their start and end apart: 5 -> 4, of which waited for: 3 -> 2; matrix products, arithmetic and copies ran while one was open for 10% -> 14% of each run, Pallas kernels for 19% -> 34%
where the time goes in v1:
time: 138 us; the launch traced here: 137 us
  Pallas kernels  66.1 us (48%)
  other arithmetic  23.5 us (17%)
  starting transfers between devices  18.6 us (13%)
  blocking collectives  11.5 us (8%)
  local copies, waits for them, and re-layouts  9.86 us (7%)
  waiting for transfers between devices  5.21 us (4%)
  matrix products  1.78 us (1%)
    pallas_call x4, Pallas kernels, band_conv(): pl.pallas_call(kernel, grid=(chans // block,), in_specs=in_specs, out_spe...  29.8 us
    pallas_call x2, Pallas kernels, modal_out(): pl.pallas_call(kernel, grid=(chans // block,), in_specs=[pl.BlockSpec((gr...  15.9 us
    all_to_all x2, starting transfers between devices, gather_seq(): return lax.all_to_all(tiled, 'seq', split_axis=0, concat_axis=0, tiled=True)  12.4 us
    pallas_call x1, Pallas kernels, gram_diag(): pl.pallas_call(kernel, grid=(chans // block,), in_specs=[pl.BlockSpec((ro...  11.4 us
    pallas_call x2, Pallas kernels, modal_states(): pl.pallas_call(kernel, grid=(chans // block,), in_specs=[pl.BlockSpec((gr...  9.05 us
    ppermute x2, starting transfers between devices, from_behind(): lax.ppermute(value, axis, [(source, source + steps) for source in range(i...  6.18 us
    psum x1, blocking collectives, on_device(): squares = lax.psum(jnp.sum(out_full * out_full, axis=1), 'chan')  5.83 us
    psum x1, blocking collectives, on_device(): cross_dots = lax.psum(jnp.sum(weighted * out_full, axis=1), 'chan')[:, None]  5.63 us
  transfers between devices with their start and end apart: 4, of which 2 were waited for; matrix products, arithmetic and copies ran while one was open for 14% of the time, Pallas kernels for 34%

profile of v1, /device:TPU:0, one launch (start us, length us, event | category | flops | bytes accessed | tf_op | source)
XLA Modules:
  0.0 137.4 jit_solution(12230198506497312778)
XLA Ops:
  0.7 1.4 %fusion.7.refs_2_.bot_ref = bf16[128,2048]{1,0:T(8,128)(2,1)S(1)} fusion(bf16[128,2048]{1,0:T(8,128)(2,1)} %param.12, bf16[128,2048]{1,0:T(8,128)(2,1)} %param.11), kind=kLoop, calls=%fused_computation.22 | loop fusion | flops 1048576 | bytes 1572864 | tf_op jit(solution)/shard_map/convert_element_type | solution.py:320
  2.1 4.9 %collective-permute-start = (bf16[128,2048]{1,0:T(8,128)(2,1)S(1)}, bf16[128,2048]{1,0:T(8,128)(2,1)S(1)}, u32[]{:S(2)}, u32[]{:S(2)}) collective-permute-start(bf16[128,2048]{1,0:T(8,128)(2,1)S(1)} %fusion.7.refs_2_.bot_ref), channel_id=1, source_target_pairs={{0,4},{4,8},{8,12},{12,16},{16,20},{20,24},{24,28},{1,5},{5,9},{9,... | collective-permute-start | bytes 1572872 | tf_op jit(solution)/shard_map/ppermute | solution.py:20
  9.7 1.7 %multiply_exponential_fusion.1 = (f32[128,16,128]{2,1,0:T(8,128)}, f32[128,16,128]{2,1,0:T(8,128)}) fusion(f32[128,16]{1,0:T(8,128)S(1)} %copy.45, f32[128]{0:T(128)S(1)} %iota_subtract_fusion), kind=kLoop, calls=%fused_computation.40 | loop fusion | flops 524288 | bytes 2105856 | tf_op jit(solution)/shard_map/exp | solution.py:339
  11.4 4.6 %shard_map.161 = f32[16,2048]{1,0:T(8,128)} custom-call(f32[128,16,128]{2,1,0:T(8,128)} %get-tuple-element.21.e_ref, bf16[128,2048]{1,0:T(8,128)(2,1)} %fusion.1.x_ref.refs_1_), custom_call_target="tpu_custom_call" | custom-call | tf_op jit(solution)/shard_map/pallas_call | solution.py:158
  18.9 7.5 %shard_map.162 = f32[128,2048]{1,0:T(8,128)} custom-call(f32[128,256]{1,0:T(8,128)} %maximum_maximum_fusion.refs_0_, bf16[128,2048]{1,0:T(8,128)(2,1)} %copy-done.5, bf16[128,2048]{1,0:T(8,128)(2,1)} %copy-done.2), custom_call_target="tpu_custom_call" | custom-call | tf_op jit(solution)/shard_map/pallas_call | solution.py:121
  26.4 1.5 %fusion.9 = (f32[128]{0:T(128)S(1)}, bf16[128,2048]{1,0:T(8,128)(2,1)S(1)}) fusion(f32[128,2048]{1,0:T(8,128)} %shard_map.162, bf16[128,2048]{1,0:T(8,128)(2,1)S(1)} %copy-done.12), kind=kLoop, calls=%fused_computation.24 | loop fusion | flops 1572736 | bytes 2097664 | tf_op jit(solution)/shard_map/reduce_sum | solution.py:325
  27.9 5.8 %psum.14 = f32[128]{0:T(128)S(1)} all-reduce(f32[128]{0:T(128)S(1)} %get-tuple-element.12), channel_id=1, replica_groups=mesh['seq'=8,'chan'=4] {'chan'}, use_global_device_ids=true, to_apply=%region_1.2 | all-reduce | flops 128 | bytes 1024 | tf_op jit(solution)/shard_map/psum | solution.py:325
  34.8 4.5 %shard_map.163 = f32[16,2048]{1,0:T(8,128)} custom-call(f32[128,16,128]{2,1,0:T(8,128)} %get-tuple-element.22.e_ref, bf16[128,2048]{1,0:T(8,128)(2,1)} %fusion.3.x_ref.refs_1_), custom_call_target="tpu_custom_call" | custom-call | tf_op jit(solution)/shard_map/pallas_call | solution.py:158
  41.3 6.7 %all-to-all-start = ((bf16[8,32,2048]{2,1,0:T(8,128)(2,1)}), bf16[8,32,2048]{2,1,0:T(8,128)(2,1)S(1)}, u32[]{:S(2)}, u32[]{:S(2)}) async-start(bf16[8,32,2048]{2,1,0:T(8,128)(2,1)} %broadcast_in_dim.33), calls=%async_computation | async-start | bytes 2097152 | tf_op jit(solution)/shard_map/all_to_all | solution.py:276
  49.6 1.8 %fusion.21 = f32[128,1,128]{2,1,0:T(1,128)} fusion(f32[128,16,1]{1,2,0:T(1,128)S(1)} %bitcast.13, f32[128,16]{1,0:T(8,128)S(1)} %copy.45), kind=kOutput, calls=%fused_computation.41 | convolution fusion | flops 3407872 | bytes 81920 | tf_op jit(solution)/shard_map/gr,grd->gd/dot_general | solution.py:334
  51.4 7.4 %shard_map.166.loc_ref = f32[128,2048]{1,0:T(8,128)} custom-call(f32[128,128]{1,0:T(8,128)} %bitcast.14, bf16[128,2048]{1,0:T(8,128)(2,1)} %fusion.1.x_ref.refs_1_), custom_call_target="tpu_custom_call" | custom-call | tf_op jit(solution)/shard_map/pallas_call | solution.py:121
  61.6 7.4 %shard_map.164.loc_ref = f32[128,2048]{1,0:T(8,128)} custom-call(f32[128,128]{1,0:T(8,128)} %pad_maximum_fusion.2.refs_0_, bf16[128,2048]{1,0:T(8,128)(2,1)} %fusion.3.x_ref.refs_1_), custom_call_target="tpu_custom_call" | custom-call | tf_op jit(solution)/shard_map/pallas_call | solution.py:121
  69.0 4.7 %all-to-all-done = bf16[8,32,2048]{2,1,0:T(8,128)(2,1)S(1)} async-done(((bf16[8,32,2048]{2,1,0:T(8,128)(2,1)}), bf16[8,32,2048]{2,1,0:T(8,128)(2,1)S(1)}, u32[]{:S(2)}, u32[]{:S(2)}) %all-to-all-start) | async-done | bytes 1048608 | tf_op jit(solution)/shard_map/all_to_all | solution.py:276
  75.2 7.9 %shard_map.167 = f32[128,2048]{1,0:T(8,128)} custom-call(f32[128,16]{1,0:T(8,128)} %copy.46.dec_ref, f32[128,16]{1,0:T(8,128)} %copy-done.13, f32[16,2048]{1,0:T(8,128)} %get-tuple-element.8.ent_ref, f32[128,2048]{1,0:T(8,128)} %shard_map.166.loc_ref), custom_call_target="tpu_custom_call" | custom-call | tf_op jit(solution)/shard_map/pallas_call | solution.py:208
  83.1 2.5 %fusion.18 = (f32[2048]{0:T(1024)S(1)}, f32[128]{0:T(128)S(1)}, bf16[128,2048]{1,0:T(8,128)(2,1)}) fusion(bf16[128,2048]{1,0:T(8,128)(2,1)S(1)} %get-tuple-element.13, f32[128]{0:T(128)S(1)} %get-tuple-element.27, f32[128,2048]{1,0:T(8,128)} %shard_map.167, bf16[128,2048]{1,0:T(8,128)(2,1)S(1)} %copy-done.4, f32[2048]{0:T(1024)S(1)} %copy-done.16), kind=kLoop, calls=%fused_computation.33 | loop fusion | flops 3405696 | bytes 2638848 | tf_op jit(solution)/shard_map/reduce_sum | solution.py:361
  85.6 5.6 %psum.15 = f32[128]{0:T(128)S(1)} all-reduce(f32[128]{0:T(128)S(1)} %get-tuple-element.11), channel_id=1, replica_groups=mesh['seq'=8,'chan'=4] {'chan'}, use_global_device_ids=true, to_apply=%region_5.6 | all-reduce | flops 128 | bytes 1024 | tf_op jit(solution)/shard_map/psum | solution.py:363
  91.3 2.6 %fusion.5 = (bf16[128,2048]{1,0:T(8,128)(2,1)}, bf16[128,2048]{1,0:T(8,128)(2,1)}) fusion(bf16[128,2048]{1,0:T(8,128)(2,1)} %param.10, f32[128]{0:T(128)S(1)} %psum.15, f32[128]{0:T(128)S(1)} %get-tuple-element.26, bf16[128,2048]{1,0:T(8,128)(2,1)S(1)} %get-tuple-element.13, f32[2048]{0:T(1024)S(1)} %copy-done.16, f32[128]{0:T(128)S(1)} %get-tuple-element.27, ...), kind=kLoop, calls=%fused_computation.20 | loop fusion | flops 3670016 | bytes 4728320 | tf_op jit(solution)/shard_map/convert_element_type | solution.py:366
  93.9 1.3 collective-permute-start.1
  95.1 11.4 %shard_map.169 = f32[128,256]{1,0:T(8,128)} custom-call(bf16[128,2048]{1,0:T(8,128)(2,1)} %get-tuple-element.14.refs_1_.back_ref, bf16[128,2048]{1,0:T(8,128)(2,1)} %copy-done.5, bf16[128,2048]{1,0:T(8,128)(2,1)} %copy-done.2), custom_call_target="tpu_custom_call" | custom-call | tf_op jit(solution)/shard_map/pallas_call | solution.py:259
  108.7 5.7 %all-to-all-start.1 = ((f32[8,1,18432]{2,1,0:T(1,128)}), f32[8,1,18432]{2,1,0:T(1,128)S(1)}, u32[]{:S(2)}, u32[]{:S(2)}) async-start(f32[8,1,18432]{2,1,0:T(1,128)} %broadcast_in_dim.62), calls=%async_computation.1 | async-start | bytes 1179648 | tf_op jit(solution)/shard_map/all_to_all | solution.py:276
  114.4 8.0 %shard_map.165 = f32[128,2048]{1,0:T(8,128)} custom-call(f32[128,16]{1,0:T(8,128)} %copy.46.dec_ref, f32[128,16]{1,0:T(8,128)} %copy-done.13, f32[16,2048]{1,0:T(8,128)} %get-tuple-element.9.ent_ref, f32[128,2048]{1,0:T(8,128)} %shard_map.164.loc_ref), custom_call_target="tpu_custom_call" | custom-call | tf_op jit(solution)/shard_map/pallas_call | solution.py:208
  122.4 2.5 %fusion.2 = (bf16[128,2048]{1,0:T(8,128)(2,1)}, bf16[128,2048]{1,0:T(8,128)(2,1)}) fusion(f32[128,2048]{1,0:T(8,128)} %shard_map.165, bf16[128,2048]{1,0:T(8,128)(2,1)S(1)} %copy-done.9, bf16[128,2048]{1,0:T(8,128)(2,1)S(1)} %copy-done.7), kind=kLoop, calls=%fused_computation.17 | loop fusion | flops 1572864 | bytes 3145728 | tf_op jit(solution)/shard_map/convert_element_type | solution.py:358
  125.7 7.5 %shard_map.168 = f32[128,2048]{1,0:T(8,128)} custom-call(f32[128,256]{1,0:T(8,128)} %concatenate.23.refs_0_, bf16[128,2048]{1,0:T(8,128)(2,1)} %get-tuple-element.14.refs_1_.back_ref, bf16[128,2048]{1,0:T(8,128)(2,1)} %copy-done.15), custom_call_target="tpu_custom_call" | custom-call | tf_op jit(solution)/shard_map/pallas_call | solution.py:121
  133.2 2.5 %fusion.6 = (bf16[128,2048]{1,0:T(8,128)(2,1)}, bf16[128,2048]{1,0:T(8,128)(2,1)}) fusion(f32[128,2048]{1,0:T(8,128)} %shard_map.168, bf16[128,2048]{1,0:T(8,128)(2,1)S(1)} %copy-done.11, bf16[128,2048]{1,0:T(8,128)(2,1)S(1)} %copy-done.10), kind=kLoop, calls=%fused_computation.21 | loop fusion | flops 1572864 | bytes 3145728 | tf_op jit(solution)/shard_map/convert_element_type | solution.py:370
  (79 shorter events, 19.1 us)
Async XLA Ops:
  0.6 7.9 %copy-start.6 = (bf16[128,2048]{1,0:T(8,128)(2,1)S(1)}, bf16[128,2048]{1,0:T(8,128)(2,1)}, u32[]{:S(2)}) copy-start(bf16[128,2048]{1,0:T(8,128)(2,1)} %param.13) | copy-start | bytes 1572868
  0.6 7.9 %copy-start.8 = (bf16[128,2048]{1,0:T(8,128)(2,1)S(1)}, bf16[128,2048]{1,0:T(8,128)(2,1)}, u32[]{:S(2)}) copy-start(bf16[128,2048]{1,0:T(8,128)(2,1)} %param.15) | copy-start | bytes 1572868
  2.1 13.9 %copy-start.2 = (bf16[128,2048]{1,0:T(8,128)(2,1)}, bf16[128,2048]{1,0:T(8,128)(2,1)S(1)}, u32[]{:S(2)}) copy-start(bf16[128,2048]{1,0:T(8,128)(2,1)S(1)} %fusion.7.refs_2_.bot_ref) | copy-start | bytes 1572868
  2.1 16.0 %collective-permute-start = (bf16[128,2048]{1,0:T(8,128)(2,1)S(1)}, bf16[128,2048]{1,0:T(8,128)(2,1)S(1)}, u32[]{:S(2)}, u32[]{:S(2)}) collective-permute-start(bf16[128,2048]{1,0:T(8,128)(2,1)S(1)} %fusion.7.refs_2_.bot_ref), channel_id=1, source_target_pairs={{0,4},{4,8},{8,12},{12,16},{16,20},{20,24},{24,28},{1,5},{5,9},{9,... | collective-permute-start | bytes 1572872 | tf_op jit(solution)/shard_map/ppermute | solution.py:20
  11.4 15.0 %copy-start.12 = (bf16[128,2048]{1,0:T(8,128)(2,1)S(1)}, bf16[128,2048]{1,0:T(8,128)(2,1)}, u32[]{:S(2)}) copy-start(bf16[128,2048]{1,0:T(8,128)(2,1)} %param.10) | copy-start | bytes 1572868
  17.7 16.0 %copy-start.3 = (bf16[128,2048]{1,0:T(8,128)(2,1)S(1)}, bf16[128,2048]{1,0:T(8,128)(2,1)}, u32[]{:S(2)}) copy-start(bf16[128,2048]{1,0:T(8,128)(2,1)} %param.14) | copy-start | bytes 1572868
  17.7 16.0 %copy-start.16 = (f32[2048]{0:T(1024)S(1)}, f32[2048]{0:T(1024)}, u32[]{:S(2)}) copy-start(f32[2048]{0:T(1024)} %param.17) | copy-start | bytes 24580
  18.1 0.8 copy-start.5
  39.3 8.7 %copy-start.17 = (f32[128,16]{0,1:T(8,128)S(1)}, f32[128,16]{0,1:T(8,128)}, u32[]{:S(2)}) copy-start(f32[128,16]{0,1:T(8,128)} %param.18) | copy-start | bytes 24580
  39.3 10.2 %copy-start.18 = (f32[128,16]{0,1:T(8,128)S(1)}, f32[128,16]{0,1:T(8,128)}, u32[]{:S(2)}) copy-start(f32[128,16]{0,1:T(8,128)} %param.19) | copy-start | bytes 24580
  41.3 32.4 %all-to-all-start = ((bf16[8,32,2048]{2,1,0:T(8,128)(2,1)}), bf16[8,32,2048]{2,1,0:T(8,128)(2,1)S(1)}, u32[]{:S(2)}, u32[]{:S(2)}) async-start(bf16[8,32,2048]{2,1,0:T(8,128)(2,1)} %broadcast_in_dim.33), calls=%async_computation | async-start | bytes 2097152 | tf_op jit(solution)/shard_map/all_to_all | solution.py:276
  49.6 11.1 %copy-start.13 = (f32[128,16]{1,0:T(8,128)}, f32[128,16]{1,0:T(8,128)S(1)}, u32[]{:S(2)}) copy-start(f32[128,16]{1,0:T(8,128)S(1)} %sqrt_multiply_fusion.wt_ref) | copy-start | bytes 24580
  51.4 9.5 %copy-start.14 = (f32[128,1,128]{2,1,0:T(1,128)S(1)}, f32[128,1,128]{2,1,0:T(1,128)}, u32[]{:S(2)}) copy-start(f32[128,1,128]{2,1,0:T(1,128)} %fusion.21) | copy-start | bytes 196612
  74.0 9.1 %copy-start.4 = (bf16[128,2048]{1,0:T(8,128)(2,1)S(1)}, bf16[128,2048]{1,0:T(8,128)(2,1)}, u32[]{:S(2)}) copy-start(bf16[128,2048]{1,0:T(8,128)(2,1)} %param.14) | copy-start | bytes 1572868
  75.2 16.1 %copy-start.1 = (f32[128,2048]{1,0:T(8,128)S(1)}, f32[128,2048]{1,0:T(8,128)}, u32[]{:S(2)}) copy-start(f32[128,2048]{1,0:T(8,128)} %shard_map.162) | copy-start | bytes 3145732
  83.1 8.2 %copy-start = (f32[128,2048]{1,0:T(8,128)S(1)}, f32[128,2048]{1,0:T(8,128)}, u32[]{:S(2)}) copy-start(f32[128,2048]{1,0:T(8,128)} %shard_map.167) | copy-start | bytes 3145732
  93.9 31.1 %collective-permute-start.1 = (bf16[128,2048]{1,0:T(8,128)(2,1)}, bf16[128,2048]{1,0:T(8,128)(2,1)S(1)}, u32[]{:S(2)}, u32[]{:S(2)}) collective-permute-start(bf16[128,2048]{1,0:T(8,128)(2,1)} %get-tuple-element.14.refs_1_.back_ref), channel_id=1, source_target_pairs={{4,0},{8,4},{12,8},{16,12},{20,16},{24,20},{28,24},{5,1},{9,5},{13... | collective-permute-start | bytes 1572872 | tf_op jit(solution)/shard_map/ppermute | solution.py:20
  107.5 14.9 %copy-start.7 = (bf16[128,2048]{1,0:T(8,128)(2,1)S(1)}, bf16[128,2048]{1,0:T(8,128)(2,1)}, u32[]{:S(2)}) copy-start(bf16[128,2048]{1,0:T(8,128)(2,1)} %param.13) | copy-start | bytes 1572868
  107.5 14.9 %copy-start.9 = (bf16[128,2048]{1,0:T(8,128)(2,1)S(1)}, bf16[128,2048]{1,0:T(8,128)(2,1)}, u32[]{:S(2)}) copy-start(bf16[128,2048]{1,0:T(8,128)(2,1)} %param.15) | copy-start | bytes 1572868
  108.7 27.0 %all-to-all-start.1 = ((f32[8,1,18432]{2,1,0:T(1,128)}), f32[8,1,18432]{2,1,0:T(1,128)S(1)}, u32[]{:S(2)}, u32[]{:S(2)}) async-start(f32[8,1,18432]{2,1,0:T(1,128)} %broadcast_in_dim.62), calls=%async_computation.1 | async-start | bytes 1179648 | tf_op jit(solution)/shard_map/all_to_all | solution.py:276
  122.4 10.8 %copy-start.10 = (bf16[128,2048]{1,0:T(8,128)(2,1)S(1)}, bf16[128,2048]{1,0:T(8,128)(2,1)}, u32[]{:S(2)}) copy-start(bf16[128,2048]{1,0:T(8,128)(2,1)} %param.12) | copy-start | bytes 1572868
  122.4 10.8 %copy-start.11 = (bf16[128,2048]{1,0:T(8,128)(2,1)S(1)}, bf16[128,2048]{1,0:T(8,128)(2,1)}, u32[]{:S(2)}) copy-start(bf16[128,2048]{1,0:T(8,128)(2,1)} %param.11) | copy-start | bytes 1572868
  125.0 0.8 copy-start.15

commit v2 on v1

--- a/solution.py
+++ b/solution.py
@@ -170,28 +170,28 @@
 
 def _modal_kernel(dec_ref, wt_ref, ent_ref, loc_ref, out_ref, *, group_size, forward, sub):
     rows = out_ref.shape[0]
-    modes = dec_ref.shape[1]
+    modes = ent_ref.shape[0]
     groups_here = LANES // group_size
-    lane_group = lax.broadcasted_iota(jnp.int32, (rows, LANES), 1) // group_size
-    offsets = lax.broadcasted_iota(jnp.int32, (rows, modes), 0).astype(jnp.float32)
+    width = groups_here * modes
+    offsets = lax.broadcasted_iota(jnp.int32, (rows, width), 0).astype(jnp.float32)
     dist = offsets + 1.0 if forward else float(rows) - offsets
+    row_group = lax.broadcasted_iota(jnp.int32, (width, LANES), 0) // modes
+    lane_group = lax.broadcasted_iota(jnp.int32, (width, LANES), 1) // group_size
 
     def body(j, carry):
         lanes = pl.ds(pl.multiple_of(j * LANES, LANES), LANES)
-        ent_high, ent_low = _split(ent_ref[:, lanes])
-        out_w = []
-        for k in range(groups_here):
-            rate = dec_ref[pl.ds(j * groups_here + k, 1), :]
-            weight = wt_ref[pl.ds(j * groups_here + k, 1), :]
-            out_w.append(weight * jnp.exp(-rate * dist))
-        a_high, a_low = _split(jnp.concatenate(out_w, axis=0))
+        row = pl.program_id(0) * sub + j
+        rate = dec_ref[pl.ds(row, 1), :]
+        weight = wt_ref[pl.ds(row, 1), :]
+        a_high, a_low = _split(weight * jnp.exp(-rate * dist))
+        entering = ent_ref[:, lanes]
+        tiled = jnp.concatenate([entering] * groups_here, axis=0)
+        diag = jnp.where(row_group == lane_group, tiled, 0.0)
+        ent_high, ent_low = _split(diag)
         y = jnp.dot(a_high, ent_high, preferred_element_type=jnp.float32)
         y = y + jnp.dot(a_low, ent_high, preferred_element_type=jnp.float32)
         y = y + jnp.dot(a_high, ent_low, preferred_element_type=jnp.float32)
-        acc = y[:rows]
-        for k in range(1, groups_here):
-            acc = jnp.where(lane_group == k, y[k * rows:(k + 1) * rows], acc)
-        out_ref[:, lanes] = loc_ref[:, lanes] + acc
+        out_ref[:, lanes] = loc_ref[:, lanes] + y
         return carry
 
     lax.fori_loop(0, sub, body, 0)
@@ -202,22 +202,24 @@
     block = min(BLOCK_LANES, chans)
     groups_block = block // group_size
     modes = decays.shape[1]
-    kernel = functools.partial(
-        _modal_kernel, group_size=group_size, forward=forward, sub=block // LANES
-    )
+    per_row = (LANES // group_size) * modes
+    flat_decays = decays.reshape(-1, per_row)
+    flat_weights = weights.reshape(-1, per_row)
+    sub = block // LANES
+    kernel = functools.partial(_modal_kernel, group_size=group_size, forward=forward, sub=sub)
     return pl.pallas_call(
         kernel,
         grid=(chans // block,),
         in_specs=[
-            pl.BlockSpec((groups_block, modes), lambda b: (b, 0)),
-            pl.BlockSpec((groups_block, modes), lambda b: (b, 0)),
+            pl.BlockSpec(flat_decays.shape, lambda b: (0, 0)),
+            pl.BlockSpec(flat_weights.shape, lambda b: (0, 0)),
             pl.BlockSpec((modes, block), lambda b: (0, b)),
             pl.BlockSpec((rows, block), lambda b: (0, b)),
         ],
         out_specs=pl.BlockSpec((rows, block), lambda b: (0, b)),
         out_shape=jax.ShapeDtypeStruct((rows, chans), jnp.float32),
         compiler_params=pltpu.CompilerParams(dimension_semantics=("parallel",)),
-    )(decays, weights, entering, local)
+    )(flat_decays, flat_weights, entering, local)
 
 
 def _gram_kernel(back_ref, top_ref, bot_ref, f_ref, *, group_size, sub):

time: 138 us -> 133 us (0.964)
  Pallas kernels: 66.1 us -> 60.3 us
    pallas_call x2, Pallas kernels: 15.9 us -> 10 us  [modal_out(): pl.pallas_call(kernel, grid=(chans // block,), in_specs=[pl.BlockSpec(fla...]
  transfers between devices with their start and end apart: 4 -> 4, of which waited for: 2 -> 2; matrix products, arithmetic and copies ran while one was open for 14% -> 15% of each run, Pallas kernels for 34% -> 33%
where the time goes in v2:
time: 133 us; the launch traced here: 131 us
  Pallas kernels  60.3 us (45%)
  other arithmetic  23.5 us (18%)
  starting transfers between devices  18.6 us (14%)
  blocking collectives  11.5 us (9%)
  local copies, waits for them, and re-layouts  10.6 us (8%)
  waiting for transfers between devices  4.51 us (3%)
  matrix products  1.78 us (1%)
    pallas_call x4, Pallas kernels, band_conv(): pl.pallas_call(kernel, grid=(chans // block,), in_specs=in_specs, out_spe...  29.8 us
    all_to_all x2, starting transfers between devices, gather_seq(): return lax.all_to_all(tiled, 'seq', split_axis=0, concat_axis=0, tiled=True)  12.4 us
    pallas_call x1, Pallas kernels, gram_diag(): pl.pallas_call(kernel, grid=(chans // block,), in_specs=[pl.BlockSpec((ro...  11.4 us
    pallas_call x2, Pallas kernels, modal_out(): pl.pallas_call(kernel, grid=(chans // block,), in_specs=[pl.BlockSpec(fla...  10 us
    pallas_call x2, Pallas kernels, modal_states(): pl.pallas_call(kernel, grid=(chans // block,), in_specs=[pl.BlockSpec((gr...  9.05 us
    ppermute x2, starting transfers between devices, from_behind(): lax.ppermute(value, axis, [(source, source + steps) for source in range(i...  6.18 us
    psum x1, blocking collectives, on_device(): squares = lax.psum(jnp.sum(out_full * out_full, axis=1), 'chan')  5.87 us
    psum x1, blocking collectives, on_device(): cross_dots = lax.psum(jnp.sum(weighted * out_full, axis=1), 'chan')[:, None]  5.63 us
  transfers between devices with their start and end apart: 4, of which 2 were waited for; matrix products, arithmetic and copies ran while one was open for 15% of the time, Pallas kernels for 33%

profile of v2, /device:TPU:0, one launch (start us, length us, event | category | flops | bytes accessed | tf_op | source)
XLA Modules:
  0.0 131.5 jit_solution(994173744575948532)
XLA Ops:
  0.7 1.4 %fusion.7.refs_2_.bot_ref = bf16[128,2048]{1,0:T(8,128)(2,1)S(1)} fusion(bf16[128,2048]{1,0:T(8,128)(2,1)} %param.12, bf16[128,2048]{1,0:T(8,128)(2,1)} %param.11), kind=kLoop, calls=%fused_computation.22 | loop fusion | flops 1048576 | bytes 1572864 | tf_op jit(solution)/shard_map/convert_element_type | solution.py:322
  2.1 4.9 %collective-permute-start = (bf16[128,2048]{1,0:T(8,128)(2,1)S(1)}, bf16[128,2048]{1,0:T(8,128)(2,1)S(1)}, u32[]{:S(2)}, u32[]{:S(2)}) collective-permute-start(bf16[128,2048]{1,0:T(8,128)(2,1)S(1)} %fusion.7.refs_2_.bot_ref), channel_id=1, source_target_pairs={{0,4},{4,8},{8,12},{12,16},{16,20},{20,24},{24,28},{1,5},{5,9},{9,... | collective-permute-start | bytes 1572872 | tf_op jit(solution)/shard_map/ppermute | solution.py:20
  9.8 1.7 %multiply_exponential_fusion.1 = (f32[128,16,128]{2,1,0:T(8,128)}, f32[128,16,128]{2,1,0:T(8,128)}) fusion(f32[128,16]{1,0:T(8,128)S(1)} %copy.29, f32[128]{0:T(128)S(1)} %iota_subtract_fusion), kind=kLoop, calls=%fused_computation.40 | loop fusion | flops 524288 | bytes 2105856 | tf_op jit(solution)/shard_map/exp | solution.py:341
  11.5 4.6 %shard_map.161 = f32[16,2048]{1,0:T(8,128)} custom-call(f32[128,16,128]{2,1,0:T(8,128)} %get-tuple-element.21.e_ref, bf16[128,2048]{1,0:T(8,128)(2,1)} %fusion.1.x_ref.refs_1_), custom_call_target="tpu_custom_call" | custom-call | tf_op jit(solution)/shard_map/pallas_call | solution.py:158
  18.9 7.5 %shard_map.162 = f32[128,2048]{1,0:T(8,128)} custom-call(f32[128,256]{1,0:T(8,128)} %maximum_maximum_fusion.refs_0_, bf16[128,2048]{1,0:T(8,128)(2,1)} %copy-done.5, bf16[128,2048]{1,0:T(8,128)(2,1)} %copy-done.2), custom_call_target="tpu_custom_call" | custom-call | tf_op jit(solution)/shard_map/pallas_call | solution.py:121
  26.4 1.5 %fusion.9 = (f32[128]{0:T(128)S(1)}, bf16[128,2048]{1,0:T(8,128)(2,1)S(1)}) fusion(f32[128,2048]{1,0:T(8,128)} %shard_map.162, bf16[128,2048]{1,0:T(8,128)(2,1)S(1)} %copy-done.12), kind=kLoop, calls=%fused_computation.24 | loop fusion | flops 1572736 | bytes 2097664 | tf_op jit(solution)/shard_map/reduce_sum | solution.py:327
  27.9 5.9 %psum.14 = f32[128]{0:T(128)S(1)} all-reduce(f32[128]{0:T(128)S(1)} %get-tuple-element.12), channel_id=1, replica_groups=mesh['seq'=8,'chan'=4] {'chan'}, use_global_device_ids=true, to_apply=%region_1.2 | all-reduce | flops 128 | bytes 1024 | tf_op jit(solution)/shard_map/psum | solution.py:327
  34.8 4.5 %shard_map.163 = f32[16,2048]{1,0:T(8,128)} custom-call(f32[128,16,128]{2,1,0:T(8,128)} %get-tuple-element.22.e_ref, bf16[128,2048]{1,0:T(8,128)(2,1)} %fusion.3.x_ref.refs_1_), custom_call_target="tpu_custom_call" | custom-call | tf_op jit(solution)/shard_map/pallas_call | solution.py:158
  41.4 6.6 %all-to-all-start = ((bf16[8,32,2048]{2,1,0:T(8,128)(2,1)}), bf16[8,32,2048]{2,1,0:T(8,128)(2,1)S(1)}, u32[]{:S(2)}, u32[]{:S(2)}) async-start(bf16[8,32,2048]{2,1,0:T(8,128)(2,1)} %broadcast_in_dim.33), calls=%async_computation | async-start | bytes 2097152 | tf_op jit(solution)/shard_map/all_to_all | solution.py:278
  48.9 1.8 %fusion.21 = f32[128,1,128]{2,1,0:T(1,128)} fusion(f32[128,16,1]{1,2,0:T(1,128)S(1)} %copy.31, f32[128,16]{1,0:T(8,128)S(1)} %copy.29), kind=kOutput, calls=%fused_computation.41 | convolution fusion | flops 3407872 | bytes 81920 | tf_op jit(solution)/shard_map/gr,grd->gd/dot_general | solution.py:336
  50.7 7.4 %shard_map.166.loc_ref = f32[128,2048]{1,0:T(8,128)} custom-call(f32[128,128]{1,0:T(8,128)} %bitcast.11, bf16[128,2048]{1,0:T(8,128)(2,1)} %fusion.1.x_ref.refs_1_), custom_call_target="tpu_custom_call" | custom-call | tf_op jit(solution)/shard_map/pallas_call | solution.py:121
  62.2 7.4 %shard_map.164.loc_ref = f32[128,2048]{1,0:T(8,128)} custom-call(f32[128,128]{1,0:T(8,128)} %pad_maximum_fusion.2.refs_0_, bf16[128,2048]{1,0:T(8,128)(2,1)} %fusion.3.x_ref.refs_1_), custom_call_target="tpu_custom_call" | custom-call | tf_op jit(solution)/shard_map/pallas_call | solution.py:121
  69.7 4.1 %all-to-all-done = bf16[8,32,2048]{2,1,0:T(8,128)(2,1)S(1)} async-done(((bf16[8,32,2048]{2,1,0:T(8,128)(2,1)}), bf16[8,32,2048]{2,1,0:T(8,128)(2,1)S(1)}, u32[]{:S(2)}, u32[]{:S(2)}) %all-to-all-start) | async-done | bytes 1048608 | tf_op jit(solution)/shard_map/all_to_all | solution.py:278
  75.2 5.1 %shard_map.167 = f32[128,2048]{1,0:T(8,128)} custom-call(f32[16,128]{1,0:T(8,128)} %reshape.95.dec_ref, f32[16,128]{1,0:T(8,128)} %reshape.96.wt_ref, f32[16,2048]{1,0:T(8,128)} %get-tuple-element.8.ent_ref, f32[128,2048]{1,0:T(8,128)} %shard_map.166.loc_ref), custom_call_target="tpu_custom_call" | custom-call | tf_op jit(solution)/shard_map/pallas_call | solution.py:210
  80.2 2.5 %fusion.18 = (f32[2048]{0:T(1024)S(1)}, f32[128]{0:T(128)S(1)}, bf16[128,2048]{1,0:T(8,128)(2,1)}) fusion(bf16[128,2048]{1,0:T(8,128)(2,1)S(1)} %get-tuple-element.13, f32[128]{0:T(128)S(1)} %get-tuple-element.27, f32[128,2048]{1,0:T(8,128)} %shard_map.167, bf16[128,2048]{1,0:T(8,128)(2,1)S(1)} %copy-done.4, f32[2048]{0:T(1024)S(1)} %copy-done.15), kind=kLoop, calls=%fused_computation.33 | loop fusion | flops 3405696 | bytes 2638848 | tf_op jit(solution)/shard_map/reduce_sum | solution.py:363
  82.8 5.6 %psum.15 = f32[128]{0:T(128)S(1)} all-reduce(f32[128]{0:T(128)S(1)} %get-tuple-element.11), channel_id=1, replica_groups=mesh['seq'=8,'chan'=4] {'chan'}, use_global_device_ids=true, to_apply=%region_5.6 | all-reduce | flops 128 | bytes 1024 | tf_op jit(solution)/shard_map/psum | solution.py:365
  88.4 2.6 %fusion.5 = (bf16[128,2048]{1,0:T(8,128)(2,1)}, bf16[128,2048]{1,0:T(8,128)(2,1)}) fusion(bf16[128,2048]{1,0:T(8,128)(2,1)} %param.10, f32[128]{0:T(128)S(1)} %psum.15, f32[128]{0:T(128)S(1)} %get-tuple-element.26, bf16[128,2048]{1,0:T(8,128)(2,1)S(1)} %get-tuple-element.13, f32[2048]{0:T(1024)S(1)} %copy-done.15, f32[128]{0:T(128)S(1)} %get-tuple-element.27, ...), kind=kLoop, calls=%fused_computation.20 | loop fusion | flops 3670016 | bytes 4728320 | tf_op jit(solution)/shard_map/convert_element_type | solution.py:368
  91.0 1.3 collective-permute-start.1
  92.3 11.4 %shard_map.169 = f32[128,256]{1,0:T(8,128)} custom-call(bf16[128,2048]{1,0:T(8,128)(2,1)} %get-tuple-element.14.refs_1_.back_ref, bf16[128,2048]{1,0:T(8,128)(2,1)} %copy-done.5, bf16[128,2048]{1,0:T(8,128)(2,1)} %copy-done.2), custom_call_target="tpu_custom_call" | custom-call | tf_op jit(solution)/shard_map/pallas_call | solution.py:261
  105.8 5.7 %all-to-all-start.1 = ((f32[8,1,18432]{2,1,0:T(1,128)}), f32[8,1,18432]{2,1,0:T(1,128)S(1)}, u32[]{:S(2)}, u32[]{:S(2)}) async-start(f32[8,1,18432]{2,1,0:T(1,128)} %broadcast_in_dim.62), calls=%async_computation.1 | async-start | bytes 1179648 | tf_op jit(solution)/shard_map/all_to_all | solution.py:278
  111.5 5.0 %shard_map.165 = f32[128,2048]{1,0:T(8,128)} custom-call(f32[16,128]{1,0:T(8,128)} %reshape.95.dec_ref, f32[16,128]{1,0:T(8,128)} %reshape.96.wt_ref, f32[16,2048]{1,0:T(8,128)} %get-tuple-element.9.ent_ref, f32[128,2048]{1,0:T(8,128)} %shard_map.164.loc_ref), custom_call_target="tpu_custom_call" | custom-call | tf_op jit(solution)/shard_map/pallas_call | solution.py:210
  116.5 2.5 %fusion.2 = (bf16[128,2048]{1,0:T(8,128)(2,1)}, bf16[128,2048]{1,0:T(8,128)(2,1)}) fusion(f32[128,2048]{1,0:T(8,128)} %shard_map.165, bf16[128,2048]{1,0:T(8,128)(2,1)S(1)} %copy-done.9, bf16[128,2048]{1,0:T(8,128)(2,1)S(1)} %copy-done.7), kind=kLoop, calls=%fused_computation.17 | loop fusion | flops 1572864 | bytes 3145728 | tf_op jit(solution)/shard_map/convert_element_type | solution.py:360
  119.9 7.5 %shard_map.168 = f32[128,2048]{1,0:T(8,128)} custom-call(f32[128,256]{1,0:T(8,128)} %concatenate.23.refs_0_, bf16[128,2048]{1,0:T(8,128)(2,1)} %get-tuple-element.14.refs_1_.back_ref, bf16[128,2048]{1,0:T(8,128)(2,1)} %copy-done.14), custom_call_target="tpu_custom_call" | custom-call | tf_op jit(solution)/shard_map/pallas_call | solution.py:121
  127.3 2.5 %fusion.6 = (bf16[128,2048]{1,0:T(8,128)(2,1)}, bf16[128,2048]{1,0:T(8,128)(2,1)}) fusion(f32[128,2048]{1,0:T(8,128)} %shard_map.168, bf16[128,2048]{1,0:T(8,128)(2,1)S(1)} %copy-done.11, bf16[128,2048]{1,0:T(8,128)(2,1)S(1)} %copy-done.10), kind=kLoop, calls=%fused_computation.21 | loop fusion | flops 1572864 | bytes 3145728 | tf_op jit(solution)/shard_map/convert_element_type | solution.py:372
  (76 shorter events, 19.8 us)
Async XLA Ops:
  0.6 7.9 %copy-start.6 = (bf16[128,2048]{1,0:T(8,128)(2,1)S(1)}, bf16[128,2048]{1,0:T(8,128)(2,1)}, u32[]{:S(2)}) copy-start(bf16[128,2048]{1,0:T(8,128)(2,1)} %param.13) | copy-start | bytes 1572868
  0.6 7.9 %copy-start.8 = (bf16[128,2048]{1,0:T(8,128)(2,1)S(1)}, bf16[128,2048]{1,0:T(8,128)(2,1)}, u32[]{:S(2)}) copy-start(bf16[128,2048]{1,0:T(8,128)(2,1)} %param.15) | copy-start | bytes 1572868
  2.1 13.9 %copy-start.2 = (bf16[128,2048]{1,0:T(8,128)(2,1)}, bf16[128,2048]{1,0:T(8,128)(2,1)S(1)}, u32[]{:S(2)}) copy-start(bf16[128,2048]{1,0:T(8,128)(2,1)S(1)} %fusion.7.refs_2_.bot_ref) | copy-start | bytes 1572868
  2.1 16.0 %collective-permute-start = (bf16[128,2048]{1,0:T(8,128)(2,1)S(1)}, bf16[128,2048]{1,0:T(8,128)(2,1)S(1)}, u32[]{:S(2)}, u32[]{:S(2)}) collective-permute-start(bf16[128,2048]{1,0:T(8,128)(2,1)S(1)} %fusion.7.refs_2_.bot_ref), channel_id=1, source_target_pairs={{0,4},{4,8},{8,12},{12,16},{16,20},{20,24},{24,28},{1,5},{5,9},{9,... | collective-permute-start | bytes 1572872 | tf_op jit(solution)/shard_map/ppermute | solution.py:20
  11.5 14.9 %copy-start.12 = (bf16[128,2048]{1,0:T(8,128)(2,1)S(1)}, bf16[128,2048]{1,0:T(8,128)(2,1)}, u32[]{:S(2)}) copy-start(bf16[128,2048]{1,0:T(8,128)(2,1)} %param.10) | copy-start | bytes 1572868
  17.7 16.0 %copy-start.3 = (bf16[128,2048]{1,0:T(8,128)(2,1)S(1)}, bf16[128,2048]{1,0:T(8,128)(2,1)}, u32[]{:S(2)}) copy-start(bf16[128,2048]{1,0:T(8,128)(2,1)} %param.14) | copy-start | bytes 1572868
  17.7 16.0 %copy-start.15 = (f32[2048]{0:T(1024)S(1)}, f32[2048]{0:T(1024)}, u32[]{:S(2)}) copy-start(f32[2048]{0:T(1024)} %param.17) | copy-start | bytes 24580
  18.1 0.8 copy-start.5
  39.3 8.7 %copy-start.16 = (f32[128,16]{0,1:T(8,128)S(1)}, f32[128,16]{0,1:T(8,128)}, u32[]{:S(2)}) copy-start(f32[128,16]{0,1:T(8,128)} %param.18) | copy-start | bytes 24580
  41.4 32.4 %all-to-all-start = ((bf16[8,32,2048]{2,1,0:T(8,128)(2,1)}), bf16[8,32,2048]{2,1,0:T(8,128)(2,1)S(1)}, u32[]{:S(2)}, u32[]{:S(2)}) async-start(bf16[8,32,2048]{2,1,0:T(8,128)(2,1)} %broadcast_in_dim.33), calls=%async_computation | async-start | bytes 2097152 | tf_op jit(solution)/shard_map/all_to_all | solution.py:278
  50.7 10.8 %copy-start.13 = (f32[128,1,128]{2,1,0:T(1,128)S(1)}, f32[128,1,128]{2,1,0:T(1,128)}, u32[]{:S(2)}) copy-start(f32[128,1,128]{2,1,0:T(1,128)} %fusion.21) | copy-start | bytes 196612
  74.0 6.2 %copy-start.4 = (bf16[128,2048]{1,0:T(8,128)(2,1)S(1)}, bf16[128,2048]{1,0:T(8,128)(2,1)}, u32[]{:S(2)}) copy-start(bf16[128,2048]{1,0:T(8,128)(2,1)} %param.14) | copy-start | bytes 1572868
  75.2 13.2 %copy-start.1 = (f32[128,2048]{1,0:T(8,128)S(1)}, f32[128,2048]{1,0:T(8,128)}, u32[]{:S(2)}) copy-start(f32[128,2048]{1,0:T(8,128)} %shard_map.162) | copy-start | bytes 3145732
  80.2 8.2 %copy-start = (f32[128,2048]{1,0:T(8,128)S(1)}, f32[128,2048]{1,0:T(8,128)}, u32[]{:S(2)}) copy-start(f32[128,2048]{1,0:T(8,128)} %shard_map.167) | copy-start | bytes 3145732
  91.0 28.1 %collective-permute-start.1 = (bf16[128,2048]{1,0:T(8,128)(2,1)}, bf16[128,2048]{1,0:T(8,128)(2,1)S(1)}, u32[]{:S(2)}, u32[]{:S(2)}) collective-permute-start(bf16[128,2048]{1,0:T(8,128)(2,1)} %get-tuple-element.14.refs_1_.back_ref), channel_id=1, source_target_pairs={{4,0},{8,4},{12,8},{16,12},{20,16},{24,20},{28,24},{5,1},{9,5},{13... | collective-permute-start | bytes 1572872 | tf_op jit(solution)/shard_map/ppermute | solution.py:20
  104.6 11.9 %copy-start.7 = (bf16[128,2048]{1,0:T(8,128)(2,1)S(1)}, bf16[128,2048]{1,0:T(8,128)(2,1)}, u32[]{:S(2)}) copy-start(bf16[128,2048]{1,0:T(8,128)(2,1)} %param.13) | copy-start | bytes 1572868
  104.6 11.9 %copy-start.9 = (bf16[128,2048]{1,0:T(8,128)(2,1)S(1)}, bf16[128,2048]{1,0:T(8,128)(2,1)}, u32[]{:S(2)}) copy-start(bf16[128,2048]{1,0:T(8,128)(2,1)} %param.15) | copy-start | bytes 1572868
  105.8 24.0 %all-to-all-start.1 = ((f32[8,1,18432]{2,1,0:T(1,128)}), f32[8,1,18432]{2,1,0:T(1,128)S(1)}, u32[]{:S(2)}, u32[]{:S(2)}) async-start(f32[8,1,18432]{2,1,0:T(1,128)} %broadcast_in_dim.62), calls=%async_computation.1 | async-start | bytes 1179648 | tf_op jit(solution)/shard_map/all_to_all | solution.py:278
  116.5 10.8 %copy-start.10 = (bf16[128,2048]{1,0:T(8,128)(2,1)S(1)}, bf16[128,2048]{1,0:T(8,128)(2,1)}, u32[]{:S(2)}) copy-start(bf16[128,2048]{1,0:T(8,128)(2,1)} %param.12) | copy-start | bytes 1572868
  116.5 10.8 %copy-start.11 = (bf16[128,2048]{1,0:T(8,128)(2,1)S(1)}, bf16[128,2048]{1,0:T(8,128)(2,1)}, u32[]{:S(2)}) copy-start(bf16[128,2048]{1,0:T(8,128)(2,1)} %param.11) | copy-start | bytes 1572868
  119.1 0.8 copy-start.14

commit v3 on v2

--- a/solution.py
+++ b/solution.py
@@ -319,18 +319,6 @@
     )
     bwd_rows = jnp.concatenate([taps_mr, jnp.zeros_like(taps_mr)], 1)
 
-    mixed_mr = (key_mr.astype(jnp.float32) * value_mr.astype(jnp.float32)).astype(jnp.bfloat16)
-    rim_rows = from_behind(mixed_mr, "seq", 1)
-    conv_mr = band_conv(fwd_rows, rim_rows, mixed_mr, group_size=group_size, split=False, tri=None)
-    out_mr = (query_mr.astype(jnp.float32) * conv_mr).astype(jnp.bfloat16)
-    out_full = out_mr.astype(jnp.float32)
-    squares = lax.psum(jnp.sum(out_full * out_full, axis=1), "chan")
-    inv_rms = lax.rsqrt(squares / D + 1e-06)[:, None]
-    normed = out_full * inv_rms * norm_gain
-    mixed_li = key_li.astype(jnp.float32) * normed
-    cotan_full = cotangent.astype(jnp.float32)
-    back_li = cotan_full * query_li.astype(jnp.float32)
-
     offsets = jnp.arange(row_count, dtype=jnp.float32)
     weights_res = li_residue * jnp.sqrt(2.0 * li_decay)
     taps_li = jnp.einsum(
@@ -340,29 +328,43 @@
     fwd_states = jnp.exp(-li_decay[:, :, None] * (row_count - 1.0 - offsets))
     bwd_states = jnp.exp(-li_decay[:, :, None] * offsets)
 
-    back_li_bf = back_li.astype(jnp.bfloat16)
-    mixed_li_bf = mixed_li.astype(jnp.bfloat16)
-    modes = li_decay.shape[1]
+    cotan_full = cotangent.astype(jnp.float32)
+    back_li_bf = (cotan_full * query_li.astype(jnp.float32)).astype(jnp.bfloat16)
     grad_st = modal_states(bwd_states, back_li_bf, group_size=group_size)
-    conv_st = modal_states(fwd_states, mixed_li_bf, group_size=group_size)
-    both_st = gather_seq(jnp.concatenate([grad_st, conv_st], 0).astype(jnp.bfloat16))
-    both_st = both_st.astype(jnp.float32)
+    grad_gathered = gather_seq(grad_st.astype(jnp.bfloat16)).astype(jnp.float32)
+
+    mixed_mr = (key_mr.astype(jnp.float32) * value_mr.astype(jnp.float32)).astype(jnp.bfloat16)
+    rim_rows = from_behind(mixed_mr, "seq", 1)
     grad_loc = band_conv(taps_li, back_li_bf, group_size=group_size, split=True, tri="upper")
-    conv_loc = band_conv(li_fwd_rows, mixed_li_bf, group_size=group_size, split=True, tri="lower")
-    grad_ent = entering_states(both_st[:, :modes], li_decay, row_count, group_size, False)
-    conv_ent = entering_states(both_st[:, modes:], li_decay, row_count, group_size, True)
+    conv_mr = band_conv(fwd_rows, rim_rows, mixed_mr, group_size=group_size, split=False, tri=None)
+    grad_ent = entering_states(grad_gathered, li_decay, row_count, group_size, False)
     grad_mixed_li = modal_out(
         li_decay, weights_res, grad_ent, grad_loc, group_size=group_size, forward=False
     )
+    out_mr = (query_mr.astype(jnp.float32) * conv_mr).astype(jnp.bfloat16)
+    out_full = out_mr.astype(jnp.float32)
+    key_full = key_li.astype(jnp.float32)
+    grad_normed = grad_mixed_li * key_full
+    weighted = grad_normed * norm_gain
+    row_sums = jnp.stack(
+        [jnp.sum(out_full * out_full, axis=1), jnp.sum(weighted * out_full, axis=1)]
+    )
+    row_sums = lax.psum(row_sums, "chan")
+    squares = row_sums[0]
+    cross_dots = row_sums[1][:, None]
+    inv_rms = lax.rsqrt(squares / D + 1e-06)[:, None]
+    normed = out_full * inv_rms * norm_gain
+    mixed_li_bf = (key_full * normed).astype(jnp.bfloat16)
+    conv_st = modal_states(fwd_states, mixed_li_bf, group_size=group_size)
+    conv_gathered = gather_seq(conv_st.astype(jnp.bfloat16)).astype(jnp.float32)
+    conv_loc = band_conv(li_fwd_rows, mixed_li_bf, group_size=group_size, split=True, tri="lower")
+    conv_ent = entering_states(conv_gathered, li_decay, row_count, group_size, True)
     conv_li = modal_out(li_decay, weights_res, conv_ent, conv_loc, group_size=group_size, forward=True)
 
     out_li = (query_li.astype(jnp.float32) * conv_li).astype(jnp.bfloat16)
     grad_query_li = (cotan_full * conv_li).astype(jnp.bfloat16)
     grad_key_li = (grad_mixed_li * normed).astype(jnp.bfloat16)
-    grad_normed = grad_mixed_li * key_li.astype(jnp.float32)
     gain_part = jnp.sum(grad_normed * out_full * inv_rms, axis=0)
-    weighted = grad_normed * norm_gain
-    cross_dots = lax.psum(jnp.sum(weighted * out_full, axis=1), "chan")[:, None]
     grad_out_mr = inv_rms * weighted - out_full * inv_rms**3 * cross_dots / D
     grad_query_mr = (grad_out_mr * conv_mr).astype(jnp.bfloat16)
     back_mr = (grad_out_mr * query_mr.astype(jnp.float32)).astype(jnp.bfloat16)

time: 133 us -> 136 us (1.023)
  starting transfers between devices: 18.6 us -> 31.8 us
  blocking collectives: 11.5 us -> 6.14 us
  other arithmetic: 23.5 us -> 18.4 us
    all_to_all x2 -> x3, starting transfers between devices: 12.4 us -> 26.5 us  [gather_seq(): return lax.all_to_all(tiled, 'seq', split_axis=0, concat_axis=0, tiled=True)]
    psum x2 -> x1, blocking collectives: 11.5 us -> 6.14 us  [on_device(): row_sums = lax.psum(row_sums, 'chan')]
    another operation x2 -> x1, other arithmetic: 1.84 us -> 0.01 us  [on_device(): jnp.stack([jnp.sum(out_full * out_full, axis=1), jnp.sum(weighted * out_f...]
    reduce_sum x2 -> x1, other arithmetic: 4.01 us -> 2.42 us  [on_device(): jnp.sum(out_full * out_full, axis=1)]
    broadcast_in_dim x2 -> x3, local copies, waits for them, and re-layouts: 2.24 us -> 2.81 us  [gather_seq(): tiled = jnp.broadcast_to(value[None], (count,) + value.shape)]
    all_to_all x2 -> x3, waiting for transfers between devices: 4.08 us -> 4.16 us  [gather_seq(): return lax.all_to_all(tiled, 'seq', split_axis=0, concat_axis=0, tiled=True)]
  transfers between devices with their start and end apart: 4 -> 5, of which waited for: 2 -> 1; matrix products, arithmetic and copies ran while one was open for 15% -> 9% of each run, Pallas kernels for 33% -> 34%
where the time goes in v3:
time: 136 us; the launch traced here: 135 us
  Pallas kernels  60.6 us (45%)
  starting transfers between devices  31.8 us (23%)
  other arithmetic  18.4 us (14%)
  local copies, waits for them, and re-layouts  11 us (8%)
  blocking collectives  6.14 us (5%)
  waiting for transfers between devices  4.17 us (3%)
  matrix products  1.78 us (1%)
    pallas_call x4, Pallas kernels, band_conv(): pl.pallas_call(kernel, grid=(chans // block,), in_specs=in_specs, out_spe...  29.8 us
    all_to_all x3, starting transfers between devices, gather_seq(): return lax.all_to_all(tiled, 'seq', split_axis=0, concat_axis=0, tiled=True)  26.5 us
    pallas_call x1, Pallas kernels, gram_diag(): pl.pallas_call(kernel, grid=(chans // block,), in_specs=[pl.BlockSpec((ro...  11.4 us
    pallas_call x2, Pallas kernels, modal_out(): pl.pallas_call(kernel, grid=(chans // block,), in_specs=[pl.BlockSpec(fla...  10.2 us
    pallas_call x2, Pallas kernels, modal_states(): pl.pallas_call(kernel, grid=(chans // block,), in_specs=[pl.BlockSpec((gr...  9.18 us
    psum x1, blocking collectives, on_device(): row_sums = lax.psum(row_sums, 'chan')  6.14 us
    ppermute x2, starting transfers between devices, from_behind(): lax.ppermute(value, axis, [(source, source + steps) for source in range(i...  5.24 us
    all_to_all x3, waiting for transfers between devices, gather_seq(): return lax.all_to_all(tiled, 'seq', split_axis=0, concat_axis=0, tiled=True)  4.16 us
  transfers between devices with their start and end apart: 5, of which 1 were waited for; matrix products, arithmetic and copies ran while one was open for 9% of the time, Pallas kernels for 34%

profile of v3, /device:TPU:0, one launch (start us, length us, event | category | flops | bytes accessed | tf_op | source)
XLA Modules:
  0.0 134.7 jit_solution(6201579390145064884)
XLA Ops:
  1.5 1.7 %multiply_exponential_fusion = (f32[128,16,128]{2,1,0:T(8,128)}, f32[128,16,128]{2,1,0:T(8,128)}) fusion(f32[128,16]{1,0:T(8,128)S(1)} %copy.29, f32[128]{0:T(128)S(1)} %iota_subtract_fusion), kind=kLoop, calls=%fused_computation.37 | loop fusion | flops 524288 | bytes 2105856 | tf_op jit(solution)/shard_map/exp | solution.py:329
  4.1 4.5 %shard_map.162 = f32[16,2048]{1,0:T(8,128)} custom-call(f32[128,16,128]{2,1,0:T(8,128)} %get-tuple-element.22.e_ref, bf16[128,2048]{1,0:T(8,128)(2,1)} %fusion.7.x_ref.refs_1_), custom_call_target="tpu_custom_call" | custom-call | tf_op jit(solution)/shard_map/pallas_call | solution.py:158
  10.3 7.4 %all-to-all-start = ((bf16[8,16,2048]{2,1,0:T(8,128)(2,1)}), bf16[8,16,2048]{2,1,0:T(8,128)(2,1)S(1)}, u32[]{:S(2)}, u32[]{:S(2)}) async-start(bf16[8,16,2048]{2,1,0:T(8,128)(2,1)} %broadcast_in_dim.36), calls=%async_computation | async-start | bytes 1048576 | tf_op jit(solution)/shard_map/all_to_all | solution.py:278
  17.9 4.0 %collective-permute-start = (bf16[128,2048]{1,0:T(8,128)(2,1)S(1)}, bf16[128,2048]{1,0:T(8,128)(2,1)S(1)}, u32[]{:S(2)}, u32[]{:S(2)}) collective-permute-start(bf16[128,2048]{1,0:T(8,128)(2,1)S(1)} %fusion.5.refs_2_.bot_ref), channel_id=1, source_target_pairs={{0,4},{4,8},{8,12},{12,16},{16,20},{20,24},{24,28},{1,5},{5,9},{9,... | collective-permute-start | bytes 1572872 | tf_op jit(solution)/shard_map/ppermute | solution.py:20
  22.0 1.8 %fusion.19 = f32[128,1,128]{2,1,0:T(1,128)} fusion(f32[128,16,1]{1,2,0:T(1,128)S(1)} %copy.31, f32[128,16]{1,0:T(8,128)S(1)} %copy.29), kind=kOutput, calls=%fused_computation.39 | convolution fusion | flops 3407872 | bytes 81920 | tf_op jit(solution)/shard_map/gr,grd->gd/dot_general | solution.py:324
  27.0 7.4 %shard_map.163.loc_ref = f32[128,2048]{1,0:T(8,128)} custom-call(f32[128,128]{1,0:T(8,128)} %bitcast.18, bf16[128,2048]{1,0:T(8,128)(2,1)} %fusion.7.x_ref.refs_1_), custom_call_target="tpu_custom_call" | custom-call | tf_op jit(solution)/shard_map/pallas_call | solution.py:121
  36.2 7.5 %shard_map.161 = f32[128,2048]{1,0:T(8,128)} custom-call(f32[128,256]{1,0:T(8,128)} %maximum_maximum_fusion.refs_0_, bf16[128,2048]{1,0:T(8,128)(2,1)} %copy-done.5, bf16[128,2048]{1,0:T(8,128)(2,1)} %copy-done.2), custom_call_target="tpu_custom_call" | custom-call | tf_op jit(solution)/shard_map/pallas_call | solution.py:121
  43.6 1.0 multiply_reduce_fusion.1.ent_ref
  44.6 5.1 %shard_map.164 = f32[128,2048]{1,0:T(8,128)} custom-call(f32[16,128]{1,0:T(8,128)} %reshape.97.dec_ref, f32[16,128]{1,0:T(8,128)} %reshape.98.wt_ref, f32[16,2048]{1,0:T(8,128)} %multiply_reduce_fusion.1.ent_ref, f32[128,2048]{1,0:T(8,128)} %shard_map.163.loc_ref), custom_call_target="tpu_custom_call" | custom-call | tf_op jit(solution)/shard_map/pallas_call | solution.py:210
  49.8 2.4 %fusion.9 = (f32[128]{0:T(128)S(1)}, f32[128]{0:T(128)S(1)}, bf16[128,2048]{1,0:T(8,128)(2,1)}) fusion(f32[2048]{0:T(1024)S(1)} %copy-done.19, f32[128,2048]{1,0:T(8,128)} %shard_map.164, bf16[128,2048]{1,0:T(8,128)(2,1)S(1)} %copy-done.7, f32[128,2048]{1,0:T(8,128)S(1)} %copy-done, bf16[128,2048]{1,0:T(8,128)(2,1)S(1)} %copy-done.6), kind=kLoop, calls=%fused_computation.24 | loop fusion | flops 2883328 | bytes 3679232 | tf_op jit(solution)/shard_map/reduce_sum | solution.py:350
  52.2 6.1 %psum.7 = f32[2,128]{1,0:T(2,128)S(1)} all-reduce(f32[2,128]{1,0:T(2,128)S(1)} %pad_maximum_fusion.2), channel_id=1, replica_groups=mesh['seq'=8,'chan'=4] {'chan'}, use_global_device_ids=true, to_apply=%region_3.4 | all-reduce | flops 256 | bytes 2048 | tf_op jit(solution)/shard_map/psum | solution.py:352
  58.4 3.1 %fusion.3 = (bf16[128,2048]{1,0:T(8,128)(2,1)S(1)}, bf16[128,2048]{1,0:T(8,128)(2,1)}, f32[2048]{0:T(1024)S(1)}, bf16[128,2048]{1,0:T(8,128)(2,1)}, bf16[128,2048]{1,0:T(8,128)(2,1)}) fusion(bf16[128,2048]{1,0:T(8,128)(2,1)S(1)} %copy-done.6, f32[128]{0:T(128)S(1)} %slice_bitcast_fusion.1, f32[128]{0:T(128)S(1)} %get-tuple-element.10, ...), kind=kLoop, calls=%fused_computation.18 | loop fusion | flops 6027264 | bytes 5785088 | tf_op jit(solution)/shard_map/convert_element_type | solution.py:370
  61.5 4.7 %shard_map.165 = f32[16,2048]{1,0:T(8,128)} custom-call(f32[128,16,128]{2,1,0:T(8,128)} %get-tuple-element.23.e_ref, bf16[128,2048]{1,0:T(8,128)(2,1)} %get-tuple-element.17.x_ref.refs_1_), custom_call_target="tpu_custom_call" | custom-call | tf_op jit(solution)/shard_map/pallas_call | solution.py:158
  67.9 11.8 %all-to-all-start.1 = ((bf16[8,16,2048]{2,1,0:T(8,128)(2,1)}), bf16[8,16,2048]{2,1,0:T(8,128)(2,1)S(1)}, u32[]{:S(2)}, u32[]{:S(2)}) async-start(bf16[8,16,2048]{2,1,0:T(8,128)(2,1)} %broadcast_in_dim.37), calls=%async_computation.1 | async-start | bytes 1048576 | tf_op jit(solution)/shard_map/all_to_all | solution.py:278
  80.6 1.3 collective-permute-start.1
  82.6 7.4 %shard_map.166.loc_ref = f32[128,2048]{1,0:T(8,128)} custom-call(f32[128,128]{1,0:T(8,128)} %pad_maximum_fusion.1.refs_0_, bf16[128,2048]{1,0:T(8,128)(2,1)} %get-tuple-element.17.x_ref.refs_1_), custom_call_target="tpu_custom_call" | custom-call | tf_op jit(solution)/shard_map/pallas_call | solution.py:121
  90.0 11.4 %shard_map.169 = f32[128,256]{1,0:T(8,128)} custom-call(bf16[128,2048]{1,0:T(8,128)(2,1)} %copy-done.3, bf16[128,2048]{1,0:T(8,128)(2,1)} %copy-done.5, bf16[128,2048]{1,0:T(8,128)(2,1)} %copy-done.2), custom_call_target="tpu_custom_call" | custom-call | tf_op jit(solution)/shard_map/pallas_call | solution.py:261
  103.1 7.5 %shard_map.168 = f32[128,2048]{1,0:T(8,128)} custom-call(f32[128,256]{1,0:T(8,128)} %concatenate.14.refs_0_, bf16[128,2048]{1,0:T(8,128)(2,1)} %copy-done.3, bf16[128,2048]{1,0:T(8,128)(2,1)} %copy-done.17), custom_call_target="tpu_custom_call" | custom-call | tf_op jit(solution)/shard_map/pallas_call | solution.py:121
  110.6 1.1 broadcast_in_dim.68
  111.8 7.3 %all-to-all-start.2 = ((f32[8,1,18432]{2,1,0:T(1,128)}), f32[8,1,18432]{2,1,0:T(1,128)S(1)}, u32[]{:S(2)}, u32[]{:S(2)}) async-start(f32[8,1,18432]{2,1,0:T(1,128)} %broadcast_in_dim.68), calls=%async_computation.2 | async-start | bytes 1179648 | tf_op jit(solution)/shard_map/all_to_all | solution.py:278
  119.1 1.2 fusion.4
  121.3 5.1 %shard_map.167 = f32[128,2048]{1,0:T(8,128)} custom-call(f32[16,128]{1,0:T(8,128)} %reshape.97.dec_ref, f32[16,128]{1,0:T(8,128)} %reshape.98.wt_ref, f32[16,2048]{1,0:T(8,128)} %multiply_reduce_fusion.ent_ref, f32[128,2048]{1,0:T(8,128)} %shard_map.166.loc_ref), custom_call_target="tpu_custom_call" | custom-call | tf_op jit(solution)/shard_map/pallas_call | solution.py:210
  126.4 2.5 %fusion.8 = (bf16[128,2048]{1,0:T(8,128)(2,1)}, bf16[128,2048]{1,0:T(8,128)(2,1)}) fusion(f32[128,2048]{1,0:T(8,128)} %shard_map.167, bf16[128,2048]{1,0:T(8,128)(2,1)S(1)} %copy-done.15, bf16[128,2048]{1,0:T(8,128)(2,1)S(1)} %copy-done.13), kind=kLoop, calls=%fused_computation.23 | loop fusion | flops 1572864 | bytes 3145728 | tf_op jit(solution)/shard_map/convert_element_type | solution.py:365
  128.9 4.2 %all-to-all-done.2 = f32[8,1,18432]{2,1,0:T(1,128)S(1)} async-done(((f32[8,1,18432]{2,1,0:T(1,128)}), f32[8,1,18432]{2,1,0:T(1,128)S(1)}, u32[]{:S(2)}, u32[]{:S(2)}) %all-to-all-start.2) | async-done | bytes 589856 | tf_op jit(solution)/shard_map/all_to_all | solution.py:278
  (88 shorter events, 16.4 us)
Async XLA Ops:
  1.5 1.7 %copy-start.12 = (bf16[128,2048]{1,0:T(8,128)(2,1)S(1)}, bf16[128,2048]{1,0:T(8,128)(2,1)}, u32[]{:S(2)}) copy-start(bf16[128,2048]{1,0:T(8,128)(2,1)} %param.13) | copy-start | bytes 1572868
  1.5 1.7 %copy-start.14 = (bf16[128,2048]{1,0:T(8,128)(2,1)S(1)}, bf16[128,2048]{1,0:T(8,128)(2,1)}, u32[]{:S(2)}) copy-start(bf16[128,2048]{1,0:T(8,128)(2,1)} %param.15) | copy-start | bytes 1572868
  10.3 7.4 %copy-start.8 = (bf16[128,2048]{1,0:T(8,128)(2,1)S(1)}, bf16[128,2048]{1,0:T(8,128)(2,1)}, u32[]{:S(2)}) copy-start(bf16[128,2048]{1,0:T(8,128)(2,1)} %param.12) | copy-start | bytes 1572868
  10.3 7.4 %copy-start.10 = (bf16[128,2048]{1,0:T(8,128)(2,1)S(1)}, bf16[128,2048]{1,0:T(8,128)(2,1)}, u32[]{:S(2)}) copy-start(bf16[128,2048]{1,0:T(8,128)(2,1)} %param.11) | copy-start | bytes 1572868
  10.3 33.3 %all-to-all-start = ((bf16[8,16,2048]{2,1,0:T(8,128)(2,1)}), bf16[8,16,2048]{2,1,0:T(8,128)(2,1)S(1)}, u32[]{:S(2)}, u32[]{:S(2)}) async-start(bf16[8,16,2048]{2,1,0:T(8,128)(2,1)} %broadcast_in_dim.36), calls=%async_computation | async-start | bytes 1048576 | tf_op jit(solution)/shard_map/all_to_all | solution.py:278
  17.9 5.9 %copy-start.2 = (bf16[128,2048]{1,0:T(8,128)(2,1)}, bf16[128,2048]{1,0:T(8,128)(2,1)S(1)}, u32[]{:S(2)}) copy-start(bf16[128,2048]{1,0:T(8,128)(2,1)S(1)} %fusion.5.refs_2_.bot_ref) | copy-start | bytes 1572868
  17.9 17.4 %collective-permute-start = (bf16[128,2048]{1,0:T(8,128)(2,1)S(1)}, bf16[128,2048]{1,0:T(8,128)(2,1)S(1)}, u32[]{:S(2)}, u32[]{:S(2)}) collective-permute-start(bf16[128,2048]{1,0:T(8,128)(2,1)S(1)} %fusion.5.refs_2_.bot_ref), channel_id=1, source_target_pairs={{0,4},{4,8},{8,12},{12,16},{16,20},{20,24},{24,28},{1,5},{5,9},{9,... | collective-permute-start | bytes 1572872 | tf_op jit(solution)/shard_map/ppermute | solution.py:20
  22.0 1.8 %copy-start.18 = (f32[128,128]{1,0:T(8,128)S(1)}, f32[128,128]{1,0:T(8,128)}, u32[]{:S(2)}) copy-start(f32[128,128]{1,0:T(8,128)} %param.16) | copy-start | bytes 196612
  44.6 5.2 %copy-start = (f32[128,2048]{1,0:T(8,128)S(1)}, f32[128,2048]{1,0:T(8,128)}, u32[]{:S(2)}) copy-start(f32[128,2048]{1,0:T(8,128)} %shard_map.161) | copy-start | bytes 3145732
  44.6 5.2 %copy-start.6 = (bf16[128,2048]{1,0:T(8,128)(2,1)S(1)}, bf16[128,2048]{1,0:T(8,128)(2,1)}, u32[]{:S(2)}) copy-start(bf16[128,2048]{1,0:T(8,128)(2,1)} %param.10) | copy-start | bytes 1572868
  44.6 5.2 %copy-start.7 = (bf16[128,2048]{1,0:T(8,128)(2,1)S(1)}, bf16[128,2048]{1,0:T(8,128)(2,1)}, u32[]{:S(2)}) copy-start(bf16[128,2048]{1,0:T(8,128)(2,1)} %param.14) | copy-start | bytes 1572868
  44.6 5.2 %copy-start.19 = (f32[2048]{0:T(1024)S(1)}, f32[2048]{0:T(1024)}, u32[]{:S(2)}) copy-start(f32[2048]{0:T(1024)} %param.17) | copy-start | bytes 24580
  49.8 8.6 %copy-start.1 = (f32[128,2048]{1,0:T(8,128)S(1)}, f32[128,2048]{1,0:T(8,128)}, u32[]{:S(2)}) copy-start(f32[128,2048]{1,0:T(8,128)} %shard_map.164) | copy-start | bytes 3145732
  61.5 19.1 %copy-start.3 = (bf16[128,2048]{1,0:T(8,128)(2,1)}, bf16[128,2048]{1,0:T(8,128)(2,1)S(1)}, u32[]{:S(2)}) copy-start(bf16[128,2048]{1,0:T(8,128)(2,1)S(1)} %get-tuple-element.13.refs_1_.back_ref) | copy-start | bytes 1572868
  67.9 11.8 %copy-start.16 = (f32[128,1,128]{2,1,0:T(1,128)S(1)}, f32[128,1,128]{2,1,0:T(1,128)}, u32[]{:S(2)}) copy-start(f32[128,1,128]{2,1,0:T(1,128)} %fusion.19) | copy-start | bytes 196612
  67.9 42.7 %all-to-all-start.1 = ((bf16[8,16,2048]{2,1,0:T(8,128)(2,1)}), bf16[8,16,2048]{2,1,0:T(8,128)(2,1)S(1)}, u32[]{:S(2)}, u32[]{:S(2)}) async-start(bf16[8,16,2048]{2,1,0:T(8,128)(2,1)} %broadcast_in_dim.37), calls=%async_computation.1 | async-start | bytes 1048576 | tf_op jit(solution)/shard_map/all_to_all | solution.py:278
  80.6 21.8 %collective-permute-start.1 = (bf16[128,2048]{1,0:T(8,128)(2,1)S(1)}, bf16[128,2048]{1,0:T(8,128)(2,1)S(1)}, u32[]{:S(2)}, u32[]{:S(2)}) collective-permute-start(bf16[128,2048]{1,0:T(8,128)(2,1)S(1)} %get-tuple-element.13.refs_1_.back_ref), channel_id=1, source_target_pairs={{4,0},{8,4},{12,8},{16,12},{20,16},{24,20},{28,24},{5,1},{9,5},{13... | collective-permute-start | bytes 1572872 | tf_op jit(solution)/shard_map/ppermute | solution.py:20
  101.4 0.8 slice-start
  103.1 16.0 %copy-start.11 = (bf16[128,2048]{1,0:T(8,128)(2,1)S(1)}, bf16[128,2048]{1,0:T(8,128)(2,1)}, u32[]{:S(2)}) copy-start(bf16[128,2048]{1,0:T(8,128)(2,1)} %param.11) | copy-start | bytes 1572868
  110.6 8.5 %copy-start.4 = (f32[128,2048]{1,0:T(8,128)S(1)}, f32[128,2048]{1,0:T(8,128)}, u32[]{:S(2)}) copy-start(f32[128,2048]{1,0:T(8,128)} %shard_map.168) | copy-start | bytes 3145732
  111.8 7.4 %copy-start.9 = (bf16[128,2048]{1,0:T(8,128)(2,1)S(1)}, bf16[128,2048]{1,0:T(8,128)(2,1)}, u32[]{:S(2)}) copy-start(bf16[128,2048]{1,0:T(8,128)(2,1)} %param.12) | copy-start | bytes 1572868
  111.8 21.3 %all-to-all-start.2 = ((f32[8,1,18432]{2,1,0:T(1,128)}), f32[8,1,18432]{2,1,0:T(1,128)S(1)}, u32[]{:S(2)}, u32[]{:S(2)}) async-start(f32[8,1,18432]{2,1,0:T(1,128)} %broadcast_in_dim.68), calls=%async_computation.2 | async-start | bytes 1179648 | tf_op jit(solution)/shard_map/all_to_all | solution.py:278
  121.3 5.1 %copy-start.13 = (bf16[128,2048]{1,0:T(8,128)(2,1)S(1)}, bf16[128,2048]{1,0:T(8,128)(2,1)}, u32[]{:S(2)}) copy-start(bf16[128,2048]{1,0:T(8,128)(2,1)} %param.13) | copy-start | bytes 1572868
  121.3 5.1 %copy-start.15 = (bf16[128,2048]{1,0:T(8,128)(2,1)S(1)}, bf16[128,2048]{1,0:T(8,128)(2,1)}, u32[]{:S(2)}) copy-start(bf16[128,2048]{1,0:T(8,128)(2,1)} %param.15) | copy-start | bytes 1572868
  (3 other events, 2.3 us)

commit v4 on v3

--- a/solution.py
+++ b/solution.py
@@ -356,28 +356,35 @@
     normed = out_full * inv_rms * norm_gain
     mixed_li_bf = (key_full * normed).astype(jnp.bfloat16)
     conv_st = modal_states(fwd_states, mixed_li_bf, group_size=group_size)
-    conv_gathered = gather_seq(conv_st.astype(jnp.bfloat16)).astype(jnp.float32)
     conv_loc = band_conv(li_fwd_rows, mixed_li_bf, group_size=group_size, split=True, tri="lower")
-    conv_ent = entering_states(conv_gathered, li_decay, row_count, group_size, True)
-    conv_li = modal_out(li_decay, weights_res, conv_ent, conv_loc, group_size=group_size, forward=True)
-
-    out_li = (query_li.astype(jnp.float32) * conv_li).astype(jnp.bfloat16)
-    grad_query_li = (cotan_full * conv_li).astype(jnp.bfloat16)
+
     grad_key_li = (grad_mixed_li * normed).astype(jnp.bfloat16)
     gain_part = jnp.sum(grad_normed * out_full * inv_rms, axis=0)
     grad_out_mr = inv_rms * weighted - out_full * inv_rms**3 * cross_dots / D
     grad_query_mr = (grad_out_mr * conv_mr).astype(jnp.bfloat16)
     back_mr = (grad_out_mr * query_mr.astype(jnp.float32)).astype(jnp.bfloat16)
     after_rim = from_behind(back_mr, "seq", -1)
+    diag_sums = gram_diag(back_mr, rim_rows, mixed_mr, group_size=group_size)
+    filter_part = jnp.flip(diag_sums[:, tap_count:], 1)
+    params = jnp.concatenate([gain_part, filter_part.reshape(-1)])
+    params_high = params.astype(jnp.bfloat16)
+    params_low = (params - params_high.astype(jnp.float32)).astype(jnp.bfloat16)
+    state_len = conv_st.size
+    packed = jnp.concatenate([conv_st.reshape(-1).astype(jnp.bfloat16), params_high, params_low])
+    gathered = gather_seq(packed).astype(jnp.float32)
+    conv_gathered = gathered[:, :state_len].reshape((-1,) + conv_st.shape)
+    param_count = params.shape[0]
+    param_rows = gathered[:, state_len:state_len + param_count] + gathered[:, state_len + param_count:]
+    param_sums = jnp.sum(param_rows, axis=0) * grad_scale
+    grad_gain = param_sums[:chan_count]
+    grad_filter = param_sums[chan_count:].reshape(group_count, tap_count)
     grad_mixed_mr = band_conv(bwd_rows, back_mr, after_rim, group_size=group_size, split=False, tri=None)
     grad_key_mr = (grad_mixed_mr * value_mr.astype(jnp.float32)).astype(jnp.bfloat16)
     grad_value_mr = (grad_mixed_mr * key_mr.astype(jnp.float32)).astype(jnp.bfloat16)
-    diag_sums = gram_diag(back_mr, rim_rows, mixed_mr, group_size=group_size)
-    filter_part = jnp.flip(diag_sums[:, tap_count:], 1)
-    packed = jnp.concatenate([gain_part, filter_part.reshape(-1)])
-    param_sums = jnp.sum(gather_seq(packed), axis=0) * grad_scale
-    grad_gain = param_sums[:chan_count]
-    grad_filter = param_sums[chan_count:].reshape(group_count, tap_count)
+    conv_ent = entering_states(conv_gathered, li_decay, row_count, group_size, True)
+    conv_li = modal_out(li_decay, weights_res, conv_ent, conv_loc, group_size=group_size, forward=True)
+    out_li = (query_li.astype(jnp.float32) * conv_li).astype(jnp.bfloat16)
+    grad_query_li = (cotan_full * conv_li).astype(jnp.bfloat16)
     return (
         out_li,
         grad_query_mr,

time: 136 us -> 170 us (1.25)
  the two profiles are of different devices: /device:TPU:0 before, /device:TPU:12 now
where the time goes in v4:
time: 170 us; the launch traced here: 169 us
  Pallas kernels  60.2 us (35%)
  waiting for transfers between devices  30.9 us (18%)
  other arithmetic  29.5 us (17%)
  local copies, waits for them, and re-layouts  19.9 us (12%)
  starting transfers between devices  18.4 us (11%)
  blocking collectives  7.04 us (4%)
  matrix products  1.78 us (1%)
    ppermute x2, waiting for transfers between devices, from_behind(): lax.ppermute(value, axis, [(source, source + steps) for source in range(i...  30.9 us
    pallas_call x4, Pallas kernels, band_conv(): pl.pallas_call(kernel, grid=(chans // block,), in_specs=in_specs, out_spe...  29.8 us
    all_to_all x2, starting transfers between devices, gather_seq(): return lax.all_to_all(tiled, 'seq', split_axis=0, concat_axis=0, tiled=True)  12.3 us
    pallas_call x1, Pallas kernels, gram_diag(): pl.pallas_call(kernel, grid=(chans // block,), in_specs=[pl.BlockSpec((ro...  11.4 us
    unnamed x37, local copies, waits for them, and re-layouts  10.6 us
    pallas_call x2, Pallas kernels, modal_out(): pl.pallas_call(kernel, grid=(chans // block,), in_specs=[pl.BlockSpec(fla...  9.99 us
    pallas_call x2, Pallas kernels, modal_states(): pl.pallas_call(kernel, grid=(chans // block,), in_specs=[pl.BlockSpec((gr...  9.09 us
    broadcast_in_dim x1, other arithmetic, gather_seq(): tiled = jnp.broadcast_to(value[None], (count,) + value.shape)  8.46 us
  transfers between devices with their start and end apart: 4, of which 2 were waited for; matrix products, arithmetic and copies ran while one was open for 6% of the time, Pallas kernels for 18%

profile of v4, /device:TPU:12, one launch (start us, length us, event | category | flops | bytes accessed | tf_op | source)
XLA Modules:
  0.0 168.6 jit_solution(9213235481312155800)
XLA Ops:
  1.5 2.1 %fusion.7.x_ref.refs_1_ = bf16[128,2048]{1,0:T(8,128)(2,1)} fusion(bf16[128,2048]{1,0:T(8,128)(2,1)} %param.13, bf16[128,2048]{1,0:T(8,128)(2,1)} %param.15), kind=kLoop, calls=%fused_computation.23 | loop fusion | flops 1048576 | bytes 1572864 | tf_op jit(solution)/shard_map/convert_element_type | solution.py:332
  5.3 4.6 %shard_map.162 = f32[16,2048]{1,0:T(8,128)} custom-call(f32[128,16,128]{2,1,0:T(8,128)} %get-tuple-element.23.e_ref, bf16[128,2048]{1,0:T(8,128)(2,1)} %fusion.7.x_ref.refs_1_), custom_call_target="tpu_custom_call" | custom-call | tf_op jit(solution)/shard_map/pallas_call | solution.py:158
  11.7 6.2 %all-to-all-start = ((bf16[8,16,2048]{2,1,0:T(8,128)(2,1)}), bf16[8,16,2048]{2,1,0:T(8,128)(2,1)S(1)}, u32[]{:S(2)}, u32[]{:S(2)}) async-start(bf16[8,16,2048]{2,1,0:T(8,128)(2,1)} %broadcast_in_dim.63), calls=%async_computation | async-start | bytes 1048576 | tf_op jit(solution)/shard_map/all_to_all | solution.py:278
  18.1 3.4 %collective-permute-start = (bf16[128,2048]{1,0:T(8,128)(2,1)S(1)}, bf16[128,2048]{1,0:T(8,128)(2,1)S(1)}, u32[]{:S(2)}, u32[]{:S(2)}) collective-permute-start(bf16[128,2048]{1,0:T(8,128)(2,1)S(1)} %fusion.5.refs_2_.bot_ref), channel_id=1, source_target_pairs={{0,4},{4,8},{8,12},{12,16},{16,20},{20,24},{24,28},{1,5},{5,9},{9,... | collective-permute-start | bytes 1572872 | tf_op jit(solution)/shard_map/ppermute | solution.py:20
  25.1 7.4 %shard_map.163.loc_ref = f32[128,2048]{1,0:T(8,128)} custom-call(f32[128,128]{1,0:T(8,128)} %bitcast.26, bf16[128,2048]{1,0:T(8,128)(2,1)} %fusion.7.x_ref.refs_1_), custom_call_target="tpu_custom_call" | custom-call | tf_op jit(solution)/shard_map/pallas_call | solution.py:121
  34.2 6.1 %collective-permute-done.refs_1_.top_ref = bf16[128,2048]{1,0:T(8,128)(2,1)S(1)} collective-permute-done((bf16[128,2048]{1,0:T(8,128)(2,1)S(1)}, bf16[128,2048]{1,0:T(8,128)(2,1)S(1)}, u32[]{:S(2)}, u32[]{:S(2)}) %collective-permute-start) | collective-permute-done | bytes 524320 | tf_op jit(solution)/shard_map/ppermute | solution.py:20
  41.1 7.4 %shard_map.161 = f32[128,2048]{1,0:T(8,128)} custom-call(f32[128,256]{1,0:T(8,128)} %maximum_maximum_fusion.refs_0_, bf16[128,2048]{1,0:T(8,128)(2,1)} %copy-done.4, bf16[128,2048]{1,0:T(8,128)(2,1)} %copy-done.2), custom_call_target="tpu_custom_call" | custom-call | tf_op jit(solution)/shard_map/pallas_call | solution.py:121
  49.5 5.0 %shard_map.164 = f32[128,2048]{1,0:T(8,128)} custom-call(f32[16,128]{1,0:T(8,128)} %reshape.106.dec_ref, f32[16,128]{1,0:T(8,128)} %reshape.107.wt_ref, f32[16,2048]{1,0:T(8,128)} %multiply_reduce_fusion.ent_ref, f32[128,2048]{1,0:T(8,128)} %shard_map.163.loc_ref), custom_call_target="tpu_custom_call" | custom-call | tf_op jit(solution)/shard_map/pallas_call | solution.py:210
  54.6 2.7 %fusion.9 = (f32[128]{0:T(128)S(1)}, f32[128]{0:T(128)S(1)}, bf16[128,2048]{1,0:T(8,128)(2,1)}) fusion(f32[2048]{0:T(1024)S(1)} %copy-done.14, f32[128,2048]{1,0:T(8,128)} %shard_map.164, bf16[128,2048]{1,0:T(8,128)(2,1)} %param.14, f32[128,2048]{1,0:T(8,128)S(1)} %copy-done, bf16[128,2048]{1,0:T(8,128)(2,1)} %param.10), kind=kLoop, calls=%fused_computation.25 | loop fusion | flops 2883328 | bytes 3679232 | tf_op jit(solution)/shard_map/reduce_sum | solution.py:350
  57.3 7.0 %psum.7 = f32[2,128]{1,0:T(2,128)S(1)} all-reduce(f32[2,128]{1,0:T(2,128)S(1)} %pad_maximum_fusion.3), channel_id=1, replica_groups=mesh['seq'=8,'chan'=4] {'chan'}, use_global_device_ids=true, to_apply=%region_3.4 | all-reduce | flops 256 | bytes 2048 | tf_op jit(solution)/shard_map/psum | solution.py:352
  64.4 3.7 %multiply_convert_fusion = (bf16[128,2048]{1,0:T(8,128)(2,1)}, bf16[128,2048]{1,0:T(8,128)(2,1)}, f32[2048]{0:T(1024)S(1)}, bf16[128,2048]{1,0:T(8,128)(2,1)}, bf16[128,2048]{1,0:T(8,128)(2,1)}) fusion(f32[128,2048]{1,0:T(8,128)S(1)} %copy-done, f32[128]{0:T(128)S(1)} %slice_bitcast_fusion.1, f32[128]{0:T(128)S(1)} %get-tuple-element.10, ...), kind=kLoop, calls=%fused_computation.37 | loop fusion | flops 6027264 | bytes 5785088 | tf_op jit(solution)/shard_map/convert_element_type | solution.py:364
  68.0 11.4 %shard_map.166 = f32[128,256]{1,0:T(8,128)} custom-call(bf16[128,2048]{1,0:T(8,128)(2,1)} %get-tuple-element.14.back_ref.refs_1_, bf16[128,2048]{1,0:T(8,128)(2,1)} %copy-done.4, bf16[128,2048]{1,0:T(8,128)(2,1)} %copy-done.2), custom_call_target="tpu_custom_call" | custom-call | tf_op jit(solution)/shard_map/pallas_call | solution.py:261
  80.4 4.5 %shard_map.165 = f32[16,2048]{1,0:T(8,128)} custom-call(f32[128,16,128]{2,1,0:T(8,128)} %get-tuple-element.22.e_ref, bf16[128,2048]{1,0:T(8,128)(2,1)} %get-tuple-element.17.x_ref.refs_1_), custom_call_target="tpu_custom_call" | custom-call | tf_op jit(solution)/shard_map/pallas_call | solution.py:158
  87.5 8.5 %reduce.1 = bf16[8,69632]{1,0:T(8,128)(2,1)} reduce(bf16[8,1,69632]{2,1,0:T(2,128)(2,1)S(1)} %broadcast_in_dim.64, bf16[]{:T(256)} %broadcast.111), dimensions={1}, to_apply=%broadcast_in_dim.64.reduce_sub_computation | reduce | bytes 2228226 | tf_op jit(solution)/shard_map/broadcast_in_dim | solution.py:277
  96.0 3.2 %reshape.113 = bf16[8,2,34816]{2,1,0:T(2,128)(2,1)} reshape(bf16[8,69632]{1,0:T(8,128)(2,1)} %reduce.1) | data formatting | bytes 2228224
  99.2 6.1 %all-to-all-start.1 = ((bf16[8,2,34816]{2,1,0:T(2,128)(2,1)}), bf16[8,2,34816]{2,1,0:T(2,128)(2,1)}, u32[]{:S(2)}, u32[]{:S(2)}) async-start(bf16[8,2,34816]{2,1,0:T(2,128)(2,1)} %reshape.113), calls=%async_computation.1 | async-start | bytes 2228224 | tf_op jit(solution)/shard_map/all_to_all | solution.py:278
  105.3 2.7 %collective-permute-start.1 = (bf16[128,2048]{1,0:T(8,128)(2,1)S(1)}, bf16[128,2048]{1,0:T(8,128)(2,1)S(1)}, u32[]{:S(2)}, u32[]{:S(2)}) collective-permute-start(bf16[128,2048]{1,0:T(8,128)(2,1)S(1)} %copy-done.3), channel_id=1, source_target_pairs={{4,0},{8,4},{12,8},{16,12},{20,16},{24,20},{28,24},{5,1},{9,5},{13... | collective-permute-start | bytes 1572872 | tf_op jit(solution)/shard_map/ppermute | solution.py:20
  109.9 7.4 %shard_map.167.loc_ref = f32[128,2048]{1,0:T(8,128)} custom-call(f32[128,128]{1,0:T(8,128)} %pad_maximum_fusion.2.refs_0_, bf16[128,2048]{1,0:T(8,128)(2,1)} %get-tuple-element.17.x_ref.refs_1_), custom_call_target="tpu_custom_call" | custom-call | tf_op jit(solution)/shard_map/pallas_call | solution.py:121
  117.3 24.8 %collective-permute-done.1.refs_2_ = bf16[128,2048]{1,0:T(8,128)(2,1)S(1)} collective-permute-done((bf16[128,2048]{1,0:T(8,128)(2,1)S(1)}, bf16[128,2048]{1,0:T(8,128)(2,1)S(1)}, u32[]{:S(2)}, u32[]{:S(2)}) %collective-permute-start.1) | collective-permute-done | bytes 524320 | tf_op jit(solution)/shard_map/ppermute | solution.py:20
  143.0 7.5 %shard_map.169 = f32[128,2048]{1,0:T(8,128)} custom-call(f32[128,256]{1,0:T(8,128)} %concatenate.19.refs_0_, bf16[128,2048]{1,0:T(8,128)(2,1)} %get-tuple-element.14.back_ref.refs_1_, bf16[128,2048]{1,0:T(8,128)(2,1)} %copy-done.12), custom_call_target="tpu_custom_call" | custom-call | tf_op jit(solution)/shard_map/pallas_call | solution.py:121
  150.5 2.5 %fusion.4 = (bf16[128,2048]{1,0:T(8,128)(2,1)}, bf16[128,2048]{1,0:T(8,128)(2,1)}) fusion(f32[128,2048]{1,0:T(8,128)} %shard_map.169, bf16[128,2048]{1,0:T(8,128)(2,1)S(1)} %copy-done.8, bf16[128,2048]{1,0:T(8,128)(2,1)S(1)} %copy-done.6), kind=kLoop, calls=%fused_computation.20 | loop fusion | flops 1572864 | bytes 3145728 | tf_op jit(solution)/shard_map/convert_element_type | solution.py:383
  152.9 4.3 %reshape.114 = bf16[8,1,69632]{2,1,0:T(2,128)(2,1)S(1)} reshape(bf16[8,2,34816]{2,1,0:T(2,128)(2,1)} %all-to-all-done.1) | data formatting | bytes 2228224
  161.2 5.0 %shard_map.168 = f32[128,2048]{1,0:T(8,128)} custom-call(f32[16,128]{1,0:T(8,128)} %reshape.106.dec_ref, f32[16,128]{1,0:T(8,128)} %reshape.107.wt_ref, f32[16,2048]{1,0:T(8,128)} %reduce_sum.61.ent_ref, f32[128,2048]{1,0:T(8,128)} %shard_map.167.loc_ref), custom_call_target="tpu_custom_call" | custom-call | tf_op jit(solution)/shard_map/pallas_call | solution.py:210
  166.2 2.5 %fusion.8 = (bf16[128,2048]{1,0:T(8,128)(2,1)}, bf16[128,2048]{1,0:T(8,128)(2,1)}) fusion(f32[128,2048]{1,0:T(8,128)} %shard_map.168, bf16[128,2048]{1,0:T(8,128)(2,1)S(1)} %copy-done.10, bf16[128,2048]{1,0:T(8,128)(2,1)S(1)} %copy-done.9), kind=kLoop, calls=%fused_computation.24 | loop fusion | flops 1572864 | bytes 3145728 | tf_op jit(solution)/shard_map/convert_element_type | solution.py:387
  (84 shorter events, 21.7 us)
Async XLA Ops:
  5.3 12.6 %copy-start.5 = (bf16[128,2048]{1,0:T(8,128)(2,1)S(1)}, bf16[128,2048]{1,0:T(8,128)(2,1)}, u32[]{:S(2)}) copy-start(bf16[128,2048]{1,0:T(8,128)(2,1)} %param.12) | copy-start | bytes 1572868
  5.3 12.6 %copy-start.7 = (bf16[128,2048]{1,0:T(8,128)(2,1)S(1)}, bf16[128,2048]{1,0:T(8,128)(2,1)}, u32[]{:S(2)}) copy-start(bf16[128,2048]{1,0:T(8,128)(2,1)} %param.11) | copy-start | bytes 1572868
  9.9 13.4 %copy-start.13 = (f32[128,128]{1,0:T(8,128)S(1)}, f32[128,128]{1,0:T(8,128)}, u32[]{:S(2)}) copy-start(f32[128,128]{1,0:T(8,128)} %param.16) | copy-start | bytes 196612
  10.8 12.6 %copy-start.15 = (f32[128,16]{0,1:T(8,128)S(1)}, f32[128,16]{0,1:T(8,128)}, u32[]{:S(2)}) copy-start(f32[128,16]{0,1:T(8,128)} %param.18) | copy-start | bytes 24580
  11.7 36.9 %all-to-all-start = ((bf16[8,16,2048]{2,1,0:T(8,128)(2,1)}), bf16[8,16,2048]{2,1,0:T(8,128)(2,1)S(1)}, u32[]{:S(2)}, u32[]{:S(2)}) async-start(bf16[8,16,2048]{2,1,0:T(8,128)(2,1)} %broadcast_in_dim.63), calls=%async_computation | async-start | bytes 1048576 | tf_op jit(solution)/shard_map/all_to_all | solution.py:278
  18.0 15.4 %copy-start.2 = (bf16[128,2048]{1,0:T(8,128)(2,1)}, bf16[128,2048]{1,0:T(8,128)(2,1)S(1)}, u32[]{:S(2)}) copy-start(bf16[128,2048]{1,0:T(8,128)(2,1)S(1)} %fusion.5.refs_2_.bot_ref) | copy-start | bytes 1572868
  18.1 22.2 %collective-permute-start = (bf16[128,2048]{1,0:T(8,128)(2,1)S(1)}, bf16[128,2048]{1,0:T(8,128)(2,1)S(1)}, u32[]{:S(2)}, u32[]{:S(2)}) collective-permute-start(bf16[128,2048]{1,0:T(8,128)(2,1)S(1)} %fusion.5.refs_2_.bot_ref), channel_id=1, source_target_pairs={{0,4},{4,8},{8,12},{12,16},{16,20},{20,24},{24,28},{1,5},{5,9},{9,... | collective-permute-start | bytes 1572872 | tf_op jit(solution)/shard_map/ppermute | solution.py:20
  34.2 20.3 %copy-start.14 = (f32[2048]{0:T(1024)S(1)}, f32[2048]{0:T(1024)}, u32[]{:S(2)}) copy-start(f32[2048]{0:T(1024)} %param.17) | copy-start | bytes 24580
  40.3 0.8 copy-start.4
  48.5 6.0 %copy-start = (f32[128,2048]{1,0:T(8,128)S(1)}, f32[128,2048]{1,0:T(8,128)}, u32[]{:S(2)}) copy-start(f32[128,2048]{1,0:T(8,128)} %shard_map.161) | copy-start | bytes 3145732
  54.6 9.8 %copy-start.1 = (f32[128,2048]{1,0:T(8,128)S(1)}, f32[128,2048]{1,0:T(8,128)}, u32[]{:S(2)}) copy-start(f32[128,2048]{1,0:T(8,128)} %shard_map.164) | copy-start | bytes 3145732
  96.0 9.3 %copy-start.3 = (bf16[128,2048]{1,0:T(8,128)(2,1)S(1)}, bf16[128,2048]{1,0:T(8,128)(2,1)}, u32[]{:S(2)}) copy-start(bf16[128,2048]{1,0:T(8,128)(2,1)} %get-tuple-element.14.back_ref.refs_1_) | copy-start | bytes 1572868
  96.0 12.7 %copy-start.11 = (f32[128,1,128]{2,1,0:T(1,128)S(1)}, f32[128,1,128]{2,1,0:T(1,128)}, u32[]{:S(2)}) copy-start(f32[128,1,128]{2,1,0:T(1,128)} %fusion.21) | copy-start | bytes 196612
  99.2 53.7 %all-to-all-start.1 = ((bf16[8,2,34816]{2,1,0:T(2,128)(2,1)}), bf16[8,2,34816]{2,1,0:T(2,128)(2,1)}, u32[]{:S(2)}, u32[]{:S(2)}) async-start(bf16[8,2,34816]{2,1,0:T(2,128)(2,1)} %reshape.113), calls=%async_computation.1 | async-start | bytes 2228224 | tf_op jit(solution)/shard_map/all_to_all | solution.py:278
  105.3 36.8 %collective-permute-start.1 = (bf16[128,2048]{1,0:T(8,128)(2,1)S(1)}, bf16[128,2048]{1,0:T(8,128)(2,1)S(1)}, u32[]{:S(2)}, u32[]{:S(2)}) collective-permute-start(bf16[128,2048]{1,0:T(8,128)(2,1)S(1)} %copy-done.3), channel_id=1, source_target_pairs={{4,0},{8,4},{12,8},{16,12},{20,16},{24,20},{28,24},{5,1},{9,5},{13... | collective-permute-start | bytes 1572872 | tf_op jit(solution)/shard_map/ppermute | solution.py:20
  109.1 41.4 %copy-start.6 = (bf16[128,2048]{1,0:T(8,128)(2,1)S(1)}, bf16[128,2048]{1,0:T(8,128)(2,1)}, u32[]{:S(2)}) copy-start(bf16[128,2048]{1,0:T(8,128)(2,1)} %param.12) | copy-start | bytes 1572868
  109.1 41.4 %copy-start.8 = (bf16[128,2048]{1,0:T(8,128)(2,1)S(1)}, bf16[128,2048]{1,0:T(8,128)(2,1)}, u32[]{:S(2)}) copy-start(bf16[128,2048]{1,0:T(8,128)(2,1)} %param.11) | copy-start | bytes 1572868
  142.2 0.8 copy-start.12
  158.7 7.4 %copy-start.9 = (bf16[128,2048]{1,0:T(8,128)(2,1)S(1)}, bf16[128,2048]{1,0:T(8,128)(2,1)}, u32[]{:S(2)}) copy-start(bf16[128,2048]{1,0:T(8,128)(2,1)} %param.13) | copy-start | bytes 1572868
  158.8 7.4 %copy-start.10 = (bf16[128,2048]{1,0:T(8,128)(2,1)S(1)}, bf16[128,2048]{1,0:T(8,128)(2,1)}, u32[]{:S(2)}) copy-start(bf16[128,2048]{1,0:T(8,128)(2,1)} %param.15) | copy-start | bytes 1572868

commit v5 on v2

--- a/solution.py
+++ b/solution.py
@@ -25,14 +25,18 @@
     return high, (value - high.astype(jnp.float32)).astype(jnp.bfloat16)
 
 
-def _band_kernel(*refs, group_size, split, tri, two_inputs, modal, sub):
+def _band_kernel(*refs, group_size, split, tri, two_inputs, modal, sub, scaled):
     refs = list(refs)
     h_ref = refs.pop(0)
     top_ref = refs.pop(0)
     bot_ref = refs.pop(0) if two_inputs else None
     if modal is not None:
         dec_ref, wt_ref, ent_ref = refs.pop(0), refs.pop(0), refs.pop(0)
+    if scaled:
+        first_ref, second_ref = refs.pop(0), refs.pop(0)
     out_ref = refs.pop(0)
+    if scaled:
+        other_ref = refs.pop(0)
     rows = out_ref.shape[0]
     width = h_ref.shape[1]
     groups_here = LANES // group_size
@@ -80,13 +84,19 @@
         acc = y[:rows]
         for k in range(1, groups_here):
             acc = jnp.where(lane_group == k, y[k * rows:(k + 1) * rows], acc)
-        out_ref[:, lanes] = acc
+        if scaled:
+            out_ref[:, lanes] = (acc * first_ref[:, lanes].astype(jnp.float32)).astype(out_ref.dtype)
+            other_ref[:, lanes] = (acc * second_ref[:, lanes].astype(jnp.float32)).astype(other_ref.dtype)
+        else:
+            out_ref[:, lanes] = acc
         return carry
 
     lax.fori_loop(0, sub, body, 0)
 
 
-def band_conv(band_rows, top, bottom=None, modal_args=None, *, group_size, split, tri, modal=None):
+def band_conv(
+    band_rows, top, bottom=None, modal_args=None, scale_pair=None, *, group_size, split, tri, modal=None
+):
     rows, chans = top.shape
     block = min(BLOCK_LANES, chans)
     groups_block = block // group_size
@@ -109,6 +119,14 @@
             pl.BlockSpec((modes, block), lambda b: (0, b)),
         ]
         args += [decays, weights, entering]
+    scaled = scale_pair is not None
+    out_specs = pl.BlockSpec((rows, block), lambda b: (0, b))
+    out_shape = jax.ShapeDtypeStruct((rows, chans), jnp.float32)
+    if scaled:
+        in_specs += [pl.BlockSpec((rows, block), lambda b: (0, b))] * 2
+        args += list(scale_pair)
+        out_specs = [out_specs, out_specs]
+        out_shape = [jax.ShapeDtypeStruct((rows, chans), jnp.bfloat16)] * 2
     kernel = functools.partial(
         _band_kernel,
         group_size=group_size,
@@ -117,13 +135,14 @@
         two_inputs=two_inputs,
         modal=modal,
         sub=block // LANES,
+        scaled=scaled,
     )
     return pl.pallas_call(
         kernel,
         grid=(chans // block,),
         in_specs=in_specs,
-        out_specs=pl.BlockSpec((rows, block), lambda b: (0, b)),
-        out_shape=jax.ShapeDtypeStruct((rows, chans), jnp.float32),
+        out_specs=out_specs,
+        out_shape=out_shape,
         compiler_params=pltpu.CompilerParams(dimension_semantics=("parallel",)),
     )(*args)
 
@@ -137,9 +156,8 @@
         lanes = pl.ds(pl.multiple_of(j * LANES, LANES), LANES)
         x = x_ref[:, lanes]
         weights = e_ref[pl.ds(j * groups_here, groups_here)]
-        high, low = _split(weights.reshape(groups_here * modes, weights.shape[2]))
-        y = jnp.dot(high, x, preferred_element_type=jnp.float32)
-        y = y + jnp.dot(low, x, preferred_element_type=jnp.float32)
+        stacked = weights.reshape(groups_here * modes, weights.shape[2]).astype(jnp.bfloat16)
+        y = jnp.dot(stacked, x, preferred_element_type=jnp.float32)
         acc = y[:modes]
         for k in range(1, groups_here):
             acc = jnp.where(state_group == k, y[k * modes:(k + 1) * modes], acc)
@@ -347,8 +365,8 @@
     conv_st = modal_states(fwd_states, mixed_li_bf, group_size=group_size)
     both_st = gather_seq(jnp.concatenate([grad_st, conv_st], 0).astype(jnp.bfloat16))
     both_st = both_st.astype(jnp.float32)
-    grad_loc = band_conv(taps_li, back_li_bf, group_size=group_size, split=True, tri="upper")
-    conv_loc = band_conv(li_fwd_rows, mixed_li_bf, group_size=group_size, split=True, tri="lower")
+    grad_loc = band_conv(taps_li, back_li_bf, group_size=group_size, split=False, tri="upper")
+    conv_loc = band_conv(li_fwd_rows, mixed_li_bf, group_size=group_size, split=False, tri="lower")
     grad_ent = entering_states(both_st[:, :modes], li_decay, row_count, group_size, False)
     conv_ent = entering_states(both_st[:, modes:], li_decay, row_count, group_size, True)
     grad_mixed_li = modal_out(
@@ -367,9 +385,10 @@
     grad_query_mr = (grad_out_mr * conv_mr).astype(jnp.bfloat16)
     back_mr = (grad_out_mr * query_mr.astype(jnp.float32)).astype(jnp.bfloat16)
     after_rim = from_behind(back_mr, "seq", -1)
-    grad_mixed_mr = band_conv(bwd_rows, back_mr, after_rim, group_size=group_size, split=False, tri=None)
-    grad_key_mr = (grad_mixed_mr * value_mr.astype(jnp.float32)).astype(jnp.bfloat16)
-    grad_value_mr = (grad_mixed_mr * key_mr.astype(jnp.float32)).astype(jnp.bfloat16)
+    grad_key_mr, grad_value_mr = band_conv(
+        bwd_rows, back_mr, after_rim, scale_pair=(value_mr, key_mr),
+        group_size=group_size, split=False, tri=None,
+    )
     diag_sums = gram_diag(back_mr, rim_rows, mixed_mr, group_size=group_size)
     filter_part = jnp.flip(diag_sums[:, tap_count:], 1)
     packed = jnp.concatenate([gain_part, filter_part.reshape(-1)])

time: 133 us -> 144 us (1.083)
  waiting for transfers between devices: 4.51 us -> 21.9 us
  other arithmetic: 23.5 us -> 20.9 us
  Pallas kernels: 60.3 us -> 57.9 us
    all_to_all x2, waiting for transfers between devices: 4.08 us -> 15 us  [gather_seq(): return lax.all_to_all(tiled, 'seq', split_axis=0, concat_axis=0, tiled=True)]
    ppermute x2, waiting for transfers between devices: 0.43 us -> 6.91 us  [from_behind(): lax.ppermute(value, axis, [(source, source + steps) for source in range(i...]
    convert_element_type x1 -> x0, other arithmetic: 2.46 us -> none  [on_device(): (grad_mixed_mr * key_mr.astype(jnp.float32)).astype(jnp.bfloat16)]
    pallas_call x4, Pallas kernels: 29.8 us -> 27.6 us  [band_conv(): pl.pallas_call(kernel, grid=(chans // block,), in_specs=in_specs, out_spe...]
  transfers between devices with their start and end apart: 4 -> 4, of which waited for: 2 -> 3; matrix products, arithmetic and copies ran while one was open for 15% -> 10% of each run, Pallas kernels for 33% -> 21%
where the time goes in v5:
time: 144 us; the launch traced here: 142 us
  Pallas kernels  57.9 us (40%)
  waiting for transfers between devices  21.9 us (15%)
  other arithmetic  20.9 us (15%)
  starting transfers between devices  17.7 us (12%)
  blocking collectives  11.4 us (8%)
  local copies, waits for them, and re-layouts  9.7 us (7%)
  matrix products  1.79 us (1%)
    pallas_call x4, Pallas kernels, band_conv(): pl.pallas_call(kernel, grid=(chans // block,), in_specs=in_specs, out_spe...  27.6 us
    all_to_all x2, waiting for transfers between devices, gather_seq(): return lax.all_to_all(tiled, 'seq', split_axis=0, concat_axis=0, tiled=True)  15 us
    all_to_all x2, starting transfers between devices, gather_seq(): return lax.all_to_all(tiled, 'seq', split_axis=0, concat_axis=0, tiled=True)  11.5 us
    pallas_call x1, Pallas kernels, gram_diag(): pl.pallas_call(kernel, grid=(chans // block,), in_specs=[pl.BlockSpec((ro...  11.4 us
    pallas_call x2, Pallas kernels, modal_out(): pl.pallas_call(kernel, grid=(chans // block,), in_specs=[pl.BlockSpec(fla...  10.1 us
    pallas_call x2, Pallas kernels, modal_states(): pl.pallas_call(kernel, grid=(chans // block,), in_specs=[pl.BlockSpec((gr...  8.82 us
    ppermute x2, waiting for transfers between devices, from_behind(): lax.ppermute(value, axis, [(source, source + steps) for source in range(i...  6.91 us
    ppermute x2, starting transfers between devices, from_behind(): lax.ppermute(value, axis, [(source, source + steps) for source in range(i...  6.18 us
  transfers between devices with their start and end apart: 4, of which 3 were waited for; matrix products, arithmetic and copies ran while one was open for 10% of the time, Pallas kernels for 21%

profile of v5, /device:TPU:0, one launch (start us, length us, event | category | flops | bytes accessed | tf_op | source)
XLA Modules:
  0.0 142.2 jit_solution(4272141155514278272)
XLA Ops:
  0.7 1.4 multiply_convert_fusion.1.refs_2_.bot_ref
  2.1 4.9 %collective-permute-start = (bf16[128,2048]{1,0:T(8,128)(2,1)S(1)}, bf16[128,2048]{1,0:T(8,128)(2,1)S(1)}, u32[]{:S(2)}, u32[]{:S(2)}) collective-permute-start(bf16[128,2048]{1,0:T(8,128)(2,1)S(1)} %multiply_convert_fusion.1.refs_2_.bot_ref), channel_id=1, source_target_pairs={{0,4},{4,8},{8,12},{12,16},{16,20},{20,24},{24,28},{1,5},{5,9},{9,... | collective-permute-start | bytes 1572872 | tf_op jit(solution)/shard_map/ppermute | solution.py:20
  9.8 1.7 %multiply_exponential_fusion.1 = (f32[128,16,128]{2,1,0:T(8,128)}, f32[128,16,128]{2,1,0:T(8,128)}) fusion(f32[128,16]{1,0:T(8,128)S(1)} %copy.29, f32[128]{0:T(128)S(1)} %iota_subtract_fusion), kind=kLoop, calls=%fused_computation.35 | loop fusion | flops 524288 | bytes 2105856 | tf_op jit(solution)/shard_map/exp | solution.py:359
  11.5 4.4 %shard_map.161 = f32[16,2048]{1,0:T(8,128)} custom-call(f32[128,16,128]{2,1,0:T(8,128)} %get-tuple-element.23.e_ref, bf16[128,2048]{1,0:T(8,128)(2,1)} %fusion.1.x_ref.refs_1_), custom_call_target="tpu_custom_call" | custom-call | tf_op jit(solution)/shard_map/pallas_call | solution.py:176
  18.9 7.4 %shard_map.162 = f32[128,2048]{1,0:T(8,128)} custom-call(f32[128,256]{1,0:T(8,128)} %maximum_maximum_fusion.refs_0_, bf16[128,2048]{1,0:T(8,128)(2,1)} %copy-done.6, bf16[128,2048]{1,0:T(8,128)(2,1)} %copy-done.2), custom_call_target="tpu_custom_call" | custom-call | tf_op jit(solution)/shard_map/pallas_call | solution.py:140
  26.4 1.5 %fusion.6 = (f32[128]{0:T(128)S(1)}, bf16[128,2048]{1,0:T(8,128)(2,1)S(1)}) fusion(f32[128,2048]{1,0:T(8,128)} %shard_map.162, bf16[128,2048]{1,0:T(8,128)(2,1)S(1)} %copy-done.11), kind=kLoop, calls=%fused_computation.18 | loop fusion | flops 1572736 | bytes 2097664 | tf_op jit(solution)/shard_map/reduce_sum | solution.py:345
  27.8 5.8 %psum.14 = f32[128]{0:T(128)S(1)} all-reduce(f32[128]{0:T(128)S(1)} %get-tuple-element.16), channel_id=1, replica_groups=mesh['seq'=8,'chan'=4] {'chan'}, use_global_device_ids=true, to_apply=%region_1.2 | all-reduce | flops 128 | bytes 1024 | tf_op jit(solution)/shard_map/psum | solution.py:345
  34.7 4.4 %shard_map.163 = f32[16,2048]{1,0:T(8,128)} custom-call(f32[128,16,128]{2,1,0:T(8,128)} %get-tuple-element.24.e_ref, bf16[128,2048]{1,0:T(8,128)(2,1)} %fusion.3.x_ref.refs_1_), custom_call_target="tpu_custom_call" | custom-call | tf_op jit(solution)/shard_map/pallas_call | solution.py:176
  41.1 6.7 %all-to-all-start = ((bf16[8,32,2048]{2,1,0:T(8,128)(2,1)}), bf16[8,32,2048]{2,1,0:T(8,128)(2,1)S(1)}, u32[]{:S(2)}, u32[]{:S(2)}) async-start(bf16[8,32,2048]{2,1,0:T(8,128)(2,1)} %broadcast_in_dim.33), calls=%async_computation | async-start | bytes 2097152 | tf_op jit(solution)/shard_map/all_to_all | solution.py:296
  49.1 1.8 %fusion.18 = f32[128,1,128]{2,1,0:T(1,128)} fusion(f32[128,16,1]{1,2,0:T(1,128)S(1)} %copy.31, f32[128,16]{1,0:T(8,128)S(1)} %copy.29), kind=kOutput, calls=%fused_computation.36 | convolution fusion | flops 3407872 | bytes 81920 | tf_op jit(solution)/shard_map/gr,grd->gd/dot_general | solution.py:354
  50.9 6.3 %shard_map.166.loc_ref = f32[128,2048]{1,0:T(8,128)} custom-call(f32[128,128]{1,0:T(8,128)} %bitcast.11, bf16[128,2048]{1,0:T(8,128)(2,1)} %fusion.1.x_ref.refs_1_), custom_call_target="tpu_custom_call" | custom-call | tf_op jit(solution)/shard_map/pallas_call | solution.py:140
  58.6 15.0 %all-to-all-done = bf16[8,32,2048]{2,1,0:T(8,128)(2,1)S(1)} async-done(((bf16[8,32,2048]{2,1,0:T(8,128)(2,1)}), bf16[8,32,2048]{2,1,0:T(8,128)(2,1)S(1)}, u32[]{:S(2)}, u32[]{:S(2)}) %all-to-all-start) | async-done | bytes 1048608 | tf_op jit(solution)/shard_map/all_to_all | solution.py:296
  75.0 5.1 %shard_map.167 = f32[128,2048]{1,0:T(8,128)} custom-call(f32[16,128]{1,0:T(8,128)} %reshape.95.dec_ref, f32[16,128]{1,0:T(8,128)} %reshape.96.wt_ref, f32[16,2048]{1,0:T(8,128)} %get-tuple-element.12.ent_ref, f32[128,2048]{1,0:T(8,128)} %shard_map.166.loc_ref), custom_call_target="tpu_custom_call" | custom-call | tf_op jit(solution)/shard_map/pallas_call | solution.py:228
  80.1 2.5 %fusion.15 = (f32[2048]{0:T(1024)S(1)}, f32[128]{0:T(128)S(1)}, bf16[128,2048]{1,0:T(8,128)(2,1)}) fusion(bf16[128,2048]{1,0:T(8,128)(2,1)S(1)} %get-tuple-element.17, f32[128]{0:T(128)S(1)} %get-tuple-element.29, f32[128,2048]{1,0:T(8,128)} %shard_map.167, bf16[128,2048]{1,0:T(8,128)(2,1)S(1)} %copy-done.4, f32[2048]{0:T(1024)S(1)} %copy-done.14), kind=kLoop, calls=%fused_computation.27 | loop fusion | flops 3405696 | bytes 2638848 | tf_op jit(solution)/shard_map/reduce_sum | solution.py:381
  82.7 5.6 %psum.15 = f32[128]{0:T(128)S(1)} all-reduce(f32[128]{0:T(128)S(1)} %get-tuple-element.15), channel_id=1, replica_groups=mesh['seq'=8,'chan'=4] {'chan'}, use_global_device_ids=true, to_apply=%region_5.6 | all-reduce | flops 128 | bytes 1024 | tf_op jit(solution)/shard_map/psum | solution.py:383
  88.3 2.6 %fusion.5 = (bf16[128,2048]{1,0:T(8,128)(2,1)}, bf16[128,2048]{1,0:T(8,128)(2,1)}) fusion(bf16[128,2048]{1,0:T(8,128)(2,1)} %param.10, f32[128]{0:T(128)S(1)} %psum.15, f32[128]{0:T(128)S(1)} %get-tuple-element.28, bf16[128,2048]{1,0:T(8,128)(2,1)S(1)} %get-tuple-element.17, f32[2048]{0:T(1024)S(1)} %copy-done.14, f32[128]{0:T(128)S(1)} %get-tuple-element.29, ...), kind=kLoop, calls=%fused_computation.17 | loop fusion | flops 3670016 | bytes 4728320 | tf_op jit(solution)/shard_map/convert_element_type | solution.py:386
  90.9 11.4 %shard_map.169 = f32[128,256]{1,0:T(8,128)} custom-call(bf16[128,2048]{1,0:T(8,128)(2,1)} %get-tuple-element.18.refs_1_.back_ref, bf16[128,2048]{1,0:T(8,128)(2,1)} %copy-done.6, bf16[128,2048]{1,0:T(8,128)(2,1)} %copy-done.2), custom_call_target="tpu_custom_call" | custom-call | tf_op jit(solution)/shard_map/pallas_call | solution.py:279
  104.4 4.8 %all-to-all-start.1 = ((f32[8,1,18432]{2,1,0:T(1,128)}), f32[8,1,18432]{2,1,0:T(1,128)S(1)}, u32[]{:S(2)}, u32[]{:S(2)}) async-start(f32[8,1,18432]{2,1,0:T(1,128)} %broadcast_in_dim.62), calls=%async_computation.1 | async-start | bytes 1179648 | tf_op jit(solution)/shard_map/all_to_all | solution.py:296
  110.7 6.3 %shard_map.164.loc_ref = f32[128,2048]{1,0:T(8,128)} custom-call(f32[128,128]{1,0:T(8,128)} %pad_maximum_fusion.2.refs_0_, bf16[128,2048]{1,0:T(8,128)(2,1)} %fusion.3.x_ref.refs_1_), custom_call_target="tpu_custom_call" | custom-call | tf_op jit(solution)/shard_map/pallas_call | solution.py:140
  117.0 1.3 collective-permute-start.1
  118.3 5.0 %shard_map.165 = f32[128,2048]{1,0:T(8,128)} custom-call(f32[16,128]{1,0:T(8,128)} %reshape.95.dec_ref, f32[16,128]{1,0:T(8,128)} %reshape.96.wt_ref, f32[16,2048]{1,0:T(8,128)} %get-tuple-element.13.ent_ref, f32[128,2048]{1,0:T(8,128)} %shard_map.164.loc_ref), custom_call_target="tpu_custom_call" | custom-call | tf_op jit(solution)/shard_map/pallas_call | solution.py:228
  123.3 2.5 %fusion.2 = (bf16[128,2048]{1,0:T(8,128)(2,1)}, bf16[128,2048]{1,0:T(8,128)(2,1)}) fusion(f32[128,2048]{1,0:T(8,128)} %shard_map.165, bf16[128,2048]{1,0:T(8,128)(2,1)S(1)} %copy-done.10, bf16[128,2048]{1,0:T(8,128)(2,1)S(1)} %copy-done.8), kind=kLoop, calls=%fused_computation.14 | loop fusion | flops 1572864 | bytes 3145728 | tf_op jit(solution)/shard_map/convert_element_type | solution.py:378
  125.8 6.4 %collective-permute-done.1.refs_2_ = bf16[128,2048]{1,0:T(8,128)(2,1)S(1)} collective-permute-done((bf16[128,2048]{1,0:T(8,128)(2,1)S(1)}, bf16[128,2048]{1,0:T(8,128)(2,1)S(1)}, u32[]{:S(2)}, u32[]{:S(2)}) %collective-permute-start.1) | collective-permute-done | bytes 524320 | tf_op jit(solution)/shard_map/ppermute | solution.py:20
  132.9 7.6 %shard_map.168 = (bf16[128,2048]{1,0:T(8,128)(2,1)}, bf16[128,2048]{1,0:T(8,128)(2,1)}) custom-call(f32[128,256]{1,0:T(8,128)} %concatenate.23.refs_0_, bf16[128,2048]{1,0:T(8,128)(2,1)} %get-tuple-element.18.refs_1_.back_ref, bf16[128,2048]{1,0:T(8,128)(2,1)} %copy-done.13, bf16[128,2048]{1,0:T(8,128)(2,1)} %refs_3_.1, bf16[128,2048]{1,0:T(8,128)(2,1)} %refs_4_.1), custom_call_target="tpu_custom_call" | custom-call | tf_op jit(solution)/shard_map/pallas_call | solution.py:140
  (73 shorter events, 19.0 us)
Async XLA Ops:
  0.6 7.9 %copy-start.7 = (bf16[128,2048]{1,0:T(8,128)(2,1)S(1)}, bf16[128,2048]{1,0:T(8,128)(2,1)}, u32[]{:S(2)}) copy-start(bf16[128,2048]{1,0:T(8,128)(2,1)} %param.13) | copy-start | bytes 1572868
  0.6 7.9 %copy-start.9 = (bf16[128,2048]{1,0:T(8,128)(2,1)S(1)}, bf16[128,2048]{1,0:T(8,128)(2,1)}, u32[]{:S(2)}) copy-start(bf16[128,2048]{1,0:T(8,128)(2,1)} %param.15) | copy-start | bytes 1572868
  2.1 13.8 %copy-start.2 = (bf16[128,2048]{1,0:T(8,128)(2,1)}, bf16[128,2048]{1,0:T(8,128)(2,1)S(1)}, u32[]{:S(2)}) copy-start(bf16[128,2048]{1,0:T(8,128)(2,1)S(1)} %multiply_convert_fusion.1.refs_2_.bot_ref) | copy-start | bytes 1572868
  2.1 16.0 %collective-permute-start = (bf16[128,2048]{1,0:T(8,128)(2,1)S(1)}, bf16[128,2048]{1,0:T(8,128)(2,1)S(1)}, u32[]{:S(2)}, u32[]{:S(2)}) collective-permute-start(bf16[128,2048]{1,0:T(8,128)(2,1)S(1)} %multiply_convert_fusion.1.refs_2_.bot_ref), channel_id=1, source_target_pairs={{0,4},{4,8},{8,12},{12,16},{16,20},{20,24},{24,28},{1,5},{5,9},{9,... | collective-permute-start | bytes 1572872 | tf_op jit(solution)/shard_map/ppermute | solution.py:20
  11.5 14.9 %copy-start.11 = (bf16[128,2048]{1,0:T(8,128)(2,1)S(1)}, bf16[128,2048]{1,0:T(8,128)(2,1)}, u32[]{:S(2)}) copy-start(bf16[128,2048]{1,0:T(8,128)(2,1)} %param.10) | copy-start | bytes 1572868
  17.6 16.0 %copy-start.3 = (bf16[128,2048]{1,0:T(8,128)(2,1)S(1)}, bf16[128,2048]{1,0:T(8,128)(2,1)}, u32[]{:S(2)}) copy-start(bf16[128,2048]{1,0:T(8,128)(2,1)} %param.14) | copy-start | bytes 1572868
  17.6 16.0 %copy-start.14 = (f32[2048]{0:T(1024)S(1)}, f32[2048]{0:T(1024)}, u32[]{:S(2)}) copy-start(f32[2048]{0:T(1024)} %param.17) | copy-start | bytes 24580
  18.1 0.8 copy-start.6
  39.1 8.8 %copy-start.15 = (f32[128,16]{0,1:T(8,128)S(1)}, f32[128,16]{0,1:T(8,128)}, u32[]{:S(2)}) copy-start(f32[128,16]{0,1:T(8,128)} %param.18) | copy-start | bytes 24580
  41.1 32.5 %all-to-all-start = ((bf16[8,32,2048]{2,1,0:T(8,128)(2,1)}), bf16[8,32,2048]{2,1,0:T(8,128)(2,1)S(1)}, u32[]{:S(2)}, u32[]{:S(2)}) async-start(bf16[8,32,2048]{2,1,0:T(8,128)(2,1)} %broadcast_in_dim.33), calls=%async_computation | async-start | bytes 2097152 | tf_op jit(solution)/shard_map/all_to_all | solution.py:296
  73.8 6.3 %copy-start.4 = (bf16[128,2048]{1,0:T(8,128)(2,1)S(1)}, bf16[128,2048]{1,0:T(8,128)(2,1)}, u32[]{:S(2)}) copy-start(bf16[128,2048]{1,0:T(8,128)(2,1)} %param.14) | copy-start | bytes 1572868
  75.0 13.3 %copy-start.1 = (f32[128,2048]{1,0:T(8,128)S(1)}, f32[128,2048]{1,0:T(8,128)}, u32[]{:S(2)}) copy-start(f32[128,2048]{1,0:T(8,128)} %shard_map.162) | copy-start | bytes 3145732
  80.1 8.2 %copy-start = (f32[128,2048]{1,0:T(8,128)S(1)}, f32[128,2048]{1,0:T(8,128)}, u32[]{:S(2)}) copy-start(f32[128,2048]{1,0:T(8,128)} %shard_map.167) | copy-start | bytes 3145732
  90.9 18.9 %copy-start.12 = (f32[128,1,128]{2,1,0:T(1,128)S(1)}, f32[128,1,128]{2,1,0:T(1,128)}, u32[]{:S(2)}) copy-start(f32[128,1,128]{2,1,0:T(1,128)} %fusion.18) | copy-start | bytes 196612
  103.2 13.8 %copy-start.5 = (bf16[128,2048]{1,0:T(8,128)(2,1)S(1)}, bf16[128,2048]{1,0:T(8,128)(2,1)}, u32[]{:S(2)}) copy-start(bf16[128,2048]{1,0:T(8,128)(2,1)} %get-tuple-element.18.refs_1_.back_ref) | copy-start | bytes 1572868
  104.4 36.1 %all-to-all-start.1 = ((f32[8,1,18432]{2,1,0:T(1,128)}), f32[8,1,18432]{2,1,0:T(1,128)S(1)}, u32[]{:S(2)}, u32[]{:S(2)}) async-start(f32[8,1,18432]{2,1,0:T(1,128)} %broadcast_in_dim.62), calls=%async_computation.1 | async-start | bytes 1179648 | tf_op jit(solution)/shard_map/all_to_all | solution.py:296
  109.9 13.4 %copy-start.8 = (bf16[128,2048]{1,0:T(8,128)(2,1)S(1)}, bf16[128,2048]{1,0:T(8,128)(2,1)}, u32[]{:S(2)}) copy-start(bf16[128,2048]{1,0:T(8,128)(2,1)} %param.13) | copy-start | bytes 1572868
  109.9 13.4 %copy-start.10 = (bf16[128,2048]{1,0:T(8,128)(2,1)S(1)}, bf16[128,2048]{1,0:T(8,128)(2,1)}, u32[]{:S(2)}) copy-start(bf16[128,2048]{1,0:T(8,128)(2,1)} %param.15) | copy-start | bytes 1572868
  117.0 15.1 %collective-permute-start.1 = (bf16[128,2048]{1,0:T(8,128)(2,1)S(1)}, bf16[128,2048]{1,0:T(8,128)(2,1)S(1)}, u32[]{:S(2)}, u32[]{:S(2)}) collective-permute-start(bf16[128,2048]{1,0:T(8,128)(2,1)S(1)} %copy-done.5), channel_id=1, source_target_pairs={{4,0},{8,4},{12,8},{16,12},{20,16},{24,20},{28,24},{5,1},{9,5},{13... | collective-permute-start | bytes 1572872 | tf_op jit(solution)/shard_map/ppermute | solution.py:20
  132.1 0.8 copy-start.13

commit v6 on v5

--- a/solution.py
+++ b/solution.py
@@ -367,6 +367,7 @@
     both_st = both_st.astype(jnp.float32)
     grad_loc = band_conv(taps_li, back_li_bf, group_size=group_size, split=False, tri="upper")
     conv_loc = band_conv(li_fwd_rows, mixed_li_bf, group_size=group_size, split=False, tri="lower")
+    both_st, grad_loc, conv_loc = lax.optimization_barrier((both_st, grad_loc, conv_loc))
     grad_ent = entering_states(both_st[:, :modes], li_decay, row_count, group_size, False)
     conv_ent = entering_states(both_st[:, modes:], li_decay, row_count, group_size, True)
     grad_mixed_li = modal_out(

time: 144 us -> 144 us (level)
  the two profiles are of different devices: /device:TPU:0 before, /device:TPU:14 now
where the time goes in v6:
time: 144 us; the launch traced here: 143 us
  Pallas kernels  58 us (40%)
  waiting for transfers between devices  21.1 us (15%)
  other arithmetic  20.9 us (15%)
  starting transfers between devices  19.1 us (13%)
  blocking collectives  11.8 us (8%)
  local copies, waits for them, and re-layouts  10.3 us (7%)
    pallas_call x4, Pallas kernels, band_conv(): pl.pallas_call(kernel, grid=(chans // block,), in_specs=in_specs, out_spe...  27.6 us
    ppermute x2, waiting for transfers between devices, from_behind(): lax.ppermute(value, axis, [(source, source + steps) for source in range(i...  16.7 us
    all_to_all x2, starting transfers between devices, gather_seq(): return lax.all_to_all(tiled, 'seq', split_axis=0, concat_axis=0, tiled=True)  13.3 us
    pallas_call x1, Pallas kernels, gram_diag(): pl.pallas_call(kernel, grid=(chans // block,), in_specs=[pl.BlockSpec((ro...  11.5 us
    pallas_call x2, Pallas kernels, modal_out(): pl.pallas_call(kernel, grid=(chans // block,), in_specs=[pl.BlockSpec(fla...  10 us
    pallas_call x2, Pallas kernels, modal_states(): pl.pallas_call(kernel, grid=(chans // block,), in_specs=[pl.BlockSpec((gr...  8.82 us
    psum x1, blocking collectives, on_device(): squares = lax.psum(jnp.sum(out_full * out_full, axis=1), 'chan')  5.9 us
    ppermute x2, starting transfers between devices, from_behind(): lax.ppermute(value, axis, [(source, source + steps) for source in range(i...  5.89 us
  transfers between devices with their start and end apart: 4, of which 3 were waited for; matrix products, arithmetic and copies ran while one was open for 10% of the time, Pallas kernels for 21%

profile of v6, /device:TPU:14, one launch (start us, length us, event | category | flops | bytes accessed | tf_op | source)
XLA Modules:
  0.0 143.1 jit_solution(7063672002903893560)
XLA Ops:
  0.7 1.4 multiply_convert_fusion.1.refs_2_.bot_ref
  2.1 3.4 %collective-permute-start = (bf16[128,2048]{1,0:T(8,128)(2,1)S(1)}, bf16[128,2048]{1,0:T(8,128)(2,1)S(1)}, u32[]{:S(2)}, u32[]{:S(2)}) collective-permute-start(bf16[128,2048]{1,0:T(8,128)(2,1)S(1)} %multiply_convert_fusion.1.refs_2_.bot_ref), channel_id=1, source_target_pairs={{0,4},{4,8},{8,12},{12,16},{16,20},{20,24},{24,28},{1,5},{5,9},{9,... | collective-permute-start | bytes 1572872 | tf_op jit(solution)/shard_map/ppermute | solution.py:20
  8.3 1.7 %multiply_exponential_fusion.1 = (f32[128,16,128]{2,1,0:T(8,128)}, f32[128,16,128]{2,1,0:T(8,128)}) fusion(f32[128,16]{1,0:T(8,128)S(1)} %copy.29, f32[128]{0:T(128)S(1)} %iota_subtract_fusion), kind=kLoop, calls=%fused_computation.33 | loop fusion | flops 524288 | bytes 2105856 | tf_op jit(solution)/shard_map/exp | solution.py:359
  10.0 4.4 %shard_map.161 = f32[16,2048]{1,0:T(8,128)} custom-call(f32[128,16,128]{2,1,0:T(8,128)} %get-tuple-element.29.e_ref, bf16[128,2048]{1,0:T(8,128)(2,1)} %fusion.1.x_ref.refs_1_), custom_call_target="tpu_custom_call" | custom-call | tf_op jit(solution)/shard_map/pallas_call | solution.py:176
  16.1 1.6 %collective-permute-done.refs_1_.top_ref = bf16[128,2048]{1,0:T(8,128)(2,1)S(1)} collective-permute-done((bf16[128,2048]{1,0:T(8,128)(2,1)S(1)}, bf16[128,2048]{1,0:T(8,128)(2,1)S(1)}, u32[]{:S(2)}, u32[]{:S(2)}) %collective-permute-start) | collective-permute-done | bytes 524320 | tf_op jit(solution)/shard_map/ppermute | solution.py:20
  18.4 7.5 %shard_map.162 = f32[128,2048]{1,0:T(8,128)} custom-call(f32[128,256]{1,0:T(8,128)} %maximum_maximum_fusion.refs_0_, bf16[128,2048]{1,0:T(8,128)(2,1)} %copy-done.6, bf16[128,2048]{1,0:T(8,128)(2,1)} %copy-done.2), custom_call_target="tpu_custom_call" | custom-call | tf_op jit(solution)/shard_map/pallas_call | solution.py:140
  25.9 1.5 %fusion.6 = (f32[128]{0:T(128)S(1)}, bf16[128,2048]{1,0:T(8,128)(2,1)S(1)}) fusion(f32[128,2048]{1,0:T(8,128)} %shard_map.162, bf16[128,2048]{1,0:T(8,128)(2,1)S(1)} %copy-done.11), kind=kLoop, calls=%fused_computation.18 | loop fusion | flops 1572736 | bytes 2097664 | tf_op jit(solution)/shard_map/reduce_sum | solution.py:345
  27.4 5.9 %psum.14 = f32[128]{0:T(128)S(1)} all-reduce(f32[128]{0:T(128)S(1)} %get-tuple-element.22), channel_id=1, replica_groups=mesh['seq'=8,'chan'=4] {'chan'}, use_global_device_ids=true, to_apply=%region_1.2 | all-reduce | flops 128 | bytes 1024 | tf_op jit(solution)/shard_map/psum | solution.py:345
  34.3 4.4 %shard_map.163 = f32[16,2048]{1,0:T(8,128)} custom-call(f32[128,16,128]{2,1,0:T(8,128)} %get-tuple-element.30.e_ref, bf16[128,2048]{1,0:T(8,128)(2,1)} %fusion.3.x_ref.refs_1_), custom_call_target="tpu_custom_call" | custom-call | tf_op jit(solution)/shard_map/pallas_call | solution.py:176
  40.8 6.4 %all-to-all-start = ((bf16[8,32,2048]{2,1,0:T(8,128)(2,1)}), bf16[8,32,2048]{2,1,0:T(8,128)(2,1)S(1)}, u32[]{:S(2)}, u32[]{:S(2)}) async-start(bf16[8,32,2048]{2,1,0:T(8,128)(2,1)} %broadcast_in_dim.33), calls=%async_computation | async-start | bytes 2097152 | tf_op jit(solution)/shard_map/all_to_all | solution.py:296
  49.0 6.3 %shard_map.164.loc_ref = f32[128,2048]{1,0:T(8,128)} custom-call(f32[128,128]{1,0:T(8,128)} %bitcast.12, bf16[128,2048]{1,0:T(8,128)(2,1)} %fusion.1.x_ref.refs_1_), custom_call_target="tpu_custom_call" | custom-call | tf_op jit(solution)/shard_map/pallas_call | solution.py:140
  58.7 6.3 %shard_map.165.loc_ref = f32[128,2048]{1,0:T(8,128)} custom-call(f32[128,128]{1,0:T(8,128)} %pad_maximum_fusion.2.refs_0_, bf16[128,2048]{1,0:T(8,128)(2,1)} %fusion.3.x_ref.refs_1_), custom_call_target="tpu_custom_call" | custom-call | tf_op jit(solution)/shard_map/pallas_call | solution.py:140
  65.0 4.4 %all-to-all-done = bf16[8,32,2048]{2,1,0:T(8,128)(2,1)S(1)} async-done(((bf16[8,32,2048]{2,1,0:T(8,128)(2,1)}), bf16[8,32,2048]{2,1,0:T(8,128)(2,1)S(1)}, u32[]{:S(2)}, u32[]{:S(2)}) %all-to-all-start) | async-done | bytes 1048608 | tf_op jit(solution)/shard_map/all_to_all | solution.py:296
  70.8 5.1 %shard_map.167 = f32[128,2048]{1,0:T(8,128)} custom-call(f32[16,128]{1,0:T(8,128)} %reshape.95.dec_ref, f32[16,128]{1,0:T(8,128)} %reshape.96.wt_ref, f32[16,2048]{1,0:T(8,128)} %get-tuple-element.18.ent_ref, f32[128,2048]{1,0:T(8,128)} %shard_map.164.loc_ref), custom_call_target="tpu_custom_call" | custom-call | tf_op jit(solution)/shard_map/pallas_call | solution.py:228
  75.9 2.5 %fusion.15 = (f32[2048]{0:T(1024)S(1)}, f32[128]{0:T(128)S(1)}, bf16[128,2048]{1,0:T(8,128)(2,1)}) fusion(bf16[128,2048]{1,0:T(8,128)(2,1)S(1)} %get-tuple-element.23, f32[128]{0:T(128)S(1)} %get-tuple-element.35, f32[128,2048]{1,0:T(8,128)} %shard_map.167, bf16[128,2048]{1,0:T(8,128)(2,1)S(1)} %copy-done.4, f32[2048]{0:T(1024)S(1)} %copy-done.15), kind=kLoop, calls=%fused_computation.27 | loop fusion | flops 3405696 | bytes 2638848 | tf_op jit(solution)/shard_map/reduce_sum | solution.py:382
  78.4 5.9 %psum.15 = f32[128]{0:T(128)S(1)} all-reduce(f32[128]{0:T(128)S(1)} %get-tuple-element.21), channel_id=1, replica_groups=mesh['seq'=8,'chan'=4] {'chan'}, use_global_device_ids=true, to_apply=%region_5.6 | all-reduce | flops 128 | bytes 1024 | tf_op jit(solution)/shard_map/psum | solution.py:384
  84.3 2.6 %fusion.5 = (bf16[128,2048]{1,0:T(8,128)(2,1)}, bf16[128,2048]{1,0:T(8,128)(2,1)}) fusion(bf16[128,2048]{1,0:T(8,128)(2,1)} %param.10, f32[128]{0:T(128)S(1)} %psum.15, f32[128]{0:T(128)S(1)} %get-tuple-element.34, bf16[128,2048]{1,0:T(8,128)(2,1)S(1)} %get-tuple-element.23, f32[2048]{0:T(1024)S(1)} %copy-done.15, f32[128]{0:T(128)S(1)} %get-tuple-element.35, ...), kind=kLoop, calls=%fused_computation.17 | loop fusion | flops 3670016 | bytes 4728320 | tf_op jit(solution)/shard_map/convert_element_type | solution.py:387
  86.9 11.5 %shard_map.169 = f32[128,256]{1,0:T(8,128)} custom-call(bf16[128,2048]{1,0:T(8,128)(2,1)} %get-tuple-element.24.refs_1_.back_ref, bf16[128,2048]{1,0:T(8,128)(2,1)} %copy-done.6, bf16[128,2048]{1,0:T(8,128)(2,1)} %copy-done.2), custom_call_target="tpu_custom_call" | custom-call | tf_op jit(solution)/shard_map/pallas_call | solution.py:279
  100.4 6.9 %all-to-all-start.1 = ((f32[8,1,18432]{2,1,0:T(1,128)}), f32[8,1,18432]{2,1,0:T(1,128)S(1)}, u32[]{:S(2)}, u32[]{:S(2)}) async-start(f32[8,1,18432]{2,1,0:T(1,128)} %broadcast_in_dim.62), calls=%async_computation.1 | async-start | bytes 1179648 | tf_op jit(solution)/shard_map/all_to_all | solution.py:296
  108.0 2.5 %collective-permute-start.1 = (bf16[128,2048]{1,0:T(8,128)(2,1)S(1)}, bf16[128,2048]{1,0:T(8,128)(2,1)S(1)}, u32[]{:S(2)}, u32[]{:S(2)}) collective-permute-start(bf16[128,2048]{1,0:T(8,128)(2,1)S(1)} %copy-done.5), channel_id=1, source_target_pairs={{4,0},{8,4},{12,8},{16,12},{20,16},{24,20},{28,24},{5,1},{9,5},{13... | collective-permute-start | bytes 1572872 | tf_op jit(solution)/shard_map/ppermute | solution.py:20
  110.4 5.0 %shard_map.166 = f32[128,2048]{1,0:T(8,128)} custom-call(f32[16,128]{1,0:T(8,128)} %reshape.95.dec_ref, f32[16,128]{1,0:T(8,128)} %reshape.96.wt_ref, f32[16,2048]{1,0:T(8,128)} %get-tuple-element.19.ent_ref, f32[128,2048]{1,0:T(8,128)} %shard_map.165.loc_ref), custom_call_target="tpu_custom_call" | custom-call | tf_op jit(solution)/shard_map/pallas_call | solution.py:228
  115.4 2.5 %fusion.2 = (bf16[128,2048]{1,0:T(8,128)(2,1)}, bf16[128,2048]{1,0:T(8,128)(2,1)}) fusion(f32[128,2048]{1,0:T(8,128)} %shard_map.166, bf16[128,2048]{1,0:T(8,128)(2,1)S(1)} %copy-done.10, bf16[128,2048]{1,0:T(8,128)(2,1)S(1)} %copy-done.8), kind=kLoop, calls=%fused_computation.14 | loop fusion | flops 1572864 | bytes 3145728 | tf_op jit(solution)/shard_map/convert_element_type | solution.py:379
  117.9 15.1 %collective-permute-done.1.refs_2_ = bf16[128,2048]{1,0:T(8,128)(2,1)S(1)} collective-permute-done((bf16[128,2048]{1,0:T(8,128)(2,1)S(1)}, bf16[128,2048]{1,0:T(8,128)(2,1)S(1)}, u32[]{:S(2)}, u32[]{:S(2)}) %collective-permute-start.1) | collective-permute-done | bytes 524320 | tf_op jit(solution)/shard_map/ppermute | solution.py:20
  133.8 7.6 %shard_map.168 = (bf16[128,2048]{1,0:T(8,128)(2,1)}, bf16[128,2048]{1,0:T(8,128)(2,1)}) custom-call(f32[128,256]{1,0:T(8,128)} %concatenate.23.refs_0_, bf16[128,2048]{1,0:T(8,128)(2,1)} %get-tuple-element.24.refs_1_.back_ref, bf16[128,2048]{1,0:T(8,128)(2,1)} %copy-done.14, bf16[128,2048]{1,0:T(8,128)(2,1)} %refs_3_.1, bf16[128,2048]{1,0:T(8,128)(2,1)} %refs_4_.1), custom_call_target="tpu_custom_call" | custom-call | tf_op jit(solution)/shard_map/pallas_call | solution.py:140
  (75 shorter events, 20.2 us)
Async XLA Ops:
  0.6 6.5 %copy-start.7 = (bf16[128,2048]{1,0:T(8,128)(2,1)S(1)}, bf16[128,2048]{1,0:T(8,128)(2,1)}, u32[]{:S(2)}) copy-start(bf16[128,2048]{1,0:T(8,128)(2,1)} %param.13) | copy-start | bytes 1572868
  0.6 6.5 %copy-start.9 = (bf16[128,2048]{1,0:T(8,128)(2,1)S(1)}, bf16[128,2048]{1,0:T(8,128)(2,1)}, u32[]{:S(2)}) copy-start(bf16[128,2048]{1,0:T(8,128)(2,1)} %param.15) | copy-start | bytes 1572868
  2.1 12.3 %copy-start.2 = (bf16[128,2048]{1,0:T(8,128)(2,1)}, bf16[128,2048]{1,0:T(8,128)(2,1)S(1)}, u32[]{:S(2)}) copy-start(bf16[128,2048]{1,0:T(8,128)(2,1)S(1)} %multiply_convert_fusion.1.refs_2_.bot_ref) | copy-start | bytes 1572868
  2.1 15.6 %collective-permute-start = (bf16[128,2048]{1,0:T(8,128)(2,1)S(1)}, bf16[128,2048]{1,0:T(8,128)(2,1)S(1)}, u32[]{:S(2)}, u32[]{:S(2)}) collective-permute-start(bf16[128,2048]{1,0:T(8,128)(2,1)S(1)} %multiply_convert_fusion.1.refs_2_.bot_ref), channel_id=1, source_target_pairs={{0,4},{4,8},{8,12},{12,16},{16,20},{20,24},{24,28},{1,5},{5,9},{9,... | collective-permute-start | bytes 1572872 | tf_op jit(solution)/shard_map/ppermute | solution.py:20
  10.0 15.9 %copy-start.11 = (bf16[128,2048]{1,0:T(8,128)(2,1)S(1)}, bf16[128,2048]{1,0:T(8,128)(2,1)}, u32[]{:S(2)}) copy-start(bf16[128,2048]{1,0:T(8,128)(2,1)} %param.10) | copy-start | bytes 1572868
  16.1 17.2 %copy-start.3 = (bf16[128,2048]{1,0:T(8,128)(2,1)S(1)}, bf16[128,2048]{1,0:T(8,128)(2,1)}, u32[]{:S(2)}) copy-start(bf16[128,2048]{1,0:T(8,128)(2,1)} %param.14) | copy-start | bytes 1572868
  16.1 17.2 %copy-start.15 = (f32[2048]{0:T(1024)S(1)}, f32[2048]{0:T(1024)}, u32[]{:S(2)}) copy-start(f32[2048]{0:T(1024)} %param.17) | copy-start | bytes 24580
  17.6 0.8 copy-start.6
  40.8 14.6 %copy-start.16 = (f32[128,16]{0,1:T(8,128)S(1)}, f32[128,16]{0,1:T(8,128)}, u32[]{:S(2)}) copy-start(f32[128,16]{0,1:T(8,128)} %param.18) | copy-start | bytes 24580
  40.8 28.6 %all-to-all-start = ((bf16[8,32,2048]{2,1,0:T(8,128)(2,1)}), bf16[8,32,2048]{2,1,0:T(8,128)(2,1)S(1)}, u32[]{:S(2)}, u32[]{:S(2)}) async-start(bf16[8,32,2048]{2,1,0:T(8,128)(2,1)} %broadcast_in_dim.33), calls=%async_computation | async-start | bytes 2097152 | tf_op jit(solution)/shard_map/all_to_all | solution.py:296
  48.4 0.6 copy-start.12
  55.3 2.6 %copy-start.13 = (f32[128,1,128]{2,1,0:T(1,128)S(1)}, f32[128,1,128]{2,1,0:T(1,128)}, u32[]{:S(2)}) copy-start(f32[128,1,128]{2,1,0:T(1,128)} %copy-done.12) | copy-start | bytes 196612
  69.6 6.2 %copy-start.4 = (bf16[128,2048]{1,0:T(8,128)(2,1)S(1)}, bf16[128,2048]{1,0:T(8,128)(2,1)}, u32[]{:S(2)}) copy-start(bf16[128,2048]{1,0:T(8,128)(2,1)} %param.14) | copy-start | bytes 1572868
  70.8 13.5 %copy-start.1 = (f32[128,2048]{1,0:T(8,128)S(1)}, f32[128,2048]{1,0:T(8,128)}, u32[]{:S(2)}) copy-start(f32[128,2048]{1,0:T(8,128)} %shard_map.162) | copy-start | bytes 3145732
  75.8 8.4 %copy-start = (f32[128,2048]{1,0:T(8,128)S(1)}, f32[128,2048]{1,0:T(8,128)}, u32[]{:S(2)}) copy-start(f32[128,2048]{1,0:T(8,128)} %shard_map.167) | copy-start | bytes 3145732
  86.8 21.1 %copy-start.5 = (bf16[128,2048]{1,0:T(8,128)(2,1)S(1)}, bf16[128,2048]{1,0:T(8,128)(2,1)}, u32[]{:S(2)}) copy-start(bf16[128,2048]{1,0:T(8,128)(2,1)} %get-tuple-element.24.refs_1_.back_ref) | copy-start | bytes 1572868
  99.2 16.2 %copy-start.8 = (bf16[128,2048]{1,0:T(8,128)(2,1)S(1)}, bf16[128,2048]{1,0:T(8,128)(2,1)}, u32[]{:S(2)}) copy-start(bf16[128,2048]{1,0:T(8,128)(2,1)} %param.13) | copy-start | bytes 1572868
  99.3 16.2 %copy-start.10 = (bf16[128,2048]{1,0:T(8,128)(2,1)S(1)}, bf16[128,2048]{1,0:T(8,128)(2,1)}, u32[]{:S(2)}) copy-start(bf16[128,2048]{1,0:T(8,128)(2,1)} %param.15) | copy-start | bytes 1572868
  100.4 41.0 %all-to-all-start.1 = ((f32[8,1,18432]{2,1,0:T(1,128)}), f32[8,1,18432]{2,1,0:T(1,128)S(1)}, u32[]{:S(2)}, u32[]{:S(2)}) async-start(f32[8,1,18432]{2,1,0:T(1,128)} %broadcast_in_dim.62), calls=%async_computation.1 | async-start | bytes 1179648 | tf_op jit(solution)/shard_map/all_to_all | solution.py:296
  108.0 25.0 %collective-permute-start.1 = (bf16[128,2048]{1,0:T(8,128)(2,1)S(1)}, bf16[128,2048]{1,0:T(8,128)(2,1)S(1)}, u32[]{:S(2)}, u32[]{:S(2)}) collective-permute-start(bf16[128,2048]{1,0:T(8,128)(2,1)S(1)} %copy-done.5), channel_id=1, source_target_pairs={{4,0},{8,4},{12,8},{16,12},{20,16},{24,20},{28,24},{5,1},{9,5},{13... | collective-permute-start | bytes 1572872 | tf_op jit(solution)/shard_map/ppermute | solution.py:20
  133.0 0.8 copy-start.14

commit v7 on v6

--- a/solution.py
+++ b/solution.py
@@ -393,6 +393,7 @@
     diag_sums = gram_diag(back_mr, rim_rows, mixed_mr, group_size=group_size)
     filter_part = jnp.flip(diag_sums[:, tap_count:], 1)
     packed = jnp.concatenate([gain_part, filter_part.reshape(-1)])
+    packed, after_rim = lax.optimization_barrier((packed, after_rim))
     param_sums = jnp.sum(gather_seq(packed), axis=0) * grad_scale
     grad_gain = param_sums[:chan_count]
     grad_filter = param_sums[chan_count:].reshape(group_count, tap_count)

time: 144 us -> 130 us (0.903)
  the two profiles are of different devices: /device:TPU:14 before, /device:TPU:0 now
where the time goes in v7:
time: 130 us; the launch traced here: 129 us
  Pallas kernels  58 us (45%)
  other arithmetic  20.9 us (16%)
  starting transfers between devices  16.7 us (13%)
  blocking collectives  11.4 us (9%)
  waiting for transfers between devices  10.6 us (8%)
  local copies, waits for them, and re-layouts  9.48 us (7%)
    pallas_call x4, Pallas kernels, band_conv(): pl.pallas_call(kernel, grid=(chans // block,), in_specs=in_specs, out_spe...  27.7 us
    pallas_call x1, Pallas kernels, gram_diag(): pl.pallas_call(kernel, grid=(chans // block,), in_specs=[pl.BlockSpec((ro...  11.4 us
    all_to_all x2, starting transfers between devices, gather_seq(): return lax.all_to_all(tiled, 'seq', split_axis=0, concat_axis=0, tiled=True)  10.5 us
    pallas_call x2, Pallas kernels, modal_out(): pl.pallas_call(kernel, grid=(chans // block,), in_specs=[pl.BlockSpec(fla...  10.1 us
    pallas_call x2, Pallas kernels, modal_states(): pl.pallas_call(kernel, grid=(chans // block,), in_specs=[pl.BlockSpec((gr...  8.82 us
    all_to_all x2, waiting for transfers between devices, gather_seq(): return lax.all_to_all(tiled, 'seq', split_axis=0, concat_axis=0, tiled=True)  7.89 us
    ppermute x2, starting transfers between devices, from_behind(): lax.ppermute(value, axis, [(source, source + steps) for source in range(i...  6.18 us
    psum x1, blocking collectives, on_device(): squares = lax.psum(jnp.sum(out_full * out_full, axis=1), 'chan')  5.74 us
  transfers between devices with their start and end apart: 4, of which 3 were waited for; matrix products, arithmetic and copies ran while one was open for 11% of the time, Pallas kernels for 32%

profile of v7, /device:TPU:0, one launch (start us, length us, event | category | flops | bytes accessed | tf_op | source)
XLA Modules:
  0.0 129.0 jit_solution(3979708913229878808)
XLA Ops:
  0.7 1.4 %multiply_convert_fusion.1.refs_2_.bot_ref = bf16[128,2048]{1,0:T(8,128)(2,1)S(1)} fusion(bf16[128,2048]{1,0:T(8,128)(2,1)} %refs_3_.1, bf16[128,2048]{1,0:T(8,128)(2,1)} %refs_4_.1), kind=kLoop, calls=%fused_computation.31 | loop fusion | flops 1048576 | bytes 1572864 | tf_op jit(solution)/shard_map/convert_element_type | solution.py:340
  2.1 4.9 %collective-permute-start = (bf16[128,2048]{1,0:T(8,128)(2,1)S(1)}, bf16[128,2048]{1,0:T(8,128)(2,1)S(1)}, u32[]{:S(2)}, u32[]{:S(2)}) collective-permute-start(bf16[128,2048]{1,0:T(8,128)(2,1)S(1)} %multiply_convert_fusion.1.refs_2_.bot_ref), channel_id=1, source_target_pairs={{0,4},{4,8},{8,12},{12,16},{16,20},{20,24},{24,28},{1,5},{5,9},{9,... | collective-permute-start | bytes 1572872 | tf_op jit(solution)/shard_map/ppermute | solution.py:20
  9.8 1.7 %multiply_exponential_fusion.1 = (f32[128,16,128]{2,1,0:T(8,128)}, f32[128,16,128]{2,1,0:T(8,128)}) fusion(f32[128,16]{1,0:T(8,128)S(1)} %copy.29, f32[128]{0:T(128)S(1)} %iota_subtract_fusion), kind=kLoop, calls=%fused_computation.33 | loop fusion | flops 524288 | bytes 2105856 | tf_op jit(solution)/shard_map/exp | solution.py:359
  11.4 4.4 %shard_map.161 = f32[16,2048]{1,0:T(8,128)} custom-call(f32[128,16,128]{2,1,0:T(8,128)} %get-tuple-element.31.e_ref, bf16[128,2048]{1,0:T(8,128)(2,1)} %fusion.1.x_ref.refs_1_), custom_call_target="tpu_custom_call" | custom-call | tf_op jit(solution)/shard_map/pallas_call | solution.py:176
  18.9 7.5 %shard_map.162 = f32[128,2048]{1,0:T(8,128)} custom-call(f32[128,256]{1,0:T(8,128)} %maximum_maximum_fusion.refs_0_, bf16[128,2048]{1,0:T(8,128)(2,1)} %copy-done.5, bf16[128,2048]{1,0:T(8,128)(2,1)} %copy-done.2), custom_call_target="tpu_custom_call" | custom-call | tf_op jit(solution)/shard_map/pallas_call | solution.py:140
  26.4 1.5 %fusion.6 = (f32[128]{0:T(128)S(1)}, bf16[128,2048]{1,0:T(8,128)(2,1)S(1)}) fusion(f32[128,2048]{1,0:T(8,128)} %shard_map.162, bf16[128,2048]{1,0:T(8,128)(2,1)S(1)} %copy-done.10), kind=kLoop, calls=%fused_computation.18 | loop fusion | flops 1572736 | bytes 2097664 | tf_op jit(solution)/shard_map/reduce_sum | solution.py:345
  27.8 5.7 %psum.14 = f32[128]{0:T(128)S(1)} all-reduce(f32[128]{0:T(128)S(1)} %get-tuple-element.24), channel_id=1, replica_groups=mesh['seq'=8,'chan'=4] {'chan'}, use_global_device_ids=true, to_apply=%region_1.2 | all-reduce | flops 128 | bytes 1024 | tf_op jit(solution)/shard_map/psum | solution.py:345
  34.7 4.4 %shard_map.163 = f32[16,2048]{1,0:T(8,128)} custom-call(f32[128,16,128]{2,1,0:T(8,128)} %get-tuple-element.32.e_ref, bf16[128,2048]{1,0:T(8,128)(2,1)} %fusion.3.x_ref.refs_1_), custom_call_target="tpu_custom_call" | custom-call | tf_op jit(solution)/shard_map/pallas_call | solution.py:176
  41.1 6.9 %all-to-all-start = ((bf16[8,32,2048]{2,1,0:T(8,128)(2,1)}), bf16[8,32,2048]{2,1,0:T(8,128)(2,1)S(1)}, u32[]{:S(2)}, u32[]{:S(2)}) async-start(bf16[8,32,2048]{2,1,0:T(8,128)(2,1)} %broadcast_in_dim.33), calls=%async_computation | async-start | bytes 2097152 | tf_op jit(solution)/shard_map/all_to_all | solution.py:296
  49.9 6.3 %shard_map.164.loc_ref = f32[128,2048]{1,0:T(8,128)} custom-call(f32[128,128]{1,0:T(8,128)} %bitcast.12, bf16[128,2048]{1,0:T(8,128)(2,1)} %fusion.1.x_ref.refs_1_), custom_call_target="tpu_custom_call" | custom-call | tf_op jit(solution)/shard_map/pallas_call | solution.py:140
  59.6 6.3 %shard_map.165.loc_ref = f32[128,2048]{1,0:T(8,128)} custom-call(f32[128,128]{1,0:T(8,128)} %pad_maximum_fusion.2.refs_0_, bf16[128,2048]{1,0:T(8,128)(2,1)} %fusion.3.x_ref.refs_1_), custom_call_target="tpu_custom_call" | custom-call | tf_op jit(solution)/shard_map/pallas_call | solution.py:140
  65.8 7.9 %all-to-all-done = bf16[8,32,2048]{2,1,0:T(8,128)(2,1)S(1)} async-done(((bf16[8,32,2048]{2,1,0:T(8,128)(2,1)}), bf16[8,32,2048]{2,1,0:T(8,128)(2,1)S(1)}, u32[]{:S(2)}, u32[]{:S(2)}) %all-to-all-start) | async-done | bytes 1048608 | tf_op jit(solution)/shard_map/all_to_all | solution.py:296
  74.0 1.2 multiply_reduce_fusion
  75.2 5.1 %shard_map.167 = f32[128,2048]{1,0:T(8,128)} custom-call(f32[16,128]{1,0:T(8,128)} %reshape.95.dec_ref, f32[16,128]{1,0:T(8,128)} %reshape.96.wt_ref, f32[16,2048]{1,0:T(8,128)} %get-tuple-element.20.ent_ref, f32[128,2048]{1,0:T(8,128)} %shard_map.164.loc_ref), custom_call_target="tpu_custom_call" | custom-call | tf_op jit(solution)/shard_map/pallas_call | solution.py:228
  80.3 2.5 %fusion.15 = (f32[2048]{0:T(1024)S(1)}, f32[128]{0:T(128)S(1)}, bf16[128,2048]{1,0:T(8,128)(2,1)}) fusion(bf16[128,2048]{1,0:T(8,128)(2,1)S(1)} %get-tuple-element.25, f32[128]{0:T(128)S(1)} %get-tuple-element.37, f32[128,2048]{1,0:T(8,128)} %shard_map.167, bf16[128,2048]{1,0:T(8,128)(2,1)S(1)} %copy-done.4, f32[2048]{0:T(1024)S(1)} %copy-done.14), kind=kLoop, calls=%fused_computation.27 | loop fusion | flops 3405696 | bytes 2638848 | tf_op jit(solution)/shard_map/reduce_sum | solution.py:382
  82.8 5.6 %psum.15 = f32[128]{0:T(128)S(1)} all-reduce(f32[128]{0:T(128)S(1)} %get-tuple-element.23), channel_id=1, replica_groups=mesh['seq'=8,'chan'=4] {'chan'}, use_global_device_ids=true, to_apply=%region_5.6 | all-reduce | flops 128 | bytes 1024 | tf_op jit(solution)/shard_map/psum | solution.py:384
  88.5 2.6 %fusion.5 = (bf16[128,2048]{1,0:T(8,128)(2,1)}, bf16[128,2048]{1,0:T(8,128)(2,1)}) fusion(bf16[128,2048]{1,0:T(8,128)(2,1)} %param.10, f32[128]{0:T(128)S(1)} %psum.15, f32[128]{0:T(128)S(1)} %get-tuple-element.36, bf16[128,2048]{1,0:T(8,128)(2,1)S(1)} %get-tuple-element.25, f32[2048]{0:T(1024)S(1)} %copy-done.14, f32[128]{0:T(128)S(1)} %get-tuple-element.37, ...), kind=kLoop, calls=%fused_computation.17 | loop fusion | flops 3670016 | bytes 4728320 | tf_op jit(solution)/shard_map/convert_element_type | solution.py:387
  91.1 1.3 collective-permute-start.1
  92.3 11.4 %shard_map.169 = f32[128,256]{1,0:T(8,128)} custom-call(bf16[128,2048]{1,0:T(8,128)(2,1)} %get-tuple-element.26.refs_1_.back_ref, bf16[128,2048]{1,0:T(8,128)(2,1)} %copy-done.5, bf16[128,2048]{1,0:T(8,128)(2,1)} %copy-done.2), custom_call_target="tpu_custom_call" | custom-call | tf_op jit(solution)/shard_map/pallas_call | solution.py:279
  104.7 2.1 %collective-permute-done.1.refs_2_ = bf16[128,2048]{1,0:T(8,128)(2,1)S(1)} collective-permute-done((bf16[128,2048]{1,0:T(8,128)(2,1)}, bf16[128,2048]{1,0:T(8,128)(2,1)S(1)}, u32[]{:S(2)}, u32[]{:S(2)}) %collective-permute-start.1) | collective-permute-done | bytes 524320 | tf_op jit(solution)/shard_map/ppermute | solution.py:20
  108.0 3.6 %all-to-all-start.1 = ((f32[8,1,18432]{2,1,0:T(1,128)}), f32[8,1,18432]{2,1,0:T(1,128)S(1)}, u32[]{:S(2)}, u32[]{:S(2)}) async-start(f32[8,1,18432]{2,1,0:T(1,128)} %broadcast_in_dim.62), calls=%async_computation.1 | async-start | bytes 1179648 | tf_op jit(solution)/shard_map/all_to_all | solution.py:296
  112.2 5.0 %shard_map.166 = f32[128,2048]{1,0:T(8,128)} custom-call(f32[16,128]{1,0:T(8,128)} %reshape.95.dec_ref, f32[16,128]{1,0:T(8,128)} %reshape.96.wt_ref, f32[16,2048]{1,0:T(8,128)} %get-tuple-element.21.ent_ref, f32[128,2048]{1,0:T(8,128)} %shard_map.165.loc_ref), custom_call_target="tpu_custom_call" | custom-call | tf_op jit(solution)/shard_map/pallas_call | solution.py:228
  117.2 2.5 %fusion.2 = (bf16[128,2048]{1,0:T(8,128)(2,1)}, bf16[128,2048]{1,0:T(8,128)(2,1)}) fusion(f32[128,2048]{1,0:T(8,128)} %shard_map.166, bf16[128,2048]{1,0:T(8,128)(2,1)S(1)} %copy-done.9, bf16[128,2048]{1,0:T(8,128)(2,1)S(1)} %copy-done.7), kind=kLoop, calls=%fused_computation.14 | loop fusion | flops 1572864 | bytes 3145728 | tf_op jit(solution)/shard_map/convert_element_type | solution.py:379
  119.7 7.6 %shard_map.168 = (bf16[128,2048]{1,0:T(8,128)(2,1)}, bf16[128,2048]{1,0:T(8,128)(2,1)}) custom-call(f32[128,256]{1,0:T(8,128)} %concatenate.23.refs_0_, bf16[128,2048]{1,0:T(8,128)(2,1)} %get-tuple-element.26.refs_1_.back_ref, bf16[128,2048]{1,0:T(8,128)(2,1)} %copy-done.13, bf16[128,2048]{1,0:T(8,128)(2,1)} %refs_3_.1, bf16[128,2048]{1,0:T(8,128)(2,1)} %refs_4_.1), custom_call_target="tpu_custom_call" | custom-call | tf_op jit(solution)/shard_map/pallas_call | solution.py:140
  (73 shorter events, 18.8 us)
Async XLA Ops:
  0.6 7.9 %copy-start.6 = (bf16[128,2048]{1,0:T(8,128)(2,1)S(1)}, bf16[128,2048]{1,0:T(8,128)(2,1)}, u32[]{:S(2)}) copy-start(bf16[128,2048]{1,0:T(8,128)(2,1)} %param.13) | copy-start | bytes 1572868
  0.6 7.9 %copy-start.8 = (bf16[128,2048]{1,0:T(8,128)(2,1)S(1)}, bf16[128,2048]{1,0:T(8,128)(2,1)}, u32[]{:S(2)}) copy-start(bf16[128,2048]{1,0:T(8,128)(2,1)} %param.15) | copy-start | bytes 1572868
  2.1 13.8 %copy-start.2 = (bf16[128,2048]{1,0:T(8,128)(2,1)}, bf16[128,2048]{1,0:T(8,128)(2,1)S(1)}, u32[]{:S(2)}) copy-start(bf16[128,2048]{1,0:T(8,128)(2,1)S(1)} %multiply_convert_fusion.1.refs_2_.bot_ref) | copy-start | bytes 1572868
  2.1 16.0 %collective-permute-start = (bf16[128,2048]{1,0:T(8,128)(2,1)S(1)}, bf16[128,2048]{1,0:T(8,128)(2,1)S(1)}, u32[]{:S(2)}, u32[]{:S(2)}) collective-permute-start(bf16[128,2048]{1,0:T(8,128)(2,1)S(1)} %multiply_convert_fusion.1.refs_2_.bot_ref), channel_id=1, source_target_pairs={{0,4},{4,8},{8,12},{12,16},{16,20},{20,24},{24,28},{1,5},{5,9},{9,... | collective-permute-start | bytes 1572872 | tf_op jit(solution)/shard_map/ppermute | solution.py:20
  11.4 14.9 %copy-start.10 = (bf16[128,2048]{1,0:T(8,128)(2,1)S(1)}, bf16[128,2048]{1,0:T(8,128)(2,1)}, u32[]{:S(2)}) copy-start(bf16[128,2048]{1,0:T(8,128)(2,1)} %param.10) | copy-start | bytes 1572868
  17.6 16.0 %copy-start.3 = (bf16[128,2048]{1,0:T(8,128)(2,1)S(1)}, bf16[128,2048]{1,0:T(8,128)(2,1)}, u32[]{:S(2)}) copy-start(bf16[128,2048]{1,0:T(8,128)(2,1)} %param.14) | copy-start | bytes 1572868
  17.6 16.0 %copy-start.14 = (f32[2048]{0:T(1024)S(1)}, f32[2048]{0:T(1024)}, u32[]{:S(2)}) copy-start(f32[2048]{0:T(1024)} %param.17) | copy-start | bytes 24580
  18.1 0.8 copy-start.5
  41.1 15.2 %copy-start.15 = (f32[128,16]{0,1:T(8,128)S(1)}, f32[128,16]{0,1:T(8,128)}, u32[]{:S(2)}) copy-start(f32[128,16]{0,1:T(8,128)} %param.18) | copy-start | bytes 24580
  41.1 32.6 %all-to-all-start = ((bf16[8,32,2048]{2,1,0:T(8,128)(2,1)}), bf16[8,32,2048]{2,1,0:T(8,128)(2,1)S(1)}, u32[]{:S(2)}, u32[]{:S(2)}) async-start(bf16[8,32,2048]{2,1,0:T(8,128)(2,1)} %broadcast_in_dim.33), calls=%async_computation | async-start | bytes 2097152 | tf_op jit(solution)/shard_map/all_to_all | solution.py:296
  49.2 0.6 copy-start.11
  56.2 2.6 %copy-start.12 = (f32[128,1,128]{2,1,0:T(1,128)S(1)}, f32[128,1,128]{2,1,0:T(1,128)}, u32[]{:S(2)}) copy-start(f32[128,1,128]{2,1,0:T(1,128)} %copy-done.11) | copy-start | bytes 196612
  74.0 6.3 %copy-start.4 = (bf16[128,2048]{1,0:T(8,128)(2,1)S(1)}, bf16[128,2048]{1,0:T(8,128)(2,1)}, u32[]{:S(2)}) copy-start(bf16[128,2048]{1,0:T(8,128)(2,1)} %param.14) | copy-start | bytes 1572868
  75.2 13.3 %copy-start.1 = (f32[128,2048]{1,0:T(8,128)S(1)}, f32[128,2048]{1,0:T(8,128)}, u32[]{:S(2)}) copy-start(f32[128,2048]{1,0:T(8,128)} %shard_map.162) | copy-start | bytes 3145732
  80.3 8.2 %copy-start = (f32[128,2048]{1,0:T(8,128)S(1)}, f32[128,2048]{1,0:T(8,128)}, u32[]{:S(2)}) copy-start(f32[128,2048]{1,0:T(8,128)} %shard_map.167) | copy-start | bytes 3145732
  91.1 15.8 %collective-permute-start.1 = (bf16[128,2048]{1,0:T(8,128)(2,1)}, bf16[128,2048]{1,0:T(8,128)(2,1)S(1)}, u32[]{:S(2)}, u32[]{:S(2)}) collective-permute-start(bf16[128,2048]{1,0:T(8,128)(2,1)} %get-tuple-element.26.refs_1_.back_ref), channel_id=1, source_target_pairs={{4,0},{8,4},{12,8},{16,12},{20,16},{24,20},{28,24},{5,1},{9,5},{13... | collective-permute-start | bytes 1572872 | tf_op jit(solution)/shard_map/ppermute | solution.py:20
  104.7 12.5 %copy-start.7 = (bf16[128,2048]{1,0:T(8,128)(2,1)S(1)}, bf16[128,2048]{1,0:T(8,128)(2,1)}, u32[]{:S(2)}) copy-start(bf16[128,2048]{1,0:T(8,128)(2,1)} %param.13) | copy-start | bytes 1572868
  104.7 12.5 %copy-start.9 = (bf16[128,2048]{1,0:T(8,128)(2,1)S(1)}, bf16[128,2048]{1,0:T(8,128)(2,1)}, u32[]{:S(2)}) copy-start(bf16[128,2048]{1,0:T(8,128)(2,1)} %param.15) | copy-start | bytes 1572868
  106.8 10.4 %copy-start.13 = (bf16[128,2048]{1,0:T(8,128)(2,1)}, bf16[128,2048]{1,0:T(8,128)(2,1)S(1)}, u32[]{:S(2)}) copy-start(bf16[128,2048]{1,0:T(8,128)(2,1)S(1)} %collective-permute-done.1.refs_2_) | copy-start | bytes 1572868
  108.0 19.3 %all-to-all-start.1 = ((f32[8,1,18432]{2,1,0:T(1,128)}), f32[8,1,18432]{2,1,0:T(1,128)S(1)}, u32[]{:S(2)}, u32[]{:S(2)}) async-start(f32[8,1,18432]{2,1,0:T(1,128)} %broadcast_in_dim.62), calls=%async_computation.1 | async-start | bytes 1179648 | tf_op jit(solution)/shard_map/all_to_all | solution.py:296

commit v8 on v7

--- a/solution.py
+++ b/solution.py
@@ -186,7 +186,11 @@
     )(state_rows, x)
 
 
-def _modal_kernel(dec_ref, wt_ref, ent_ref, loc_ref, out_ref, *, group_size, forward, sub):
+def _modal_kernel(*refs, group_size, forward, sub, scaled):
+    if scaled:
+        dec_ref, wt_ref, ent_ref, loc_ref, first_ref, second_ref, out_ref, other_ref = refs
+    else:
+        dec_ref, wt_ref, ent_ref, loc_ref, out_ref = refs
     rows = out_ref.shape[0]
     modes = ent_ref.shape[0]
     groups_here = LANES // group_size
@@ -209,13 +213,18 @@
         y = jnp.dot(a_high, ent_high, preferred_element_type=jnp.float32)
         y = y + jnp.dot(a_low, ent_high, preferred_element_type=jnp.float32)
         y = y + jnp.dot(a_high, ent_low, preferred_element_type=jnp.float32)
-        out_ref[:, lanes] = loc_ref[:, lanes] + y
+        total = loc_ref[:, lanes] + y
+        if scaled:
+            out_ref[:, lanes] = (total * first_ref[:, lanes].astype(jnp.float32)).astype(out_ref.dtype)
+            other_ref[:, lanes] = (total * second_ref[:, lanes].astype(jnp.float32)).astype(other_ref.dtype)
+        else:
+            out_ref[:, lanes] = total
         return carry
 
     lax.fori_loop(0, sub, body, 0)
 
 
-def modal_out(decays, weights, entering, local, *, group_size, forward):
+def modal_out(decays, weights, entering, local, scale_pair=None, *, group_size, forward):
     rows, chans = local.shape
     block = min(BLOCK_LANES, chans)
     groups_block = block // group_size
@@ -224,20 +233,32 @@
     flat_decays = decays.reshape(-1, per_row)
     flat_weights = weights.reshape(-1, per_row)
     sub = block // LANES
-    kernel = functools.partial(_modal_kernel, group_size=group_size, forward=forward, sub=sub)
+    scaled = scale_pair is not None
+    kernel = functools.partial(
+        _modal_kernel, group_size=group_size, forward=forward, sub=sub, scaled=scaled
+    )
+    in_specs = [
+        pl.BlockSpec(flat_decays.shape, lambda b: (0, 0)),
+        pl.BlockSpec(flat_weights.shape, lambda b: (0, 0)),
+        pl.BlockSpec((modes, block), lambda b: (0, b)),
+        pl.BlockSpec((rows, block), lambda b: (0, b)),
+    ]
+    args = [flat_decays, flat_weights, entering, local]
+    out_specs = pl.BlockSpec((rows, block), lambda b: (0, b))
+    out_shape = jax.ShapeDtypeStruct((rows, chans), jnp.float32)
+    if scaled:
+        in_specs += [pl.BlockSpec((rows, block), lambda b: (0, b))] * 2
+        args += list(scale_pair)
+        out_specs = [out_specs, out_specs]
+        out_shape = [jax.ShapeDtypeStruct((rows, chans), jnp.bfloat16)] * 2
     return pl.pallas_call(
         kernel,
         grid=(chans // block,),
-        in_specs=[
-            pl.BlockSpec(flat_decays.shape, lambda b: (0, 0)),
-            pl.BlockSpec(flat_weights.shape, lambda b: (0, 0)),
-            pl.BlockSpec((modes, block), lambda b: (0, b)),
-            pl.BlockSpec((rows, block), lambda b: (0, b)),
-        ],
-        out_specs=pl.BlockSpec((rows, block), lambda b: (0, b)),
-        out_shape=jax.ShapeDtypeStruct((rows, chans), jnp.float32),
+        in_specs=in_specs,
+        out_specs=out_specs,
+        out_shape=out_shape,
         compiler_params=pltpu.CompilerParams(dimension_semantics=("parallel",)),
-    )(flat_decays, flat_weights, entering, local)
+    )(*args)
 
 
 def _gram_kernel(back_ref, top_ref, bot_ref, f_ref, *, group_size, sub):
@@ -373,10 +394,11 @@
     grad_mixed_li = modal_out(
         li_decay, weights_res, grad_ent, grad_loc, group_size=group_size, forward=False
     )
-    conv_li = modal_out(li_decay, weights_res, conv_ent, conv_loc, group_size=group_size, forward=True)
-
-    out_li = (query_li.astype(jnp.float32) * conv_li).astype(jnp.bfloat16)
-    grad_query_li = (cotan_full * conv_li).astype(jnp.bfloat16)
+    out_li, grad_query_li = modal_out(
+        li_decay, weights_res, conv_ent, conv_loc, (query_li, cotangent),
+        group_size=group_size, forward=True,
+    )
+
     grad_key_li = (grad_mixed_li * normed).astype(jnp.bfloat16)
     grad_normed = grad_mixed_li * key_li.astype(jnp.float32)
     gain_part = jnp.sum(grad_normed * out_full * inv_rms, axis=0)

time: 130 us -> 129 us (level)
  other arithmetic: 20.9 us -> 18.4 us
  waiting for transfers between devices: 10.6 us -> 12.3 us
    convert_element_type x1 -> x0, other arithmetic: 2.46 us -> none  [on_device(): grad_query_li = (cotan_full * conv_li).astype(jnp.bfloat16)]
    all_to_all x2, waiting for transfers between devices: 7.89 us -> 9.59 us  [gather_seq(): return lax.all_to_all(tiled, 'seq', split_axis=0, concat_axis=0, tiled=True)]
  transfers between devices with their start and end apart: 4 -> 4, of which waited for: 3 -> 4; matrix products, arithmetic and copies ran while one was open for 11% -> 10% of each run, Pallas kernels for 32% -> 32%
where the time goes in v8:
time: 129 us; the launch traced here: 128 us
  Pallas kernels  58.2 us (45%)
  other arithmetic  18.4 us (14%)
  starting transfers between devices  16.7 us (13%)
  waiting for transfers between devices  12.3 us (10%)
  blocking collectives  11.4 us (9%)
  local copies, waits for them, and re-layouts  9.48 us (7%)
    pallas_call x4, Pallas kernels, band_conv(): pl.pallas_call(kernel, grid=(chans // block,), in_specs=in_specs, out_spe...  27.7 us
    pallas_call x1, Pallas kernels, gram_diag(): pl.pallas_call(kernel, grid=(chans // block,), in_specs=[pl.BlockSpec((ro...  11.4 us
    all_to_all x2, starting transfers between devices, gather_seq(): return lax.all_to_all(tiled, 'seq', split_axis=0, concat_axis=0, tiled=True)  10.5 us
    pallas_call x2, Pallas kernels, modal_out(): pl.pallas_call(kernel, grid=(chans // block,), in_specs=in_specs, out_spe...  10.3 us
    all_to_all x2, waiting for transfers between devices, gather_seq(): return lax.all_to_all(tiled, 'seq', split_axis=0, concat_axis=0, tiled=True)  9.59 us
    pallas_call x2, Pallas kernels, modal_states(): pl.pallas_call(kernel, grid=(chans // block,), in_specs=[pl.BlockSpec((gr...  8.82 us
    ppermute x2, starting transfers between devices, from_behind(): lax.ppermute(value, axis, [(source, source + steps) for source in range(i...  6.18 us
    psum x1, blocking collectives, on_device(): squares = lax.psum(jnp.sum(out_full * out_full, axis=1), 'chan')  5.75 us
  transfers between devices with their start and end apart: 4, of which 4 were waited for; matrix products, arithmetic and copies ran while one was open for 10% of the time, Pallas kernels for 32%

profile of v8, /device:TPU:0, one launch (start us, length us, event | category | flops | bytes accessed | tf_op | source)
XLA Modules:
  0.0 128.4 jit_solution(6266193305818815754)
XLA Ops:
  0.7 1.4 %multiply_convert_fusion.1.refs_2_.bot_ref = bf16[128,2048]{1,0:T(8,128)(2,1)S(1)} fusion(bf16[128,2048]{1,0:T(8,128)(2,1)} %refs_3_.1, bf16[128,2048]{1,0:T(8,128)(2,1)} %refs_4_.3), kind=kLoop, calls=%fused_computation.25 | loop fusion | flops 1048576 | bytes 1572864 | tf_op jit(solution)/shard_map/convert_element_type | solution.py:361
  2.1 4.9 %collective-permute-start = (bf16[128,2048]{1,0:T(8,128)(2,1)S(1)}, bf16[128,2048]{1,0:T(8,128)(2,1)S(1)}, u32[]{:S(2)}, u32[]{:S(2)}) collective-permute-start(bf16[128,2048]{1,0:T(8,128)(2,1)S(1)} %multiply_convert_fusion.1.refs_2_.bot_ref), channel_id=1, source_target_pairs={{0,4},{4,8},{8,12},{12,16},{16,20},{20,24},{24,28},{1,5},{5,9},{9,... | collective-permute-start | bytes 1572872 | tf_op jit(solution)/shard_map/ppermute | solution.py:20
  9.8 1.7 %multiply_exponential_fusion.1 = (f32[128,16,128]{2,1,0:T(8,128)}, f32[128,16,128]{2,1,0:T(8,128)}) fusion(f32[128,16]{1,0:T(8,128)S(1)} %copy.29, f32[128]{0:T(128)S(1)} %iota_subtract_fusion), kind=kLoop, calls=%fused_computation.28 | loop fusion | flops 524288 | bytes 2105856 | tf_op jit(solution)/shard_map/exp | solution.py:380
  11.5 4.4 %shard_map.161 = f32[16,2048]{1,0:T(8,128)} custom-call(f32[128,16,128]{2,1,0:T(8,128)} %get-tuple-element.33.e_ref, bf16[128,2048]{1,0:T(8,128)(2,1)} %multiply_convert_fusion.2.x_ref.refs_1_), custom_call_target="tpu_custom_call" | custom-call | tf_op jit(solution)/shard_map/pallas_call | solution.py:176
  18.9 7.4 %shard_map.162 = f32[128,2048]{1,0:T(8,128)} custom-call(f32[128,256]{1,0:T(8,128)} %maximum_maximum_fusion.refs_0_, bf16[128,2048]{1,0:T(8,128)(2,1)} %copy-done.7, bf16[128,2048]{1,0:T(8,128)(2,1)} %copy-done.2), custom_call_target="tpu_custom_call" | custom-call | tf_op jit(solution)/shard_map/pallas_call | solution.py:140
  26.4 1.5 %fusion.3 = (f32[128]{0:T(128)S(1)}, bf16[128,2048]{1,0:T(8,128)(2,1)S(1)}) fusion(f32[128,2048]{1,0:T(8,128)} %shard_map.162, bf16[128,2048]{1,0:T(8,128)(2,1)S(1)} %copy-done.8), kind=kLoop, calls=%fused_computation.12 | loop fusion | flops 1572736 | bytes 2097664 | tf_op jit(solution)/shard_map/reduce_sum | solution.py:366
  27.8 5.8 %psum.14 = f32[128]{0:T(128)S(1)} all-reduce(f32[128]{0:T(128)S(1)} %get-tuple-element.28), channel_id=1, replica_groups=mesh['seq'=8,'chan'=4] {'chan'}, use_global_device_ids=true, to_apply=%region_1.2 | all-reduce | flops 128 | bytes 1024 | tf_op jit(solution)/shard_map/psum | solution.py:366
  34.7 4.4 %shard_map.163 = f32[16,2048]{1,0:T(8,128)} custom-call(f32[128,16,128]{2,1,0:T(8,128)} %get-tuple-element.34.e_ref, bf16[128,2048]{1,0:T(8,128)(2,1)} %fusion.x_ref.refs_1_), custom_call_target="tpu_custom_call" | custom-call | tf_op jit(solution)/shard_map/pallas_call | solution.py:176
  41.1 6.9 %all-to-all-start = ((bf16[8,32,2048]{2,1,0:T(8,128)(2,1)}), bf16[8,32,2048]{2,1,0:T(8,128)(2,1)S(1)}, u32[]{:S(2)}, u32[]{:S(2)}) async-start(bf16[8,32,2048]{2,1,0:T(8,128)(2,1)} %broadcast_in_dim.33), calls=%async_computation | async-start | bytes 2097152 | tf_op jit(solution)/shard_map/all_to_all | solution.py:317
  49.9 6.3 %shard_map.164.refs_3_ = f32[128,2048]{1,0:T(8,128)} custom-call(f32[128,128]{1,0:T(8,128)} %bitcast.12, bf16[128,2048]{1,0:T(8,128)(2,1)} %multiply_convert_fusion.2.x_ref.refs_1_), custom_call_target="tpu_custom_call" | custom-call | tf_op jit(solution)/shard_map/pallas_call | solution.py:140
  59.5 6.3 %shard_map.165.refs_3_ = f32[128,2048]{1,0:T(8,128)} custom-call(f32[128,128]{1,0:T(8,128)} %pad_maximum_fusion.2.refs_0_, bf16[128,2048]{1,0:T(8,128)(2,1)} %fusion.x_ref.refs_1_), custom_call_target="tpu_custom_call" | custom-call | tf_op jit(solution)/shard_map/pallas_call | solution.py:140
  65.8 7.9 %all-to-all-done = bf16[8,32,2048]{2,1,0:T(8,128)(2,1)S(1)} async-done(((bf16[8,32,2048]{2,1,0:T(8,128)(2,1)}), bf16[8,32,2048]{2,1,0:T(8,128)(2,1)S(1)}, u32[]{:S(2)}, u32[]{:S(2)}) %all-to-all-start) | async-done | bytes 1048608 | tf_op jit(solution)/shard_map/all_to_all | solution.py:317
  74.0 1.2 multiply_reduce_fusion
  75.1 5.1 %shard_map.167 = f32[128,2048]{1,0:T(8,128)} custom-call(f32[16,128]{1,0:T(8,128)} %reshape.95.refs_0_, f32[16,128]{1,0:T(8,128)} %reshape.96.refs_1_, f32[16,2048]{1,0:T(8,128)} %get-tuple-element.24.refs_2_, f32[128,2048]{1,0:T(8,128)} %shard_map.164.refs_3_), custom_call_target="tpu_custom_call" | custom-call | tf_op jit(solution)/shard_map/pallas_call | solution.py:254
  80.2 2.5 %fusion.12 = (f32[2048]{0:T(1024)S(1)}, f32[128]{0:T(128)S(1)}, bf16[128,2048]{1,0:T(8,128)(2,1)}) fusion(bf16[128,2048]{1,0:T(8,128)(2,1)S(1)} %get-tuple-element.29, f32[128]{0:T(128)S(1)} %get-tuple-element.39, f32[128,2048]{1,0:T(8,128)} %shard_map.167, bf16[128,2048]{1,0:T(8,128)(2,1)S(1)} %copy-done.4, f32[2048]{0:T(1024)S(1)} %copy-done.12), kind=kLoop, calls=%fused_computation.21 | loop fusion | flops 3405696 | bytes 2638848 | tf_op jit(solution)/shard_map/reduce_sum | solution.py:404
  82.7 5.6 %psum.15 = f32[128]{0:T(128)S(1)} all-reduce(f32[128]{0:T(128)S(1)} %get-tuple-element.27), channel_id=1, replica_groups=mesh['seq'=8,'chan'=4] {'chan'}, use_global_device_ids=true, to_apply=%region_5.6 | all-reduce | flops 128 | bytes 1024 | tf_op jit(solution)/shard_map/psum | solution.py:406
  88.4 2.6 %fusion.2 = (bf16[128,2048]{1,0:T(8,128)(2,1)}, bf16[128,2048]{1,0:T(8,128)(2,1)}) fusion(bf16[128,2048]{1,0:T(8,128)(2,1)} %param.10, f32[128]{0:T(128)S(1)} %psum.15, f32[128]{0:T(128)S(1)} %get-tuple-element.38, bf16[128,2048]{1,0:T(8,128)(2,1)S(1)} %get-tuple-element.29, f32[2048]{0:T(1024)S(1)} %copy-done.12, f32[128]{0:T(128)S(1)} %get-tuple-element.39, ...), kind=kLoop, calls=%fused_computation.11 | loop fusion | flops 3670016 | bytes 4728320 | tf_op jit(solution)/shard_map/convert_element_type | solution.py:409
  90.9 1.3 collective-permute-start.1
  92.2 11.4 %shard_map.169 = f32[128,256]{1,0:T(8,128)} custom-call(bf16[128,2048]{1,0:T(8,128)(2,1)} %get-tuple-element.30.refs_1_.back_ref, bf16[128,2048]{1,0:T(8,128)(2,1)} %copy-done.7, bf16[128,2048]{1,0:T(8,128)(2,1)} %copy-done.2), custom_call_target="tpu_custom_call" | custom-call | tf_op jit(solution)/shard_map/pallas_call | solution.py:300
  104.6 2.1 %collective-permute-done.1.refs_2_ = bf16[128,2048]{1,0:T(8,128)(2,1)S(1)} collective-permute-done((bf16[128,2048]{1,0:T(8,128)(2,1)}, bf16[128,2048]{1,0:T(8,128)(2,1)S(1)}, u32[]{:S(2)}, u32[]{:S(2)}) %collective-permute-start.1) | collective-permute-done | bytes 524320 | tf_op jit(solution)/shard_map/ppermute | solution.py:20
  107.9 3.6 %all-to-all-start.1 = ((f32[8,1,18432]{2,1,0:T(1,128)}), f32[8,1,18432]{2,1,0:T(1,128)S(1)}, u32[]{:S(2)}, u32[]{:S(2)}) async-start(f32[8,1,18432]{2,1,0:T(1,128)} %broadcast_in_dim.62), calls=%async_computation.1 | async-start | bytes 1179648 | tf_op jit(solution)/shard_map/all_to_all | solution.py:317
  112.2 5.3 %shard_map.166 = (bf16[128,2048]{1,0:T(8,128)(2,1)}, bf16[128,2048]{1,0:T(8,128)(2,1)}) custom-call(f32[16,128]{1,0:T(8,128)} %reshape.95.refs_0_, f32[16,128]{1,0:T(8,128)} %reshape.96.refs_1_, f32[16,2048]{1,0:T(8,128)} %get-tuple-element.25.refs_2_, f32[128,2048]{1,0:T(8,128)} %shard_map.165.refs_3_, bf16[128,2048]{1,0:T(8,128)(2,1)} %refs_4_.2, ...), custom_call_target="tpu_custom_call" | custom-call | tf_op jit(solution)/shard_map/pallas_call | solution.py:254
  117.4 7.6 %shard_map.168 = (bf16[128,2048]{1,0:T(8,128)(2,1)}, bf16[128,2048]{1,0:T(8,128)(2,1)}) custom-call(f32[128,256]{1,0:T(8,128)} %concatenate.23.refs_0_, bf16[128,2048]{1,0:T(8,128)(2,1)} %get-tuple-element.30.refs_1_.back_ref, bf16[128,2048]{1,0:T(8,128)(2,1)} %copy-done.11, bf16[128,2048]{1,0:T(8,128)(2,1)} %refs_3_.1, bf16[128,2048]{1,0:T(8,128)(2,1)} %refs_4_.3), custom_call_target="tpu_custom_call" | custom-call | tf_op jit(solution)/shard_map/pallas_call | solution.py:140
  125.0 1.7 %all-to-all-done.1 = f32[8,1,18432]{2,1,0:T(1,128)S(1)} async-done(((f32[8,1,18432]{2,1,0:T(1,128)}), f32[8,1,18432]{2,1,0:T(1,128)S(1)}, u32[]{:S(2)}, u32[]{:S(2)}) %all-to-all-start.1) | async-done | bytes 589856 | tf_op jit(solution)/shard_map/all_to_all | solution.py:317
  (68 shorter events, 18.8 us)
Async XLA Ops:
  0.6 7.9 %copy-start.5 = (bf16[128,2048]{1,0:T(8,128)(2,1)S(1)}, bf16[128,2048]{1,0:T(8,128)(2,1)}, u32[]{:S(2)}) copy-start(bf16[128,2048]{1,0:T(8,128)(2,1)} %refs_4_.2) | copy-start | bytes 1572868
  0.6 7.9 %copy-start.6 = (bf16[128,2048]{1,0:T(8,128)(2,1)S(1)}, bf16[128,2048]{1,0:T(8,128)(2,1)}, u32[]{:S(2)}) copy-start(bf16[128,2048]{1,0:T(8,128)(2,1)} %refs_5_.1) | copy-start | bytes 1572868
  2.1 13.8 %copy-start.2 = (bf16[128,2048]{1,0:T(8,128)(2,1)}, bf16[128,2048]{1,0:T(8,128)(2,1)S(1)}, u32[]{:S(2)}) copy-start(bf16[128,2048]{1,0:T(8,128)(2,1)S(1)} %multiply_convert_fusion.1.refs_2_.bot_ref) | copy-start | bytes 1572868
  2.1 16.0 %collective-permute-start = (bf16[128,2048]{1,0:T(8,128)(2,1)S(1)}, bf16[128,2048]{1,0:T(8,128)(2,1)S(1)}, u32[]{:S(2)}, u32[]{:S(2)}) collective-permute-start(bf16[128,2048]{1,0:T(8,128)(2,1)S(1)} %multiply_convert_fusion.1.refs_2_.bot_ref), channel_id=1, source_target_pairs={{0,4},{4,8},{8,12},{12,16},{16,20},{20,24},{24,28},{1,5},{5,9},{9,... | collective-permute-start | bytes 1572872 | tf_op jit(solution)/shard_map/ppermute | solution.py:20
  11.5 14.9 %copy-start.8 = (bf16[128,2048]{1,0:T(8,128)(2,1)S(1)}, bf16[128,2048]{1,0:T(8,128)(2,1)}, u32[]{:S(2)}) copy-start(bf16[128,2048]{1,0:T(8,128)(2,1)} %param.10) | copy-start | bytes 1572868
  17.6 16.0 %copy-start.3 = (bf16[128,2048]{1,0:T(8,128)(2,1)S(1)}, bf16[128,2048]{1,0:T(8,128)(2,1)}, u32[]{:S(2)}) copy-start(bf16[128,2048]{1,0:T(8,128)(2,1)} %param.14) | copy-start | bytes 1572868
  17.6 16.0 %copy-start.12 = (f32[2048]{0:T(1024)S(1)}, f32[2048]{0:T(1024)}, u32[]{:S(2)}) copy-start(f32[2048]{0:T(1024)} %param.17) | copy-start | bytes 24580
  18.1 0.8 copy-start.7
  41.1 15.2 %copy-start.13 = (f32[128,16]{0,1:T(8,128)S(1)}, f32[128,16]{0,1:T(8,128)}, u32[]{:S(2)}) copy-start(f32[128,16]{0,1:T(8,128)} %param.18) | copy-start | bytes 24580
  41.1 32.6 %all-to-all-start = ((bf16[8,32,2048]{2,1,0:T(8,128)(2,1)}), bf16[8,32,2048]{2,1,0:T(8,128)(2,1)S(1)}, u32[]{:S(2)}, u32[]{:S(2)}) async-start(bf16[8,32,2048]{2,1,0:T(8,128)(2,1)} %broadcast_in_dim.33), calls=%async_computation | async-start | bytes 2097152 | tf_op jit(solution)/shard_map/all_to_all | solution.py:317
  49.2 0.6 copy-start.9
  56.2 2.6 %copy-start.10 = (f32[128,1,128]{2,1,0:T(1,128)S(1)}, f32[128,1,128]{2,1,0:T(1,128)}, u32[]{:S(2)}) copy-start(f32[128,1,128]{2,1,0:T(1,128)} %copy-done.9) | copy-start | bytes 196612
  74.0 6.2 %copy-start.4 = (bf16[128,2048]{1,0:T(8,128)(2,1)S(1)}, bf16[128,2048]{1,0:T(8,128)(2,1)}, u32[]{:S(2)}) copy-start(bf16[128,2048]{1,0:T(8,128)(2,1)} %param.14) | copy-start | bytes 1572868
  75.1 13.2 %copy-start.1 = (f32[128,2048]{1,0:T(8,128)S(1)}, f32[128,2048]{1,0:T(8,128)}, u32[]{:S(2)}) copy-start(f32[128,2048]{1,0:T(8,128)} %shard_map.162) | copy-start | bytes 3145732
  80.2 8.2 %copy-start = (f32[128,2048]{1,0:T(8,128)S(1)}, f32[128,2048]{1,0:T(8,128)}, u32[]{:S(2)}) copy-start(f32[128,2048]{1,0:T(8,128)} %shard_map.167) | copy-start | bytes 3145732
  90.9 15.8 %collective-permute-start.1 = (bf16[128,2048]{1,0:T(8,128)(2,1)}, bf16[128,2048]{1,0:T(8,128)(2,1)S(1)}, u32[]{:S(2)}, u32[]{:S(2)}) collective-permute-start(bf16[128,2048]{1,0:T(8,128)(2,1)} %get-tuple-element.30.refs_1_.back_ref), channel_id=1, source_target_pairs={{4,0},{8,4},{12,8},{16,12},{20,16},{24,20},{28,24},{5,1},{9,5},{13... | collective-permute-start | bytes 1572872 | tf_op jit(solution)/shard_map/ppermute | solution.py:20
  106.7 10.7 %copy-start.11 = (bf16[128,2048]{1,0:T(8,128)(2,1)}, bf16[128,2048]{1,0:T(8,128)(2,1)S(1)}, u32[]{:S(2)}) copy-start(bf16[128,2048]{1,0:T(8,128)(2,1)S(1)} %collective-permute-done.1.refs_2_) | copy-start | bytes 1572868
  107.9 18.8 %all-to-all-start.1 = ((f32[8,1,18432]{2,1,0:T(1,128)}), f32[8,1,18432]{2,1,0:T(1,128)S(1)}, u32[]{:S(2)}, u32[]{:S(2)}) async-start(f32[8,1,18432]{2,1,0:T(1,128)} %broadcast_in_dim.62), calls=%async_computation.1 | async-start | bytes 1179648 | tf_op jit(solution)/shard_map/all_to_all | solution.py:317

commit v9 on v8

--- a/solution.py
+++ b/solution.py
@@ -205,14 +205,11 @@
         row = pl.program_id(0) * sub + j
         rate = dec_ref[pl.ds(row, 1), :]
         weight = wt_ref[pl.ds(row, 1), :]
-        a_high, a_low = _split(weight * jnp.exp(-rate * dist))
+        out_w = (weight * jnp.exp(-rate * dist)).astype(jnp.bfloat16)
         entering = ent_ref[:, lanes]
         tiled = jnp.concatenate([entering] * groups_here, axis=0)
-        diag = jnp.where(row_group == lane_group, tiled, 0.0)
-        ent_high, ent_low = _split(diag)
-        y = jnp.dot(a_high, ent_high, preferred_element_type=jnp.float32)
-        y = y + jnp.dot(a_low, ent_high, preferred_element_type=jnp.float32)
-        y = y + jnp.dot(a_high, ent_low, preferred_element_type=jnp.float32)
+        diag = jnp.where(row_group == lane_group, tiled, 0.0).astype(jnp.bfloat16)
+        y = jnp.dot(out_w, diag, preferred_element_type=jnp.float32)
         total = loc_ref[:, lanes] + y
         if scaled:
             out_ref[:, lanes] = (total * first_ref[:, lanes].astype(jnp.float32)).astype(out_ref.dtype)
@@ -376,8 +373,8 @@
         "gr,grd->gd", weights_res, jnp.exp(-li_decay[:, :, None] * offsets), precision=HIGHEST
     )
     li_fwd_rows = jnp.concatenate([taps_li[:, :1], jnp.flip(taps_li[:, 1:], 1)], 1)
-    fwd_states = jnp.exp(-li_decay[:, :, None] * (row_count - 1.0 - offsets))
-    bwd_states = jnp.exp(-li_decay[:, :, None] * offsets)
+    fwd_states = jnp.exp(-li_decay[:, :, None] * (row_count - 1.0 - offsets)).astype(jnp.bfloat16)
+    bwd_states = jnp.exp(-li_decay[:, :, None] * offsets).astype(jnp.bfloat16)
 
     back_li_bf = back_li.astype(jnp.bfloat16)
     mixed_li_bf = mixed_li.astype(jnp.bfloat16)

time: 129 us -> 129 us (level)
    exp x1 -> x0, other arithmetic: 1.68 us -> none  [on_device(): bwd_states = jnp.exp(-li_decay[:, :, None] * offsets)]
    convert_element_type x0 -> x1, other arithmetic: none -> 1.32 us  [on_device(): bwd_states = jnp.exp(-li_decay[:, :, None] * offsets).astype(jnp.bfloat16)]
  transfers between devices with their start and end apart: 4 -> 4, of which waited for: 4 -> 4; matrix products, arithmetic and copies ran while one was open for 10% -> 9% of each run, Pallas kernels for 32% -> 32%
where the time goes in v9:
time: 129 us; the launch traced here: 128 us
  Pallas kernels  57.4 us (44%)
  other arithmetic  18 us (14%)
  starting transfers between devices  16.7 us (13%)
  waiting for transfers between devices  13.1 us (10%)
  blocking collectives  11.3 us (9%)
  local copies, waits for them, and re-layouts  9.48 us (7%)
    pallas_call x4, Pallas kernels, band_conv(): pl.pallas_call(kernel, grid=(chans // block,), in_specs=in_specs, out_spe...  27.7 us
    pallas_call x1, Pallas kernels, gram_diag(): pl.pallas_call(kernel, grid=(chans // block,), in_specs=[pl.BlockSpec((ro...  11.4 us
    all_to_all x2, starting transfers between devices, gather_seq(): return lax.all_to_all(tiled, 'seq', split_axis=0, concat_axis=0, tiled=True)  10.5 us
    all_to_all x2, waiting for transfers between devices, gather_seq(): return lax.all_to_all(tiled, 'seq', split_axis=0, concat_axis=0, tiled=True)  9.96 us
    pallas_call x2, Pallas kernels, modal_out(): pl.pallas_call(kernel, grid=(chans // block,), in_specs=in_specs, out_spe...  9.56 us
    pallas_call x2, Pallas kernels, modal_states(): pl.pallas_call(kernel, grid=(chans // block,), in_specs=[pl.BlockSpec((gr...  8.75 us
    ppermute x2, starting transfers between devices, from_behind(): lax.ppermute(value, axis, [(source, source + steps) for source in range(i...  6.18 us
    psum x1, blocking collectives, on_device(): squares = lax.psum(jnp.sum(out_full * out_full, axis=1), 'chan')  5.71 us
  transfers between devices with their start and end apart: 4, of which 4 were waited for; matrix products, arithmetic and copies ran while one was open for 9% of the time, Pallas kernels for 32%

profile of v9, /device:TPU:0, one launch (start us, length us, event | category | flops | bytes accessed | tf_op | source)
XLA Modules:
  0.0 128.0 jit_solution(6522788517371482303)
XLA Ops:
  0.7 1.4 %multiply_convert_fusion.1.refs_2_.bot_ref = bf16[128,2048]{1,0:T(8,128)(2,1)S(1)} fusion(bf16[128,2048]{1,0:T(8,128)(2,1)} %refs_3_.1, bf16[128,2048]{1,0:T(8,128)(2,1)} %refs_4_.3), kind=kLoop, calls=%fused_computation.25 | loop fusion | flops 1048576 | bytes 1572864 | tf_op jit(solution)/shard_map/convert_element_type | solution.py:358
  2.1 4.9 %collective-permute-start = (bf16[128,2048]{1,0:T(8,128)(2,1)S(1)}, bf16[128,2048]{1,0:T(8,128)(2,1)S(1)}, u32[]{:S(2)}, u32[]{:S(2)}) collective-permute-start(bf16[128,2048]{1,0:T(8,128)(2,1)S(1)} %multiply_convert_fusion.1.refs_2_.bot_ref), channel_id=1, source_target_pairs={{0,4},{4,8},{8,12},{12,16},{16,20},{20,24},{24,28},{1,5},{5,9},{9,... | collective-permute-start | bytes 1572872 | tf_op jit(solution)/shard_map/ppermute | solution.py:20
  9.8 1.3 %fusion.14 = (bf16[128,16,128]{2,1,0:T(8,128)(2,1)}, bf16[128,16,128]{2,1,0:T(8,128)(2,1)}) fusion(f32[128,16]{1,0:T(8,128)S(1)} %copy.29, f32[128]{0:T(128)S(1)} %iota_subtract_fusion), kind=kLoop, calls=%fused_computation.30 | loop fusion | flops 1048576 | bytes 1057280 | tf_op jit(solution)/shard_map/convert_element_type | solution.py:377
  11.1 4.4 %shard_map.161 = f32[16,2048]{1,0:T(8,128)} custom-call(bf16[128,16,128]{2,1,0:T(8,128)(2,1)} %get-tuple-element.33.e_ref, bf16[128,2048]{1,0:T(8,128)(2,1)} %multiply_convert_fusion.2.x_ref.refs_1_), custom_call_target="tpu_custom_call" | custom-call | tf_op jit(solution)/shard_map/pallas_call | solution.py:176
  18.9 7.4 %shard_map.162 = f32[128,2048]{1,0:T(8,128)} custom-call(f32[128,256]{1,0:T(8,128)} %maximum_maximum_fusion.refs_0_, bf16[128,2048]{1,0:T(8,128)(2,1)} %copy-done.7, bf16[128,2048]{1,0:T(8,128)(2,1)} %copy-done.2), custom_call_target="tpu_custom_call" | custom-call | tf_op jit(solution)/shard_map/pallas_call | solution.py:140
  26.4 1.5 %fusion.3 = (f32[128]{0:T(128)S(1)}, bf16[128,2048]{1,0:T(8,128)(2,1)S(1)}) fusion(f32[128,2048]{1,0:T(8,128)} %shard_map.162, bf16[128,2048]{1,0:T(8,128)(2,1)S(1)} %copy-done.8), kind=kLoop, calls=%fused_computation.12 | loop fusion | flops 1572736 | bytes 2097664 | tf_op jit(solution)/shard_map/reduce_sum | solution.py:363
  27.8 5.7 %psum.14 = f32[128]{0:T(128)S(1)} all-reduce(f32[128]{0:T(128)S(1)} %get-tuple-element.28), channel_id=1, replica_groups=mesh['seq'=8,'chan'=4] {'chan'}, use_global_device_ids=true, to_apply=%region_1.2 | all-reduce | flops 128 | bytes 1024 | tf_op jit(solution)/shard_map/psum | solution.py:363
  34.6 4.3 %shard_map.163 = f32[16,2048]{1,0:T(8,128)} custom-call(bf16[128,16,128]{2,1,0:T(8,128)(2,1)} %get-tuple-element.34.e_ref, bf16[128,2048]{1,0:T(8,128)(2,1)} %fusion.x_ref.refs_1_), custom_call_target="tpu_custom_call" | custom-call | tf_op jit(solution)/shard_map/pallas_call | solution.py:176
  41.0 6.9 %all-to-all-start = ((bf16[8,32,2048]{2,1,0:T(8,128)(2,1)}), bf16[8,32,2048]{2,1,0:T(8,128)(2,1)S(1)}, u32[]{:S(2)}, u32[]{:S(2)}) async-start(bf16[8,32,2048]{2,1,0:T(8,128)(2,1)} %broadcast_in_dim.33), calls=%async_computation | async-start | bytes 2097152 | tf_op jit(solution)/shard_map/all_to_all | solution.py:314
  49.8 6.3 %shard_map.164.refs_3_ = f32[128,2048]{1,0:T(8,128)} custom-call(f32[128,128]{1,0:T(8,128)} %bitcast.12, bf16[128,2048]{1,0:T(8,128)(2,1)} %multiply_convert_fusion.2.x_ref.refs_1_), custom_call_target="tpu_custom_call" | custom-call | tf_op jit(solution)/shard_map/pallas_call | solution.py:140
  59.5 6.3 %shard_map.165.refs_3_ = f32[128,2048]{1,0:T(8,128)} custom-call(f32[128,128]{1,0:T(8,128)} %pad_maximum_fusion.2.refs_0_, bf16[128,2048]{1,0:T(8,128)(2,1)} %fusion.x_ref.refs_1_), custom_call_target="tpu_custom_call" | custom-call | tf_op jit(solution)/shard_map/pallas_call | solution.py:140
  65.8 7.9 %all-to-all-done = bf16[8,32,2048]{2,1,0:T(8,128)(2,1)S(1)} async-done(((bf16[8,32,2048]{2,1,0:T(8,128)(2,1)}), bf16[8,32,2048]{2,1,0:T(8,128)(2,1)S(1)}, u32[]{:S(2)}, u32[]{:S(2)}) %all-to-all-start) | async-done | bytes 1048608 | tf_op jit(solution)/shard_map/all_to_all | solution.py:314
  73.9 1.2 multiply_reduce_fusion
  75.1 4.7 %shard_map.167 = f32[128,2048]{1,0:T(8,128)} custom-call(f32[16,128]{1,0:T(8,128)} %reshape.95.refs_0_, f32[16,128]{1,0:T(8,128)} %reshape.96.refs_1_, f32[16,2048]{1,0:T(8,128)} %get-tuple-element.24.refs_2_, f32[128,2048]{1,0:T(8,128)} %shard_map.164.refs_3_), custom_call_target="tpu_custom_call" | custom-call | tf_op jit(solution)/shard_map/pallas_call | solution.py:251
  79.8 2.5 %fusion.12 = (f32[2048]{0:T(1024)S(1)}, f32[128]{0:T(128)S(1)}, bf16[128,2048]{1,0:T(8,128)(2,1)}) fusion(bf16[128,2048]{1,0:T(8,128)(2,1)S(1)} %get-tuple-element.29, f32[128]{0:T(128)S(1)} %get-tuple-element.39, f32[128,2048]{1,0:T(8,128)} %shard_map.167, bf16[128,2048]{1,0:T(8,128)(2,1)S(1)} %copy-done.4, f32[2048]{0:T(1024)S(1)} %copy-done.12), kind=kLoop, calls=%fused_computation.21 | loop fusion | flops 3405696 | bytes 2638848 | tf_op jit(solution)/shard_map/reduce_sum | solution.py:401
  82.3 5.6 %psum.15 = f32[128]{0:T(128)S(1)} all-reduce(f32[128]{0:T(128)S(1)} %get-tuple-element.27), channel_id=1, replica_groups=mesh['seq'=8,'chan'=4] {'chan'}, use_global_device_ids=true, to_apply=%region_5.6 | all-reduce | flops 128 | bytes 1024 | tf_op jit(solution)/shard_map/psum | solution.py:403
  87.9 2.6 %fusion.2 = (bf16[128,2048]{1,0:T(8,128)(2,1)}, bf16[128,2048]{1,0:T(8,128)(2,1)}) fusion(bf16[128,2048]{1,0:T(8,128)(2,1)} %param.10, f32[128]{0:T(128)S(1)} %psum.15, f32[128]{0:T(128)S(1)} %get-tuple-element.38, bf16[128,2048]{1,0:T(8,128)(2,1)S(1)} %get-tuple-element.29, f32[2048]{0:T(1024)S(1)} %copy-done.12, f32[128]{0:T(128)S(1)} %get-tuple-element.39, ...), kind=kLoop, calls=%fused_computation.11 | loop fusion | flops 3670016 | bytes 4728320 | tf_op jit(solution)/shard_map/convert_element_type | solution.py:406
  90.5 1.3 %collective-permute-start.1 = (bf16[128,2048]{1,0:T(8,128)(2,1)}, bf16[128,2048]{1,0:T(8,128)(2,1)S(1)}, u32[]{:S(2)}, u32[]{:S(2)}) collective-permute-start(bf16[128,2048]{1,0:T(8,128)(2,1)} %get-tuple-element.30.refs_1_.back_ref), channel_id=1, source_target_pairs={{4,0},{8,4},{12,8},{16,12},{20,16},{24,20},{28,24},{5,1},{9,5},{13... | collective-permute-start | bytes 1572872 | tf_op jit(solution)/shard_map/ppermute | solution.py:20
  91.8 11.4 %shard_map.169 = f32[128,256]{1,0:T(8,128)} custom-call(bf16[128,2048]{1,0:T(8,128)(2,1)} %get-tuple-element.30.refs_1_.back_ref, bf16[128,2048]{1,0:T(8,128)(2,1)} %copy-done.7, bf16[128,2048]{1,0:T(8,128)(2,1)} %copy-done.2), custom_call_target="tpu_custom_call" | custom-call | tf_op jit(solution)/shard_map/pallas_call | solution.py:297
  104.2 2.1 %collective-permute-done.1.refs_2_ = bf16[128,2048]{1,0:T(8,128)(2,1)S(1)} collective-permute-done((bf16[128,2048]{1,0:T(8,128)(2,1)}, bf16[128,2048]{1,0:T(8,128)(2,1)S(1)}, u32[]{:S(2)}, u32[]{:S(2)}) %collective-permute-start.1) | collective-permute-done | bytes 524320 | tf_op jit(solution)/shard_map/ppermute | solution.py:20
  107.5 3.6 %all-to-all-start.1 = ((f32[8,1,18432]{2,1,0:T(1,128)}), f32[8,1,18432]{2,1,0:T(1,128)S(1)}, u32[]{:S(2)}, u32[]{:S(2)}) async-start(f32[8,1,18432]{2,1,0:T(1,128)} %broadcast_in_dim.62), calls=%async_computation.1 | async-start | bytes 1179648 | tf_op jit(solution)/shard_map/all_to_all | solution.py:314
  111.7 4.9 %shard_map.166 = (bf16[128,2048]{1,0:T(8,128)(2,1)}, bf16[128,2048]{1,0:T(8,128)(2,1)}) custom-call(f32[16,128]{1,0:T(8,128)} %reshape.95.refs_0_, f32[16,128]{1,0:T(8,128)} %reshape.96.refs_1_, f32[16,2048]{1,0:T(8,128)} %get-tuple-element.25.refs_2_, f32[128,2048]{1,0:T(8,128)} %shard_map.165.refs_3_, bf16[128,2048]{1,0:T(8,128)(2,1)} %refs_4_.2, ...), custom_call_target="tpu_custom_call" | custom-call | tf_op jit(solution)/shard_map/pallas_call | solution.py:251
  116.6 7.6 %shard_map.168 = (bf16[128,2048]{1,0:T(8,128)(2,1)}, bf16[128,2048]{1,0:T(8,128)(2,1)}) custom-call(f32[128,256]{1,0:T(8,128)} %concatenate.23.refs_0_, bf16[128,2048]{1,0:T(8,128)(2,1)} %get-tuple-element.30.refs_1_.back_ref, bf16[128,2048]{1,0:T(8,128)(2,1)} %copy-done.11, bf16[128,2048]{1,0:T(8,128)(2,1)} %refs_3_.1, bf16[128,2048]{1,0:T(8,128)(2,1)} %refs_4_.3), custom_call_target="tpu_custom_call" | custom-call | tf_op jit(solution)/shard_map/pallas_call | solution.py:140
  124.2 2.1 %all-to-all-done.1 = f32[8,1,18432]{2,1,0:T(1,128)S(1)} async-done(((f32[8,1,18432]{2,1,0:T(1,128)}), f32[8,1,18432]{2,1,0:T(1,128)S(1)}, u32[]{:S(2)}, u32[]{:S(2)}) %all-to-all-start.1) | async-done | bytes 589856 | tf_op jit(solution)/shard_map/all_to_all | solution.py:314
  (68 shorter events, 19.2 us)
Async XLA Ops:
  0.6 7.9 %copy-start.5 = (bf16[128,2048]{1,0:T(8,128)(2,1)S(1)}, bf16[128,2048]{1,0:T(8,128)(2,1)}, u32[]{:S(2)}) copy-start(bf16[128,2048]{1,0:T(8,128)(2,1)} %refs_4_.2) | copy-start | bytes 1572868
  0.6 7.9 %copy-start.6 = (bf16[128,2048]{1,0:T(8,128)(2,1)S(1)}, bf16[128,2048]{1,0:T(8,128)(2,1)}, u32[]{:S(2)}) copy-start(bf16[128,2048]{1,0:T(8,128)(2,1)} %refs_5_.1) | copy-start | bytes 1572868
  2.1 13.4 %copy-start.2 = (bf16[128,2048]{1,0:T(8,128)(2,1)}, bf16[128,2048]{1,0:T(8,128)(2,1)S(1)}, u32[]{:S(2)}) copy-start(bf16[128,2048]{1,0:T(8,128)(2,1)S(1)} %multiply_convert_fusion.1.refs_2_.bot_ref) | copy-start | bytes 1572868
  2.1 16.0 %collective-permute-start = (bf16[128,2048]{1,0:T(8,128)(2,1)S(1)}, bf16[128,2048]{1,0:T(8,128)(2,1)S(1)}, u32[]{:S(2)}, u32[]{:S(2)}) collective-permute-start(bf16[128,2048]{1,0:T(8,128)(2,1)S(1)} %multiply_convert_fusion.1.refs_2_.bot_ref), channel_id=1, source_target_pairs={{0,4},{4,8},{8,12},{12,16},{16,20},{20,24},{24,28},{1,5},{5,9},{9,... | collective-permute-start | bytes 1572872 | tf_op jit(solution)/shard_map/ppermute | solution.py:20
  11.1 15.3 %copy-start.8 = (bf16[128,2048]{1,0:T(8,128)(2,1)S(1)}, bf16[128,2048]{1,0:T(8,128)(2,1)}, u32[]{:S(2)}) copy-start(bf16[128,2048]{1,0:T(8,128)(2,1)} %param.10) | copy-start | bytes 1572868
  17.2 16.4 %copy-start.3 = (bf16[128,2048]{1,0:T(8,128)(2,1)S(1)}, bf16[128,2048]{1,0:T(8,128)(2,1)}, u32[]{:S(2)}) copy-start(bf16[128,2048]{1,0:T(8,128)(2,1)} %param.14) | copy-start | bytes 1572868
  17.2 16.4 %copy-start.12 = (f32[2048]{0:T(1024)S(1)}, f32[2048]{0:T(1024)}, u32[]{:S(2)}) copy-start(f32[2048]{0:T(1024)} %param.17) | copy-start | bytes 24580
  18.1 0.8 copy-start.7
  41.0 15.2 %copy-start.13 = (f32[128,16]{0,1:T(8,128)S(1)}, f32[128,16]{0,1:T(8,128)}, u32[]{:S(2)}) copy-start(f32[128,16]{0,1:T(8,128)} %param.18) | copy-start | bytes 24580
  41.0 32.7 %all-to-all-start = ((bf16[8,32,2048]{2,1,0:T(8,128)(2,1)}), bf16[8,32,2048]{2,1,0:T(8,128)(2,1)S(1)}, u32[]{:S(2)}, u32[]{:S(2)}) async-start(bf16[8,32,2048]{2,1,0:T(8,128)(2,1)} %broadcast_in_dim.33), calls=%async_computation | async-start | bytes 2097152 | tf_op jit(solution)/shard_map/all_to_all | solution.py:314
  49.2 0.6 copy-start.9
  56.1 2.6 %copy-start.10 = (f32[128,1,128]{2,1,0:T(1,128)S(1)}, f32[128,1,128]{2,1,0:T(1,128)}, u32[]{:S(2)}) copy-start(f32[128,1,128]{2,1,0:T(1,128)} %copy-done.9) | copy-start | bytes 196612
  73.9 5.8 %copy-start.4 = (bf16[128,2048]{1,0:T(8,128)(2,1)S(1)}, bf16[128,2048]{1,0:T(8,128)(2,1)}, u32[]{:S(2)}) copy-start(bf16[128,2048]{1,0:T(8,128)(2,1)} %param.14) | copy-start | bytes 1572868
  75.1 12.9 %copy-start.1 = (f32[128,2048]{1,0:T(8,128)S(1)}, f32[128,2048]{1,0:T(8,128)}, u32[]{:S(2)}) copy-start(f32[128,2048]{1,0:T(8,128)} %shard_map.162) | copy-start | bytes 3145732
  79.8 8.2 %copy-start = (f32[128,2048]{1,0:T(8,128)S(1)}, f32[128,2048]{1,0:T(8,128)}, u32[]{:S(2)}) copy-start(f32[128,2048]{1,0:T(8,128)} %shard_map.167) | copy-start | bytes 3145732
  90.5 15.8 %collective-permute-start.1 = (bf16[128,2048]{1,0:T(8,128)(2,1)}, bf16[128,2048]{1,0:T(8,128)(2,1)S(1)}, u32[]{:S(2)}, u32[]{:S(2)}) collective-permute-start(bf16[128,2048]{1,0:T(8,128)(2,1)} %get-tuple-element.30.refs_1_.back_ref), channel_id=1, source_target_pairs={{4,0},{8,4},{12,8},{16,12},{20,16},{24,20},{28,24},{5,1},{9,5},{13... | collective-permute-start | bytes 1572872 | tf_op jit(solution)/shard_map/ppermute | solution.py:20
  106.3 10.3 %copy-start.11 = (bf16[128,2048]{1,0:T(8,128)(2,1)}, bf16[128,2048]{1,0:T(8,128)(2,1)S(1)}, u32[]{:S(2)}) copy-start(bf16[128,2048]{1,0:T(8,128)(2,1)S(1)} %collective-permute-done.1.refs_2_) | copy-start | bytes 1572868
  107.5 18.8 %all-to-all-start.1 = ((f32[8,1,18432]{2,1,0:T(1,128)}), f32[8,1,18432]{2,1,0:T(1,128)S(1)}, u32[]{:S(2)}, u32[]{:S(2)}) async-start(f32[8,1,18432]{2,1,0:T(1,128)} %broadcast_in_dim.62), calls=%async_computation.1 | async-start | bytes 1179648 | tf_op jit(solution)/shard_map/all_to_all | solution.py:314

commit v10 on v9

--- a/solution.py
+++ b/solution.py
@@ -355,18 +355,6 @@
     )
     bwd_rows = jnp.concatenate([taps_mr, jnp.zeros_like(taps_mr)], 1)
 
-    mixed_mr = (key_mr.astype(jnp.float32) * value_mr.astype(jnp.float32)).astype(jnp.bfloat16)
-    rim_rows = from_behind(mixed_mr, "seq", 1)
-    conv_mr = band_conv(fwd_rows, rim_rows, mixed_mr, group_size=group_size, split=False, tri=None)
-    out_mr = (query_mr.astype(jnp.float32) * conv_mr).astype(jnp.bfloat16)
-    out_full = out_mr.astype(jnp.float32)
-    squares = lax.psum(jnp.sum(out_full * out_full, axis=1), "chan")
-    inv_rms = lax.rsqrt(squares / D + 1e-06)[:, None]
-    normed = out_full * inv_rms * norm_gain
-    mixed_li = key_li.astype(jnp.float32) * normed
-    cotan_full = cotangent.astype(jnp.float32)
-    back_li = cotan_full * query_li.astype(jnp.float32)
-
     offsets = jnp.arange(row_count, dtype=jnp.float32)
     weights_res = li_residue * jnp.sqrt(2.0 * li_decay)
     taps_li = jnp.einsum(
@@ -376,20 +364,41 @@
     fwd_states = jnp.exp(-li_decay[:, :, None] * (row_count - 1.0 - offsets)).astype(jnp.bfloat16)
     bwd_states = jnp.exp(-li_decay[:, :, None] * offsets).astype(jnp.bfloat16)
 
-    back_li_bf = back_li.astype(jnp.bfloat16)
-    mixed_li_bf = mixed_li.astype(jnp.bfloat16)
-    modes = li_decay.shape[1]
+    cotan_full = cotangent.astype(jnp.float32)
+    back_li_bf = (cotan_full * query_li.astype(jnp.float32)).astype(jnp.bfloat16)
+    mixed_mr = (key_mr.astype(jnp.float32) * value_mr.astype(jnp.float32)).astype(jnp.bfloat16)
+    rim_rows = from_behind(mixed_mr, "seq", 1)
     grad_st = modal_states(bwd_states, back_li_bf, group_size=group_size)
-    conv_st = modal_states(fwd_states, mixed_li_bf, group_size=group_size)
-    both_st = gather_seq(jnp.concatenate([grad_st, conv_st], 0).astype(jnp.bfloat16))
-    both_st = both_st.astype(jnp.float32)
+    grad_gathered = gather_seq(grad_st.astype(jnp.bfloat16))
     grad_loc = band_conv(taps_li, back_li_bf, group_size=group_size, split=False, tri="upper")
-    conv_loc = band_conv(li_fwd_rows, mixed_li_bf, group_size=group_size, split=False, tri="lower")
-    both_st, grad_loc, conv_loc = lax.optimization_barrier((both_st, grad_loc, conv_loc))
-    grad_ent = entering_states(both_st[:, :modes], li_decay, row_count, group_size, False)
-    conv_ent = entering_states(both_st[:, modes:], li_decay, row_count, group_size, True)
+    conv_mr = band_conv(fwd_rows, rim_rows, mixed_mr, group_size=group_size, split=False, tri=None)
+    grad_gathered, grad_loc, conv_mr = lax.optimization_barrier((grad_gathered, grad_loc, conv_mr))
+    grad_ent = entering_states(
+        grad_gathered.astype(jnp.float32), li_decay, row_count, group_size, False
+    )
     grad_mixed_li = modal_out(
         li_decay, weights_res, grad_ent, grad_loc, group_size=group_size, forward=False
+    )
+    out_mr = (query_mr.astype(jnp.float32) * conv_mr).astype(jnp.bfloat16)
+    out_full = out_mr.astype(jnp.float32)
+    key_full = key_li.astype(jnp.float32)
+    grad_normed = grad_mixed_li * key_full
+    weighted = grad_normed * norm_gain
+    row_sums = jnp.stack(
+        [jnp.sum(out_full * out_full, axis=1), jnp.sum(weighted * out_full, axis=1)]
+    )
+    row_sums = lax.psum(row_sums, "chan")
+    squares = row_sums[0]
+    cross_dots = row_sums[1][:, None]
+    inv_rms = lax.rsqrt(squares / D + 1e-06)[:, None]
+    normed = out_full * inv_rms * norm_gain
+    mixed_li_bf = (key_full * normed).astype(jnp.bfloat16)
+    conv_st = modal_states(fwd_states, mixed_li_bf, group_size=group_size)
+    conv_gathered = gather_seq(conv_st.astype(jnp.bfloat16))
+    conv_loc = band_conv(li_fwd_rows, mixed_li_bf, group_size=group_size, split=False, tri="lower")
+    conv_gathered, conv_loc = lax.optimization_barrier((conv_gathered, conv_loc))
+    conv_ent = entering_states(
+        conv_gathered.astype(jnp.float32), li_decay, row_count, group_size, True
     )
     out_li, grad_query_li = modal_out(
         li_decay, weights_res, conv_ent, conv_loc, (query_li, cotangent),
@@ -397,10 +406,7 @@
     )
 
     grad_key_li = (grad_mixed_li * normed).astype(jnp.bfloat16)
-    grad_normed = grad_mixed_li * key_li.astype(jnp.float32)
     gain_part = jnp.sum(grad_normed * out_full * inv_rms, axis=0)
-    weighted = grad_normed * norm_gain
-    cross_dots = lax.psum(jnp.sum(weighted * out_full, axis=1), "chan")[:, None]
     grad_out_mr = inv_rms * weighted - out_full * inv_rms**3 * cross_dots / D
     grad_query_mr = (grad_out_mr * conv_mr).astype(jnp.bfloat16)
     back_mr = (grad_out_mr * query_mr.astype(jnp.float32)).astype(jnp.bfloat16)

time: 129 us -> 131 us (1.016)
  starting transfers between devices: 16.7 us -> 32.8 us
  waiting for transfers between devices: 13.1 us -> 6.28 us
  blocking collectives: 11.3 us -> 6.24 us
  other arithmetic: 18 us -> 14.4 us
    all_to_all x2 -> x3, starting transfers between devices: 10.5 us -> 27.5 us  [gather_seq(): return lax.all_to_all(tiled, 'seq', split_axis=0, concat_axis=0, tiled=True)]
    all_to_all x2 -> x3, waiting for transfers between devices: 9.96 us -> 0.01 us  [gather_seq(): return lax.all_to_all(tiled, 'seq', split_axis=0, concat_axis=0, tiled=True)]
    psum x2 -> x1, blocking collectives: 11.3 us -> 6.24 us  [on_device(): row_sums = lax.psum(row_sums, 'chan')]
    ppermute x2, waiting for transfers between devices: 3.1 us -> 6.28 us  [from_behind(): lax.ppermute(value, axis, [(source, source + steps) for source in range(i...]
    another operation x2 -> x1, other arithmetic: 1.82 us -> 0.01 us  [on_device(): jnp.stack([jnp.sum(out_full * out_full, axis=1), jnp.sum(weighted * out_f...]
    reduce_sum x2 -> x1, other arithmetic: 4.01 us -> 2.42 us  [on_device(): jnp.sum(out_full * out_full, axis=1)]
    broadcast_in_dim x2 -> x3, local copies, waits for them, and re-layouts: 2.26 us -> 2.84 us  [gather_seq(): tiled = jnp.broadcast_to(value[None], (count,) + value.shape)]
  transfers between devices with their start and end apart: 4 -> 5, of which waited for: 4 -> 2; matrix products, arithmetic and copies ran while one was open for 9% -> 6% of each run, Pallas kernels for 32% -> 34%
where the time goes in v10:
time: 131 us; the launch traced here: 130 us
  Pallas kernels  57.6 us (44%)
  starting transfers between devices  32.8 us (25%)
  other arithmetic  14.4 us (11%)
  local copies, waits for them, and re-layouts  10.2 us (8%)
  waiting for transfers between devices  6.28 us (5%)
  blocking collectives  6.24 us (5%)
  matrix products  1.78 us (1%)
    pallas_call x4, Pallas kernels, band_conv(): pl.pallas_call(kernel, grid=(chans // block,), in_specs=in_specs, out_spe...  27.7 us
    all_to_all x3, starting transfers between devices, gather_seq(): return lax.all_to_all(tiled, 'seq', split_axis=0, concat_axis=0, tiled=True)  27.5 us
    pallas_call x1, Pallas kernels, gram_diag(): pl.pallas_call(kernel, grid=(chans // block,), in_specs=[pl.BlockSpec((ro...  11.4 us
    pallas_call x2, Pallas kernels, modal_out(): pl.pallas_call(kernel, grid=(chans // block,), in_specs=in_specs, out_spe...  9.62 us
    pallas_call x2, Pallas kernels, modal_states(): pl.pallas_call(kernel, grid=(chans // block,), in_specs=[pl.BlockSpec((gr...  8.86 us
    ppermute x2, waiting for transfers between devices, from_behind(): lax.ppermute(value, axis, [(source, source + steps) for source in range(i...  6.28 us
    psum x1, blocking collectives, on_device(): row_sums = lax.psum(row_sums, 'chan')  6.24 us
    ppermute x2, starting transfers between devices, from_behind(): lax.ppermute(value, axis, [(source, source + steps) for source in range(i...  5.24 us
  transfers between devices with their start and end apart: 5, of which 2 were waited for; matrix products, arithmetic and copies ran while one was open for 6% of the time, Pallas kernels for 34%

profile of v10, /device:TPU:0, one launch (start us, length us, event | category | flops | bytes accessed | tf_op | source)
XLA Modules:
  0.0 130.1 jit_solution(5000779305173943878)
XLA Ops:
  1.5 1.3 %fusion.14 = (bf16[128,16,128]{2,1,0:T(8,128)(2,1)}, bf16[128,16,128]{2,1,0:T(8,128)(2,1)}) fusion(f32[128,16]{1,0:T(8,128)S(1)} %copy.29, f32[128]{0:T(128)S(1)} %iota_subtract_fusion), kind=kLoop, calls=%fused_computation.29 | loop fusion | flops 1048576 | bytes 1057280 | tf_op jit(solution)/shard_map/convert_element_type | solution.py:365
  3.7 4.3 %shard_map.161 = f32[16,2048]{1,0:T(8,128)} custom-call(bf16[128,16,128]{2,1,0:T(8,128)(2,1)} %get-tuple-element.38.e_ref, bf16[128,2048]{1,0:T(8,128)(2,1)} %multiply_convert_fusion.2.x_ref.refs_1_), custom_call_target="tpu_custom_call" | custom-call | tf_op jit(solution)/shard_map/pallas_call | solution.py:176
  9.8 7.4 %all-to-all-start = ((bf16[8,16,2048]{2,1,0:T(8,128)(2,1)}), bf16[8,16,2048]{2,1,0:T(8,128)(2,1)S(1)}, u32[]{:S(2)}, u32[]{:S(2)}) async-start(bf16[8,16,2048]{2,1,0:T(8,128)(2,1)} %broadcast_in_dim.33), calls=%async_computation | async-start | bytes 1048576 | tf_op jit(solution)/shard_map/all_to_all | solution.py:314
  17.4 4.0 %collective-permute-start = (bf16[128,2048]{1,0:T(8,128)(2,1)S(1)}, bf16[128,2048]{1,0:T(8,128)(2,1)S(1)}, u32[]{:S(2)}, u32[]{:S(2)}) collective-permute-start(bf16[128,2048]{1,0:T(8,128)(2,1)S(1)} %multiply_convert_fusion.1.refs_2_.bot_ref), channel_id=1, source_target_pairs={{0,4},{4,8},{8,12},{12,16},{16,20},{20,24},{24,28},{1,5},{5,9},{9,... | collective-permute-start | bytes 1572872 | tf_op jit(solution)/shard_map/ppermute | solution.py:20
  21.5 1.8 %fusion.13 = f32[128,1,128]{2,1,0:T(1,128)} fusion(f32[128,16,1]{1,2,0:T(1,128)S(1)} %copy.31, f32[128,16]{1,0:T(8,128)S(1)} %copy.29), kind=kOutput, calls=%fused_computation.28 | convolution fusion | flops 3407872 | bytes 81920 | tf_op jit(solution)/shard_map/gr,grd->gd/dot_general | solution.py:360
  25.5 6.3 %shard_map.162.refs_3_ = f32[128,2048]{1,0:T(8,128)} custom-call(f32[128,128]{1,0:T(8,128)} %bitcast.18, bf16[128,2048]{1,0:T(8,128)(2,1)} %multiply_convert_fusion.2.x_ref.refs_1_), custom_call_target="tpu_custom_call" | custom-call | tf_op jit(solution)/shard_map/pallas_call | solution.py:140
  33.7 1.0 collective-permute-done.refs_1_.top_ref
  35.5 7.5 %shard_map.163 = f32[128,2048]{1,0:T(8,128)} custom-call(f32[128,256]{1,0:T(8,128)} %maximum_maximum_fusion.refs_0_, bf16[128,2048]{1,0:T(8,128)(2,1)} %copy-done.8, bf16[128,2048]{1,0:T(8,128)(2,1)} %copy-done.2), custom_call_target="tpu_custom_call" | custom-call | tf_op jit(solution)/shard_map/pallas_call | solution.py:140
  43.0 1.0 multiply_reduce_fusion.1.refs_2_
  44.0 4.7 %shard_map.164 = f32[128,2048]{1,0:T(8,128)} custom-call(f32[16,128]{1,0:T(8,128)} %reshape.97.refs_0_, f32[16,128]{1,0:T(8,128)} %reshape.98.refs_1_, f32[16,2048]{1,0:T(8,128)} %multiply_reduce_fusion.1.refs_2_, f32[128,2048]{1,0:T(8,128)} %shard_map.162.refs_3_), custom_call_target="tpu_custom_call" | custom-call | tf_op jit(solution)/shard_map/pallas_call | solution.py:251
  48.8 2.4 %fusion.3 = (f32[128]{0:T(128)S(1)}, f32[128]{0:T(128)S(1)}, bf16[128,2048]{1,0:T(8,128)(2,1)}) fusion(f32[2048]{0:T(1024)S(1)} %copy-done.14, f32[128,2048]{1,0:T(8,128)} %shard_map.164, bf16[128,2048]{1,0:T(8,128)(2,1)S(1)} %copy-done.10, f32[128,2048]{1,0:T(8,128)S(1)} %copy-done, bf16[128,2048]{1,0:T(8,128)(2,1)S(1)} %copy-done.9), kind=kLoop, calls=%fused_computation.12 | loop fusion | flops 2883328 | bytes 3679232 | tf_op jit(solution)/shard_map/reduce_sum | solution.py:388
  51.2 6.2 %psum.7 = f32[2,128]{1,0:T(2,128)S(1)} all-reduce(f32[2,128]{1,0:T(2,128)S(1)} %pad_maximum_fusion.2), channel_id=1, replica_groups=mesh['seq'=8,'chan'=4] {'chan'}, use_global_device_ids=true, to_apply=%region_3.4 | all-reduce | flops 256 | bytes 2048 | tf_op jit(solution)/shard_map/psum | solution.py:390
  57.5 3.1 %fusion.2 = (bf16[128,2048]{1,0:T(8,128)(2,1)S(1)}, bf16[128,2048]{1,0:T(8,128)(2,1)}, f32[2048]{0:T(1024)S(1)}, bf16[128,2048]{1,0:T(8,128)(2,1)}, bf16[128,2048]{1,0:T(8,128)(2,1)}) fusion(bf16[128,2048]{1,0:T(8,128)(2,1)S(1)} %copy-done.9, f32[128]{0:T(128)S(1)} %slice_bitcast_fusion.1, f32[128]{0:T(128)S(1)} %get-tuple-element.30, ...), kind=kLoop, calls=%fused_computation.11 | loop fusion | flops 6027264 | bytes 5785088 | tf_op jit(solution)/shard_map/convert_element_type | solution.py:412
  60.6 4.5 %shard_map.165 = f32[16,2048]{1,0:T(8,128)} custom-call(bf16[128,16,128]{2,1,0:T(8,128)(2,1)} %get-tuple-element.39.e_ref, bf16[128,2048]{1,0:T(8,128)(2,1)} %get-tuple-element.37.x_ref.refs_1_), custom_call_target="tpu_custom_call" | custom-call | tf_op jit(solution)/shard_map/pallas_call | solution.py:176
  66.8 11.6 %all-to-all-start.1 = ((bf16[8,16,2048]{2,1,0:T(8,128)(2,1)}), bf16[8,16,2048]{2,1,0:T(8,128)(2,1)S(1)}, u32[]{:S(2)}, u32[]{:S(2)}) async-start(bf16[8,16,2048]{2,1,0:T(8,128)(2,1)} %broadcast_in_dim.37), calls=%async_computation.1 | async-start | bytes 1048576 | tf_op jit(solution)/shard_map/all_to_all | solution.py:314
  78.5 1.3 collective-permute-start.1
  79.8 11.4 %shard_map.169 = f32[128,256]{1,0:T(8,128)} custom-call(bf16[128,2048]{1,0:T(8,128)(2,1)} %copy-done.3, bf16[128,2048]{1,0:T(8,128)(2,1)} %copy-done.8, bf16[128,2048]{1,0:T(8,128)(2,1)} %copy-done.2), custom_call_target="tpu_custom_call" | custom-call | tf_op jit(solution)/shard_map/pallas_call | solution.py:297
  92.1 5.3 %collective-permute-done.1.refs_2_ = bf16[128,2048]{1,0:T(8,128)(2,1)S(1)} collective-permute-done((bf16[128,2048]{1,0:T(8,128)(2,1)S(1)}, bf16[128,2048]{1,0:T(8,128)(2,1)S(1)}, u32[]{:S(2)}, u32[]{:S(2)}) %collective-permute-start.1) | collective-permute-done | bytes 524320 | tf_op jit(solution)/shard_map/ppermute | solution.py:20
  97.4 1.2 broadcast_in_dim.68
  98.6 8.5 %all-to-all-start.2 = ((f32[8,1,18432]{2,1,0:T(1,128)}), f32[8,1,18432]{2,1,0:T(1,128)S(1)}, u32[]{:S(2)}, u32[]{:S(2)}) async-start(f32[8,1,18432]{2,1,0:T(1,128)} %broadcast_in_dim.68), calls=%async_computation.2 | async-start | bytes 1179648 | tf_op jit(solution)/shard_map/all_to_all | solution.py:314
  108.6 6.3 %shard_map.166.refs_3_ = f32[128,2048]{1,0:T(8,128)} custom-call(f32[128,128]{1,0:T(8,128)} %pad_maximum_fusion.1.refs_0_, bf16[128,2048]{1,0:T(8,128)(2,1)} %get-tuple-element.37.x_ref.refs_1_), custom_call_target="tpu_custom_call" | custom-call | tf_op jit(solution)/shard_map/pallas_call | solution.py:140
  114.9 7.6 %shard_map.168 = (bf16[128,2048]{1,0:T(8,128)(2,1)}, bf16[128,2048]{1,0:T(8,128)(2,1)}) custom-call(f32[128,256]{1,0:T(8,128)} %concatenate.14.refs_0_, bf16[128,2048]{1,0:T(8,128)(2,1)} %copy-done.3, bf16[128,2048]{1,0:T(8,128)(2,1)} %copy-done.12, bf16[128,2048]{1,0:T(8,128)(2,1)} %refs_3_.1, bf16[128,2048]{1,0:T(8,128)(2,1)} %refs_4_.3), custom_call_target="tpu_custom_call" | custom-call | tf_op jit(solution)/shard_map/pallas_call | solution.py:140
  122.5 1.0 multiply_reduce_fusion.refs_2_
  123.5 4.9 %shard_map.167 = (bf16[128,2048]{1,0:T(8,128)(2,1)}, bf16[128,2048]{1,0:T(8,128)(2,1)}) custom-call(f32[16,128]{1,0:T(8,128)} %reshape.97.refs_0_, f32[16,128]{1,0:T(8,128)} %reshape.98.refs_1_, f32[16,2048]{1,0:T(8,128)} %multiply_reduce_fusion.refs_2_, f32[128,2048]{1,0:T(8,128)} %shard_map.166.refs_3_, bf16[128,2048]{1,0:T(8,128)(2,1)} %refs_4_.2, ...), custom_call_target="tpu_custom_call" | custom-call | tf_op jit(solution)/shard_map/pallas_call | solution.py:251
  (76 shorter events, 14.7 us)
Async XLA Ops:
  1.5 1.3 %copy-start.6 = (bf16[128,2048]{1,0:T(8,128)(2,1)S(1)}, bf16[128,2048]{1,0:T(8,128)(2,1)}, u32[]{:S(2)}) copy-start(bf16[128,2048]{1,0:T(8,128)(2,1)} %refs_4_.2) | copy-start | bytes 1572868
  1.5 1.3 %copy-start.7 = (bf16[128,2048]{1,0:T(8,128)(2,1)S(1)}, bf16[128,2048]{1,0:T(8,128)(2,1)}, u32[]{:S(2)}) copy-start(bf16[128,2048]{1,0:T(8,128)(2,1)} %refs_5_.1) | copy-start | bytes 1572868
  9.8 7.4 %copy-start.4 = (bf16[128,2048]{1,0:T(8,128)(2,1)S(1)}, bf16[128,2048]{1,0:T(8,128)(2,1)}, u32[]{:S(2)}) copy-start(bf16[128,2048]{1,0:T(8,128)(2,1)} %refs_3_.1) | copy-start | bytes 1572868
  9.8 7.4 %copy-start.5 = (bf16[128,2048]{1,0:T(8,128)(2,1)S(1)}, bf16[128,2048]{1,0:T(8,128)(2,1)}, u32[]{:S(2)}) copy-start(bf16[128,2048]{1,0:T(8,128)(2,1)} %refs_4_.3) | copy-start | bytes 1572868
  9.8 33.2 %all-to-all-start = ((bf16[8,16,2048]{2,1,0:T(8,128)(2,1)}), bf16[8,16,2048]{2,1,0:T(8,128)(2,1)S(1)}, u32[]{:S(2)}, u32[]{:S(2)}) async-start(bf16[8,16,2048]{2,1,0:T(8,128)(2,1)} %broadcast_in_dim.33), calls=%async_computation | async-start | bytes 1048576 | tf_op jit(solution)/shard_map/all_to_all | solution.py:314
  17.4 5.9 %copy-start.2 = (bf16[128,2048]{1,0:T(8,128)(2,1)}, bf16[128,2048]{1,0:T(8,128)(2,1)S(1)}, u32[]{:S(2)}) copy-start(bf16[128,2048]{1,0:T(8,128)(2,1)S(1)} %multiply_convert_fusion.1.refs_2_.bot_ref) | copy-start | bytes 1572868
  17.4 17.3 %collective-permute-start = (bf16[128,2048]{1,0:T(8,128)(2,1)S(1)}, bf16[128,2048]{1,0:T(8,128)(2,1)S(1)}, u32[]{:S(2)}, u32[]{:S(2)}) collective-permute-start(bf16[128,2048]{1,0:T(8,128)(2,1)S(1)} %multiply_convert_fusion.1.refs_2_.bot_ref), channel_id=1, source_target_pairs={{0,4},{4,8},{8,12},{12,16},{16,20},{20,24},{24,28},{1,5},{5,9},{9,... | collective-permute-start | bytes 1572872 | tf_op jit(solution)/shard_map/ppermute | solution.py:20
  21.5 1.8 %copy-start.13 = (f32[128,128]{1,0:T(8,128)S(1)}, f32[128,128]{1,0:T(8,128)}, u32[]{:S(2)}) copy-start(f32[128,128]{1,0:T(8,128)} %param.16) | copy-start | bytes 196612
  23.3 0.7 copy-start.15
  34.8 0.8 copy-start.8
  44.0 4.7 %copy-start = (f32[128,2048]{1,0:T(8,128)S(1)}, f32[128,2048]{1,0:T(8,128)}, u32[]{:S(2)}) copy-start(f32[128,2048]{1,0:T(8,128)} %shard_map.163) | copy-start | bytes 3145732
  44.0 4.7 %copy-start.9 = (bf16[128,2048]{1,0:T(8,128)(2,1)S(1)}, bf16[128,2048]{1,0:T(8,128)(2,1)}, u32[]{:S(2)}) copy-start(bf16[128,2048]{1,0:T(8,128)(2,1)} %param.10) | copy-start | bytes 1572868
  44.0 4.7 %copy-start.10 = (bf16[128,2048]{1,0:T(8,128)(2,1)S(1)}, bf16[128,2048]{1,0:T(8,128)(2,1)}, u32[]{:S(2)}) copy-start(bf16[128,2048]{1,0:T(8,128)(2,1)} %param.14) | copy-start | bytes 1572868
  44.0 4.7 %copy-start.14 = (f32[2048]{0:T(1024)S(1)}, f32[2048]{0:T(1024)}, u32[]{:S(2)}) copy-start(f32[2048]{0:T(1024)} %param.17) | copy-start | bytes 24580
  48.8 8.7 %copy-start.1 = (f32[128,2048]{1,0:T(8,128)S(1)}, f32[128,2048]{1,0:T(8,128)}, u32[]{:S(2)}) copy-start(f32[128,2048]{1,0:T(8,128)} %shard_map.164) | copy-start | bytes 3145732
  60.6 17.9 %copy-start.3 = (bf16[128,2048]{1,0:T(8,128)(2,1)}, bf16[128,2048]{1,0:T(8,128)(2,1)S(1)}, u32[]{:S(2)}) copy-start(bf16[128,2048]{1,0:T(8,128)(2,1)S(1)} %get-tuple-element.33.refs_1_.back_ref) | copy-start | bytes 1572868
  66.8 30.6 %all-to-all-start.1 = ((bf16[8,16,2048]{2,1,0:T(8,128)(2,1)}), bf16[8,16,2048]{2,1,0:T(8,128)(2,1)S(1)}, u32[]{:S(2)}, u32[]{:S(2)}) async-start(bf16[8,16,2048]{2,1,0:T(8,128)(2,1)} %broadcast_in_dim.37), calls=%async_computation.1 | async-start | bytes 1048576 | tf_op jit(solution)/shard_map/all_to_all | solution.py:314
  78.5 18.9 %collective-permute-start.1 = (bf16[128,2048]{1,0:T(8,128)(2,1)S(1)}, bf16[128,2048]{1,0:T(8,128)(2,1)S(1)}, u32[]{:S(2)}, u32[]{:S(2)}) collective-permute-start(bf16[128,2048]{1,0:T(8,128)(2,1)S(1)} %get-tuple-element.33.refs_1_.back_ref), channel_id=1, source_target_pairs={{4,0},{8,4},{12,8},{16,12},{20,16},{24,20},{28,24},{5,1},{9,5},{13... | collective-permute-start | bytes 1572872 | tf_op jit(solution)/shard_map/ppermute | solution.py:20
  91.2 0.8 slice-start
  97.4 1.2 copy-start.12
  98.6 8.5 %copy-start.11 = (f32[128,1,128]{2,1,0:T(1,128)S(1)}, f32[128,1,128]{2,1,0:T(1,128)}, u32[]{:S(2)}) copy-start(f32[128,1,128]{2,1,0:T(1,128)} %fusion.13) | copy-start | bytes 196612
  98.6 29.8 %all-to-all-start.2 = ((f32[8,1,18432]{2,1,0:T(1,128)}), f32[8,1,18432]{2,1,0:T(1,128)S(1)}, u32[]{:S(2)}, u32[]{:S(2)}) async-start(f32[8,1,18432]{2,1,0:T(1,128)} %broadcast_in_dim.68), calls=%async_computation.2 | async-start | bytes 1179648 | tf_op jit(solution)/shard_map/all_to_all | solution.py:314

commit v11 on v9

--- a/solution.py
+++ b/solution.py
@@ -161,7 +161,7 @@
         acc = y[:modes]
         for k in range(1, groups_here):
             acc = jnp.where(state_group == k, y[k * modes:(k + 1) * modes], acc)
-        s_ref[:, lanes] = acc
+        s_ref[:, lanes] = acc.astype(s_ref.dtype)
         return carry
 
     lax.fori_loop(0, sub, body, 0)
@@ -181,7 +181,7 @@
             pl.BlockSpec((rows, block), lambda b: (0, b)),
         ],
         out_specs=pl.BlockSpec((modes, block), lambda b: (0, b)),
-        out_shape=jax.ShapeDtypeStruct((modes, chans), jnp.float32),
+        out_shape=jax.ShapeDtypeStruct((modes, chans), jnp.bfloat16),
         compiler_params=pltpu.CompilerParams(dimension_semantics=("parallel",)),
     )(state_rows, x)
 
@@ -381,7 +381,7 @@
     modes = li_decay.shape[1]
     grad_st = modal_states(bwd_states, back_li_bf, group_size=group_size)
     conv_st = modal_states(fwd_states, mixed_li_bf, group_size=group_size)
-    both_st = gather_seq(jnp.concatenate([grad_st, conv_st], 0).astype(jnp.bfloat16))
+    both_st = gather_seq(jnp.concatenate([grad_st, conv_st], 0))
     both_st = both_st.astype(jnp.float32)
     grad_loc = band_conv(taps_li, back_li_bf, group_size=group_size, split=False, tri="upper")
     conv_loc = band_conv(li_fwd_rows, mixed_li_bf, group_size=group_size, split=False, tri="lower")

time: 129 us -> 129 us (level)
    another operation x2 -> x0, other arithmetic: 1.82 us -> none
where the time goes in v11:
time: 129 us; the launch traced here: 128 us
  Pallas kernels  57.4 us (44%)
  other arithmetic  17.1 us (13%)
  starting transfers between devices  16.7 us (13%)
  waiting for transfers between devices  14 us (11%)
  blocking collectives  11.3 us (9%)
  local copies, waits for them, and re-layouts  9.49 us (7%)
    pallas_call x4, Pallas kernels, band_conv(): pl.pallas_call(kernel, grid=(chans // block,), in_specs=in_specs, out_spe...  27.7 us
    pallas_call x1, Pallas kernels, gram_diag(): pl.pallas_call(kernel, grid=(chans // block,), in_specs=[pl.BlockSpec((ro...  11.4 us
    all_to_all x2, starting transfers between devices, gather_seq(): return lax.all_to_all(tiled, 'seq', split_axis=0, concat_axis=0, tiled=True)  10.5 us
    all_to_all x2, waiting for transfers between devices, gather_seq(): return lax.all_to_all(tiled, 'seq', split_axis=0, concat_axis=0, tiled=True)  9.97 us
    pallas_call x2, Pallas kernels, modal_out(): pl.pallas_call(kernel, grid=(chans // block,), in_specs=in_specs, out_spe...  9.62 us
    pallas_call x2, Pallas kernels, modal_states(): pl.pallas_call(kernel, grid=(chans // block,), in_specs=[pl.BlockSpec((gr...  8.67 us
    ppermute x2, starting transfers between devices, from_behind(): lax.ppermute(value, axis, [(source, source + steps) for source in range(i...  6.18 us
    psum x1, blocking collectives, on_device(): squares = lax.psum(jnp.sum(out_full * out_full, axis=1), 'chan')  5.71 us
  transfers between devices with their start and end apart: 4, of which 4 were waited for; matrix products, arithmetic and copies ran while one was open for 9% of the time, Pallas kernels for 32%

profile of v11, /device:TPU:0, one launch (start us, length us, event | category | flops | bytes accessed | tf_op | source)
XLA Modules:
  0.0 128.0 jit_solution(15788915868815139460)
XLA Ops:
  0.7 1.4 %multiply_convert_fusion.1.refs_2_.bot_ref = bf16[128,2048]{1,0:T(8,128)(2,1)S(1)} fusion(bf16[128,2048]{1,0:T(8,128)(2,1)} %refs_3_.1, bf16[128,2048]{1,0:T(8,128)(2,1)} %refs_4_.3), kind=kLoop, calls=%fused_computation.25 | loop fusion | flops 1048576 | bytes 1572864 | tf_op jit(solution)/shard_map/convert_element_type | solution.py:358
  2.1 4.9 %collective-permute-start = (bf16[128,2048]{1,0:T(8,128)(2,1)S(1)}, bf16[128,2048]{1,0:T(8,128)(2,1)S(1)}, u32[]{:S(2)}, u32[]{:S(2)}) collective-permute-start(bf16[128,2048]{1,0:T(8,128)(2,1)S(1)} %multiply_convert_fusion.1.refs_2_.bot_ref), channel_id=1, source_target_pairs={{0,4},{4,8},{8,12},{12,16},{16,20},{20,24},{24,28},{1,5},{5,9},{9,... | collective-permute-start | bytes 1572872 | tf_op jit(solution)/shard_map/ppermute | solution.py:20
  9.8 1.3 %fusion.14 = (bf16[128,16,128]{2,1,0:T(8,128)(2,1)}, bf16[128,16,128]{2,1,0:T(8,128)(2,1)}) fusion(f32[128,16]{1,0:T(8,128)S(1)} %copy.29, f32[128]{0:T(128)S(1)} %iota_subtract_fusion), kind=kLoop, calls=%fused_computation.30 | loop fusion | flops 1048576 | bytes 1057280 | tf_op jit(solution)/shard_map/convert_element_type | solution.py:377
  11.1 4.3 %shard_map.161 = bf16[16,2048]{1,0:T(8,128)(2,1)} custom-call(bf16[128,16,128]{2,1,0:T(8,128)(2,1)} %get-tuple-element.33.e_ref, bf16[128,2048]{1,0:T(8,128)(2,1)} %multiply_convert_fusion.2.x_ref.refs_1_), custom_call_target="tpu_custom_call" | custom-call | tf_op jit(solution)/shard_map/pallas_call | solution.py:176
  16.2 1.9 %collective-permute-done.refs_1_.top_ref = bf16[128,2048]{1,0:T(8,128)(2,1)S(1)} collective-permute-done((bf16[128,2048]{1,0:T(8,128)(2,1)S(1)}, bf16[128,2048]{1,0:T(8,128)(2,1)S(1)}, u32[]{:S(2)}, u32[]{:S(2)}) %collective-permute-start) | collective-permute-done | bytes 524320 | tf_op jit(solution)/shard_map/ppermute | solution.py:20
  18.9 7.5 %shard_map.162 = f32[128,2048]{1,0:T(8,128)} custom-call(f32[128,256]{1,0:T(8,128)} %maximum_maximum_fusion.refs_0_, bf16[128,2048]{1,0:T(8,128)(2,1)} %copy-done.7, bf16[128,2048]{1,0:T(8,128)(2,1)} %copy-done.2), custom_call_target="tpu_custom_call" | custom-call | tf_op jit(solution)/shard_map/pallas_call | solution.py:140
  26.4 1.5 %fusion.3 = (f32[128]{0:T(128)S(1)}, bf16[128,2048]{1,0:T(8,128)(2,1)S(1)}) fusion(f32[128,2048]{1,0:T(8,128)} %shard_map.162, bf16[128,2048]{1,0:T(8,128)(2,1)S(1)} %copy-done.8), kind=kLoop, calls=%fused_computation.12 | loop fusion | flops 1572736 | bytes 2097664 | tf_op jit(solution)/shard_map/reduce_sum | solution.py:363
  27.9 5.7 %psum.14 = f32[128]{0:T(128)S(1)} all-reduce(f32[128]{0:T(128)S(1)} %get-tuple-element.28), channel_id=1, replica_groups=mesh['seq'=8,'chan'=4] {'chan'}, use_global_device_ids=true, to_apply=%region_1.2 | all-reduce | flops 128 | bytes 1024 | tf_op jit(solution)/shard_map/psum | solution.py:363
  34.7 4.3 %shard_map.163 = bf16[16,2048]{1,0:T(8,128)(2,1)} custom-call(bf16[128,16,128]{2,1,0:T(8,128)(2,1)} %get-tuple-element.34.e_ref, bf16[128,2048]{1,0:T(8,128)(2,1)} %fusion.x_ref.refs_1_), custom_call_target="tpu_custom_call" | custom-call | tf_op jit(solution)/shard_map/pallas_call | solution.py:176
  41.0 6.9 %all-to-all-start = ((bf16[8,32,2048]{2,1,0:T(8,128)(2,1)}), bf16[8,32,2048]{2,1,0:T(8,128)(2,1)S(1)}, u32[]{:S(2)}, u32[]{:S(2)}) async-start(bf16[8,32,2048]{2,1,0:T(8,128)(2,1)} %broadcast_in_dim.33), calls=%async_computation | async-start | bytes 2097152 | tf_op jit(solution)/shard_map/all_to_all | solution.py:314
  49.8 6.3 %shard_map.164.refs_3_ = f32[128,2048]{1,0:T(8,128)} custom-call(f32[128,128]{1,0:T(8,128)} %bitcast.12, bf16[128,2048]{1,0:T(8,128)(2,1)} %multiply_convert_fusion.2.x_ref.refs_1_), custom_call_target="tpu_custom_call" | custom-call | tf_op jit(solution)/shard_map/pallas_call | solution.py:140
  59.4 6.3 %shard_map.165.refs_3_ = f32[128,2048]{1,0:T(8,128)} custom-call(f32[128,128]{1,0:T(8,128)} %pad_maximum_fusion.2.refs_0_, bf16[128,2048]{1,0:T(8,128)(2,1)} %fusion.x_ref.refs_1_), custom_call_target="tpu_custom_call" | custom-call | tf_op jit(solution)/shard_map/pallas_call | solution.py:140
  65.7 7.9 %all-to-all-done = bf16[8,32,2048]{2,1,0:T(8,128)(2,1)S(1)} async-done(((bf16[8,32,2048]{2,1,0:T(8,128)(2,1)}), bf16[8,32,2048]{2,1,0:T(8,128)(2,1)S(1)}, u32[]{:S(2)}, u32[]{:S(2)}) %all-to-all-start) | async-done | bytes 1048608 | tf_op jit(solution)/shard_map/all_to_all | solution.py:314
  75.1 4.7 %shard_map.167 = f32[128,2048]{1,0:T(8,128)} custom-call(f32[16,128]{1,0:T(8,128)} %reshape.81.refs_0_, f32[16,128]{1,0:T(8,128)} %reshape.82.refs_1_, f32[16,2048]{1,0:T(8,128)} %get-tuple-element.24.refs_2_, f32[128,2048]{1,0:T(8,128)} %shard_map.164.refs_3_), custom_call_target="tpu_custom_call" | custom-call | tf_op jit(solution)/shard_map/pallas_call | solution.py:251
  79.8 2.5 %fusion.12 = (f32[2048]{0:T(1024)S(1)}, f32[128]{0:T(128)S(1)}, bf16[128,2048]{1,0:T(8,128)(2,1)}) fusion(bf16[128,2048]{1,0:T(8,128)(2,1)S(1)} %get-tuple-element.29, f32[128]{0:T(128)S(1)} %get-tuple-element.39, f32[128,2048]{1,0:T(8,128)} %shard_map.167, bf16[128,2048]{1,0:T(8,128)(2,1)S(1)} %copy-done.4, f32[2048]{0:T(1024)S(1)} %copy-done.13), kind=kLoop, calls=%fused_computation.21 | loop fusion | flops 3405696 | bytes 2638848 | tf_op jit(solution)/shard_map/reduce_sum | solution.py:401
  82.3 5.6 %psum.15 = f32[128]{0:T(128)S(1)} all-reduce(f32[128]{0:T(128)S(1)} %get-tuple-element.27), channel_id=1, replica_groups=mesh['seq'=8,'chan'=4] {'chan'}, use_global_device_ids=true, to_apply=%region_5.6 | all-reduce | flops 128 | bytes 1024 | tf_op jit(solution)/shard_map/psum | solution.py:403
  88.0 2.6 %fusion.2 = (bf16[128,2048]{1,0:T(8,128)(2,1)}, bf16[128,2048]{1,0:T(8,128)(2,1)}) fusion(bf16[128,2048]{1,0:T(8,128)(2,1)} %param.10, f32[128]{0:T(128)S(1)} %psum.15, f32[128]{0:T(128)S(1)} %get-tuple-element.38, bf16[128,2048]{1,0:T(8,128)(2,1)S(1)} %get-tuple-element.29, f32[2048]{0:T(1024)S(1)} %copy-done.13, f32[128]{0:T(128)S(1)} %get-tuple-element.39, ...), kind=kLoop, calls=%fused_computation.11 | loop fusion | flops 3670016 | bytes 4728320 | tf_op jit(solution)/shard_map/convert_element_type | solution.py:406
  90.6 1.3 %collective-permute-start.1 = (bf16[128,2048]{1,0:T(8,128)(2,1)}, bf16[128,2048]{1,0:T(8,128)(2,1)S(1)}, u32[]{:S(2)}, u32[]{:S(2)}) collective-permute-start(bf16[128,2048]{1,0:T(8,128)(2,1)} %get-tuple-element.30.refs_1_.back_ref), channel_id=1, source_target_pairs={{4,0},{8,4},{12,8},{16,12},{20,16},{24,20},{28,24},{5,1},{9,5},{13... | collective-permute-start | bytes 1572872 | tf_op jit(solution)/shard_map/ppermute | solution.py:20
  91.8 11.4 %shard_map.169 = f32[128,256]{1,0:T(8,128)} custom-call(bf16[128,2048]{1,0:T(8,128)(2,1)} %get-tuple-element.30.refs_1_.back_ref, bf16[128,2048]{1,0:T(8,128)(2,1)} %copy-done.7, bf16[128,2048]{1,0:T(8,128)(2,1)} %copy-done.2), custom_call_target="tpu_custom_call" | custom-call | tf_op jit(solution)/shard_map/pallas_call | solution.py:297
  104.2 2.1 %collective-permute-done.1.refs_2_ = bf16[128,2048]{1,0:T(8,128)(2,1)S(1)} collective-permute-done((bf16[128,2048]{1,0:T(8,128)(2,1)}, bf16[128,2048]{1,0:T(8,128)(2,1)S(1)}, u32[]{:S(2)}, u32[]{:S(2)}) %collective-permute-start.1) | collective-permute-done | bytes 524320 | tf_op jit(solution)/shard_map/ppermute | solution.py:20
  107.5 3.6 %all-to-all-start.1 = ((f32[8,1,18432]{2,1,0:T(1,128)}), f32[8,1,18432]{2,1,0:T(1,128)S(1)}, u32[]{:S(2)}, u32[]{:S(2)}) async-start(f32[8,1,18432]{2,1,0:T(1,128)} %broadcast_in_dim.62), calls=%async_computation.1 | async-start | bytes 1179648 | tf_op jit(solution)/shard_map/all_to_all | solution.py:314
  111.8 4.9 %shard_map.166 = (bf16[128,2048]{1,0:T(8,128)(2,1)}, bf16[128,2048]{1,0:T(8,128)(2,1)}) custom-call(f32[16,128]{1,0:T(8,128)} %reshape.81.refs_0_, f32[16,128]{1,0:T(8,128)} %reshape.82.refs_1_, f32[16,2048]{1,0:T(8,128)} %get-tuple-element.25.refs_2_, f32[128,2048]{1,0:T(8,128)} %shard_map.165.refs_3_, bf16[128,2048]{1,0:T(8,128)(2,1)} %refs_4_.2, ...), custom_call_target="tpu_custom_call" | custom-call | tf_op jit(solution)/shard_map/pallas_call | solution.py:251
  116.7 7.6 %shard_map.168 = (bf16[128,2048]{1,0:T(8,128)(2,1)}, bf16[128,2048]{1,0:T(8,128)(2,1)}) custom-call(f32[128,256]{1,0:T(8,128)} %concatenate.18.refs_0_, bf16[128,2048]{1,0:T(8,128)(2,1)} %get-tuple-element.30.refs_1_.back_ref, bf16[128,2048]{1,0:T(8,128)(2,1)} %copy-done.11, bf16[128,2048]{1,0:T(8,128)(2,1)} %refs_3_.1, bf16[128,2048]{1,0:T(8,128)(2,1)} %refs_4_.3), custom_call_target="tpu_custom_call" | custom-call | tf_op jit(solution)/shard_map/pallas_call | solution.py:140
  124.3 2.1 %all-to-all-done.1 = f32[8,1,18432]{2,1,0:T(1,128)S(1)} async-done(((f32[8,1,18432]{2,1,0:T(1,128)}), f32[8,1,18432]{2,1,0:T(1,128)S(1)}, u32[]{:S(2)}, u32[]{:S(2)}) %all-to-all-start.1) | async-done | bytes 589856 | tf_op jit(solution)/shard_map/all_to_all | solution.py:314
  (68 shorter events, 18.4 us)
Async XLA Ops:
  0.6 7.9 %copy-start.5 = (bf16[128,2048]{1,0:T(8,128)(2,1)S(1)}, bf16[128,2048]{1,0:T(8,128)(2,1)}, u32[]{:S(2)}) copy-start(bf16[128,2048]{1,0:T(8,128)(2,1)} %refs_4_.2) | copy-start | bytes 1572868
  0.6 7.9 %copy-start.6 = (bf16[128,2048]{1,0:T(8,128)(2,1)S(1)}, bf16[128,2048]{1,0:T(8,128)(2,1)}, u32[]{:S(2)}) copy-start(bf16[128,2048]{1,0:T(8,128)(2,1)} %refs_5_.1) | copy-start | bytes 1572868
  2.1 14.1 %copy-start.2 = (bf16[128,2048]{1,0:T(8,128)(2,1)}, bf16[128,2048]{1,0:T(8,128)(2,1)S(1)}, u32[]{:S(2)}) copy-start(bf16[128,2048]{1,0:T(8,128)(2,1)S(1)} %multiply_convert_fusion.1.refs_2_.bot_ref) | copy-start | bytes 1572868
  2.1 16.0 %collective-permute-start = (bf16[128,2048]{1,0:T(8,128)(2,1)S(1)}, bf16[128,2048]{1,0:T(8,128)(2,1)S(1)}, u32[]{:S(2)}, u32[]{:S(2)}) collective-permute-start(bf16[128,2048]{1,0:T(8,128)(2,1)S(1)} %multiply_convert_fusion.1.refs_2_.bot_ref), channel_id=1, source_target_pairs={{0,4},{4,8},{8,12},{12,16},{16,20},{20,24},{24,28},{1,5},{5,9},{9,... | collective-permute-start | bytes 1572872 | tf_op jit(solution)/shard_map/ppermute | solution.py:20
  9.8 16.6 %copy-start.8 = (bf16[128,2048]{1,0:T(8,128)(2,1)S(1)}, bf16[128,2048]{1,0:T(8,128)(2,1)}, u32[]{:S(2)}) copy-start(bf16[128,2048]{1,0:T(8,128)(2,1)} %param.10) | copy-start | bytes 1572868
  16.2 17.4 %copy-start.3 = (bf16[128,2048]{1,0:T(8,128)(2,1)S(1)}, bf16[128,2048]{1,0:T(8,128)(2,1)}, u32[]{:S(2)}) copy-start(bf16[128,2048]{1,0:T(8,128)(2,1)} %param.14) | copy-start | bytes 1572868
  16.2 17.4 %copy-start.13 = (f32[2048]{0:T(1024)S(1)}, f32[2048]{0:T(1024)}, u32[]{:S(2)}) copy-start(f32[2048]{0:T(1024)} %param.17) | copy-start | bytes 24580
  18.1 0.8 copy-start.7
  26.4 12.6 %copy-start.12 = (bf16[16,2048]{1,0:T(8,128)(2,1)S(1)}, bf16[16,2048]{1,0:T(8,128)(2,1)}, u32[]{:S(2)}) copy-start(bf16[16,2048]{1,0:T(8,128)(2,1)} %shard_map.161) | copy-start | bytes 196612
  41.0 15.2 %copy-start.14 = (f32[128,16]{0,1:T(8,128)S(1)}, f32[128,16]{0,1:T(8,128)}, u32[]{:S(2)}) copy-start(f32[128,16]{0,1:T(8,128)} %param.18) | copy-start | bytes 24580
  41.0 32.7 %all-to-all-start = ((bf16[8,32,2048]{2,1,0:T(8,128)(2,1)}), bf16[8,32,2048]{2,1,0:T(8,128)(2,1)S(1)}, u32[]{:S(2)}, u32[]{:S(2)}) async-start(bf16[8,32,2048]{2,1,0:T(8,128)(2,1)} %broadcast_in_dim.33), calls=%async_computation | async-start | bytes 2097152 | tf_op jit(solution)/shard_map/all_to_all | solution.py:314
  49.1 0.6 copy-start.9
  56.1 2.6 %copy-start.10 = (f32[128,1,128]{2,1,0:T(1,128)S(1)}, f32[128,1,128]{2,1,0:T(1,128)}, u32[]{:S(2)}) copy-start(f32[128,1,128]{2,1,0:T(1,128)} %copy-done.9) | copy-start | bytes 196612
  73.9 5.9 %copy-start.4 = (bf16[128,2048]{1,0:T(8,128)(2,1)S(1)}, bf16[128,2048]{1,0:T(8,128)(2,1)}, u32[]{:S(2)}) copy-start(bf16[128,2048]{1,0:T(8,128)(2,1)} %param.14) | copy-start | bytes 1572868
  75.0 12.9 %copy-start.1 = (f32[128,2048]{1,0:T(8,128)S(1)}, f32[128,2048]{1,0:T(8,128)}, u32[]{:S(2)}) copy-start(f32[128,2048]{1,0:T(8,128)} %shard_map.162) | copy-start | bytes 3145732
  79.8 8.2 %copy-start = (f32[128,2048]{1,0:T(8,128)S(1)}, f32[128,2048]{1,0:T(8,128)}, u32[]{:S(2)}) copy-start(f32[128,2048]{1,0:T(8,128)} %shard_map.167) | copy-start | bytes 3145732
  90.6 15.8 %collective-permute-start.1 = (bf16[128,2048]{1,0:T(8,128)(2,1)}, bf16[128,2048]{1,0:T(8,128)(2,1)S(1)}, u32[]{:S(2)}, u32[]{:S(2)}) collective-permute-start(bf16[128,2048]{1,0:T(8,128)(2,1)} %get-tuple-element.30.refs_1_.back_ref), channel_id=1, source_target_pairs={{4,0},{8,4},{12,8},{16,12},{20,16},{24,20},{28,24},{5,1},{9,5},{13... | collective-permute-start | bytes 1572872 | tf_op jit(solution)/shard_map/ppermute | solution.py:20
  106.3 10.3 %copy-start.11 = (bf16[128,2048]{1,0:T(8,128)(2,1)}, bf16[128,2048]{1,0:T(8,128)(2,1)S(1)}, u32[]{:S(2)}) copy-start(bf16[128,2048]{1,0:T(8,128)(2,1)S(1)} %collective-permute-done.1.refs_2_) | copy-start | bytes 1572868
  107.5 18.8 %all-to-all-start.1 = ((f32[8,1,18432]{2,1,0:T(1,128)}), f32[8,1,18432]{2,1,0:T(1,128)S(1)}, u32[]{:S(2)}, u32[]{:S(2)}) async-start(f32[8,1,18432]{2,1,0:T(1,128)} %broadcast_in_dim.62), calls=%async_computation.1 | async-start | bytes 1179648 | tf_op jit(solution)/shard_map/all_to_all | solution.py:314

commit v12 on v11

--- a/solution.py
+++ b/solution.py
@@ -381,13 +381,16 @@
     modes = li_decay.shape[1]
     grad_st = modal_states(bwd_states, back_li_bf, group_size=group_size)
     conv_st = modal_states(fwd_states, mixed_li_bf, group_size=group_size)
-    both_st = gather_seq(jnp.concatenate([grad_st, conv_st], 0))
+    count = lax.axis_size("seq")
+    later = (jnp.arange(count) > lax.axis_index("seq"))[:, None, None]
+    outgoing = jnp.where(later, conv_st[None], grad_st[None])
+    both_st = lax.all_to_all(outgoing, "seq", split_axis=0, concat_axis=0, tiled=True)
     both_st = both_st.astype(jnp.float32)
     grad_loc = band_conv(taps_li, back_li_bf, group_size=group_size, split=False, tri="upper")
     conv_loc = band_conv(li_fwd_rows, mixed_li_bf, group_size=group_size, split=False, tri="lower")
     both_st, grad_loc, conv_loc = lax.optimization_barrier((both_st, grad_loc, conv_loc))
-    grad_ent = entering_states(both_st[:, :modes], li_decay, row_count, group_size, False)
-    conv_ent = entering_states(both_st[:, modes:], li_decay, row_count, group_size, True)
+    grad_ent = entering_states(both_st, li_decay, row_count, group_size, False)
+    conv_ent = entering_states(both_st, li_decay, row_count, group_size, True)
     grad_mixed_li = modal_out(
         li_decay, weights_res, grad_ent, grad_loc, group_size=group_size, forward=False
     )

time: 129 us -> 123 us (0.953)
  waiting for transfers between devices: 14 us -> 6.34 us
  starting transfers between devices: 16.7 us -> 18.7 us
    all_to_all x2 -> x1, waiting for transfers between devices: 9.97 us -> 1.57 us  [gather_seq(): return lax.all_to_all(tiled, 'seq', split_axis=0, concat_axis=0, tiled=True)]
    all_to_all x0 -> x1, starting transfers between devices: none -> 6.8 us  [on_device(): lax.all_to_all(outgoing, 'seq', split_axis=0, concat_axis=0, tiled=True)]
    all_to_all x2 -> x1, starting transfers between devices: 10.5 us -> 5.71 us  [gather_seq(): return lax.all_to_all(tiled, 'seq', split_axis=0, concat_axis=0, tiled=True)]
    select_n x0 -> x1, other arithmetic: none -> 1.74 us  [on_device(): outgoing = jnp.where(later, conv_st[None], grad_st[None])]
  transfers between devices with their start and end apart: 4 -> 4, of which waited for: 4 -> 3; matrix products, arithmetic and copies ran while one was open for 9% -> 7% of each run, Pallas kernels for 32% -> 34%
where the time goes in v12:
time: 123 us; the launch traced here: 122 us
  Pallas kernels  57.2 us (47%)
  starting transfers between devices  18.7 us (15%)
  other arithmetic  16.4 us (13%)
  blocking collectives  12 us (10%)
  local copies, waits for them, and re-layouts  8.91 us (7%)
  waiting for transfers between devices  6.34 us (5%)
    pallas_call x4, Pallas kernels, band_conv(): pl.pallas_call(kernel, grid=(chans // block,), in_specs=in_specs, out_spe...  27.7 us
    pallas_call x1, Pallas kernels, gram_diag(): pl.pallas_call(kernel, grid=(chans // block,), in_specs=[pl.BlockSpec((ro...  11.4 us
    pallas_call x2, Pallas kernels, modal_out(): pl.pallas_call(kernel, grid=(chans // block,), in_specs=in_specs, out_spe...  9.47 us
    pallas_call x2, Pallas kernels, modal_states(): pl.pallas_call(kernel, grid=(chans // block,), in_specs=[pl.BlockSpec((gr...  8.7 us
    all_to_all x1, starting transfers between devices, on_device(): lax.all_to_all(outgoing, 'seq', split_axis=0, concat_axis=0, tiled=True)  6.8 us
    psum x1, blocking collectives, on_device(): cross_dots = lax.psum(jnp.sum(weighted * out_full, axis=1), 'chan')[:, None]  6.26 us
    ppermute x2, starting transfers between devices, from_behind(): lax.ppermute(value, axis, [(source, source + steps) for source in range(i...  6.18 us
    psum x1, blocking collectives, on_device(): squares = lax.psum(jnp.sum(out_full * out_full, axis=1), 'chan')  5.71 us
  transfers between devices with their start and end apart: 4, of which 3 were waited for; matrix products, arithmetic and copies ran while one was open for 7% of the time, Pallas kernels for 34%

profile of v12, /device:TPU:0, one launch (start us, length us, event | category | flops | bytes accessed | tf_op | source)
XLA Modules:
  0.0 121.6 jit_solution(11481351223915790114)
XLA Ops:
  0.7 1.4 %multiply_convert_fusion.2.refs_2_.bot_ref = bf16[128,2048]{1,0:T(8,128)(2,1)S(1)} fusion(bf16[128,2048]{1,0:T(8,128)(2,1)} %refs_3_.1, bf16[128,2048]{1,0:T(8,128)(2,1)} %refs_4_.3), kind=kLoop, calls=%fused_computation.29 | loop fusion | flops 1048576 | bytes 1572864 | tf_op jit(solution)/shard_map/convert_element_type | solution.py:358
  2.1 4.9 %collective-permute-start = (bf16[128,2048]{1,0:T(8,128)(2,1)S(1)}, bf16[128,2048]{1,0:T(8,128)(2,1)S(1)}, u32[]{:S(2)}, u32[]{:S(2)}) collective-permute-start(bf16[128,2048]{1,0:T(8,128)(2,1)S(1)} %multiply_convert_fusion.2.refs_2_.bot_ref), channel_id=1, source_target_pairs={{0,4},{4,8},{8,12},{12,16},{16,20},{20,24},{24,28},{1,5},{5,9},{9,... | collective-permute-start | bytes 1572872 | tf_op jit(solution)/shard_map/ppermute | solution.py:20
  8.8 1.3 %exponential_convert_fusion = (bf16[128,16,128]{2,1,0:T(8,128)(2,1)}, bf16[128,16,128]{2,1,0:T(8,128)(2,1)}) fusion(f32[128]{0:T(128)S(1)} %iota_subtract_fusion, f32[128,16]{1,0:T(8,128)S(1)} %copy.29), kind=kLoop, calls=%fused_computation.30 | loop fusion | flops 1048576 | bytes 1057280 | tf_op jit(solution)/shard_map/convert_element_type | solution.py:376
  10.1 4.3 %shard_map.163 = bf16[16,2048]{1,0:T(8,128)(2,1)} custom-call(bf16[128,16,128]{2,1,0:T(8,128)(2,1)} %get-tuple-element.34.e_ref, bf16[128,2048]{1,0:T(8,128)(2,1)} %multiply_convert_fusion.1.x_ref.refs_1_), custom_call_target="tpu_custom_call" | custom-call | tf_op jit(solution)/shard_map/pallas_call | solution.py:176
  15.2 2.9 %collective-permute-done.refs_1_.top_ref = bf16[128,2048]{1,0:T(8,128)(2,1)S(1)} collective-permute-done((bf16[128,2048]{1,0:T(8,128)(2,1)S(1)}, bf16[128,2048]{1,0:T(8,128)(2,1)S(1)}, u32[]{:S(2)}, u32[]{:S(2)}) %collective-permute-start) | collective-permute-done | bytes 524320 | tf_op jit(solution)/shard_map/ppermute | solution.py:20
  18.9 7.4 %shard_map.161 = f32[128,2048]{1,0:T(8,128)} custom-call(f32[128,256]{1,0:T(8,128)} %maximum_maximum_fusion.refs_0_, bf16[128,2048]{1,0:T(8,128)(2,1)} %copy-done.6, bf16[128,2048]{1,0:T(8,128)(2,1)} %copy-done.2), custom_call_target="tpu_custom_call" | custom-call | tf_op jit(solution)/shard_map/pallas_call | solution.py:140
  26.4 1.5 %fusion.3 = (f32[128]{0:T(128)S(1)}, bf16[128,2048]{1,0:T(8,128)(2,1)S(1)}) fusion(f32[128,2048]{1,0:T(8,128)} %shard_map.161, bf16[128,2048]{1,0:T(8,128)(2,1)S(1)} %copy-done.7), kind=kLoop, calls=%fused_computation.12 | loop fusion | flops 1572736 | bytes 2097664 | tf_op jit(solution)/shard_map/reduce_sum | solution.py:363
  27.9 5.7 %psum.14 = f32[128]{0:T(128)S(1)} all-reduce(f32[128]{0:T(128)S(1)} %get-tuple-element.28), channel_id=1, replica_groups=mesh['seq'=8,'chan'=4] {'chan'}, use_global_device_ids=true, to_apply=%region_1.2 | all-reduce | flops 128 | bytes 1024 | tf_op jit(solution)/shard_map/psum | solution.py:363
  34.7 4.4 %shard_map.162 = bf16[16,2048]{1,0:T(8,128)(2,1)} custom-call(bf16[128,16,128]{2,1,0:T(8,128)(2,1)} %get-tuple-element.33.e_ref, bf16[128,2048]{1,0:T(8,128)(2,1)} %fusion.x_ref.refs_1_), custom_call_target="tpu_custom_call" | custom-call | tf_op jit(solution)/shard_map/pallas_call | solution.py:176
  39.1 1.7 %broadcast_select_fusion = bf16[8,16,2048]{2,1,0:T(8,128)(2,1)} fusion(pred[8]{0:T(512)(128)(4,1)S(1)} %iota_compare_fusion, bf16[16,2048]{1,0:T(8,128)(2,1)S(1)} %copy-done.11, bf16[16,2048]{1,0:T(8,128)(2,1)} %shard_map.162), kind=kLoop, calls=%fused_computation.32 | loop fusion | flops 262144 | bytes 655368 | tf_op jit(solution)/shard_map/jit(_where)/select_n | solution.py:386
  40.8 6.8 %all-to-all-start = ((bf16[8,16,2048]{2,1,0:T(8,128)(2,1)}), bf16[8,16,2048]{2,1,0:T(8,128)(2,1)S(1)}, u32[]{:S(2)}, u32[]{:S(2)}) async-start(bf16[8,16,2048]{2,1,0:T(8,128)(2,1)} %broadcast_select_fusion), calls=%async_computation | async-start | bytes 1048576 | tf_op jit(solution)/shard_map/all_to_all | solution.py:387
  49.5 6.3 %shard_map.164.refs_3_ = f32[128,2048]{1,0:T(8,128)} custom-call(f32[128,128]{1,0:T(8,128)} %bitcast.12, bf16[128,2048]{1,0:T(8,128)(2,1)} %multiply_convert_fusion.1.x_ref.refs_1_), custom_call_target="tpu_custom_call" | custom-call | tf_op jit(solution)/shard_map/pallas_call | solution.py:140
  59.2 6.3 %shard_map.165.refs_3_ = f32[128,2048]{1,0:T(8,128)} custom-call(f32[128,128]{1,0:T(8,128)} %pad_maximum_fusion.1.refs_0_, bf16[128,2048]{1,0:T(8,128)(2,1)} %fusion.x_ref.refs_1_), custom_call_target="tpu_custom_call" | custom-call | tf_op jit(solution)/shard_map/pallas_call | solution.py:140
  66.7 4.6 %shard_map.167 = f32[128,2048]{1,0:T(8,128)} custom-call(f32[16,128]{1,0:T(8,128)} %reshape.86.refs_0_, f32[16,128]{1,0:T(8,128)} %reshape.87.refs_1_, f32[16,2048]{1,0:T(8,128)} %get-tuple-element.26.refs_2_, f32[128,2048]{1,0:T(8,128)} %shard_map.164.refs_3_), custom_call_target="tpu_custom_call" | custom-call | tf_op jit(solution)/shard_map/pallas_call | solution.py:251
  71.3 2.6 %fusion.12 = (f32[2048]{0:T(1024)S(1)}, f32[128]{0:T(128)S(1)}, bf16[128,2048]{1,0:T(8,128)(2,1)}) fusion(bf16[128,2048]{1,0:T(8,128)(2,1)S(1)} %get-tuple-element.29, f32[128]{0:T(128)S(1)} %get-tuple-element.39, f32[128,2048]{1,0:T(8,128)} %shard_map.167, bf16[128,2048]{1,0:T(8,128)(2,1)S(1)} %copy-done.3, f32[2048]{0:T(1024)S(1)} %copy-done.12), kind=kLoop, calls=%fused_computation.21 | loop fusion | flops 3405696 | bytes 2638848 | tf_op jit(solution)/shard_map/reduce_sum | solution.py:404
  73.9 6.3 %psum.15 = f32[128]{0:T(128)S(1)} all-reduce(f32[128]{0:T(128)S(1)} %get-tuple-element.25), channel_id=1, replica_groups=mesh['seq'=8,'chan'=4] {'chan'}, use_global_device_ids=true, to_apply=%region_5.6 | all-reduce | flops 128 | bytes 1024 | tf_op jit(solution)/shard_map/psum | solution.py:406
  80.2 2.6 %fusion.2 = (bf16[128,2048]{1,0:T(8,128)(2,1)}, bf16[128,2048]{1,0:T(8,128)(2,1)}) fusion(bf16[128,2048]{1,0:T(8,128)(2,1)} %param.10, f32[128]{0:T(128)S(1)} %psum.15, f32[128]{0:T(128)S(1)} %get-tuple-element.38, bf16[128,2048]{1,0:T(8,128)(2,1)S(1)} %get-tuple-element.29, f32[2048]{0:T(1024)S(1)} %copy-done.12, f32[128]{0:T(128)S(1)} %get-tuple-element.39, ...), kind=kLoop, calls=%fused_computation.11 | loop fusion | flops 3670016 | bytes 4728320 | tf_op jit(solution)/shard_map/convert_element_type | solution.py:409
  82.8 1.3 %collective-permute-start.1 = (bf16[128,2048]{1,0:T(8,128)(2,1)}, bf16[128,2048]{1,0:T(8,128)(2,1)S(1)}, u32[]{:S(2)}, u32[]{:S(2)}) collective-permute-start(bf16[128,2048]{1,0:T(8,128)(2,1)} %get-tuple-element.30.refs_1_.back_ref), channel_id=1, source_target_pairs={{4,0},{8,4},{12,8},{16,12},{20,16},{24,20},{28,24},{5,1},{9,5},{13... | collective-permute-start | bytes 1572872 | tf_op jit(solution)/shard_map/ppermute | solution.py:20
  84.1 11.4 %shard_map.169 = f32[128,256]{1,0:T(8,128)} custom-call(bf16[128,2048]{1,0:T(8,128)(2,1)} %get-tuple-element.30.refs_1_.back_ref, bf16[128,2048]{1,0:T(8,128)(2,1)} %copy-done.6, bf16[128,2048]{1,0:T(8,128)(2,1)} %copy-done.2), custom_call_target="tpu_custom_call" | custom-call | tf_op jit(solution)/shard_map/pallas_call | solution.py:297
  96.4 1.9 %collective-permute-done.1.refs_2_ = bf16[128,2048]{1,0:T(8,128)(2,1)S(1)} collective-permute-done((bf16[128,2048]{1,0:T(8,128)(2,1)}, bf16[128,2048]{1,0:T(8,128)(2,1)S(1)}, u32[]{:S(2)}, u32[]{:S(2)}) %collective-permute-start.1) | collective-permute-done | bytes 524320 | tf_op jit(solution)/shard_map/ppermute | solution.py:20
  99.4 5.7 %all-to-all-start.1 = ((f32[8,1,18432]{2,1,0:T(1,128)}), f32[8,1,18432]{2,1,0:T(1,128)S(1)}, u32[]{:S(2)}, u32[]{:S(2)}) async-start(f32[8,1,18432]{2,1,0:T(1,128)} %broadcast_in_dim.85), calls=%async_computation.1 | async-start | bytes 1179648 | tf_op jit(solution)/shard_map/all_to_all | solution.py:314
  105.8 4.9 %shard_map.166 = (bf16[128,2048]{1,0:T(8,128)(2,1)}, bf16[128,2048]{1,0:T(8,128)(2,1)}) custom-call(f32[16,128]{1,0:T(8,128)} %reshape.86.refs_0_, f32[16,128]{1,0:T(8,128)} %reshape.87.refs_1_, f32[16,2048]{1,0:T(8,128)} %get-tuple-element.27.refs_2_, f32[128,2048]{1,0:T(8,128)} %shard_map.165.refs_3_, bf16[128,2048]{1,0:T(8,128)(2,1)} %refs_4_.2, ...), custom_call_target="tpu_custom_call" | custom-call | tf_op jit(solution)/shard_map/pallas_call | solution.py:251
  110.7 7.6 %shard_map.168 = (bf16[128,2048]{1,0:T(8,128)(2,1)}, bf16[128,2048]{1,0:T(8,128)(2,1)}) custom-call(f32[128,256]{1,0:T(8,128)} %concatenate.14.refs_0_, bf16[128,2048]{1,0:T(8,128)(2,1)} %get-tuple-element.30.refs_1_.back_ref, bf16[128,2048]{1,0:T(8,128)(2,1)} %copy-done.10, bf16[128,2048]{1,0:T(8,128)(2,1)} %refs_3_.1, bf16[128,2048]{1,0:T(8,128)(2,1)} %refs_4_.3), custom_call_target="tpu_custom_call" | custom-call | tf_op jit(solution)/shard_map/pallas_call | solution.py:140
  118.3 1.6 %all-to-all-done.1 = f32[8,1,18432]{2,1,0:T(1,128)S(1)} async-done(((f32[8,1,18432]{2,1,0:T(1,128)}), f32[8,1,18432]{2,1,0:T(1,128)S(1)}, u32[]{:S(2)}, u32[]{:S(2)}) %all-to-all-start.1) | async-done | bytes 589856 | tf_op jit(solution)/shard_map/all_to_all | solution.py:314
  (71 shorter events, 15.3 us)
Async XLA Ops:
  0.6 6.4 %copy-start.13 = (f32[128,128]{1,0:T(8,128)S(1)}, f32[128,128]{1,0:T(8,128)}, u32[]{:S(2)}) copy-start(f32[128,128]{1,0:T(8,128)} %param.16) | copy-start | bytes 196612
  0.6 7.2 %copy-start.4 = (bf16[128,2048]{1,0:T(8,128)(2,1)S(1)}, bf16[128,2048]{1,0:T(8,128)(2,1)}, u32[]{:S(2)}) copy-start(bf16[128,2048]{1,0:T(8,128)(2,1)} %refs_4_.2) | copy-start | bytes 1572868
  0.7 7.2 %copy-start.5 = (bf16[128,2048]{1,0:T(8,128)(2,1)S(1)}, bf16[128,2048]{1,0:T(8,128)(2,1)}, u32[]{:S(2)}) copy-start(bf16[128,2048]{1,0:T(8,128)(2,1)} %refs_5_.1) | copy-start | bytes 1572868
  2.1 6.7 %copy-start.2 = (bf16[128,2048]{1,0:T(8,128)(2,1)}, bf16[128,2048]{1,0:T(8,128)(2,1)S(1)}, u32[]{:S(2)}) copy-start(bf16[128,2048]{1,0:T(8,128)(2,1)S(1)} %multiply_convert_fusion.2.refs_2_.bot_ref) | copy-start | bytes 1572868
  2.1 16.0 %collective-permute-start = (bf16[128,2048]{1,0:T(8,128)(2,1)S(1)}, bf16[128,2048]{1,0:T(8,128)(2,1)S(1)}, u32[]{:S(2)}, u32[]{:S(2)}) collective-permute-start(bf16[128,2048]{1,0:T(8,128)(2,1)S(1)} %multiply_convert_fusion.2.refs_2_.bot_ref), channel_id=1, source_target_pairs={{0,4},{4,8},{8,12},{12,16},{16,20},{20,24},{24,28},{1,5},{5,9},{9,... | collective-permute-start | bytes 1572872 | tf_op jit(solution)/shard_map/ppermute | solution.py:20
  7.1 0.7 copy-start.14
  7.1 0.7 copy-start.15
  15.2 11.2 %copy-start.7 = (bf16[128,2048]{1,0:T(8,128)(2,1)S(1)}, bf16[128,2048]{1,0:T(8,128)(2,1)}, u32[]{:S(2)}) copy-start(bf16[128,2048]{1,0:T(8,128)(2,1)} %param.10) | copy-start | bytes 1572868
  18.1 0.8 copy-start.6
  26.4 7.3 %copy-start.3 = (bf16[128,2048]{1,0:T(8,128)(2,1)S(1)}, bf16[128,2048]{1,0:T(8,128)(2,1)}, u32[]{:S(2)}) copy-start(bf16[128,2048]{1,0:T(8,128)(2,1)} %param.14) | copy-start | bytes 1572868
  27.9 5.7 %copy-start.12 = (f32[2048]{0:T(1024)S(1)}, f32[2048]{0:T(1024)}, u32[]{:S(2)}) copy-start(f32[2048]{0:T(1024)} %param.17) | copy-start | bytes 24580
  34.7 4.4 %copy-start.11 = (bf16[16,2048]{1,0:T(8,128)(2,1)S(1)}, bf16[16,2048]{1,0:T(8,128)(2,1)}, u32[]{:S(2)}) copy-start(bf16[16,2048]{1,0:T(8,128)(2,1)} %shard_map.163) | copy-start | bytes 196612
  40.8 24.7 %all-to-all-start = ((bf16[8,16,2048]{2,1,0:T(8,128)(2,1)}), bf16[8,16,2048]{2,1,0:T(8,128)(2,1)S(1)}, u32[]{:S(2)}, u32[]{:S(2)}) async-start(bf16[8,16,2048]{2,1,0:T(8,128)(2,1)} %broadcast_select_fusion), calls=%async_computation | async-start | bytes 1048576 | tf_op jit(solution)/shard_map/all_to_all | solution.py:387
  48.9 0.6 copy-start.8
  57.1 1.4 %copy-start.9 = (f32[128,1,128]{2,1,0:T(1,128)S(1)}, f32[128,1,128]{2,1,0:T(1,128)}, u32[]{:S(2)}) copy-start(f32[128,1,128]{2,1,0:T(1,128)} %copy-done.8) | copy-start | bytes 196612
  71.3 8.9 %copy-start = (f32[128,2048]{1,0:T(8,128)S(1)}, f32[128,2048]{1,0:T(8,128)}, u32[]{:S(2)}) copy-start(f32[128,2048]{1,0:T(8,128)} %shard_map.167) | copy-start | bytes 3145732
  71.3 8.9 %copy-start.1 = (f32[128,2048]{1,0:T(8,128)S(1)}, f32[128,2048]{1,0:T(8,128)}, u32[]{:S(2)}) copy-start(f32[128,2048]{1,0:T(8,128)} %shard_map.161) | copy-start | bytes 3145732
  82.8 15.5 %collective-permute-start.1 = (bf16[128,2048]{1,0:T(8,128)(2,1)}, bf16[128,2048]{1,0:T(8,128)(2,1)S(1)}, u32[]{:S(2)}, u32[]{:S(2)}) collective-permute-start(bf16[128,2048]{1,0:T(8,128)(2,1)} %get-tuple-element.30.refs_1_.back_ref), channel_id=1, source_target_pairs={{4,0},{8,4},{12,8},{16,12},{20,16},{24,20},{28,24},{5,1},{9,5},{13... | collective-permute-start | bytes 1572872 | tf_op jit(solution)/shard_map/ppermute | solution.py:20
  95.5 0.8 slice-start
  98.3 1.2 copy-start.10
  99.4 20.4 %all-to-all-start.1 = ((f32[8,1,18432]{2,1,0:T(1,128)}), f32[8,1,18432]{2,1,0:T(1,128)S(1)}, u32[]{:S(2)}, u32[]{:S(2)}) async-start(f32[8,1,18432]{2,1,0:T(1,128)} %broadcast_in_dim.85), calls=%async_computation.1 | async-start | bytes 1179648 | tf_op jit(solution)/shard_map/all_to_all | solution.py:314

commit v13 on v12

--- a/solution.py
+++ b/solution.py
@@ -416,7 +416,8 @@
     filter_part = jnp.flip(diag_sums[:, tap_count:], 1)
     packed = jnp.concatenate([gain_part, filter_part.reshape(-1)])
     packed, after_rim = lax.optimization_barrier((packed, after_rim))
-    param_sums = jnp.sum(gather_seq(packed), axis=0) * grad_scale
+    gathered = gather_seq(packed.astype(jnp.bfloat16)).astype(jnp.float32)
+    param_sums = jnp.sum(gathered, axis=0) * grad_scale
     grad_gain = param_sums[:chan_count]
     grad_filter = param_sums[chan_count:].reshape(group_count, tap_count)
     return (

time: 123 us -> 124 us (level)
  other arithmetic: 16.4 us -> 18.6 us
  waiting for transfers between devices: 6.34 us -> 4.75 us
    broadcast_in_dim x0 -> x1, other arithmetic: none -> 2.37 us  [gather_seq(): tiled = jnp.broadcast_to(value[None], (count,) + value.shape)]
    all_to_all x1, waiting for transfers between devices: 1.57 us -> 0.01 us  [gather_seq(): return lax.all_to_all(tiled, 'seq', split_axis=0, concat_axis=0, tiled=True)]
    unnamed x33 -> x35, local copies, waits for them, and re-layouts: 2.03 us -> 3.21 us
  transfers between devices with their start and end apart: 4 -> 4, of which waited for: 3 -> 2; matrix products, arithmetic and copies ran while one was open for 7% -> 8% of each run, Pallas kernels for 34% -> 33%
where the time goes in v13:
time: 124 us; the launch traced here: 123 us
  Pallas kernels  57.2 us (46%)
  starting transfers between devices  18.7 us (15%)
  other arithmetic  18.6 us (15%)
  blocking collectives  12 us (10%)
  local copies, waits for them, and re-layouts  9.79 us (8%)
  waiting for transfers between devices  4.75 us (4%)
    pallas_call x4, Pallas kernels, band_conv(): pl.pallas_call(kernel, grid=(chans // block,), in_specs=in_specs, out_spe...  27.7 us
    pallas_call x1, Pallas kernels, gram_diag(): pl.pallas_call(kernel, grid=(chans // block,), in_specs=[pl.BlockSpec((ro...  11.4 us
    pallas_call x2, Pallas kernels, modal_out(): pl.pallas_call(kernel, grid=(chans // block,), in_specs=in_specs, out_spe...  9.45 us
    pallas_call x2, Pallas kernels, modal_states(): pl.pallas_call(kernel, grid=(chans // block,), in_specs=[pl.BlockSpec((gr...  8.7 us
    all_to_all x1, starting transfers between devices, on_device(): lax.all_to_all(outgoing, 'seq', split_axis=0, concat_axis=0, tiled=True)  6.8 us
    psum x1, blocking collectives, on_device(): cross_dots = lax.psum(jnp.sum(weighted * out_full, axis=1), 'chan')[:, None]  6.26 us
    ppermute x2, starting transfers between devices, from_behind(): lax.ppermute(value, axis, [(source, source + steps) for source in range(i...  6.18 us
    psum x1, blocking collectives, on_device(): squares = lax.psum(jnp.sum(out_full * out_full, axis=1), 'chan')  5.72 us
  transfers between devices with their start and end apart: 4, of which 2 were waited for; matrix products, arithmetic and copies ran while one was open for 8% of the time, Pallas kernels for 33%

profile of v13, /device:TPU:0, one launch (start us, length us, event | category | flops | bytes accessed | tf_op | source)
XLA Modules:
  0.0 123.1 jit_solution(5092041887548770575)
XLA Ops:
  0.7 1.4 %multiply_convert_fusion.2.refs_2_.bot_ref = bf16[128,2048]{1,0:T(8,128)(2,1)S(1)} fusion(bf16[128,2048]{1,0:T(8,128)(2,1)} %refs_3_.1, bf16[128,2048]{1,0:T(8,128)(2,1)} %refs_4_.3), kind=kLoop, calls=%fused_computation.29 | loop fusion | flops 1048576 | bytes 1572864 | tf_op jit(solution)/shard_map/convert_element_type | solution.py:358
  2.1 4.9 %collective-permute-start = (bf16[128,2048]{1,0:T(8,128)(2,1)S(1)}, bf16[128,2048]{1,0:T(8,128)(2,1)S(1)}, u32[]{:S(2)}, u32[]{:S(2)}) collective-permute-start(bf16[128,2048]{1,0:T(8,128)(2,1)S(1)} %multiply_convert_fusion.2.refs_2_.bot_ref), channel_id=1, source_target_pairs={{0,4},{4,8},{8,12},{12,16},{16,20},{20,24},{24,28},{1,5},{5,9},{9,... | collective-permute-start | bytes 1572872 | tf_op jit(solution)/shard_map/ppermute | solution.py:20
  8.8 1.3 %exponential_convert_fusion = (bf16[128,16,128]{2,1,0:T(8,128)(2,1)}, bf16[128,16,128]{2,1,0:T(8,128)(2,1)}) fusion(f32[128]{0:T(128)S(1)} %iota_subtract_fusion, f32[128,16]{1,0:T(8,128)S(1)} %copy.33), kind=kLoop, calls=%fused_computation.30 | loop fusion | flops 1048576 | bytes 1057280 | tf_op jit(solution)/shard_map/convert_element_type | solution.py:376
  10.1 4.3 %shard_map.163 = bf16[16,2048]{1,0:T(8,128)(2,1)} custom-call(bf16[128,16,128]{2,1,0:T(8,128)(2,1)} %get-tuple-element.34.e_ref, bf16[128,2048]{1,0:T(8,128)(2,1)} %multiply_convert_fusion.1.x_ref.refs_1_), custom_call_target="tpu_custom_call" | custom-call | tf_op jit(solution)/shard_map/pallas_call | solution.py:176
  15.2 2.9 %collective-permute-done.refs_1_.top_ref = bf16[128,2048]{1,0:T(8,128)(2,1)S(1)} collective-permute-done((bf16[128,2048]{1,0:T(8,128)(2,1)S(1)}, bf16[128,2048]{1,0:T(8,128)(2,1)S(1)}, u32[]{:S(2)}, u32[]{:S(2)}) %collective-permute-start) | collective-permute-done | bytes 524320 | tf_op jit(solution)/shard_map/ppermute | solution.py:20
  18.9 7.5 %shard_map.161 = f32[128,2048]{1,0:T(8,128)} custom-call(f32[128,256]{1,0:T(8,128)} %maximum_maximum_fusion.refs_0_, bf16[128,2048]{1,0:T(8,128)(2,1)} %copy-done.6, bf16[128,2048]{1,0:T(8,128)(2,1)} %copy-done.2), custom_call_target="tpu_custom_call" | custom-call | tf_op jit(solution)/shard_map/pallas_call | solution.py:140
  26.4 1.5 %fusion.3 = (f32[128]{0:T(128)S(1)}, bf16[128,2048]{1,0:T(8,128)(2,1)S(1)}) fusion(f32[128,2048]{1,0:T(8,128)} %shard_map.161, bf16[128,2048]{1,0:T(8,128)(2,1)S(1)} %copy-done.7), kind=kLoop, calls=%fused_computation.12 | loop fusion | flops 1572736 | bytes 2097664 | tf_op jit(solution)/shard_map/reduce_sum | solution.py:363
  27.9 5.7 %psum.14 = f32[128]{0:T(128)S(1)} all-reduce(f32[128]{0:T(128)S(1)} %get-tuple-element.28), channel_id=1, replica_groups=mesh['seq'=8,'chan'=4] {'chan'}, use_global_device_ids=true, to_apply=%region_1.2 | all-reduce | flops 128 | bytes 1024 | tf_op jit(solution)/shard_map/psum | solution.py:363
  34.7 4.4 %shard_map.162 = bf16[16,2048]{1,0:T(8,128)(2,1)} custom-call(bf16[128,16,128]{2,1,0:T(8,128)(2,1)} %get-tuple-element.33.e_ref, bf16[128,2048]{1,0:T(8,128)(2,1)} %fusion.x_ref.refs_1_), custom_call_target="tpu_custom_call" | custom-call | tf_op jit(solution)/shard_map/pallas_call | solution.py:176
  39.1 1.7 %broadcast_select_fusion = bf16[8,16,2048]{2,1,0:T(8,128)(2,1)} fusion(pred[8]{0:T(512)(128)(4,1)S(1)} %iota_compare_fusion, bf16[16,2048]{1,0:T(8,128)(2,1)S(1)} %copy-done.11, bf16[16,2048]{1,0:T(8,128)(2,1)} %shard_map.162), kind=kLoop, calls=%fused_computation.33 | loop fusion | flops 262144 | bytes 655368 | tf_op jit(solution)/shard_map/jit(_where)/select_n | solution.py:386
  40.8 6.8 %all-to-all-start = ((bf16[8,16,2048]{2,1,0:T(8,128)(2,1)}), bf16[8,16,2048]{2,1,0:T(8,128)(2,1)S(1)}, u32[]{:S(2)}, u32[]{:S(2)}) async-start(bf16[8,16,2048]{2,1,0:T(8,128)(2,1)} %broadcast_select_fusion), calls=%async_computation | async-start | bytes 1048576 | tf_op jit(solution)/shard_map/all_to_all | solution.py:387
  49.5 6.3 %shard_map.164.refs_3_ = f32[128,2048]{1,0:T(8,128)} custom-call(f32[128,128]{1,0:T(8,128)} %bitcast.12, bf16[128,2048]{1,0:T(8,128)(2,1)} %multiply_convert_fusion.1.x_ref.refs_1_), custom_call_target="tpu_custom_call" | custom-call | tf_op jit(solution)/shard_map/pallas_call | solution.py:140
  59.2 6.3 %shard_map.165.refs_3_ = f32[128,2048]{1,0:T(8,128)} custom-call(f32[128,128]{1,0:T(8,128)} %pad_maximum_fusion.1.refs_0_, bf16[128,2048]{1,0:T(8,128)(2,1)} %fusion.x_ref.refs_1_), custom_call_target="tpu_custom_call" | custom-call | tf_op jit(solution)/shard_map/pallas_call | solution.py:140
  66.7 4.6 %shard_map.167 = f32[128,2048]{1,0:T(8,128)} custom-call(f32[16,128]{1,0:T(8,128)} %reshape.87.refs_0_, f32[16,128]{1,0:T(8,128)} %reshape.88.refs_1_, f32[16,2048]{1,0:T(8,128)} %get-tuple-element.26.refs_2_, f32[128,2048]{1,0:T(8,128)} %shard_map.164.refs_3_), custom_call_target="tpu_custom_call" | custom-call | tf_op jit(solution)/shard_map/pallas_call | solution.py:251
  71.3 2.6 %fusion.12 = (bf16[2048]{0:T(1024)(128)(2,1)S(1)}, f32[128]{0:T(128)S(1)}, bf16[128,2048]{1,0:T(8,128)(2,1)}) fusion(bf16[128,2048]{1,0:T(8,128)(2,1)S(1)} %get-tuple-element.29, f32[128]{0:T(128)S(1)} %get-tuple-element.39, f32[128,2048]{1,0:T(8,128)} %shard_map.167, bf16[128,2048]{1,0:T(8,128)(2,1)S(1)} %copy-done.3, f32[2048]{0:T(1024)S(1)} %copy-done.12), kind=kLoop, calls=%fused_computation.21 | loop fusion | flops 3405696 | bytes 2634752 | tf_op jit(solution)/shard_map/reduce_sum | solution.py:404
  73.9 6.3 %psum.15 = f32[128]{0:T(128)S(1)} all-reduce(f32[128]{0:T(128)S(1)} %get-tuple-element.25), channel_id=1, replica_groups=mesh['seq'=8,'chan'=4] {'chan'}, use_global_device_ids=true, to_apply=%region_5.6 | all-reduce | flops 128 | bytes 1024 | tf_op jit(solution)/shard_map/psum | solution.py:406
  80.2 2.6 %fusion.2 = (bf16[128,2048]{1,0:T(8,128)(2,1)}, bf16[128,2048]{1,0:T(8,128)(2,1)}) fusion(bf16[128,2048]{1,0:T(8,128)(2,1)} %param.10, f32[128]{0:T(128)S(1)} %psum.15, f32[128]{0:T(128)S(1)} %get-tuple-element.38, bf16[128,2048]{1,0:T(8,128)(2,1)S(1)} %get-tuple-element.29, f32[2048]{0:T(1024)S(1)} %copy-done.12, f32[128]{0:T(128)S(1)} %get-tuple-element.39, ...), kind=kLoop, calls=%fused_computation.11 | loop fusion | flops 3670016 | bytes 4728320 | tf_op jit(solution)/shard_map/convert_element_type | solution.py:409
  82.8 1.3 %collective-permute-start.1 = (bf16[128,2048]{1,0:T(8,128)(2,1)}, bf16[128,2048]{1,0:T(8,128)(2,1)S(1)}, u32[]{:S(2)}, u32[]{:S(2)}) collective-permute-start(bf16[128,2048]{1,0:T(8,128)(2,1)} %get-tuple-element.30.refs_1_.back_ref), channel_id=1, source_target_pairs={{4,0},{8,4},{12,8},{16,12},{20,16},{24,20},{28,24},{5,1},{9,5},{13... | collective-permute-start | bytes 1572872 | tf_op jit(solution)/shard_map/ppermute | solution.py:20
  84.0 11.4 %shard_map.169 = f32[128,256]{1,0:T(8,128)} custom-call(bf16[128,2048]{1,0:T(8,128)(2,1)} %get-tuple-element.30.refs_1_.back_ref, bf16[128,2048]{1,0:T(8,128)(2,1)} %copy-done.6, bf16[128,2048]{1,0:T(8,128)(2,1)} %copy-done.2), custom_call_target="tpu_custom_call" | custom-call | tf_op jit(solution)/shard_map/pallas_call | solution.py:297
  96.4 1.8 %collective-permute-done.1.refs_2_ = bf16[128,2048]{1,0:T(8,128)(2,1)S(1)} collective-permute-done((bf16[128,2048]{1,0:T(8,128)(2,1)}, bf16[128,2048]{1,0:T(8,128)(2,1)S(1)}, u32[]{:S(2)}, u32[]{:S(2)}) %collective-permute-start.1) | collective-permute-done | bytes 524320 | tf_op jit(solution)/shard_map/ppermute | solution.py:20
  99.1 2.4 %reduce.1 = bf16[8,18432]{1,0:T(8,128)(2,1)S(1)} reduce(bf16[8,1,18432]{2,1,0:T(2,128)(2,1)S(1)} %broadcast_in_dim.85, bf16[]{:T(256)} %broadcast.96), dimensions={1}, to_apply=%broadcast_in_dim.85.reduce_sub_computation | reduce | bytes 589826 | tf_op jit(solution)/shard_map/broadcast_in_dim | solution.py:313
  102.4 5.7 %all-to-all-start.1 = ((bf16[8,2,9216]{2,1,0:T(2,128)(2,1)}), bf16[8,2,9216]{2,1,0:T(2,128)(2,1)S(1)}, u32[]{:S(2)}, u32[]{:S(2)}) async-start(bf16[8,2,9216]{2,1,0:T(2,128)(2,1)} %reshape.93), calls=%async_computation.1 | async-start | bytes 589824 | tf_op jit(solution)/shard_map/all_to_all | solution.py:314
  108.8 4.9 %shard_map.166 = (bf16[128,2048]{1,0:T(8,128)(2,1)}, bf16[128,2048]{1,0:T(8,128)(2,1)}) custom-call(f32[16,128]{1,0:T(8,128)} %reshape.87.refs_0_, f32[16,128]{1,0:T(8,128)} %reshape.88.refs_1_, f32[16,2048]{1,0:T(8,128)} %get-tuple-element.27.refs_2_, f32[128,2048]{1,0:T(8,128)} %shard_map.165.refs_3_, bf16[128,2048]{1,0:T(8,128)(2,1)} %refs_4_.2, ...), custom_call_target="tpu_custom_call" | custom-call | tf_op jit(solution)/shard_map/pallas_call | solution.py:251
  113.7 7.6 %shard_map.168 = (bf16[128,2048]{1,0:T(8,128)(2,1)}, bf16[128,2048]{1,0:T(8,128)(2,1)}) custom-call(f32[128,256]{1,0:T(8,128)} %concatenate.14.refs_0_, bf16[128,2048]{1,0:T(8,128)(2,1)} %get-tuple-element.30.refs_1_.back_ref, bf16[128,2048]{1,0:T(8,128)(2,1)} %copy-done.10, bf16[128,2048]{1,0:T(8,128)(2,1)} %refs_3_.1, bf16[128,2048]{1,0:T(8,128)(2,1)} %refs_4_.3), custom_call_target="tpu_custom_call" | custom-call | tf_op jit(solution)/shard_map/pallas_call | solution.py:140
  (74 shorter events, 16.0 us)
Async XLA Ops:
  0.6 6.4 %copy-start.13 = (f32[128,128]{1,0:T(8,128)S(1)}, f32[128,128]{1,0:T(8,128)}, u32[]{:S(2)}) copy-start(f32[128,128]{1,0:T(8,128)} %param.16) | copy-start | bytes 196612
  0.6 7.2 %copy-start.4 = (bf16[128,2048]{1,0:T(8,128)(2,1)S(1)}, bf16[128,2048]{1,0:T(8,128)(2,1)}, u32[]{:S(2)}) copy-start(bf16[128,2048]{1,0:T(8,128)(2,1)} %refs_4_.2) | copy-start | bytes 1572868
  0.7 7.2 %copy-start.5 = (bf16[128,2048]{1,0:T(8,128)(2,1)S(1)}, bf16[128,2048]{1,0:T(8,128)(2,1)}, u32[]{:S(2)}) copy-start(bf16[128,2048]{1,0:T(8,128)(2,1)} %refs_5_.1) | copy-start | bytes 1572868
  2.1 6.7 %copy-start.2 = (bf16[128,2048]{1,0:T(8,128)(2,1)}, bf16[128,2048]{1,0:T(8,128)(2,1)S(1)}, u32[]{:S(2)}) copy-start(bf16[128,2048]{1,0:T(8,128)(2,1)S(1)} %multiply_convert_fusion.2.refs_2_.bot_ref) | copy-start | bytes 1572868
  2.1 16.0 %collective-permute-start = (bf16[128,2048]{1,0:T(8,128)(2,1)S(1)}, bf16[128,2048]{1,0:T(8,128)(2,1)S(1)}, u32[]{:S(2)}, u32[]{:S(2)}) collective-permute-start(bf16[128,2048]{1,0:T(8,128)(2,1)S(1)} %multiply_convert_fusion.2.refs_2_.bot_ref), channel_id=1, source_target_pairs={{0,4},{4,8},{8,12},{12,16},{16,20},{20,24},{24,28},{1,5},{5,9},{9,... | collective-permute-start | bytes 1572872 | tf_op jit(solution)/shard_map/ppermute | solution.py:20
  7.1 0.7 copy-start.14
  7.1 0.7 copy-start.15
  15.2 11.2 %copy-start.7 = (bf16[128,2048]{1,0:T(8,128)(2,1)S(1)}, bf16[128,2048]{1,0:T(8,128)(2,1)}, u32[]{:S(2)}) copy-start(bf16[128,2048]{1,0:T(8,128)(2,1)} %param.10) | copy-start | bytes 1572868
  18.1 0.8 copy-start.6
  26.4 7.3 %copy-start.3 = (bf16[128,2048]{1,0:T(8,128)(2,1)S(1)}, bf16[128,2048]{1,0:T(8,128)(2,1)}, u32[]{:S(2)}) copy-start(bf16[128,2048]{1,0:T(8,128)(2,1)} %param.14) | copy-start | bytes 1572868
  27.9 5.7 %copy-start.12 = (f32[2048]{0:T(1024)S(1)}, f32[2048]{0:T(1024)}, u32[]{:S(2)}) copy-start(f32[2048]{0:T(1024)} %param.17) | copy-start | bytes 24580
  34.7 4.4 %copy-start.11 = (bf16[16,2048]{1,0:T(8,128)(2,1)S(1)}, bf16[16,2048]{1,0:T(8,128)(2,1)}, u32[]{:S(2)}) copy-start(bf16[16,2048]{1,0:T(8,128)(2,1)} %shard_map.163) | copy-start | bytes 196612
  40.8 24.6 %all-to-all-start = ((bf16[8,16,2048]{2,1,0:T(8,128)(2,1)}), bf16[8,16,2048]{2,1,0:T(8,128)(2,1)S(1)}, u32[]{:S(2)}, u32[]{:S(2)}) async-start(bf16[8,16,2048]{2,1,0:T(8,128)(2,1)} %broadcast_select_fusion), calls=%async_computation | async-start | bytes 1048576 | tf_op jit(solution)/shard_map/all_to_all | solution.py:387
  48.9 0.6 copy-start.8
  57.1 1.4 %copy-start.9 = (f32[128,1,128]{2,1,0:T(1,128)S(1)}, f32[128,1,128]{2,1,0:T(1,128)}, u32[]{:S(2)}) copy-start(f32[128,1,128]{2,1,0:T(1,128)} %copy-done.8) | copy-start | bytes 196612
  71.3 8.9 %copy-start = (f32[128,2048]{1,0:T(8,128)S(1)}, f32[128,2048]{1,0:T(8,128)}, u32[]{:S(2)}) copy-start(f32[128,2048]{1,0:T(8,128)} %shard_map.161) | copy-start | bytes 3145732
  71.3 8.9 %copy-start.1 = (f32[128,2048]{1,0:T(8,128)S(1)}, f32[128,2048]{1,0:T(8,128)}, u32[]{:S(2)}) copy-start(f32[128,2048]{1,0:T(8,128)} %shard_map.167) | copy-start | bytes 3145732
  82.8 15.5 %collective-permute-start.1 = (bf16[128,2048]{1,0:T(8,128)(2,1)}, bf16[128,2048]{1,0:T(8,128)(2,1)S(1)}, u32[]{:S(2)}, u32[]{:S(2)}) collective-permute-start(bf16[128,2048]{1,0:T(8,128)(2,1)} %get-tuple-element.30.refs_1_.back_ref), channel_id=1, source_target_pairs={{4,0},{8,4},{12,8},{16,12},{20,16},{24,20},{28,24},{5,1},{9,5},{13... | collective-permute-start | bytes 1572872 | tf_op jit(solution)/shard_map/ppermute | solution.py:20
  98.3 3.2 %copy-start.10 = (bf16[128,2048]{1,0:T(8,128)(2,1)}, bf16[128,2048]{1,0:T(8,128)(2,1)S(1)}, u32[]{:S(2)}) copy-start(bf16[128,2048]{1,0:T(8,128)(2,1)S(1)} %collective-permute-done.1.refs_2_) | copy-start | bytes 1572868
  102.4 18.9 %all-to-all-start.1 = ((bf16[8,2,9216]{2,1,0:T(2,128)(2,1)}), bf16[8,2,9216]{2,1,0:T(2,128)(2,1)S(1)}, u32[]{:S(2)}, u32[]{:S(2)}) async-start(bf16[8,2,9216]{2,1,0:T(2,128)(2,1)} %reshape.93), calls=%async_computation.1 | async-start | bytes 589824 | tf_op jit(solution)/shard_map/all_to_all | solution.py:314

commit v14 on v12

--- a/solution.py
+++ b/solution.py
@@ -10,7 +10,7 @@
 D = 8192
 G = 512
 LANES = 128
-BLOCK_LANES = 512
+BLOCK_LANES = 1024
 HIGHEST = lax.Precision.HIGHEST
 
 

time: 123 us -> 122 us (level)
  transfers between devices with their start and end apart: 4 -> 4, of which waited for: 3 -> 3; matrix products, arithmetic and copies ran while one was open for 7% -> 7% of each run, Pallas kernels for 34% -> 33%
where the time goes in v14:
time: 122 us; the launch traced here: 121 us
  Pallas kernels  56.1 us (46%)
  starting transfers between devices  18.7 us (15%)
  other arithmetic  16.4 us (13%)
  blocking collectives  12 us (10%)
  local copies, waits for them, and re-layouts  8.91 us (7%)
  waiting for transfers between devices  6.92 us (6%)
    pallas_call x4, Pallas kernels, band_conv(): pl.pallas_call(kernel, grid=(chans // block,), in_specs=in_specs, out_spe...  27.9 us
    pallas_call x1, Pallas kernels, gram_diag(): pl.pallas_call(kernel, grid=(chans // block,), in_specs=[pl.BlockSpec((ro...  11.5 us
    pallas_call x2, Pallas kernels, modal_out(): pl.pallas_call(kernel, grid=(chans // block,), in_specs=in_specs, out_spe...  8.79 us
    pallas_call x2, Pallas kernels, modal_states(): pl.pallas_call(kernel, grid=(chans // block,), in_specs=[pl.BlockSpec((gr...  7.99 us
    all_to_all x1, starting transfers between devices, on_device(): lax.all_to_all(outgoing, 'seq', split_axis=0, concat_axis=0, tiled=True)  6.8 us
    psum x1, blocking collectives, on_device(): cross_dots = lax.psum(jnp.sum(weighted * out_full, axis=1), 'chan')[:, None]  6.25 us
    ppermute x2, starting transfers between devices, from_behind(): lax.ppermute(value, axis, [(source, source + steps) for source in range(i...  6.18 us
    psum x1, blocking collectives, on_device(): squares = lax.psum(jnp.sum(out_full * out_full, axis=1), 'chan')  5.71 us
  transfers between devices with their start and end apart: 4, of which 3 were waited for; matrix products, arithmetic and copies ran while one was open for 7% of the time, Pallas kernels for 33%

profile of v14, /device:TPU:0, one launch (start us, length us, event | category | flops | bytes accessed | tf_op | source)
XLA Modules:
  0.0 121.0 jit_solution(12918923198484971649)
XLA Ops:
  0.7 1.4 %multiply_convert_fusion.2.refs_2_.bot_ref = bf16[128,2048]{1,0:T(8,128)(2,1)S(1)} fusion(bf16[128,2048]{1,0:T(8,128)(2,1)} %refs_3_.1, bf16[128,2048]{1,0:T(8,128)(2,1)} %refs_4_.3), kind=kLoop, calls=%fused_computation.29 | loop fusion | flops 1048576 | bytes 1572864 | tf_op jit(solution)/shard_map/convert_element_type | solution.py:358
  2.1 4.9 %collective-permute-start = (bf16[128,2048]{1,0:T(8,128)(2,1)S(1)}, bf16[128,2048]{1,0:T(8,128)(2,1)S(1)}, u32[]{:S(2)}, u32[]{:S(2)}) collective-permute-start(bf16[128,2048]{1,0:T(8,128)(2,1)S(1)} %multiply_convert_fusion.2.refs_2_.bot_ref), channel_id=1, source_target_pairs={{0,4},{4,8},{8,12},{12,16},{16,20},{20,24},{24,28},{1,5},{5,9},{9,... | collective-permute-start | bytes 1572872 | tf_op jit(solution)/shard_map/ppermute | solution.py:20
  8.8 1.3 %exponential_convert_fusion = (bf16[128,16,128]{2,1,0:T(8,128)(2,1)}, bf16[128,16,128]{2,1,0:T(8,128)(2,1)}) fusion(f32[128]{0:T(128)S(1)} %iota_subtract_fusion, f32[128,16]{1,0:T(8,128)S(1)} %copy.29), kind=kLoop, calls=%fused_computation.30 | loop fusion | flops 1048576 | bytes 1057280 | tf_op jit(solution)/shard_map/convert_element_type | solution.py:376
  10.1 4.0 %shard_map.163 = bf16[16,2048]{1,0:T(8,128)(2,1)} custom-call(bf16[128,16,128]{2,1,0:T(8,128)(2,1)} %get-tuple-element.34.e_ref, bf16[128,2048]{1,0:T(8,128)(2,1)} %multiply_convert_fusion.1.x_ref.refs_1_), custom_call_target="tpu_custom_call" | custom-call | tf_op jit(solution)/shard_map/pallas_call | solution.py:176
  14.9 3.3 %collective-permute-done.refs_1_.top_ref = bf16[128,2048]{1,0:T(8,128)(2,1)S(1)} collective-permute-done((bf16[128,2048]{1,0:T(8,128)(2,1)S(1)}, bf16[128,2048]{1,0:T(8,128)(2,1)S(1)}, u32[]{:S(2)}, u32[]{:S(2)}) %collective-permute-start) | collective-permute-done | bytes 524320 | tf_op jit(solution)/shard_map/ppermute | solution.py:20
  18.9 7.4 %shard_map.161 = f32[128,2048]{1,0:T(8,128)} custom-call(f32[128,256]{1,0:T(8,128)} %maximum_maximum_fusion.refs_0_, bf16[128,2048]{1,0:T(8,128)(2,1)} %copy-done.6, bf16[128,2048]{1,0:T(8,128)(2,1)} %copy-done.2), custom_call_target="tpu_custom_call" | custom-call | tf_op jit(solution)/shard_map/pallas_call | solution.py:140
  26.4 1.5 %fusion.3 = (f32[128]{0:T(128)S(1)}, bf16[128,2048]{1,0:T(8,128)(2,1)S(1)}) fusion(f32[128,2048]{1,0:T(8,128)} %shard_map.161, bf16[128,2048]{1,0:T(8,128)(2,1)S(1)} %copy-done.7), kind=kLoop, calls=%fused_computation.12 | loop fusion | flops 1572736 | bytes 2097664 | tf_op jit(solution)/shard_map/reduce_sum | solution.py:363
  27.9 5.7 %psum.14 = f32[128]{0:T(128)S(1)} all-reduce(f32[128]{0:T(128)S(1)} %get-tuple-element.28), channel_id=1, replica_groups=mesh['seq'=8,'chan'=4] {'chan'}, use_global_device_ids=true, to_apply=%region_1.2 | all-reduce | flops 128 | bytes 1024 | tf_op jit(solution)/shard_map/psum | solution.py:363
  34.7 4.0 %shard_map.162 = bf16[16,2048]{1,0:T(8,128)(2,1)} custom-call(bf16[128,16,128]{2,1,0:T(8,128)(2,1)} %get-tuple-element.33.e_ref, bf16[128,2048]{1,0:T(8,128)(2,1)} %fusion.x_ref.refs_1_), custom_call_target="tpu_custom_call" | custom-call | tf_op jit(solution)/shard_map/pallas_call | solution.py:176
  38.7 1.7 %broadcast_select_fusion = bf16[8,16,2048]{2,1,0:T(8,128)(2,1)} fusion(pred[8]{0:T(512)(128)(4,1)S(1)} %iota_compare_fusion, bf16[16,2048]{1,0:T(8,128)(2,1)S(1)} %copy-done.11, bf16[16,2048]{1,0:T(8,128)(2,1)} %shard_map.162), kind=kLoop, calls=%fused_computation.32 | loop fusion | flops 262144 | bytes 655368 | tf_op jit(solution)/shard_map/jit(_where)/select_n | solution.py:386
  40.4 6.8 %all-to-all-start = ((bf16[8,16,2048]{2,1,0:T(8,128)(2,1)}), bf16[8,16,2048]{2,1,0:T(8,128)(2,1)S(1)}, u32[]{:S(2)}, u32[]{:S(2)}) async-start(bf16[8,16,2048]{2,1,0:T(8,128)(2,1)} %broadcast_select_fusion), calls=%async_computation | async-start | bytes 1048576 | tf_op jit(solution)/shard_map/all_to_all | solution.py:387
  49.1 6.4 %shard_map.164.refs_3_ = f32[128,2048]{1,0:T(8,128)} custom-call(f32[128,128]{1,0:T(8,128)} %bitcast.12, bf16[128,2048]{1,0:T(8,128)(2,1)} %multiply_convert_fusion.1.x_ref.refs_1_), custom_call_target="tpu_custom_call" | custom-call | tf_op jit(solution)/shard_map/pallas_call | solution.py:140
  58.9 6.4 %shard_map.165.refs_3_ = f32[128,2048]{1,0:T(8,128)} custom-call(f32[128,128]{1,0:T(8,128)} %pad_maximum_fusion.1.refs_0_, bf16[128,2048]{1,0:T(8,128)(2,1)} %fusion.x_ref.refs_1_), custom_call_target="tpu_custom_call" | custom-call | tf_op jit(solution)/shard_map/pallas_call | solution.py:140
  66.5 4.2 %shard_map.167 = f32[128,2048]{1,0:T(8,128)} custom-call(f32[16,128]{1,0:T(8,128)} %reshape.86.refs_0_, f32[16,128]{1,0:T(8,128)} %reshape.87.refs_1_, f32[16,2048]{1,0:T(8,128)} %get-tuple-element.26.refs_2_, f32[128,2048]{1,0:T(8,128)} %shard_map.164.refs_3_), custom_call_target="tpu_custom_call" | custom-call | tf_op jit(solution)/shard_map/pallas_call | solution.py:251
  70.7 2.6 %fusion.12 = (f32[2048]{0:T(1024)S(1)}, f32[128]{0:T(128)S(1)}, bf16[128,2048]{1,0:T(8,128)(2,1)}) fusion(bf16[128,2048]{1,0:T(8,128)(2,1)S(1)} %get-tuple-element.29, f32[128]{0:T(128)S(1)} %get-tuple-element.39, f32[128,2048]{1,0:T(8,128)} %shard_map.167, bf16[128,2048]{1,0:T(8,128)(2,1)S(1)} %copy-done.3, f32[2048]{0:T(1024)S(1)} %copy-done.12), kind=kLoop, calls=%fused_computation.21 | loop fusion | flops 3405696 | bytes 2638848 | tf_op jit(solution)/shard_map/reduce_sum | solution.py:404
  73.3 6.3 %psum.15 = f32[128]{0:T(128)S(1)} all-reduce(f32[128]{0:T(128)S(1)} %get-tuple-element.25), channel_id=1, replica_groups=mesh['seq'=8,'chan'=4] {'chan'}, use_global_device_ids=true, to_apply=%region_5.6 | all-reduce | flops 128 | bytes 1024 | tf_op jit(solution)/shard_map/psum | solution.py:406
  79.6 2.6 %fusion.2 = (bf16[128,2048]{1,0:T(8,128)(2,1)}, bf16[128,2048]{1,0:T(8,128)(2,1)}) fusion(bf16[128,2048]{1,0:T(8,128)(2,1)} %param.10, f32[128]{0:T(128)S(1)} %psum.15, f32[128]{0:T(128)S(1)} %get-tuple-element.38, bf16[128,2048]{1,0:T(8,128)(2,1)S(1)} %get-tuple-element.29, f32[2048]{0:T(1024)S(1)} %copy-done.12, f32[128]{0:T(128)S(1)} %get-tuple-element.39, ...), kind=kLoop, calls=%fused_computation.11 | loop fusion | flops 3670016 | bytes 4728320 | tf_op jit(solution)/shard_map/convert_element_type | solution.py:409
  82.2 1.3 %collective-permute-start.1 = (bf16[128,2048]{1,0:T(8,128)(2,1)}, bf16[128,2048]{1,0:T(8,128)(2,1)S(1)}, u32[]{:S(2)}, u32[]{:S(2)}) collective-permute-start(bf16[128,2048]{1,0:T(8,128)(2,1)} %get-tuple-element.30.refs_1_.back_ref), channel_id=1, source_target_pairs={{4,0},{8,4},{12,8},{16,12},{20,16},{24,20},{28,24},{5,1},{9,5},{13... | collective-permute-start | bytes 1572872 | tf_op jit(solution)/shard_map/ppermute | solution.py:20
  83.4 11.5 %shard_map.169 = f32[128,256]{1,0:T(8,128)} custom-call(bf16[128,2048]{1,0:T(8,128)(2,1)} %get-tuple-element.30.refs_1_.back_ref, bf16[128,2048]{1,0:T(8,128)(2,1)} %copy-done.6, bf16[128,2048]{1,0:T(8,128)(2,1)} %copy-done.2), custom_call_target="tpu_custom_call" | custom-call | tf_op jit(solution)/shard_map/pallas_call | solution.py:297
  95.9 1.8 %collective-permute-done.1.refs_2_ = bf16[128,2048]{1,0:T(8,128)(2,1)S(1)} collective-permute-done((bf16[128,2048]{1,0:T(8,128)(2,1)}, bf16[128,2048]{1,0:T(8,128)(2,1)S(1)}, u32[]{:S(2)}, u32[]{:S(2)}) %collective-permute-start.1) | collective-permute-done | bytes 524320 | tf_op jit(solution)/shard_map/ppermute | solution.py:20
  98.8 5.7 %all-to-all-start.1 = ((f32[8,1,18432]{2,1,0:T(1,128)}), f32[8,1,18432]{2,1,0:T(1,128)S(1)}, u32[]{:S(2)}, u32[]{:S(2)}) async-start(f32[8,1,18432]{2,1,0:T(1,128)} %broadcast_in_dim.85), calls=%async_computation.1 | async-start | bytes 1179648 | tf_op jit(solution)/shard_map/all_to_all | solution.py:314
  105.2 4.6 %shard_map.166 = (bf16[128,2048]{1,0:T(8,128)(2,1)}, bf16[128,2048]{1,0:T(8,128)(2,1)}) custom-call(f32[16,128]{1,0:T(8,128)} %reshape.86.refs_0_, f32[16,128]{1,0:T(8,128)} %reshape.87.refs_1_, f32[16,2048]{1,0:T(8,128)} %get-tuple-element.27.refs_2_, f32[128,2048]{1,0:T(8,128)} %shard_map.165.refs_3_, bf16[128,2048]{1,0:T(8,128)(2,1)} %refs_4_.2, ...), custom_call_target="tpu_custom_call" | custom-call | tf_op jit(solution)/shard_map/pallas_call | solution.py:251
  109.8 7.7 %shard_map.168 = (bf16[128,2048]{1,0:T(8,128)(2,1)}, bf16[128,2048]{1,0:T(8,128)(2,1)}) custom-call(f32[128,256]{1,0:T(8,128)} %concatenate.14.refs_0_, bf16[128,2048]{1,0:T(8,128)(2,1)} %get-tuple-element.30.refs_1_.back_ref, bf16[128,2048]{1,0:T(8,128)(2,1)} %copy-done.10, bf16[128,2048]{1,0:T(8,128)(2,1)} %refs_3_.1, bf16[128,2048]{1,0:T(8,128)(2,1)} %refs_4_.3), custom_call_target="tpu_custom_call" | custom-call | tf_op jit(solution)/shard_map/pallas_call | solution.py:140
  117.5 1.9 %all-to-all-done.1 = f32[8,1,18432]{2,1,0:T(1,128)S(1)} async-done(((f32[8,1,18432]{2,1,0:T(1,128)}), f32[8,1,18432]{2,1,0:T(1,128)S(1)}, u32[]{:S(2)}, u32[]{:S(2)}) %all-to-all-start.1) | async-done | bytes 589856 | tf_op jit(solution)/shard_map/all_to_all | solution.py:314
  (71 shorter events, 15.3 us)
Async XLA Ops:
  0.6 6.4 %copy-start.13 = (f32[128,128]{1,0:T(8,128)S(1)}, f32[128,128]{1,0:T(8,128)}, u32[]{:S(2)}) copy-start(f32[128,128]{1,0:T(8,128)} %param.16) | copy-start | bytes 196612
  0.6 7.2 %copy-start.4 = (bf16[128,2048]{1,0:T(8,128)(2,1)S(1)}, bf16[128,2048]{1,0:T(8,128)(2,1)}, u32[]{:S(2)}) copy-start(bf16[128,2048]{1,0:T(8,128)(2,1)} %refs_4_.2) | copy-start | bytes 1572868
  0.7 7.2 %copy-start.5 = (bf16[128,2048]{1,0:T(8,128)(2,1)S(1)}, bf16[128,2048]{1,0:T(8,128)(2,1)}, u32[]{:S(2)}) copy-start(bf16[128,2048]{1,0:T(8,128)(2,1)} %refs_5_.1) | copy-start | bytes 1572868
  2.1 6.7 %copy-start.2 = (bf16[128,2048]{1,0:T(8,128)(2,1)}, bf16[128,2048]{1,0:T(8,128)(2,1)S(1)}, u32[]{:S(2)}) copy-start(bf16[128,2048]{1,0:T(8,128)(2,1)S(1)} %multiply_convert_fusion.2.refs_2_.bot_ref) | copy-start | bytes 1572868
  2.1 16.0 %collective-permute-start = (bf16[128,2048]{1,0:T(8,128)(2,1)S(1)}, bf16[128,2048]{1,0:T(8,128)(2,1)S(1)}, u32[]{:S(2)}, u32[]{:S(2)}) collective-permute-start(bf16[128,2048]{1,0:T(8,128)(2,1)S(1)} %multiply_convert_fusion.2.refs_2_.bot_ref), channel_id=1, source_target_pairs={{0,4},{4,8},{8,12},{12,16},{16,20},{20,24},{24,28},{1,5},{5,9},{9,... | collective-permute-start | bytes 1572872 | tf_op jit(solution)/shard_map/ppermute | solution.py:20
  7.1 0.7 copy-start.14
  7.1 0.7 copy-start.15
  14.9 11.5 %copy-start.7 = (bf16[128,2048]{1,0:T(8,128)(2,1)S(1)}, bf16[128,2048]{1,0:T(8,128)(2,1)}, u32[]{:S(2)}) copy-start(bf16[128,2048]{1,0:T(8,128)(2,1)} %param.10) | copy-start | bytes 1572868
  18.1 0.8 copy-start.6
  26.4 7.3 %copy-start.3 = (bf16[128,2048]{1,0:T(8,128)(2,1)S(1)}, bf16[128,2048]{1,0:T(8,128)(2,1)}, u32[]{:S(2)}) copy-start(bf16[128,2048]{1,0:T(8,128)(2,1)} %param.14) | copy-start | bytes 1572868
  27.9 5.7 %copy-start.12 = (f32[2048]{0:T(1024)S(1)}, f32[2048]{0:T(1024)}, u32[]{:S(2)}) copy-start(f32[2048]{0:T(1024)} %param.17) | copy-start | bytes 24580
  34.7 4.0 %copy-start.11 = (bf16[16,2048]{1,0:T(8,128)(2,1)S(1)}, bf16[16,2048]{1,0:T(8,128)(2,1)}, u32[]{:S(2)}) copy-start(bf16[16,2048]{1,0:T(8,128)(2,1)} %shard_map.163) | copy-start | bytes 196612
  40.4 24.8 %all-to-all-start = ((bf16[8,16,2048]{2,1,0:T(8,128)(2,1)}), bf16[8,16,2048]{2,1,0:T(8,128)(2,1)S(1)}, u32[]{:S(2)}, u32[]{:S(2)}) async-start(bf16[8,16,2048]{2,1,0:T(8,128)(2,1)} %broadcast_select_fusion), calls=%async_computation | async-start | bytes 1048576 | tf_op jit(solution)/shard_map/all_to_all | solution.py:387
  48.5 0.6 copy-start.8
  56.7 1.4 %copy-start.9 = (f32[128,1,128]{2,1,0:T(1,128)S(1)}, f32[128,1,128]{2,1,0:T(1,128)}, u32[]{:S(2)}) copy-start(f32[128,1,128]{2,1,0:T(1,128)} %copy-done.8) | copy-start | bytes 196612
  70.7 8.9 %copy-start = (f32[128,2048]{1,0:T(8,128)S(1)}, f32[128,2048]{1,0:T(8,128)}, u32[]{:S(2)}) copy-start(f32[128,2048]{1,0:T(8,128)} %shard_map.167) | copy-start | bytes 3145732
  70.7 8.9 %copy-start.1 = (f32[128,2048]{1,0:T(8,128)S(1)}, f32[128,2048]{1,0:T(8,128)}, u32[]{:S(2)}) copy-start(f32[128,2048]{1,0:T(8,128)} %shard_map.161) | copy-start | bytes 3145732
  82.2 15.5 %collective-permute-start.1 = (bf16[128,2048]{1,0:T(8,128)(2,1)}, bf16[128,2048]{1,0:T(8,128)(2,1)S(1)}, u32[]{:S(2)}, u32[]{:S(2)}) collective-permute-start(bf16[128,2048]{1,0:T(8,128)(2,1)} %get-tuple-element.30.refs_1_.back_ref), channel_id=1, source_target_pairs={{4,0},{8,4},{12,8},{16,12},{20,16},{24,20},{28,24},{5,1},{9,5},{13... | collective-permute-start | bytes 1572872 | tf_op jit(solution)/shard_map/ppermute | solution.py:20
  94.9 0.8 slice-start
  97.7 1.2 copy-start.10
  98.8 20.5 %all-to-all-start.1 = ((f32[8,1,18432]{2,1,0:T(1,128)}), f32[8,1,18432]{2,1,0:T(1,128)S(1)}, u32[]{:S(2)}, u32[]{:S(2)}) async-start(f32[8,1,18432]{2,1,0:T(1,128)} %broadcast_in_dim.85), calls=%async_computation.1 | async-start | bytes 1179648 | tf_op jit(solution)/shard_map/all_to_all | solution.py:314

commit v15 on v14

--- a/solution.py
+++ b/solution.py
@@ -25,7 +25,7 @@
     return high, (value - high.astype(jnp.float32)).astype(jnp.bfloat16)
 
 
-def _band_kernel(*refs, group_size, split, tri, two_inputs, modal, sub, scaled):
+def _band_kernel(*refs, group_size, split, tri, two_inputs, modal, sub, scaled, keep):
     refs = list(refs)
     h_ref = refs.pop(0)
     top_ref = refs.pop(0)
@@ -34,8 +34,10 @@
         dec_ref, wt_ref, ent_ref = refs.pop(0), refs.pop(0), refs.pop(0)
     if scaled:
         first_ref, second_ref = refs.pop(0), refs.pop(0)
+    if keep:
+        first_ref = refs.pop(0)
     out_ref = refs.pop(0)
-    if scaled:
+    if scaled or keep:
         other_ref = refs.pop(0)
     rows = out_ref.shape[0]
     width = h_ref.shape[1]
@@ -87,6 +89,9 @@
         if scaled:
             out_ref[:, lanes] = (acc * first_ref[:, lanes].astype(jnp.float32)).astype(out_ref.dtype)
             other_ref[:, lanes] = (acc * second_ref[:, lanes].astype(jnp.float32)).astype(other_ref.dtype)
+        elif keep:
+            out_ref[:, lanes] = acc
+            other_ref[:, lanes] = (acc * first_ref[:, lanes].astype(jnp.float32)).astype(other_ref.dtype)
         else:
             out_ref[:, lanes] = acc
         return carry
@@ -95,7 +100,8 @@
 
 
 def band_conv(
-    band_rows, top, bottom=None, modal_args=None, scale_pair=None, *, group_size, split, tri, modal=None
+    band_rows, top, bottom=None, modal_args=None, scale_pair=None, gate=None,
+    *, group_size, split, tri, modal=None
 ):
     rows, chans = top.shape
     block = min(BLOCK_LANES, chans)
@@ -127,6 +133,12 @@
         args += list(scale_pair)
         out_specs = [out_specs, out_specs]
         out_shape = [jax.ShapeDtypeStruct((rows, chans), jnp.bfloat16)] * 2
+    keep = gate is not None
+    if keep:
+        in_specs.append(pl.BlockSpec((rows, block), lambda b: (0, b)))
+        args.append(gate)
+        out_specs = [out_specs, out_specs]
+        out_shape = [out_shape, jax.ShapeDtypeStruct((rows, chans), jnp.bfloat16)]
     kernel = functools.partial(
         _band_kernel,
         group_size=group_size,
@@ -136,6 +148,7 @@
         modal=modal,
         sub=block // LANES,
         scaled=scaled,
+        keep=keep,
     )
     return pl.pallas_call(
         kernel,
@@ -357,8 +370,9 @@
 
     mixed_mr = (key_mr.astype(jnp.float32) * value_mr.astype(jnp.float32)).astype(jnp.bfloat16)
     rim_rows = from_behind(mixed_mr, "seq", 1)
-    conv_mr = band_conv(fwd_rows, rim_rows, mixed_mr, group_size=group_size, split=False, tri=None)
-    out_mr = (query_mr.astype(jnp.float32) * conv_mr).astype(jnp.bfloat16)
+    conv_mr, out_mr = band_conv(
+        fwd_rows, rim_rows, mixed_mr, gate=query_mr, group_size=group_size, split=False, tri=None
+    )
     out_full = out_mr.astype(jnp.float32)
     squares = lax.psum(jnp.sum(out_full * out_full, axis=1), "chan")
     inv_rms = lax.rsqrt(squares / D + 1e-06)[:, None]

time: 122 us -> 122 us (level)
  no operation moved by 1% of the time
where the time goes in v15:
time: 122 us; the launch traced here: 121 us
  Pallas kernels  56.5 us (46%)
  starting transfers between devices  18.7 us (15%)
  other arithmetic  16.1 us (13%)
  blocking collectives  12 us (10%)
  local copies, waits for them, and re-layouts  9.19 us (8%)
  waiting for transfers between devices  6.86 us (6%)
    pallas_call x4, Pallas kernels, band_conv(): pl.pallas_call(kernel, grid=(chans // block,), in_specs=in_specs, out_spe...  28.2 us
    pallas_call x1, Pallas kernels, gram_diag(): pl.pallas_call(kernel, grid=(chans // block,), in_specs=[pl.BlockSpec((ro...  11.5 us
    pallas_call x2, Pallas kernels, modal_out(): pl.pallas_call(kernel, grid=(chans // block,), in_specs=in_specs, out_spe...  8.8 us
    pallas_call x2, Pallas kernels, modal_states(): pl.pallas_call(kernel, grid=(chans // block,), in_specs=[pl.BlockSpec((gr...  7.99 us
    all_to_all x1, starting transfers between devices, on_device(): lax.all_to_all(outgoing, 'seq', split_axis=0, concat_axis=0, tiled=True)  6.78 us
    psum x1, blocking collectives, on_device(): cross_dots = lax.psum(jnp.sum(weighted * out_full, axis=1), 'chan')[:, None]  6.26 us
    ppermute x2, starting transfers between devices, from_behind(): lax.ppermute(value, axis, [(source, source + steps) for source in range(i...  6.18 us
    psum x1, blocking collectives, on_device(): squares = lax.psum(jnp.sum(out_full * out_full, axis=1), 'chan')  5.72 us
  transfers between devices with their start and end apart: 4, of which 3 were waited for; matrix products, arithmetic and copies ran while one was open for 7% of the time, Pallas kernels for 33%

profile of v15, /device:TPU:0, one launch (start us, length us, event | category | flops | bytes accessed | tf_op | source)
XLA Modules:
  0.0 121.3 jit_solution(16804917005173089654)
XLA Ops:
  0.7 1.4 %multiply_convert_fusion.3.refs_2_.bot_ref = bf16[128,2048]{1,0:T(8,128)(2,1)S(1)} fusion(bf16[128,2048]{1,0:T(8,128)(2,1)} %refs_3_.3, bf16[128,2048]{1,0:T(8,128)(2,1)} %refs_4_.3), kind=kLoop, calls=%fused_computation.26 | loop fusion | flops 1048576 | bytes 1572864 | tf_op jit(solution)/shard_map/convert_element_type | solution.py:371
  2.1 4.9 %collective-permute-start = (bf16[128,2048]{1,0:T(8,128)(2,1)S(1)}, bf16[128,2048]{1,0:T(8,128)(2,1)S(1)}, u32[]{:S(2)}, u32[]{:S(2)}) collective-permute-start(bf16[128,2048]{1,0:T(8,128)(2,1)S(1)} %multiply_convert_fusion.3.refs_2_.bot_ref), channel_id=1, source_target_pairs={{0,4},{4,8},{8,12},{12,16},{16,20},{20,24},{24,28},{1,5},{5,9},{9,... | collective-permute-start | bytes 1572872 | tf_op jit(solution)/shard_map/ppermute | solution.py:20
  8.9 1.3 %exponential_convert_fusion = (bf16[128,16,128]{2,1,0:T(8,128)(2,1)}, bf16[128,16,128]{2,1,0:T(8,128)(2,1)}) fusion(f32[128]{0:T(128)S(1)} %iota_subtract_fusion, f32[128,16]{1,0:T(8,128)S(1)} %copy.29), kind=kLoop, calls=%fused_computation.27 | loop fusion | flops 1048576 | bytes 1057280 | tf_op jit(solution)/shard_map/convert_element_type | solution.py:390
  10.2 4.0 %shard_map.163 = bf16[16,2048]{1,0:T(8,128)(2,1)} custom-call(bf16[128,16,128]{2,1,0:T(8,128)(2,1)} %get-tuple-element.36.e_ref, bf16[128,2048]{1,0:T(8,128)(2,1)} %multiply_convert_fusion.2.x_ref.refs_1_), custom_call_target="tpu_custom_call" | custom-call | tf_op jit(solution)/shard_map/pallas_call | solution.py:189
  15.0 3.2 %collective-permute-done.refs_1_.top_ref = bf16[128,2048]{1,0:T(8,128)(2,1)S(1)} collective-permute-done((bf16[128,2048]{1,0:T(8,128)(2,1)S(1)}, bf16[128,2048]{1,0:T(8,128)(2,1)S(1)}, u32[]{:S(2)}, u32[]{:S(2)}) %collective-permute-start) | collective-permute-done | bytes 524320 | tf_op jit(solution)/shard_map/ppermute | solution.py:20
  18.9 7.7 %shard_map.161 = (f32[128,2048]{1,0:T(8,128)}, bf16[128,2048]{1,0:T(8,128)(2,1)}) custom-call(f32[128,256]{1,0:T(8,128)} %maximum_maximum_fusion.refs_0_, bf16[128,2048]{1,0:T(8,128)(2,1)} %copy-done.7, bf16[128,2048]{1,0:T(8,128)(2,1)} %copy-done.2, bf16[128,2048]{1,0:T(8,128)(2,1)} %refs_3_.2), custom_call_target="tpu_custom_call" | custom-call | tf_op jit(solution)/shard_map/pallas_call | solution.py:153
  26.7 1.3 %fusion.1 = f32[128]{0:T(128)S(1)} fusion(bf16[128,2048]{1,0:T(8,128)(2,1)} %get-tuple-element.18), kind=kLoop, calls=%fused_computation.8 | loop fusion | flops 786304 | bytes 524800 | tf_op jit(solution)/shard_map/reduce_sum | solution.py:377
  27.9 5.7 %psum.14 = f32[128]{0:T(128)S(1)} all-reduce(f32[128]{0:T(128)S(1)} %fusion.1), channel_id=1, replica_groups=mesh['seq'=8,'chan'=4] {'chan'}, use_global_device_ids=true, to_apply=%region_1.2 | all-reduce | flops 128 | bytes 1024 | tf_op jit(solution)/shard_map/psum | solution.py:377
  34.8 4.0 %shard_map.162 = bf16[16,2048]{1,0:T(8,128)(2,1)} custom-call(bf16[128,16,128]{2,1,0:T(8,128)(2,1)} %get-tuple-element.35.e_ref, bf16[128,2048]{1,0:T(8,128)(2,1)} %fusion.x_ref.refs_1_), custom_call_target="tpu_custom_call" | custom-call | tf_op jit(solution)/shard_map/pallas_call | solution.py:189
  38.8 1.7 %broadcast_select_fusion = bf16[8,16,2048]{2,1,0:T(8,128)(2,1)} fusion(pred[8]{0:T(512)(128)(4,1)S(1)} %iota_compare_fusion, bf16[16,2048]{1,0:T(8,128)(2,1)S(1)} %copy-done.12, bf16[16,2048]{1,0:T(8,128)(2,1)} %shard_map.162), kind=kLoop, calls=%fused_computation.29 | loop fusion | flops 262144 | bytes 655368 | tf_op jit(solution)/shard_map/jit(_where)/select_n | solution.py:400
  40.5 6.8 %all-to-all-start = ((bf16[8,16,2048]{2,1,0:T(8,128)(2,1)}), bf16[8,16,2048]{2,1,0:T(8,128)(2,1)S(1)}, u32[]{:S(2)}, u32[]{:S(2)}) async-start(bf16[8,16,2048]{2,1,0:T(8,128)(2,1)} %broadcast_select_fusion), calls=%async_computation | async-start | bytes 1048576 | tf_op jit(solution)/shard_map/all_to_all | solution.py:401
  49.4 6.4 %shard_map.164.refs_3_ = f32[128,2048]{1,0:T(8,128)} custom-call(f32[128,128]{1,0:T(8,128)} %bitcast.12, bf16[128,2048]{1,0:T(8,128)(2,1)} %multiply_convert_fusion.2.x_ref.refs_1_), custom_call_target="tpu_custom_call" | custom-call | tf_op jit(solution)/shard_map/pallas_call | solution.py:153
  59.1 6.4 %shard_map.165.refs_3_ = f32[128,2048]{1,0:T(8,128)} custom-call(f32[128,128]{1,0:T(8,128)} %pad_maximum_fusion.1.refs_0_, bf16[128,2048]{1,0:T(8,128)(2,1)} %fusion.x_ref.refs_1_), custom_call_target="tpu_custom_call" | custom-call | tf_op jit(solution)/shard_map/pallas_call | solution.py:153
  66.8 4.2 %shard_map.167 = f32[128,2048]{1,0:T(8,128)} custom-call(f32[16,128]{1,0:T(8,128)} %reshape.86.refs_0_, f32[16,128]{1,0:T(8,128)} %reshape.87.refs_1_, f32[16,2048]{1,0:T(8,128)} %get-tuple-element.30.refs_2_, f32[128,2048]{1,0:T(8,128)} %shard_map.164.refs_3_), custom_call_target="tpu_custom_call" | custom-call | tf_op jit(solution)/shard_map/pallas_call | solution.py:264
  71.0 2.6 %fusion.10 = (f32[2048]{0:T(1024)S(1)}, f32[128]{0:T(128)S(1)}, bf16[128,2048]{1,0:T(8,128)(2,1)}) fusion(bf16[128,2048]{1,0:T(8,128)(2,1)S(1)} %copy-done.1, f32[128]{0:T(128)S(1)} %get-tuple-element.41, f32[128,2048]{1,0:T(8,128)} %shard_map.167, bf16[128,2048]{1,0:T(8,128)(2,1)S(1)} %copy-done.3, f32[2048]{0:T(1024)S(1)} %copy-done.13), kind=kLoop, calls=%fused_computation.17 | loop fusion | flops 3405696 | bytes 2638848 | tf_op jit(solution)/shard_map/reduce_sum | solution.py:418
  73.6 6.3 %psum.15 = f32[128]{0:T(128)S(1)} all-reduce(f32[128]{0:T(128)S(1)} %get-tuple-element.29), channel_id=1, replica_groups=mesh['seq'=8,'chan'=4] {'chan'}, use_global_device_ids=true, to_apply=%region_5.6 | all-reduce | flops 128 | bytes 1024 | tf_op jit(solution)/shard_map/psum | solution.py:420
  79.9 2.6 %multiply_convert_fusion = (bf16[128,2048]{1,0:T(8,128)(2,1)S(1)}, bf16[128,2048]{1,0:T(8,128)(2,1)}) fusion(bf16[128,2048]{1,0:T(8,128)(2,1)S(1)} %copy-done.8, f32[128]{0:T(128)S(1)} %psum.15, f32[128]{0:T(128)S(1)} %get-tuple-element.40, bf16[128,2048]{1,0:T(8,128)(2,1)S(1)} %copy-done.1, f32[2048]{0:T(1024)S(1)} %copy-done.13, ...), kind=kLoop, calls=%fused_computation.18 | loop fusion | flops 3670016 | bytes 4728320 | tf_op jit(solution)/shard_map/convert_element_type | solution.py:423
  82.4 1.3 %collective-permute-start.1 = (bf16[128,2048]{1,0:T(8,128)(2,1)S(1)}, bf16[128,2048]{1,0:T(8,128)(2,1)S(1)}, u32[]{:S(2)}, u32[]{:S(2)}) collective-permute-start(bf16[128,2048]{1,0:T(8,128)(2,1)S(1)} %get-tuple-element.32.refs_1_.back_ref), channel_id=1, source_target_pairs={{4,0},{8,4},{12,8},{16,12},{20,16},{24,20},{28,24},{5,1},{9,5},{13... | collective-permute-start | bytes 1572872 | tf_op jit(solution)/shard_map/ppermute | solution.py:20
  83.7 11.5 %shard_map.169 = f32[128,256]{1,0:T(8,128)} custom-call(bf16[128,2048]{1,0:T(8,128)(2,1)} %copy-done.4, bf16[128,2048]{1,0:T(8,128)(2,1)} %copy-done.7, bf16[128,2048]{1,0:T(8,128)(2,1)} %copy-done.2), custom_call_target="tpu_custom_call" | custom-call | tf_op jit(solution)/shard_map/pallas_call | solution.py:310
  96.2 1.6 %collective-permute-done.1.refs_2_ = bf16[128,2048]{1,0:T(8,128)(2,1)S(1)} collective-permute-done((bf16[128,2048]{1,0:T(8,128)(2,1)S(1)}, bf16[128,2048]{1,0:T(8,128)(2,1)S(1)}, u32[]{:S(2)}, u32[]{:S(2)}) %collective-permute-start.1) | collective-permute-done | bytes 524320 | tf_op jit(solution)/shard_map/ppermute | solution.py:20
  98.9 5.7 %all-to-all-start.1 = ((f32[8,1,18432]{2,1,0:T(1,128)}), f32[8,1,18432]{2,1,0:T(1,128)S(1)}, u32[]{:S(2)}, u32[]{:S(2)}) async-start(f32[8,1,18432]{2,1,0:T(1,128)} %broadcast_in_dim.85), calls=%async_computation.1 | async-start | bytes 1179648 | tf_op jit(solution)/shard_map/all_to_all | solution.py:327
  105.2 4.6 %shard_map.166 = (bf16[128,2048]{1,0:T(8,128)(2,1)}, bf16[128,2048]{1,0:T(8,128)(2,1)}) custom-call(f32[16,128]{1,0:T(8,128)} %reshape.86.refs_0_, f32[16,128]{1,0:T(8,128)} %reshape.87.refs_1_, f32[16,2048]{1,0:T(8,128)} %get-tuple-element.31.refs_2_, f32[128,2048]{1,0:T(8,128)} %shard_map.165.refs_3_, bf16[128,2048]{1,0:T(8,128)(2,1)} %refs_4_.2, ...), custom_call_target="tpu_custom_call" | custom-call | tf_op jit(solution)/shard_map/pallas_call | solution.py:264
  109.8 7.7 %shard_map.168 = (bf16[128,2048]{1,0:T(8,128)(2,1)}, bf16[128,2048]{1,0:T(8,128)(2,1)}) custom-call(f32[128,256]{1,0:T(8,128)} %concatenate.14.refs_0_, bf16[128,2048]{1,0:T(8,128)(2,1)} %copy-done.4, bf16[128,2048]{1,0:T(8,128)(2,1)} %copy-done.11, bf16[128,2048]{1,0:T(8,128)(2,1)} %refs_3_.3, bf16[128,2048]{1,0:T(8,128)(2,1)} %refs_4_.3), custom_call_target="tpu_custom_call" | custom-call | tf_op jit(solution)/shard_map/pallas_call | solution.py:153
  117.5 2.1 %all-to-all-done.1 = f32[8,1,18432]{2,1,0:T(1,128)S(1)} async-done(((f32[8,1,18432]{2,1,0:T(1,128)}), f32[8,1,18432]{2,1,0:T(1,128)S(1)}, u32[]{:S(2)}, u32[]{:S(2)}) %all-to-all-start.1) | async-done | bytes 589856 | tf_op jit(solution)/shard_map/all_to_all | solution.py:327
  (73 shorter events, 15.6 us)
Async XLA Ops:
  0.6 7.3 %copy-start.5 = (bf16[128,2048]{1,0:T(8,128)(2,1)S(1)}, bf16[128,2048]{1,0:T(8,128)(2,1)}, u32[]{:S(2)}) copy-start(bf16[128,2048]{1,0:T(8,128)(2,1)} %refs_4_.2) | copy-start | bytes 1572868
  0.6 7.3 %copy-start.6 = (bf16[128,2048]{1,0:T(8,128)(2,1)S(1)}, bf16[128,2048]{1,0:T(8,128)(2,1)}, u32[]{:S(2)}) copy-start(bf16[128,2048]{1,0:T(8,128)(2,1)} %refs_5_.1) | copy-start | bytes 1572868
  2.1 6.8 %copy-start.2 = (bf16[128,2048]{1,0:T(8,128)(2,1)}, bf16[128,2048]{1,0:T(8,128)(2,1)S(1)}, u32[]{:S(2)}) copy-start(bf16[128,2048]{1,0:T(8,128)(2,1)S(1)} %multiply_convert_fusion.3.refs_2_.bot_ref) | copy-start | bytes 1572868
  2.1 16.0 %collective-permute-start = (bf16[128,2048]{1,0:T(8,128)(2,1)S(1)}, bf16[128,2048]{1,0:T(8,128)(2,1)S(1)}, u32[]{:S(2)}, u32[]{:S(2)}) collective-permute-start(bf16[128,2048]{1,0:T(8,128)(2,1)S(1)} %multiply_convert_fusion.3.refs_2_.bot_ref), channel_id=1, source_target_pairs={{0,4},{4,8},{8,12},{12,16},{16,20},{20,24},{24,28},{1,5},{5,9},{9,... | collective-permute-start | bytes 1572872 | tf_op jit(solution)/shard_map/ppermute | solution.py:20
  7.0 0.7 copy-start.16
  7.0 0.7 copy-start.15
  7.0 0.8 copy-start.14
  18.1 0.8 copy-start.7
  18.9 14.8 %copy-start.3 = (bf16[128,2048]{1,0:T(8,128)(2,1)S(1)}, bf16[128,2048]{1,0:T(8,128)(2,1)}, u32[]{:S(2)}) copy-start(bf16[128,2048]{1,0:T(8,128)(2,1)} %param.14) | copy-start | bytes 1572868
  26.6 7.0 %copy-start.1 = (bf16[128,2048]{1,0:T(8,128)(2,1)S(1)}, bf16[128,2048]{1,0:T(8,128)(2,1)}, u32[]{:S(2)}) copy-start(bf16[128,2048]{1,0:T(8,128)(2,1)} %get-tuple-element.18) | copy-start | bytes 1572868
  26.6 7.0 %copy-start.13 = (f32[2048]{0:T(1024)S(1)}, f32[2048]{0:T(1024)}, u32[]{:S(2)}) copy-start(f32[2048]{0:T(1024)} %param.17) | copy-start | bytes 24580
  34.8 4.0 %copy-start.12 = (bf16[16,2048]{1,0:T(8,128)(2,1)S(1)}, bf16[16,2048]{1,0:T(8,128)(2,1)}, u32[]{:S(2)}) copy-start(bf16[16,2048]{1,0:T(8,128)(2,1)} %shard_map.163) | copy-start | bytes 196612
  40.5 25.0 %all-to-all-start = ((bf16[8,16,2048]{2,1,0:T(8,128)(2,1)}), bf16[8,16,2048]{2,1,0:T(8,128)(2,1)S(1)}, u32[]{:S(2)}, u32[]{:S(2)}) async-start(bf16[8,16,2048]{2,1,0:T(8,128)(2,1)} %broadcast_select_fusion), calls=%async_computation | async-start | bytes 1048576 | tf_op jit(solution)/shard_map/all_to_all | solution.py:401
  48.8 0.6 copy-start.9
  57.6 0.8 copy-start.10
  71.0 8.8 %copy-start = (f32[128,2048]{1,0:T(8,128)S(1)}, f32[128,2048]{1,0:T(8,128)}, u32[]{:S(2)}) copy-start(f32[128,2048]{1,0:T(8,128)} %shard_map.167) | copy-start | bytes 3145732
  71.0 8.8 %copy-start.8 = (bf16[128,2048]{1,0:T(8,128)(2,1)S(1)}, bf16[128,2048]{1,0:T(8,128)(2,1)}, u32[]{:S(2)}) copy-start(bf16[128,2048]{1,0:T(8,128)(2,1)} %refs_3_.2) | copy-start | bytes 1572868
  82.4 1.3 %copy-start.4 = (bf16[128,2048]{1,0:T(8,128)(2,1)}, bf16[128,2048]{1,0:T(8,128)(2,1)S(1)}, u32[]{:S(2)}) copy-start(bf16[128,2048]{1,0:T(8,128)(2,1)S(1)} %get-tuple-element.32.refs_1_.back_ref) | copy-start | bytes 1572868
  82.4 15.3 %collective-permute-start.1 = (bf16[128,2048]{1,0:T(8,128)(2,1)S(1)}, bf16[128,2048]{1,0:T(8,128)(2,1)S(1)}, u32[]{:S(2)}, u32[]{:S(2)}) collective-permute-start(bf16[128,2048]{1,0:T(8,128)(2,1)S(1)} %get-tuple-element.32.refs_1_.back_ref), channel_id=1, source_target_pairs={{4,0},{8,4},{12,8},{16,12},{20,16},{24,20},{28,24},{5,1},{9,5},{13... | collective-permute-start | bytes 1572872 | tf_op jit(solution)/shard_map/ppermute | solution.py:20
  95.2 0.8 slice-start
  97.7 1.2 copy-start.11
  98.9 20.8 %all-to-all-start.1 = ((f32[8,1,18432]{2,1,0:T(1,128)}), f32[8,1,18432]{2,1,0:T(1,128)S(1)}, u32[]{:S(2)}, u32[]{:S(2)}) async-start(f32[8,1,18432]{2,1,0:T(1,128)} %broadcast_in_dim.85), calls=%async_computation.1 | async-start | bytes 1179648 | tf_op jit(solution)/shard_map/all_to_all | solution.py:327

commit v16 on v14

--- a/solution.py
+++ b/solution.py
@@ -10,7 +10,7 @@
 D = 8192
 G = 512
 LANES = 128
-BLOCK_LANES = 1024
+BLOCK_LANES = 2048
 HIGHEST = lax.Precision.HIGHEST
 
 

time: 122 us -> 123 us (level)
  Pallas kernels: 56.1 us -> 58.8 us
  transfers between devices with their start and end apart: 4 -> 4, of which waited for: 3 -> 3; matrix products, arithmetic and copies ran while one was open for 7% -> 7% of each run, Pallas kernels for 33% -> 34%
where the time goes in v16:
time: 123 us
  Pallas kernels  58.8 us (48%)
  starting transfers between devices  18.7 us (15%)
  other arithmetic  16.4 us (13%)
  blocking collectives  12 us (10%)
  local copies, waits for them, and re-layouts  8.91 us (7%)
  waiting for transfers between devices  5.83 us (5%)
    pallas_call x4, Pallas kernels, band_conv(): pl.pallas_call(kernel, grid=(chans // block,), in_specs=in_specs, out_spe...  29.1 us
    pallas_call x1, Pallas kernels, gram_diag(): pl.pallas_call(kernel, grid=(chans // block,), in_specs=[pl.BlockSpec((ro...  11.7 us
    pallas_call x2, Pallas kernels, modal_out(): pl.pallas_call(kernel, grid=(chans // block,), in_specs=in_specs, out_spe...  9.7 us
    pallas_call x2, Pallas kernels, modal_states(): pl.pallas_call(kernel, grid=(chans // block,), in_specs=[pl.BlockSpec((gr...  8.34 us
    all_to_all x1, starting transfers between devices, on_device(): lax.all_to_all(outgoing, 'seq', split_axis=0, concat_axis=0, tiled=True)  6.8 us
    psum x1, blocking collectives, on_device(): cross_dots = lax.psum(jnp.sum(weighted * out_full, axis=1), 'chan')[:, None]  6.28 us
    ppermute x2, starting transfers between devices, from_behind(): lax.ppermute(value, axis, [(source, source + steps) for source in range(i...  6.18 us
    psum x1, blocking collectives, on_device(): squares = lax.psum(jnp.sum(out_full * out_full, axis=1), 'chan')  5.71 us
  transfers between devices with their start and end apart: 4, of which 3 were waited for; matrix products, arithmetic and copies ran while one was open for 7% of the time, Pallas kernels for 34%

profile of v16, /device:TPU:0, one launch (start us, length us, event | category | flops | bytes accessed | tf_op | source)
XLA Modules:
  0.0 122.6 jit_solution(11672683867356740200)
XLA Ops:
  0.7 1.4 %multiply_convert_fusion.2.refs_2_.bot_ref = bf16[128,2048]{1,0:T(8,128)(2,1)S(1)} fusion(bf16[128,2048]{1,0:T(8,128)(2,1)} %refs_3_.1, bf16[128,2048]{1,0:T(8,128)(2,1)} %refs_4_.3), kind=kLoop, calls=%fused_computation.29 | loop fusion | flops 1048576 | bytes 1572864 | tf_op jit(solution)/shard_map/convert_element_type | solution.py:358
  2.1 4.9 %collective-permute-start = (bf16[128,2048]{1,0:T(8,128)(2,1)S(1)}, bf16[128,2048]{1,0:T(8,128)(2,1)S(1)}, u32[]{:S(2)}, u32[]{:S(2)}) collective-permute-start(bf16[128,2048]{1,0:T(8,128)(2,1)S(1)} %multiply_convert_fusion.2.refs_2_.bot_ref), channel_id=1, source_target_pairs={{0,4},{4,8},{8,12},{12,16},{16,20},{20,24},{24,28},{1,5},{5,9},{9,... | collective-permute-start | bytes 1572872 | tf_op jit(solution)/shard_map/ppermute | solution.py:20
  8.8 1.3 %exponential_convert_fusion = (bf16[128,16,128]{2,1,0:T(8,128)(2,1)}, bf16[128,16,128]{2,1,0:T(8,128)(2,1)}) fusion(f32[128]{0:T(128)S(1)} %iota_subtract_fusion, f32[128,16]{1,0:T(8,128)S(1)} %copy.29), kind=kLoop, calls=%fused_computation.30 | loop fusion | flops 1048576 | bytes 1057280 | tf_op jit(solution)/shard_map/convert_element_type | solution.py:376
  10.1 4.2 %shard_map.163 = bf16[16,2048]{1,0:T(8,128)(2,1)} custom-call(bf16[128,16,128]{2,1,0:T(8,128)(2,1)} %get-tuple-element.34.e_ref, bf16[128,2048]{1,0:T(8,128)(2,1)} %multiply_convert_fusion.1.x_ref.refs_1_), custom_call_target="tpu_custom_call" | custom-call | tf_op jit(solution)/shard_map/pallas_call | solution.py:176
  15.1 3.1 %collective-permute-done.refs_1_.top_ref = bf16[128,2048]{1,0:T(8,128)(2,1)S(1)} collective-permute-done((bf16[128,2048]{1,0:T(8,128)(2,1)S(1)}, bf16[128,2048]{1,0:T(8,128)(2,1)S(1)}, u32[]{:S(2)}, u32[]{:S(2)}) %collective-permute-start) | collective-permute-done | bytes 524320 | tf_op jit(solution)/shard_map/ppermute | solution.py:20
  18.9 7.8 %shard_map.161 = f32[128,2048]{1,0:T(8,128)} custom-call(f32[128,256]{1,0:T(8,128)} %maximum_maximum_fusion.refs_0_, bf16[128,2048]{1,0:T(8,128)(2,1)} %copy-done.6, bf16[128,2048]{1,0:T(8,128)(2,1)} %copy-done.2), custom_call_target="tpu_custom_call" | custom-call | tf_op jit(solution)/shard_map/pallas_call | solution.py:140
  26.7 1.5 %fusion.3 = (f32[128]{0:T(128)S(1)}, bf16[128,2048]{1,0:T(8,128)(2,1)S(1)}) fusion(f32[128,2048]{1,0:T(8,128)} %shard_map.161, bf16[128,2048]{1,0:T(8,128)(2,1)S(1)} %copy-done.7), kind=kLoop, calls=%fused_computation.12 | loop fusion | flops 1572736 | bytes 2097664 | tf_op jit(solution)/shard_map/reduce_sum | solution.py:363
  28.2 5.7 %psum.14 = f32[128]{0:T(128)S(1)} all-reduce(f32[128]{0:T(128)S(1)} %get-tuple-element.28), channel_id=1, replica_groups=mesh['seq'=8,'chan'=4] {'chan'}, use_global_device_ids=true, to_apply=%region_1.2 | all-reduce | flops 128 | bytes 1024 | tf_op jit(solution)/shard_map/psum | solution.py:363
  35.0 4.2 %shard_map.162 = bf16[16,2048]{1,0:T(8,128)(2,1)} custom-call(bf16[128,16,128]{2,1,0:T(8,128)(2,1)} %get-tuple-element.33.e_ref, bf16[128,2048]{1,0:T(8,128)(2,1)} %fusion.x_ref.refs_1_), custom_call_target="tpu_custom_call" | custom-call | tf_op jit(solution)/shard_map/pallas_call | solution.py:176
  39.2 1.7 %broadcast_select_fusion = bf16[8,16,2048]{2,1,0:T(8,128)(2,1)} fusion(pred[8]{0:T(512)(128)(4,1)S(1)} %iota_compare_fusion, bf16[16,2048]{1,0:T(8,128)(2,1)S(1)} %copy-done.11, bf16[16,2048]{1,0:T(8,128)(2,1)} %shard_map.162), kind=kLoop, calls=%fused_computation.32 | loop fusion | flops 262144 | bytes 655368 | tf_op jit(solution)/shard_map/jit(_where)/select_n | solution.py:386
  41.0 6.8 %all-to-all-start = ((bf16[8,16,2048]{2,1,0:T(8,128)(2,1)}), bf16[8,16,2048]{2,1,0:T(8,128)(2,1)S(1)}, u32[]{:S(2)}, u32[]{:S(2)}) async-start(bf16[8,16,2048]{2,1,0:T(8,128)(2,1)} %broadcast_select_fusion), calls=%async_computation | async-start | bytes 1048576 | tf_op jit(solution)/shard_map/all_to_all | solution.py:387
  49.6 6.6 %shard_map.164.refs_3_ = f32[128,2048]{1,0:T(8,128)} custom-call(f32[128,128]{1,0:T(8,128)} %bitcast.12, bf16[128,2048]{1,0:T(8,128)(2,1)} %multiply_convert_fusion.1.x_ref.refs_1_), custom_call_target="tpu_custom_call" | custom-call | tf_op jit(solution)/shard_map/pallas_call | solution.py:140
  59.6 6.6 %shard_map.165.refs_3_ = f32[128,2048]{1,0:T(8,128)} custom-call(f32[128,128]{1,0:T(8,128)} %pad_maximum_fusion.1.refs_0_, bf16[128,2048]{1,0:T(8,128)(2,1)} %fusion.x_ref.refs_1_), custom_call_target="tpu_custom_call" | custom-call | tf_op jit(solution)/shard_map/pallas_call | solution.py:140
  67.4 4.6 %shard_map.167 = f32[128,2048]{1,0:T(8,128)} custom-call(f32[16,128]{1,0:T(8,128)} %reshape.86.refs_0_, f32[16,128]{1,0:T(8,128)} %reshape.87.refs_1_, f32[16,2048]{1,0:T(8,128)} %get-tuple-element.26.refs_2_, f32[128,2048]{1,0:T(8,128)} %shard_map.164.refs_3_), custom_call_target="tpu_custom_call" | custom-call | tf_op jit(solution)/shard_map/pallas_call | solution.py:251
  72.1 2.6 %fusion.12 = (f32[2048]{0:T(1024)S(1)}, f32[128]{0:T(128)S(1)}, bf16[128,2048]{1,0:T(8,128)(2,1)}) fusion(bf16[128,2048]{1,0:T(8,128)(2,1)S(1)} %get-tuple-element.29, f32[128]{0:T(128)S(1)} %get-tuple-element.39, f32[128,2048]{1,0:T(8,128)} %shard_map.167, bf16[128,2048]{1,0:T(8,128)(2,1)S(1)} %copy-done.3, f32[2048]{0:T(1024)S(1)} %copy-done.12), kind=kLoop, calls=%fused_computation.21 | loop fusion | flops 3405696 | bytes 2638848 | tf_op jit(solution)/shard_map/reduce_sum | solution.py:404
  74.7 6.3 %psum.15 = f32[128]{0:T(128)S(1)} all-reduce(f32[128]{0:T(128)S(1)} %get-tuple-element.25), channel_id=1, replica_groups=mesh['seq'=8,'chan'=4] {'chan'}, use_global_device_ids=true, to_apply=%region_5.6 | all-reduce | flops 128 | bytes 1024 | tf_op jit(solution)/shard_map/psum | solution.py:406
  81.0 2.6 %fusion.2 = (bf16[128,2048]{1,0:T(8,128)(2,1)}, bf16[128,2048]{1,0:T(8,128)(2,1)}) fusion(bf16[128,2048]{1,0:T(8,128)(2,1)} %param.10, f32[128]{0:T(128)S(1)} %psum.15, f32[128]{0:T(128)S(1)} %get-tuple-element.38, bf16[128,2048]{1,0:T(8,128)(2,1)S(1)} %get-tuple-element.29, f32[2048]{0:T(1024)S(1)} %copy-done.12, f32[128]{0:T(128)S(1)} %get-tuple-element.39, ...), kind=kLoop, calls=%fused_computation.11 | loop fusion | flops 3670016 | bytes 4728320 | tf_op jit(solution)/shard_map/convert_element_type | solution.py:409
  83.6 1.3 %collective-permute-start.1 = (bf16[128,2048]{1,0:T(8,128)(2,1)}, bf16[128,2048]{1,0:T(8,128)(2,1)S(1)}, u32[]{:S(2)}, u32[]{:S(2)}) collective-permute-start(bf16[128,2048]{1,0:T(8,128)(2,1)} %get-tuple-element.30.refs_1_.back_ref), channel_id=1, source_target_pairs={{4,0},{8,4},{12,8},{16,12},{20,16},{24,20},{28,24},{5,1},{9,5},{13... | collective-permute-start | bytes 1572872 | tf_op jit(solution)/shard_map/ppermute | solution.py:20
  84.8 11.7 %shard_map.169 = f32[128,256]{1,0:T(8,128)} custom-call(bf16[128,2048]{1,0:T(8,128)(2,1)} %get-tuple-element.30.refs_1_.back_ref, bf16[128,2048]{1,0:T(8,128)(2,1)} %copy-done.6, bf16[128,2048]{1,0:T(8,128)(2,1)} %copy-done.2), custom_call_target="tpu_custom_call" | custom-call | tf_op jit(solution)/shard_map/pallas_call | solution.py:297
  97.5 1.5 %collective-permute-done.1.refs_2_ = bf16[128,2048]{1,0:T(8,128)(2,1)S(1)} collective-permute-done((bf16[128,2048]{1,0:T(8,128)(2,1)}, bf16[128,2048]{1,0:T(8,128)(2,1)S(1)}, u32[]{:S(2)}, u32[]{:S(2)}) %collective-permute-start.1) | collective-permute-done | bytes 524320 | tf_op jit(solution)/shard_map/ppermute | solution.py:20
  100.2 5.7 %all-to-all-start.1 = ((f32[8,1,18432]{2,1,0:T(1,128)}), f32[8,1,18432]{2,1,0:T(1,128)S(1)}, u32[]{:S(2)}, u32[]{:S(2)}) async-start(f32[8,1,18432]{2,1,0:T(1,128)} %broadcast_in_dim.85), calls=%async_computation.1 | async-start | bytes 1179648 | tf_op jit(solution)/shard_map/all_to_all | solution.py:314
  106.6 5.1 %shard_map.166 = (bf16[128,2048]{1,0:T(8,128)(2,1)}, bf16[128,2048]{1,0:T(8,128)(2,1)}) custom-call(f32[16,128]{1,0:T(8,128)} %reshape.86.refs_0_, f32[16,128]{1,0:T(8,128)} %reshape.87.refs_1_, f32[16,2048]{1,0:T(8,128)} %get-tuple-element.27.refs_2_, f32[128,2048]{1,0:T(8,128)} %shard_map.165.refs_3_, bf16[128,2048]{1,0:T(8,128)(2,1)} %refs_4_.2, ...), custom_call_target="tpu_custom_call" | custom-call | tf_op jit(solution)/shard_map/pallas_call | solution.py:251
  111.6 8.1 %shard_map.168 = (bf16[128,2048]{1,0:T(8,128)(2,1)}, bf16[128,2048]{1,0:T(8,128)(2,1)}) custom-call(f32[128,256]{1,0:T(8,128)} %concatenate.14.refs_0_, bf16[128,2048]{1,0:T(8,128)(2,1)} %get-tuple-element.30.refs_1_.back_ref, bf16[128,2048]{1,0:T(8,128)(2,1)} %copy-done.10, bf16[128,2048]{1,0:T(8,128)(2,1)} %refs_3_.1, bf16[128,2048]{1,0:T(8,128)(2,1)} %refs_4_.3), custom_call_target="tpu_custom_call" | custom-call | tf_op jit(solution)/shard_map/pallas_call | solution.py:140
  119.8 1.2 all-to-all-done.1
  (71 shorter events, 15.3 us)
Async XLA Ops:
  0.6 6.4 %copy-start.13 = (f32[128,128]{1,0:T(8,128)S(1)}, f32[128,128]{1,0:T(8,128)}, u32[]{:S(2)}) copy-start(f32[128,128]{1,0:T(8,128)} %param.16) | copy-start | bytes 196612
  0.6 7.2 %copy-start.4 = (bf16[128,2048]{1,0:T(8,128)(2,1)S(1)}, bf16[128,2048]{1,0:T(8,128)(2,1)}, u32[]{:S(2)}) copy-start(bf16[128,2048]{1,0:T(8,128)(2,1)} %refs_4_.2) | copy-start | bytes 1572868
  0.7 7.2 %copy-start.5 = (bf16[128,2048]{1,0:T(8,128)(2,1)S(1)}, bf16[128,2048]{1,0:T(8,128)(2,1)}, u32[]{:S(2)}) copy-start(bf16[128,2048]{1,0:T(8,128)(2,1)} %refs_5_.1) | copy-start | bytes 1572868
  2.1 6.7 %copy-start.2 = (bf16[128,2048]{1,0:T(8,128)(2,1)}, bf16[128,2048]{1,0:T(8,128)(2,1)S(1)}, u32[]{:S(2)}) copy-start(bf16[128,2048]{1,0:T(8,128)(2,1)S(1)} %multiply_convert_fusion.2.refs_2_.bot_ref) | copy-start | bytes 1572868
  2.1 16.0 %collective-permute-start = (bf16[128,2048]{1,0:T(8,128)(2,1)S(1)}, bf16[128,2048]{1,0:T(8,128)(2,1)S(1)}, u32[]{:S(2)}, u32[]{:S(2)}) collective-permute-start(bf16[128,2048]{1,0:T(8,128)(2,1)S(1)} %multiply_convert_fusion.2.refs_2_.bot_ref), channel_id=1, source_target_pairs={{0,4},{4,8},{8,12},{12,16},{16,20},{20,24},{24,28},{1,5},{5,9},{9,... | collective-permute-start | bytes 1572872 | tf_op jit(solution)/shard_map/ppermute | solution.py:20
  7.1 0.7 copy-start.14
  7.1 0.7 copy-start.15
  15.1 11.7 %copy-start.7 = (bf16[128,2048]{1,0:T(8,128)(2,1)S(1)}, bf16[128,2048]{1,0:T(8,128)(2,1)}, u32[]{:S(2)}) copy-start(bf16[128,2048]{1,0:T(8,128)(2,1)} %param.10) | copy-start | bytes 1572868
  18.1 0.8 copy-start.6
  26.7 7.3 %copy-start.3 = (bf16[128,2048]{1,0:T(8,128)(2,1)S(1)}, bf16[128,2048]{1,0:T(8,128)(2,1)}, u32[]{:S(2)}) copy-start(bf16[128,2048]{1,0:T(8,128)(2,1)} %param.14) | copy-start | bytes 1572868
  28.2 5.7 %copy-start.12 = (f32[2048]{0:T(1024)S(1)}, f32[2048]{0:T(1024)}, u32[]{:S(2)}) copy-start(f32[2048]{0:T(1024)} %param.17) | copy-start | bytes 24580
  35.0 4.2 %copy-start.11 = (bf16[16,2048]{1,0:T(8,128)(2,1)S(1)}, bf16[16,2048]{1,0:T(8,128)(2,1)}, u32[]{:S(2)}) copy-start(bf16[16,2048]{1,0:T(8,128)(2,1)} %shard_map.163) | copy-start | bytes 196612
  41.0 25.2 %all-to-all-start = ((bf16[8,16,2048]{2,1,0:T(8,128)(2,1)}), bf16[8,16,2048]{2,1,0:T(8,128)(2,1)S(1)}, u32[]{:S(2)}, u32[]{:S(2)}) async-start(bf16[8,16,2048]{2,1,0:T(8,128)(2,1)} %broadcast_select_fusion), calls=%async_computation | async-start | bytes 1048576 | tf_op jit(solution)/shard_map/all_to_all | solution.py:387
  49.0 0.6 copy-start.8
  57.5 1.4 %copy-start.9 = (f32[128,1,128]{2,1,0:T(1,128)S(1)}, f32[128,1,128]{2,1,0:T(1,128)}, u32[]{:S(2)}) copy-start(f32[128,1,128]{2,1,0:T(1,128)} %copy-done.8) | copy-start | bytes 196612
  72.1 8.9 %copy-start = (f32[128,2048]{1,0:T(8,128)S(1)}, f32[128,2048]{1,0:T(8,128)}, u32[]{:S(2)}) copy-start(f32[128,2048]{1,0:T(8,128)} %shard_map.167) | copy-start | bytes 3145732
  72.1 8.9 %copy-start.1 = (f32[128,2048]{1,0:T(8,128)S(1)}, f32[128,2048]{1,0:T(8,128)}, u32[]{:S(2)}) copy-start(f32[128,2048]{1,0:T(8,128)} %shard_map.161) | copy-start | bytes 3145732
  83.6 15.5 %collective-permute-start.1 = (bf16[128,2048]{1,0:T(8,128)(2,1)}, bf16[128,2048]{1,0:T(8,128)(2,1)S(1)}, u32[]{:S(2)}, u32[]{:S(2)}) collective-permute-start(bf16[128,2048]{1,0:T(8,128)(2,1)} %get-tuple-element.30.refs_1_.back_ref), channel_id=1, source_target_pairs={{4,0},{8,4},{12,8},{16,12},{20,16},{24,20},{28,24},{5,1},{9,5},{13... | collective-permute-start | bytes 1572872 | tf_op jit(solution)/shard_map/ppermute | solution.py:20
  96.5 0.8 slice-start
  99.0 1.2 copy-start.10
  100.2 20.8 %all-to-all-start.1 = ((f32[8,1,18432]{2,1,0:T(1,128)}), f32[8,1,18432]{2,1,0:T(1,128)S(1)}, u32[]{:S(2)}, u32[]{:S(2)}) async-start(f32[8,1,18432]{2,1,0:T(1,128)} %broadcast_in_dim.85), calls=%async_computation.1 | async-start | bytes 1179648 | tf_op jit(solution)/shard_map/all_to_all | solution.py:314

commit v17 on v14

--- a/solution.py
+++ b/solution.py
@@ -314,20 +314,19 @@
     return lax.all_to_all(tiled, "seq", split_axis=0, concat_axis=0, tiled=True)
 
 
-def entering_states(gathered, decays, block_len, group_size, forward):
+def entering_both(gathered, decays, block_len, group_size):
     count = gathered.shape[0]
     here = lax.axis_index("seq")
     rates = jnp.repeat(decays.T, group_size, axis=1)
     source = jnp.arange(count)
-    if forward:
-        gap = here - 1 - source
-    else:
-        gap = source - here - 1
-    valid = gap >= 0
-    steps = jnp.maximum(gap, 0).astype(jnp.float32)
+    steps = jnp.maximum(jnp.abs(here - source) - 1, 0).astype(jnp.float32)
     coef = jnp.exp(-rates[None] * (float(block_len) * steps)[:, None, None])
-    coef = jnp.where(valid[:, None, None], coef, 0.0)
-    return jnp.sum(coef * gathered, axis=0)
+    weighted_states = coef * gathered
+    earlier = (source < here)[:, None, None]
+    later = (source > here)[:, None, None]
+    forward = jnp.sum(jnp.where(earlier, weighted_states, 0.0), axis=0)
+    backward = jnp.sum(jnp.where(later, weighted_states, 0.0), axis=0)
+    return forward, backward
 
 
 def on_device(
@@ -389,8 +388,7 @@
     grad_loc = band_conv(taps_li, back_li_bf, group_size=group_size, split=False, tri="upper")
     conv_loc = band_conv(li_fwd_rows, mixed_li_bf, group_size=group_size, split=False, tri="lower")
     both_st, grad_loc, conv_loc = lax.optimization_barrier((both_st, grad_loc, conv_loc))
-    grad_ent = entering_states(both_st, li_decay, row_count, group_size, False)
-    conv_ent = entering_states(both_st, li_decay, row_count, group_size, True)
+    conv_ent, grad_ent = entering_both(both_st, li_decay, row_count, group_size)
     grad_mixed_li = modal_out(
         li_decay, weights_res, grad_ent, grad_loc, group_size=group_size, forward=False
     )

time: 122 us -> 122 us (level)
  transfers between devices with their start and end apart: 4 -> 4, of which waited for: 3 -> 3; matrix products, arithmetic and copies ran while one was open for 7% -> 7% of each run, Pallas kernels for 33% -> 34%
where the time goes in v17:
time: 122 us; the launch traced here: 121 us
  Pallas kernels  56.1 us (46%)
  starting transfers between devices  18.7 us (15%)
  other arithmetic  16.3 us (13%)
  blocking collectives  12 us (10%)
  local copies, waits for them, and re-layouts  8.9 us (7%)
  waiting for transfers between devices  6.91 us (6%)
    pallas_call x4, Pallas kernels, band_conv(): pl.pallas_call(kernel, grid=(chans // block,), in_specs=in_specs, out_spe...  27.8 us
    pallas_call x1, Pallas kernels, gram_diag(): pl.pallas_call(kernel, grid=(chans // block,), in_specs=[pl.BlockSpec((ro...  11.5 us
    pallas_call x2, Pallas kernels, modal_out(): pl.pallas_call(kernel, grid=(chans // block,), in_specs=in_specs, out_spe...  8.8 us
    pallas_call x2, Pallas kernels, modal_states(): pl.pallas_call(kernel, grid=(chans // block,), in_specs=[pl.BlockSpec((gr...  7.99 us
    all_to_all x1, starting transfers between devices, on_device(): lax.all_to_all(outgoing, 'seq', split_axis=0, concat_axis=0, tiled=True)  6.8 us
    psum x1, blocking collectives, on_device(): cross_dots = lax.psum(jnp.sum(weighted * out_full, axis=1), 'chan')[:, None]  6.25 us
    ppermute x2, starting transfers between devices, from_behind(): lax.ppermute(value, axis, [(source, source + steps) for source in range(i...  6.18 us
    psum x1, blocking collectives, on_device(): squares = lax.psum(jnp.sum(out_full * out_full, axis=1), 'chan')  5.71 us
  transfers between devices with their start and end apart: 4, of which 3 were waited for; matrix products, arithmetic and copies ran while one was open for 7% of the time, Pallas kernels for 34%

profile of v17, /device:TPU:0, one launch (start us, length us, event | category | flops | bytes accessed | tf_op | source)
XLA Modules:
  0.0 120.8 jit_solution(5443681568243357541)
XLA Ops:
  0.7 1.4 %multiply_convert_fusion.2.refs_2_.bot_ref = bf16[128,2048]{1,0:T(8,128)(2,1)S(1)} fusion(bf16[128,2048]{1,0:T(8,128)(2,1)} %refs_3_.1, bf16[128,2048]{1,0:T(8,128)(2,1)} %refs_4_.3), kind=kLoop, calls=%fused_computation.29 | loop fusion | flops 1048576 | bytes 1572864 | tf_op jit(solution)/shard_map/convert_element_type | solution.py:357
  2.1 4.9 %collective-permute-start = (bf16[128,2048]{1,0:T(8,128)(2,1)S(1)}, bf16[128,2048]{1,0:T(8,128)(2,1)S(1)}, u32[]{:S(2)}, u32[]{:S(2)}) collective-permute-start(bf16[128,2048]{1,0:T(8,128)(2,1)S(1)} %multiply_convert_fusion.2.refs_2_.bot_ref), channel_id=1, source_target_pairs={{0,4},{4,8},{8,12},{12,16},{16,20},{20,24},{24,28},{1,5},{5,9},{9,... | collective-permute-start | bytes 1572872 | tf_op jit(solution)/shard_map/ppermute | solution.py:20
  8.8 1.3 %exponential_convert_fusion = (bf16[128,16,128]{2,1,0:T(8,128)(2,1)}, bf16[128,16,128]{2,1,0:T(8,128)(2,1)}) fusion(f32[128]{0:T(128)S(1)} %iota_subtract_fusion, f32[128,16]{1,0:T(8,128)S(1)} %copy.29), kind=kLoop, calls=%fused_computation.30 | loop fusion | flops 1048576 | bytes 1057280 | tf_op jit(solution)/shard_map/convert_element_type | solution.py:375
  10.1 4.0 %shard_map.163 = bf16[16,2048]{1,0:T(8,128)(2,1)} custom-call(bf16[128,16,128]{2,1,0:T(8,128)(2,1)} %get-tuple-element.34.e_ref, bf16[128,2048]{1,0:T(8,128)(2,1)} %multiply_convert_fusion.1.x_ref.refs_1_), custom_call_target="tpu_custom_call" | custom-call | tf_op jit(solution)/shard_map/pallas_call | solution.py:176
  14.9 3.3 %collective-permute-done.refs_1_.top_ref = bf16[128,2048]{1,0:T(8,128)(2,1)S(1)} collective-permute-done((bf16[128,2048]{1,0:T(8,128)(2,1)S(1)}, bf16[128,2048]{1,0:T(8,128)(2,1)S(1)}, u32[]{:S(2)}, u32[]{:S(2)}) %collective-permute-start) | collective-permute-done | bytes 524320 | tf_op jit(solution)/shard_map/ppermute | solution.py:20
  18.9 7.4 %shard_map.161 = f32[128,2048]{1,0:T(8,128)} custom-call(f32[128,256]{1,0:T(8,128)} %maximum_maximum_fusion.refs_0_, bf16[128,2048]{1,0:T(8,128)(2,1)} %copy-done.6, bf16[128,2048]{1,0:T(8,128)(2,1)} %copy-done.2), custom_call_target="tpu_custom_call" | custom-call | tf_op jit(solution)/shard_map/pallas_call | solution.py:140
  26.4 1.5 %fusion.3 = (f32[128]{0:T(128)S(1)}, bf16[128,2048]{1,0:T(8,128)(2,1)S(1)}) fusion(f32[128,2048]{1,0:T(8,128)} %shard_map.161, bf16[128,2048]{1,0:T(8,128)(2,1)S(1)} %copy-done.7), kind=kLoop, calls=%fused_computation.12 | loop fusion | flops 1572736 | bytes 2097664 | tf_op jit(solution)/shard_map/reduce_sum | solution.py:362
  27.9 5.7 %psum.14 = f32[128]{0:T(128)S(1)} all-reduce(f32[128]{0:T(128)S(1)} %get-tuple-element.28), channel_id=1, replica_groups=mesh['seq'=8,'chan'=4] {'chan'}, use_global_device_ids=true, to_apply=%region_1.2 | all-reduce | flops 128 | bytes 1024 | tf_op jit(solution)/shard_map/psum | solution.py:362
  34.7 4.0 %shard_map.162 = bf16[16,2048]{1,0:T(8,128)(2,1)} custom-call(bf16[128,16,128]{2,1,0:T(8,128)(2,1)} %get-tuple-element.33.e_ref, bf16[128,2048]{1,0:T(8,128)(2,1)} %fusion.x_ref.refs_1_), custom_call_target="tpu_custom_call" | custom-call | tf_op jit(solution)/shard_map/pallas_call | solution.py:176
  38.7 1.7 %broadcast_select_fusion = bf16[8,16,2048]{2,1,0:T(8,128)(2,1)} fusion(pred[8]{0:T(512)(128)(4,1)S(1)} %iota_compare_fusion, bf16[16,2048]{1,0:T(8,128)(2,1)S(1)} %copy-done.11, bf16[16,2048]{1,0:T(8,128)(2,1)} %shard_map.162), kind=kLoop, calls=%fused_computation.33 | loop fusion | flops 262144 | bytes 655368 | tf_op jit(solution)/shard_map/jit(_where)/select_n | solution.py:385
  40.4 6.8 %all-to-all-start = ((bf16[8,16,2048]{2,1,0:T(8,128)(2,1)}), bf16[8,16,2048]{2,1,0:T(8,128)(2,1)S(1)}, u32[]{:S(2)}, u32[]{:S(2)}) async-start(bf16[8,16,2048]{2,1,0:T(8,128)(2,1)} %broadcast_select_fusion), calls=%async_computation | async-start | bytes 1048576 | tf_op jit(solution)/shard_map/all_to_all | solution.py:386
  49.1 6.4 %shard_map.164.refs_3_ = f32[128,2048]{1,0:T(8,128)} custom-call(f32[128,128]{1,0:T(8,128)} %bitcast.12, bf16[128,2048]{1,0:T(8,128)(2,1)} %multiply_convert_fusion.1.x_ref.refs_1_), custom_call_target="tpu_custom_call" | custom-call | tf_op jit(solution)/shard_map/pallas_call | solution.py:140
  58.8 6.3 %shard_map.165.refs_3_ = f32[128,2048]{1,0:T(8,128)} custom-call(f32[128,128]{1,0:T(8,128)} %pad_maximum_fusion.1.refs_0_, bf16[128,2048]{1,0:T(8,128)(2,1)} %fusion.x_ref.refs_1_), custom_call_target="tpu_custom_call" | custom-call | tf_op jit(solution)/shard_map/pallas_call | solution.py:140
  66.3 4.2 %shard_map.167 = f32[128,2048]{1,0:T(8,128)} custom-call(f32[16,128]{1,0:T(8,128)} %reshape.78.refs_0_, f32[16,128]{1,0:T(8,128)} %reshape.79.refs_1_, f32[16,2048]{1,0:T(8,128)} %get-tuple-element.26.refs_2_, f32[128,2048]{1,0:T(8,128)} %shard_map.164.refs_3_), custom_call_target="tpu_custom_call" | custom-call | tf_op jit(solution)/shard_map/pallas_call | solution.py:251
  70.5 2.6 %fusion.12 = (f32[2048]{0:T(1024)S(1)}, f32[128]{0:T(128)S(1)}, bf16[128,2048]{1,0:T(8,128)(2,1)}) fusion(bf16[128,2048]{1,0:T(8,128)(2,1)S(1)} %get-tuple-element.29, f32[128]{0:T(128)S(1)} %get-tuple-element.39, f32[128,2048]{1,0:T(8,128)} %shard_map.167, bf16[128,2048]{1,0:T(8,128)(2,1)S(1)} %copy-done.3, f32[2048]{0:T(1024)S(1)} %copy-done.12), kind=kLoop, calls=%fused_computation.21 | loop fusion | flops 3405696 | bytes 2638848 | tf_op jit(solution)/shard_map/reduce_sum | solution.py:402
  73.2 6.3 %psum.15 = f32[128]{0:T(128)S(1)} all-reduce(f32[128]{0:T(128)S(1)} %get-tuple-element.25), channel_id=1, replica_groups=mesh['seq'=8,'chan'=4] {'chan'}, use_global_device_ids=true, to_apply=%region_5.6 | all-reduce | flops 128 | bytes 1024 | tf_op jit(solution)/shard_map/psum | solution.py:404
  79.4 2.6 %fusion.2 = (bf16[128,2048]{1,0:T(8,128)(2,1)}, bf16[128,2048]{1,0:T(8,128)(2,1)}) fusion(bf16[128,2048]{1,0:T(8,128)(2,1)} %param.10, f32[128]{0:T(128)S(1)} %psum.15, f32[128]{0:T(128)S(1)} %get-tuple-element.38, bf16[128,2048]{1,0:T(8,128)(2,1)S(1)} %get-tuple-element.29, f32[2048]{0:T(1024)S(1)} %copy-done.12, f32[128]{0:T(128)S(1)} %get-tuple-element.39, ...), kind=kLoop, calls=%fused_computation.11 | loop fusion | flops 3670016 | bytes 4728320 | tf_op jit(solution)/shard_map/convert_element_type | solution.py:407
  82.0 1.3 %collective-permute-start.1 = (bf16[128,2048]{1,0:T(8,128)(2,1)}, bf16[128,2048]{1,0:T(8,128)(2,1)S(1)}, u32[]{:S(2)}, u32[]{:S(2)}) collective-permute-start(bf16[128,2048]{1,0:T(8,128)(2,1)} %get-tuple-element.30.refs_1_.back_ref), channel_id=1, source_target_pairs={{4,0},{8,4},{12,8},{16,12},{20,16},{24,20},{28,24},{5,1},{9,5},{13... | collective-permute-start | bytes 1572872 | tf_op jit(solution)/shard_map/ppermute | solution.py:20
  83.3 11.5 %shard_map.169 = f32[128,256]{1,0:T(8,128)} custom-call(bf16[128,2048]{1,0:T(8,128)(2,1)} %get-tuple-element.30.refs_1_.back_ref, bf16[128,2048]{1,0:T(8,128)(2,1)} %copy-done.6, bf16[128,2048]{1,0:T(8,128)(2,1)} %copy-done.2), custom_call_target="tpu_custom_call" | custom-call | tf_op jit(solution)/shard_map/pallas_call | solution.py:297
  95.7 1.8 %collective-permute-done.1.refs_2_ = bf16[128,2048]{1,0:T(8,128)(2,1)S(1)} collective-permute-done((bf16[128,2048]{1,0:T(8,128)(2,1)}, bf16[128,2048]{1,0:T(8,128)(2,1)S(1)}, u32[]{:S(2)}, u32[]{:S(2)}) %collective-permute-start.1) | collective-permute-done | bytes 524320 | tf_op jit(solution)/shard_map/ppermute | solution.py:20
  98.7 5.7 %all-to-all-start.1 = ((f32[8,1,18432]{2,1,0:T(1,128)}), f32[8,1,18432]{2,1,0:T(1,128)S(1)}, u32[]{:S(2)}, u32[]{:S(2)}) async-start(f32[8,1,18432]{2,1,0:T(1,128)} %broadcast_in_dim.80), calls=%async_computation.1 | async-start | bytes 1179648 | tf_op jit(solution)/shard_map/all_to_all | solution.py:314
  105.0 4.6 %shard_map.166 = (bf16[128,2048]{1,0:T(8,128)(2,1)}, bf16[128,2048]{1,0:T(8,128)(2,1)}) custom-call(f32[16,128]{1,0:T(8,128)} %reshape.78.refs_0_, f32[16,128]{1,0:T(8,128)} %reshape.79.refs_1_, f32[16,2048]{1,0:T(8,128)} %get-tuple-element.27.refs_2_, f32[128,2048]{1,0:T(8,128)} %shard_map.165.refs_3_, bf16[128,2048]{1,0:T(8,128)(2,1)} %refs_4_.2, ...), custom_call_target="tpu_custom_call" | custom-call | tf_op jit(solution)/shard_map/pallas_call | solution.py:251
  109.6 7.7 %shard_map.168 = (bf16[128,2048]{1,0:T(8,128)(2,1)}, bf16[128,2048]{1,0:T(8,128)(2,1)}) custom-call(f32[128,256]{1,0:T(8,128)} %concatenate.14.refs_0_, bf16[128,2048]{1,0:T(8,128)(2,1)} %get-tuple-element.30.refs_1_.back_ref, bf16[128,2048]{1,0:T(8,128)(2,1)} %copy-done.10, bf16[128,2048]{1,0:T(8,128)(2,1)} %refs_3_.1, bf16[128,2048]{1,0:T(8,128)(2,1)} %refs_4_.3), custom_call_target="tpu_custom_call" | custom-call | tf_op jit(solution)/shard_map/pallas_call | solution.py:140
  117.3 1.9 %all-to-all-done.1 = f32[8,1,18432]{2,1,0:T(1,128)S(1)} async-done(((f32[8,1,18432]{2,1,0:T(1,128)}), f32[8,1,18432]{2,1,0:T(1,128)S(1)}, u32[]{:S(2)}, u32[]{:S(2)}) %all-to-all-start.1) | async-done | bytes 589856 | tf_op jit(solution)/shard_map/all_to_all | solution.py:314
  (71 shorter events, 15.1 us)
Async XLA Ops:
  0.6 6.4 %copy-start.13 = (f32[128,128]{1,0:T(8,128)S(1)}, f32[128,128]{1,0:T(8,128)}, u32[]{:S(2)}) copy-start(f32[128,128]{1,0:T(8,128)} %param.16) | copy-start | bytes 196612
  0.6 7.2 %copy-start.4 = (bf16[128,2048]{1,0:T(8,128)(2,1)S(1)}, bf16[128,2048]{1,0:T(8,128)(2,1)}, u32[]{:S(2)}) copy-start(bf16[128,2048]{1,0:T(8,128)(2,1)} %refs_4_.2) | copy-start | bytes 1572868
  0.7 7.2 %copy-start.5 = (bf16[128,2048]{1,0:T(8,128)(2,1)S(1)}, bf16[128,2048]{1,0:T(8,128)(2,1)}, u32[]{:S(2)}) copy-start(bf16[128,2048]{1,0:T(8,128)(2,1)} %refs_5_.1) | copy-start | bytes 1572868
  2.1 6.7 %copy-start.2 = (bf16[128,2048]{1,0:T(8,128)(2,1)}, bf16[128,2048]{1,0:T(8,128)(2,1)S(1)}, u32[]{:S(2)}) copy-start(bf16[128,2048]{1,0:T(8,128)(2,1)S(1)} %multiply_convert_fusion.2.refs_2_.bot_ref) | copy-start | bytes 1572868
  2.1 16.0 %collective-permute-start = (bf16[128,2048]{1,0:T(8,128)(2,1)S(1)}, bf16[128,2048]{1,0:T(8,128)(2,1)S(1)}, u32[]{:S(2)}, u32[]{:S(2)}) collective-permute-start(bf16[128,2048]{1,0:T(8,128)(2,1)S(1)} %multiply_convert_fusion.2.refs_2_.bot_ref), channel_id=1, source_target_pairs={{0,4},{4,8},{8,12},{12,16},{16,20},{20,24},{24,28},{1,5},{5,9},{9,... | collective-permute-start | bytes 1572872 | tf_op jit(solution)/shard_map/ppermute | solution.py:20
  7.1 0.7 copy-start.14
  7.1 0.7 copy-start.15
  14.9 11.5 %copy-start.7 = (bf16[128,2048]{1,0:T(8,128)(2,1)S(1)}, bf16[128,2048]{1,0:T(8,128)(2,1)}, u32[]{:S(2)}) copy-start(bf16[128,2048]{1,0:T(8,128)(2,1)} %param.10) | copy-start | bytes 1572868
  18.1 0.8 copy-start.6
  26.4 7.3 %copy-start.3 = (bf16[128,2048]{1,0:T(8,128)(2,1)S(1)}, bf16[128,2048]{1,0:T(8,128)(2,1)}, u32[]{:S(2)}) copy-start(bf16[128,2048]{1,0:T(8,128)(2,1)} %param.14) | copy-start | bytes 1572868
  27.9 5.7 %copy-start.12 = (f32[2048]{0:T(1024)S(1)}, f32[2048]{0:T(1024)}, u32[]{:S(2)}) copy-start(f32[2048]{0:T(1024)} %param.17) | copy-start | bytes 24580
  34.7 4.0 %copy-start.11 = (bf16[16,2048]{1,0:T(8,128)(2,1)S(1)}, bf16[16,2048]{1,0:T(8,128)(2,1)}, u32[]{:S(2)}) copy-start(bf16[16,2048]{1,0:T(8,128)(2,1)} %shard_map.163) | copy-start | bytes 196612
  40.4 24.8 %all-to-all-start = ((bf16[8,16,2048]{2,1,0:T(8,128)(2,1)}), bf16[8,16,2048]{2,1,0:T(8,128)(2,1)S(1)}, u32[]{:S(2)}, u32[]{:S(2)}) async-start(bf16[8,16,2048]{2,1,0:T(8,128)(2,1)} %broadcast_select_fusion), calls=%async_computation | async-start | bytes 1048576 | tf_op jit(solution)/shard_map/all_to_all | solution.py:386
  48.5 0.6 copy-start.8
  56.7 1.4 %copy-start.9 = (f32[128,1,128]{2,1,0:T(1,128)S(1)}, f32[128,1,128]{2,1,0:T(1,128)}, u32[]{:S(2)}) copy-start(f32[128,1,128]{2,1,0:T(1,128)} %copy-done.8) | copy-start | bytes 196612
  70.5 8.9 %copy-start = (f32[128,2048]{1,0:T(8,128)S(1)}, f32[128,2048]{1,0:T(8,128)}, u32[]{:S(2)}) copy-start(f32[128,2048]{1,0:T(8,128)} %shard_map.167) | copy-start | bytes 3145732
  70.5 8.9 %copy-start.1 = (f32[128,2048]{1,0:T(8,128)S(1)}, f32[128,2048]{1,0:T(8,128)}, u32[]{:S(2)}) copy-start(f32[128,2048]{1,0:T(8,128)} %shard_map.161) | copy-start | bytes 3145732
  82.0 15.5 %collective-permute-start.1 = (bf16[128,2048]{1,0:T(8,128)(2,1)}, bf16[128,2048]{1,0:T(8,128)(2,1)S(1)}, u32[]{:S(2)}, u32[]{:S(2)}) collective-permute-start(bf16[128,2048]{1,0:T(8,128)(2,1)} %get-tuple-element.30.refs_1_.back_ref), channel_id=1, source_target_pairs={{4,0},{8,4},{12,8},{16,12},{20,16},{24,20},{28,24},{5,1},{9,5},{13... | collective-permute-start | bytes 1572872 | tf_op jit(solution)/shard_map/ppermute | solution.py:20
  94.8 0.8 slice-start
  97.5 1.2 copy-start.10
  98.7 20.5 %all-to-all-start.1 = ((f32[8,1,18432]{2,1,0:T(1,128)}), f32[8,1,18432]{2,1,0:T(1,128)S(1)}, u32[]{:S(2)}, u32[]{:S(2)}) async-start(f32[8,1,18432]{2,1,0:T(1,128)} %broadcast_in_dim.80), calls=%async_computation.1 | async-start | bytes 1179648 | tf_op jit(solution)/shard_map/all_to_all | solution.py:314
